TPU v7x, 256 devices: a whole 4x4x8 slice. The times are simulated.
256 devices in a mesh: cent: 8 (over z), dp: 32 (over x, y, core).
Axes of the slice: x: 4, y: 4, z: 8, core: 2. Of those that a mesh axis runs over, the one named last changes fastest.
Arguments:
- points: bfloat16 [32768, 1024], P('dp'), may hold values from -6 to 6
- cluster_ids: int32 [32768, 1], P('dp'), may hold values from 0 to 63; in each aligned block of 1024 rows (0 to 1023, 1024 to 2047, ...) at most 64 rows name the same one
- centroids: bfloat16 [8192, 1024], P('cent'), may hold values from -6 to 6
- sub_centroids: bfloat16 [64, 1024, 1024], P('dp', 'cent'), may hold values from -6 to 6
Outputs:
- assign: bfloat16 [32768, 8192], P('dp', 'cent')
- sub_assign: bfloat16 [32768, 1024], P('dp', 'cent')
Inputs may be any that keep to these rules, and one draw needn't show every extreme that they name: `cluster_ids`: among the 1024 points of one index of dp, no level-two cluster holds more than 64 points; some cluster holds exactly 64 in some block.
All inputs are finite; a program needn't handle non-finite values.
Results may differ from a plain program's by a relative error of at most 0.001.
Values may be sent and summed in bfloat16 or wider, within the bound.
No kernel may reach another device: no remote copies, remote signals or barrier semaphores. Data moves between devices by JAX's collectives and lax.ppermute only.
A program may use at most 128 MiB of HBM per device.

v0:
```python
import jax
import jax.numpy as jnp
from jax import lax
from jax.sharding import PartitionSpec as P

CAP = 64
ITERS = 3


EPS = 1e-06
TAU = 0.05


def inverse_norm(rows):
    values = rows.astype(jnp.float32)
    return lax.rsqrt(jnp.mean(values * values, axis=-1) + EPS)


def shards(points, cluster_ids, centroids, sub_centroids):
    pts_count = points.shape[0]
    width = points.shape[1]
    dp_count = lax.axis_size("dp")
    cent_count = lax.axis_size("cent")
    group_dev = sub_centroids.shape[0]
    sub_dev = sub_centroids.shape[1]
    clusters = group_dev * dp_count
    total_cent = centroids.shape[0] * cent_count
    total_sub = sub_dev * cent_count
    inv_x = inverse_norm(points)
    inv_c = inverse_norm(centroids)
    inv_u = inverse_norm(sub_centroids)
    scores = jnp.einsum("pd,kd->pk", points, centroids, preferred_element_type=jnp.float32)
    expo = jnp.exp(scores * inv_x[:, None] * inv_c[None, :] * (1.0 / (width * TAU)))
    row_scale = jnp.ones((pts_count,), jnp.float32)
    col_scale = jnp.ones((centroids.shape[0],), jnp.float32)
    row_part = row_scale
    for step in range(ITERS):
        col_part = jnp.dot(row_scale, expo, precision=lax.Precision.HIGHEST)
        col_scale = 1.0 / lax.psum(col_part, "dp")
        row_part = jnp.dot(expo, col_scale, precision=lax.Precision.HIGHEST)
        if step + 1 < ITERS:
            row_scale = 1.0 / lax.psum(row_part, "cent")
    ids = cluster_ids[:, 0]
    labels = lax.broadcasted_iota(jnp.int32, (pts_count, clusters), 1)
    onehot = ids[:, None] == labels
    positions = lax.broadcasted_iota(jnp.int32, (pts_count, pts_count), 0)
    earlier = (positions > positions.T).astype(jnp.bfloat16)
    before = jnp.dot(earlier, onehot.astype(jnp.bfloat16), preferred_element_type=jnp.float32)
    rank = jnp.sum(before * onehot.astype(jnp.float32), axis=1).astype(jnp.int32)
    slot = ids * CAP + rank
    buffer = jnp.zeros((clusters * CAP, width), jnp.bfloat16).at[slot].set(points)
    scale_two = 1.0 / (width * TAU)
    outgoing = buffer.reshape(dp_count, group_dev * CAP, width)
    arrived = lax.all_to_all(outgoing, "dp", split_axis=0, concat_axis=0, tiled=True)
    arrived = arrived.reshape(dp_count, group_dev, CAP, width)
    inv_rows = inverse_norm(arrived)
    dots = jnp.einsum("sgcd,gkd->sgck", arrived, sub_centroids, preferred_element_type=jnp.float32)
    weights = jnp.exp(dots * inv_rows[..., None] * inv_u[None, :, None, :] * scale_two)
    weights = weights.reshape(dp_count, group_dev * CAP, sub_dev)
    returned = lax.all_to_all(weights, "dp", split_axis=0, concat_axis=0, tiled=True)
    slot_weights = returned.reshape(clusters * CAP, sub_dev)
    point_weights = slot_weights[slot]
    denom_part = jnp.sum(point_weights, axis=1)
    row_total = lax.psum(row_part, "cent")
    denominator = lax.psum(denom_part, "cent")
    row_scale = 1.0 / row_total
    assign = (expo * row_scale[:, None] * col_scale[None, :] * total_cent).astype(jnp.bfloat16)
    sub_assign = (total_sub * point_weights / denominator[:, None]).astype(jnp.bfloat16)
    return (assign, sub_assign)


def solution(mesh):
    return jax.shard_map(
        shards,
        mesh=mesh,
        in_specs=(P("dp", None), P("dp", None), P("cent", None), P("dp", "cent", None)),
        out_specs=(P("dp", "cent"), P("dp", "cent")),
        check_vma=False,
    )
```

profile of v0, /device:TPU:32, one launch (start us, length us, event | category | flops | bytes accessed | tf_op | source)
XLA Modules:
  0.0 412.6 jit_solution(17542967821555174308)
XLA Ops:
  0.6 1.4 fusion.11
  2.0 0.7 compare_select_fusion
  2.7 10.8 %scatter_custom_fusion = bf16[4096,1024]{1,0:T(8,128)(2,1)} fusion(s32[1024]{0:T(1024)S(1)} %bitcast.56, bf16[1024,1024]{1,0:T(8,128)(2,1)} %param.4, bf16[]{:T(256)} %constant.6.clone.1), kind=kCustom, calls=%fused_computation.6 | custom fusion | bytes 8389120 | tf_op jit(solution)/shard_map/scatter | solution.py:51
  13.5 7.8 %all-to-all-start = ((bf16[32,128,1024]{2,1,0:T(8,128)(2,1)}), bf16[32,128,1024]{2,1,0:T(8,128)(2,1)}, u32[]{:S(2)}, u32[]{:S(2)}) async-start(bf16[32,128,1024]{2,1,0:T(8,128)(2,1)} %bitcast.51), calls=%async_computation | async-start | bytes 16777216 | tf_op jit(solution)/shard_map/all_to_all | solution.py:54
  21.3 0.0 copy-start.2
  21.3 2.2 multiply_reduce_fusion.1
  23.5 0.5 multiply_reduce_fusion.2
  24.0 2.6 multiply_exponential_fusion
  26.7 1.9 copy-done
  28.6 2.1 fusion.14
  30.6 141.6 %psum.49 = f32[1024]{0:T(1024)S(1)} all-reduce(f32[1024]{0:T(1024)S(1)} %bitcast.55), channel_id=1, replica_groups=mesh['cent'=8,'dp'=32] {'dp'}, use_global_device_ids=true, to_apply=%region_2.0 | all-reduce | flops 1024 | bytes 8192 | tf_op jit(solution)/shard_map/psum | solution.py:39
  172.2 5.8 %fusion.17 = f32[1,1024]{1,0:T(1,128)S(1)} fusion(f32[1024,1024]{1,0:T(8,128)} %copy-done, f32[1024,1]{0,1:T(1,128)S(1)} %bitcast.61), kind=kOutput, calls=%fused_computation.39 | convolution fusion | flops 12582912 | bytes 4202496 | tf_op jit(solution)/shard_map/dot_general | solution.py:40
  178.0 17.9 %psum.50 = f32[1024]{0:T(1024)S(1)} all-reduce(f32[1024]{0:T(1024)S(1)} %bitcast.62), channel_id=1, replica_groups=mesh['cent'=8,'dp'=32] {'cent'}, use_global_device_ids=true, to_apply=%region_3.0 | all-reduce | flops 1024 | bytes 8192 | tf_op jit(solution)/shard_map/psum | solution.py:42
  195.9 0.2 multiply_reduce_fusion.3
  196.1 0.0 all-to-all-done
  196.1 5.1 %multiply_reduce_fusion = f32[32,128]{1,0:T(8,128)S(1)} fusion(bf16[32,128,1024]{2,1,0:T(8,128)(2,1)} %all-to-all-done), kind=kLoop, calls=%fused_computation.2 | loop fusion | flops 12578816 | bytes 8404992 | tf_op jit(solution)/shard_map/reduce_sum | solution.py:16
  201.2 0.1 rsqrt.34
  201.3 4.8 %fusion.7 = f32[32,2,64,128]{3,2,0,1:T(8,128)S(1)} fusion(bf16[32,2,64,1024]{3,2,1,0:T(8,128)(2,1)} %bitcast.16, f32[2,128]{1,0:T(2,128)S(1)} %add_rsqrt_fusion.3, f32[32,2,64]{2,0,1:T(8,128)S(1)} %copy.7, bf16[2,128,1024]{2,1,0:T(8,128)(2,1)S(1)} %copy-done.3), kind=kOutput, calls=%fused_computation.16 | convolution fusion | flops 1075314688 | bytes 11027456 | tf_op jit(solution)/shard_map/sgcd,gkd->sgck/dot_general | solution.py:57
  206.1 1.5 copy.8
  207.6 5.4 %all-to-all-start.1 = ((f32[32,128,128]{2,1,0:T(8,128)}), f32[32,128,128]{2,1,0:T(8,128)S(1)}, u32[]{:S(2)}, u32[]{:S(2)}) async-start(f32[32,128,128]{2,1,0:T(8,128)} %bitcast.53), calls=%async_computation.1 | async-start | bytes 4194304 | tf_op jit(solution)/shard_map/all_to_all | solution.py:60
  213.0 4.3 %fusion.18 = f32[1,1024]{1,0:T(1,128)S(1)} fusion(f32[1024,1]{0,1:T(1,128)S(1)} %bitcast.59, f32[1024,1024]{1,0:T(8,128)} %copy-done), kind=kOutput, calls=%fused_computation.40 | convolution fusion | flops 12582912 | bytes 4202496 | tf_op jit(solution)/shard_map/dot_general | solution.py:38
  217.2 78.1 %psum.51 = f32[1024]{0:T(1024)S(1)} all-reduce(f32[1024]{0:T(1024)S(1)} %bitcast.63), channel_id=1, replica_groups=mesh['cent'=8,'dp'=32] {'dp'}, use_global_device_ids=true, to_apply=%region_4.0 | all-reduce | flops 1024 | bytes 8192 | tf_op jit(solution)/shard_map/psum | solution.py:39
  295.3 5.8 %fusion.19 = f32[1,1024]{1,0:T(1,128)S(1)} fusion(f32[1024,1024]{1,0:T(8,128)} %copy-done, f32[1024,1]{0,1:T(1,128)S(1)} %bitcast.64), kind=kOutput, calls=%fused_computation.41 | convolution fusion | flops 12582912 | bytes 4202496 | tf_op jit(solution)/shard_map/dot_general | solution.py:40
  301.1 16.4 %psum.52 = f32[1024]{0:T(1024)S(1)} all-reduce(f32[1024]{0:T(1024)S(1)} %bitcast.65), channel_id=1, replica_groups=mesh['cent'=8,'dp'=32] {'cent'}, use_global_device_ids=true, to_apply=%region_5.0 | all-reduce | flops 1024 | bytes 8192 | tf_op jit(solution)/shard_map/psum | solution.py:42
  317.5 4.3 %fusion.20 = f32[1,1024]{1,0:T(1,128)S(1)} fusion(f32[1024,1]{0,1:T(1,128)S(1)} %bitcast.66, f32[1024,1024]{1,0:T(8,128)} %copy-done), kind=kOutput, calls=%fused_computation.42 | convolution fusion | flops 12582912 | bytes 4202496 | tf_op jit(solution)/shard_map/dot_general | solution.py:38
  321.7 62.7 %psum.53 = f32[1024]{0:T(1024)S(1)} all-reduce(f32[1024]{0:T(1024)S(1)} %bitcast.67), channel_id=1, replica_groups=mesh['cent'=8,'dp'=32] {'dp'}, use_global_device_ids=true, to_apply=%region_6.0 | all-reduce | flops 1024 | bytes 8192 | tf_op jit(solution)/shard_map/psum | solution.py:39
  384.4 5.8 %fusion.21 = f32[1,1024]{1,0:T(1,128)S(1)} fusion(f32[1024,1024]{1,0:T(8,128)} %copy-done, f32[1024,1]{0,1:T(1,128)S(1)} %bitcast.54), kind=kOutput, calls=%fused_computation.43 | convolution fusion | flops 12582912 | bytes 4202496 | tf_op jit(solution)/shard_map/dot_general | solution.py:40
  390.2 2.8 gather_fusion
  393.0 0.2 reduce_sum.59
  393.2 14.4 %all-reduce = (f32[1024]{0:T(1024)S(1)}, f32[1024]{0:T(1024)S(1)}) all-reduce(f32[1024]{0:T(1024)S(1)} %bitcast.60, f32[1024]{0:T(1024)S(1)} %reduce_sum.59), channel_id=1, replica_groups=mesh['cent'=8,'dp'=32] {'cent'}, use_global_device_ids=true, to_apply=%region_7.0 | all-reduce | flops 2048 | bytes 16384 | tf_op jit(solution)/shard_map/psum | solution.py:64
  407.7 4.0 multiply_convert_fusion
  411.7 0.9 divide_convert_fusion
  (20 shorter events, 0.1 us)
Async XLA Ops:
  13.5 10.0 %copy-start.1 = (bf16[1024,1024]{1,0:T(8,128)(2,1)S(1)}, bf16[1024,1024]{1,0:T(8,128)(2,1)}, u32[]{:S(2)}) copy-start(bf16[1024,1024]{1,0:T(8,128)(2,1)} %param.4) | copy-start | bytes 6291460
  13.5 182.6 %all-to-all-start = ((bf16[32,128,1024]{2,1,0:T(8,128)(2,1)}), bf16[32,128,1024]{2,1,0:T(8,128)(2,1)}, u32[]{:S(2)}, u32[]{:S(2)}) async-start(bf16[32,128,1024]{2,1,0:T(8,128)(2,1)} %bitcast.51), calls=%async_computation | async-start | bytes 16777216 | tf_op jit(solution)/shard_map/all_to_all | solution.py:54
  21.3 2.7 copy-start.2
  26.6 1.9 copy-start
  28.6 167.3 %copy-start.3 = (bf16[2,128,1024]{2,1,0:T(8,128)(2,1)S(1)}, bf16[2,128,1024]{2,1,0:T(8,128)(2,1)}, u32[]{:S(2)}) copy-start(bf16[2,128,1024]{2,1,0:T(8,128)(2,1)} %param.7) | copy-start | bytes 1572868
  207.6 182.6 %all-to-all-start.1 = ((f32[32,128,128]{2,1,0:T(8,128)}), f32[32,128,128]{2,1,0:T(8,128)S(1)}, u32[]{:S(2)}, u32[]{:S(2)}) async-start(f32[32,128,128]{2,1,0:T(8,128)} %bitcast.53), calls=%async_computation.1 | async-start | bytes 4194304 | tf_op jit(solution)/shard_map/all_to_all | solution.py:60
where the time goes:
time: 414 us; the launch traced here: 413 us
  blocking collectives  331 us (80%)
  matrix products  36.6 us (9%)
  local copies, waits for them, and re-layouts  17.1 us (4%)
  other arithmetic  13.9 us (3%)
  starting transfers between devices  13.2 us (3%)
    psum x3, blocking collectives, shards(): col_scale = 1.0 / lax.psum(col_part, 'dp')  282 us
    psum x2, blocking collectives, shards(): row_scale = 1.0 / lax.psum(row_part, 'cent')  34.3 us
    dot_general x3, matrix products, shards(): row_part = jnp.dot(expo, col_scale, precision=lax.Precision.HIGHEST)  17.3 us
    psum x1, blocking collectives, shards(): row_total = lax.psum(row_part, 'cent')  14.4 us
    scatter x1, local copies, waits for them, and re-layouts, shards(): jnp.zeros((clusters * CAP, width), jnp.bfloat16).at[slot].set(points)  10.8 us
    dot_general x3, matrix products, shards(): col_part = jnp.dot(row_scale, expo, precision=lax.Precision.HIGHEST)  10.6 us
  transfers between devices with their start and end apart: 2, of which 0 were waited for; matrix products, arithmetic and copies ran while one was open for 8% of the time, Pallas kernels for 0%

commit v1 on v0

--- a/solution.py
+++ b/solution.py
@@ -26,20 +26,8 @@
     clusters = group_dev * dp_count
     total_cent = centroids.shape[0] * cent_count
     total_sub = sub_dev * cent_count
-    inv_x = inverse_norm(points)
-    inv_c = inverse_norm(centroids)
-    inv_u = inverse_norm(sub_centroids)
-    scores = jnp.einsum("pd,kd->pk", points, centroids, preferred_element_type=jnp.float32)
-    expo = jnp.exp(scores * inv_x[:, None] * inv_c[None, :] * (1.0 / (width * TAU)))
-    row_scale = jnp.ones((pts_count,), jnp.float32)
-    col_scale = jnp.ones((centroids.shape[0],), jnp.float32)
-    row_part = row_scale
-    for step in range(ITERS):
-        col_part = jnp.dot(row_scale, expo, precision=lax.Precision.HIGHEST)
-        col_scale = 1.0 / lax.psum(col_part, "dp")
-        row_part = jnp.dot(expo, col_scale, precision=lax.Precision.HIGHEST)
-        if step + 1 < ITERS:
-            row_scale = 1.0 / lax.psum(row_part, "cent")
+    scale_two = 1.0 / (width * TAU)
+
     ids = cluster_ids[:, 0]
     labels = lax.broadcasted_iota(jnp.int32, (pts_count, clusters), 1)
     onehot = ids[:, None] == labels
@@ -49,15 +37,31 @@
     rank = jnp.sum(before * onehot.astype(jnp.float32), axis=1).astype(jnp.int32)
     slot = ids * CAP + rank
     buffer = jnp.zeros((clusters * CAP, width), jnp.bfloat16).at[slot].set(points)
-    scale_two = 1.0 / (width * TAU)
     outgoing = buffer.reshape(dp_count, group_dev * CAP, width)
     arrived = lax.all_to_all(outgoing, "dp", split_axis=0, concat_axis=0, tiled=True)
     arrived = arrived.reshape(dp_count, group_dev, CAP, width)
+    inv_u = inverse_norm(sub_centroids)
     inv_rows = inverse_norm(arrived)
     dots = jnp.einsum("sgcd,gkd->sgck", arrived, sub_centroids, preferred_element_type=jnp.float32)
     weights = jnp.exp(dots * inv_rows[..., None] * inv_u[None, :, None, :] * scale_two)
     weights = weights.reshape(dp_count, group_dev * CAP, sub_dev)
     returned = lax.all_to_all(weights, "dp", split_axis=0, concat_axis=0, tiled=True)
+
+    inv_x = inverse_norm(points)
+    inv_c = inverse_norm(centroids)
+    scores = jnp.einsum("pd,kd->pk", points, centroids, preferred_element_type=jnp.float32)
+    expo = jnp.exp(scores * inv_x[:, None] * inv_c[None, :] * (1.0 / (width * TAU)))
+    col_part = jnp.sum(expo, axis=0)
+    col_part, returned = lax.optimization_barrier((col_part, returned))
+    row_part = None
+    for step in range(ITERS):
+        if step > 0:
+            col_part = jnp.sum(expo * row_scale[:, None], axis=0)
+        col_scale = 1.0 / lax.psum(col_part, "dp")
+        row_part = jnp.sum(expo * col_scale[None, :], axis=1)
+        if step + 1 < ITERS:
+            row_scale = 1.0 / lax.psum(row_part, "cent")
+
     slot_weights = returned.reshape(clusters * CAP, sub_dev)
     point_weights = slot_weights[slot]
     denom_part = jnp.sum(point_weights, axis=1)

time: 414 us -> 448 us (1.082)
  waiting for transfers between devices: 0.01 us -> 133 us
  blocking collectives: 331 us -> 237 us
  matrix products: 36.6 us -> 10.7 us
  other arithmetic: 13.9 us -> 28.2 us
  starting transfers between devices: 13.2 us -> 21.8 us
    all_to_all x1, waiting for transfers between devices: 0.01 us -> 113 us  [shards(): lax.all_to_all(outgoing, 'dp', split_axis=0, concat_axis=0, tiled=True)]
    psum x3, blocking collectives: 282 us -> 189 us  [shards(): col_scale = 1.0 / lax.psum(col_part, 'dp')]
    dot_general x6 -> x0, matrix products: 27.9 us -> none  [the longest x3 17.3 us: shards(): row_part = jnp.dot(expo, col_scale, precision=lax.Precision.HIGHEST)]
    all_to_all x1, waiting for transfers between devices: 0.01 us -> 19.8 us  [shards(): lax.all_to_all(weights, 'dp', split_axis=0, concat_axis=0, tiled=True)]
    reduce_sum x0 -> x5, other arithmetic: none -> 12.7 us  [the longest x3 7.62 us: shards(): row_part = jnp.sum(expo * col_scale[None, :], axis=1)]
    all_to_all x1, starting transfers between devices: 5.39 us -> 14.2 us  [shards(): lax.all_to_all(weights, 'dp', split_axis=0, concat_axis=0, tiled=True)]
  transfers between devices with their start and end apart: 2 -> 2, of which waited for: 0 -> 2; matrix products, arithmetic and copies ran while one was open for 8% -> 2% of each run, Pallas kernels for 0% -> 0%
where the time goes in v1:
time: 448 us; the launch traced here: 447 us
  blocking collectives  237 us (53%)
  waiting for transfers between devices  133 us (30%)
  other arithmetic  28.2 us (6%)
  starting transfers between devices  21.8 us (5%)
  local copies, waits for them, and re-layouts  15.2 us (3%)
  matrix products  10.7 us (2%)
    psum x3, blocking collectives, shards(): col_scale = 1.0 / lax.psum(col_part, 'dp')  189 us
    all_to_all x1, waiting for transfers between devices, shards(): lax.all_to_all(outgoing, 'dp', split_axis=0, concat_axis=0, tiled=True)  113 us
    psum x2, blocking collectives, shards(): row_scale = 1.0 / lax.psum(row_part, 'cent')  34.3 us
    all_to_all x1, waiting for transfers between devices, shards(): lax.all_to_all(weights, 'dp', split_axis=0, concat_axis=0, tiled=True)  19.8 us
    psum x1, blocking collectives, shards(): row_total = lax.psum(row_part, 'cent')  14.4 us
    all_to_all x1, starting transfers between devices, shards(): lax.all_to_all(weights, 'dp', split_axis=0, concat_axis=0, tiled=True)  14.2 us
    scatter x1, local copies, waits for them, and re-layouts, shards(): jnp.zeros((clusters * CAP, width), jnp.bfloat16).at[slot].set(points)  10.8 us
    reduce_sum x4, other arithmetic, inverse_norm(): return lax.rsqrt(jnp.mean(values * values, axis=-1) + EPS)  9.56 us
  transfers between devices with their start and end apart: 2, of which 2 were waited for; matrix products, arithmetic and copies ran while one was open for 2% of the time, Pallas kernels for 0%

profile of v1, /device:TPU:32, one launch (start us, length us, event | category | flops | bytes accessed | tf_op | source)
XLA Modules:
  0.0 447.2 jit_solution(16847889719878286994)
XLA Ops:
  0.6 1.4 fusion.11
  2.0 0.7 compare_select_fusion
  2.7 10.8 %scatter_custom_fusion = bf16[4096,1024]{1,0:T(8,128)(2,1)} fusion(s32[1024]{0:T(1024)S(1)} %bitcast.32, bf16[1024,1024]{1,0:T(8,128)(2,1)} %param.4, bf16[]{:T(256)} %constant.5.clone.1), kind=kCustom, calls=%fused_computation.12 | custom fusion | bytes 8389120 | tf_op jit(solution)/shard_map/scatter | solution.py:39
  13.5 7.6 %all-to-all-start = ((bf16[32,128,1024]{2,1,0:T(8,128)(2,1)}), bf16[32,128,1024]{2,1,0:T(8,128)(2,1)}, u32[]{:S(2)}, u32[]{:S(2)}) async-start(bf16[32,128,1024]{2,1,0:T(8,128)(2,1)} %bitcast.29), calls=%async_computation | async-start | bytes 16777216 | tf_op jit(solution)/shard_map/all_to_all | solution.py:41
  21.1 0.2 multiply_reduce_fusion.8
  21.3 113.3 %all-to-all-done = bf16[32,128,1024]{2,1,0:T(8,128)(2,1)} async-done(((bf16[32,128,1024]{2,1,0:T(8,128)(2,1)}), bf16[32,128,1024]{2,1,0:T(8,128)(2,1)}, u32[]{:S(2)}, u32[]{:S(2)}) %all-to-all-start) | async-done | bytes 8388640 | tf_op jit(solution)/shard_map/all_to_all | solution.py:41
  134.6 5.1 %multiply_reduce_fusion = f32[32,128]{1,0:T(8,128)S(1)} fusion(bf16[32,128,1024]{2,1,0:T(8,128)(2,1)} %all-to-all-done), kind=kLoop, calls=%fused_computation.2 | loop fusion | flops 12578816 | bytes 8404992 | tf_op jit(solution)/shard_map/reduce_sum | solution.py:16
  139.7 0.1 rsqrt.34
  139.8 4.8 %fusion.7 = f32[32,2,64,128]{3,2,0,1:T(8,128)S(1)} fusion(bf16[32,2,64,1024]{3,2,1,0:T(8,128)(2,1)} %bitcast.5, f32[2,128]{1,0:T(2,128)S(1)} %add_rsqrt_fusion.3, f32[32,2,64]{2,0,1:T(8,128)S(1)} %copy.7, bf16[2,128,1024]{2,1,0:T(8,128)(2,1)S(1)} %copy-done.2), kind=kOutput, calls=%fused_computation.21 | convolution fusion | flops 1075314688 | bytes 11027456 | tf_op jit(solution)/shard_map/sgcd,gkd->sgck/dot_general | solution.py:45
  144.6 1.5 copy.8
  146.0 14.2 %all-to-all-start.1 = ((f32[32,128,128]{2,1,0:T(8,128)}), f32[32,128,128]{2,1,0:T(8,128)S(1)}, u32[]{:S(2)}, u32[]{:S(2)}) async-start(f32[32,128,128]{2,1,0:T(8,128)} %bitcast.31), calls=%async_computation.1 | async-start | bytes 4194304 | tf_op jit(solution)/shard_map/all_to_all | solution.py:48
  160.3 0.0 copy-start
  160.3 0.0 copy-start.1
  160.3 2.2 multiply_reduce_fusion.6
  162.5 2.1 multiply_reduce_fusion.7
  164.7 4.6 %fusion.14 = (f32[1024]{0:T(1024)S(1)}, f32[1024,1024]{1,0:T(8,128)}) fusion(f32[1024]{0:T(1024)S(1)} %add_rsqrt_fusion.1, f32[1024]{0:T(1024)S(1)} %add_rsqrt_fusion.2, bf16[1024,1024]{1,0:T(8,128)(2,1)S(1)} %copy-done.1, bf16[1024,1024]{1,0:T(8,128)(2,1)S(1)} %copy-done), kind=kOutput, calls=%fused_computation.41 | convolution fusion | flops 2151676928 | bytes 8400896 | tf_op jit(solution)/shard_map/pd,kd->pk/dot_general | solution.py:52
  169.3 19.8 %all-to-all-done.1 = f32[32,128,128]{2,1,0:T(8,128)S(1)} async-done(((f32[32,128,128]{2,1,0:T(8,128)}), f32[32,128,128]{2,1,0:T(8,128)S(1)}, u32[]{:S(2)}, u32[]{:S(2)}) %all-to-all-start.1) | async-done | bytes 2097184 | tf_op jit(solution)/shard_map/all_to_all | solution.py:48
  189.0 63.4 %psum.49 = f32[1024]{0:T(1024)S(1)} all-reduce(f32[1024]{0:T(1024)S(1)} %get-tuple-element.4), channel_id=1, replica_groups=mesh['cent'=8,'dp'=32] {'dp'}, use_global_device_ids=true, to_apply=%region_7.0 | all-reduce | flops 1024 | bytes 8192 | tf_op jit(solution)/shard_map/psum | solution.py:60
  252.4 2.5 multiply_reduce_fusion.5
  254.9 17.9 %psum.50 = f32[1024]{0:T(1024)S(1)} all-reduce(f32[1024]{0:T(1024)S(1)} %multiply_reduce_fusion.5), channel_id=1, replica_groups=mesh['cent'=8,'dp'=32] {'cent'}, use_global_device_ids=true, to_apply=%region_9.0 | all-reduce | flops 1024 | bytes 8192 | tf_op jit(solution)/shard_map/psum | solution.py:63
  272.8 2.5 multiply_reduce_fusion.4
  275.4 62.7 %psum.51 = f32[1024]{0:T(1024)S(1)} all-reduce(f32[1024]{0:T(1024)S(1)} %multiply_reduce_fusion.4), channel_id=1, replica_groups=mesh['cent'=8,'dp'=32] {'dp'}, use_global_device_ids=true, to_apply=%region_11.0 | all-reduce | flops 1024 | bytes 8192 | tf_op jit(solution)/shard_map/psum | solution.py:60
  338.1 2.5 multiply_reduce_fusion.3
  340.6 16.4 %psum.52 = f32[1024]{0:T(1024)S(1)} all-reduce(f32[1024]{0:T(1024)S(1)} %multiply_reduce_fusion.3), channel_id=1, replica_groups=mesh['cent'=8,'dp'=32] {'cent'}, use_global_device_ids=true, to_apply=%region_13.0 | all-reduce | flops 1024 | bytes 8192 | tf_op jit(solution)/shard_map/psum | solution.py:63
  357.0 2.5 multiply_reduce_fusion.2
  359.5 62.7 %psum.53 = f32[1024]{0:T(1024)S(1)} all-reduce(f32[1024]{0:T(1024)S(1)} %multiply_reduce_fusion.2), channel_id=1, replica_groups=mesh['cent'=8,'dp'=32] {'dp'}, use_global_device_ids=true, to_apply=%region_15.0 | all-reduce | flops 1024 | bytes 8192 | tf_op jit(solution)/shard_map/psum | solution.py:60
  422.2 2.5 multiply_reduce_fusion.1
  424.8 2.8 gather_fusion
  427.6 0.2 reduce_sum.119
  427.8 14.4 %all-reduce = (f32[1024]{0:T(1024)S(1)}, f32[1024]{0:T(1024)S(1)}) all-reduce(f32[1024]{0:T(1024)S(1)} %multiply_reduce_fusion.1, f32[1024]{0:T(1024)S(1)} %reduce_sum.119), channel_id=1, replica_groups=mesh['cent'=8,'dp'=32] {'cent'}, use_global_device_ids=true, to_apply=%region_17.0 | all-reduce | flops 2048 | bytes 16384 | tf_op jit(solution)/shard_map/psum | solution.py:68
  442.3 4.0 multiply_convert_fusion
  446.3 0.9 divide_convert_fusion
  (17 shorter events, 0.1 us)
Async XLA Ops:
  13.5 7.6 %copy-start.2 = (bf16[2,128,1024]{2,1,0:T(8,128)(2,1)S(1)}, bf16[2,128,1024]{2,1,0:T(8,128)(2,1)}, u32[]{:S(2)}) copy-start(bf16[2,128,1024]{2,1,0:T(8,128)(2,1)} %param.7) | copy-start | bytes 1572868
  13.5 121.1 %all-to-all-start = ((bf16[32,128,1024]{2,1,0:T(8,128)(2,1)}), bf16[32,128,1024]{2,1,0:T(8,128)(2,1)}, u32[]{:S(2)}, u32[]{:S(2)}) async-start(bf16[32,128,1024]{2,1,0:T(8,128)(2,1)} %bitcast.29), calls=%async_computation | async-start | bytes 16777216 | tf_op jit(solution)/shard_map/all_to_all | solution.py:41
  146.0 43.0 %all-to-all-start.1 = ((f32[32,128,128]{2,1,0:T(8,128)}), f32[32,128,128]{2,1,0:T(8,128)S(1)}, u32[]{:S(2)}, u32[]{:S(2)}) async-start(f32[32,128,128]{2,1,0:T(8,128)} %bitcast.31), calls=%async_computation.1 | async-start | bytes 4194304 | tf_op jit(solution)/shard_map/all_to_all | solution.py:48
  160.3 4.4 copy-start
  160.3 4.4 copy-start.1

commit v2 on v1

v2 whole, which is shorter than its diff:
```python
import jax
import jax.numpy as jnp
from jax import lax
from jax.sharding import PartitionSpec as P

CAP = 64
ITERS = 3


EPS = 1e-06
TAU = 0.05


def inverse_norm(rows):
    values = rows.astype(jnp.float32)
    return lax.rsqrt(jnp.mean(values * values, axis=-1) + EPS)


def shift_pairs(count, stride, size, step):
    pairs = []
    for i in range(count):
        digit = (i // stride) % size
        pairs.append((i, i + (((digit + step) % size) - digit) * stride))
    return pairs


def dp_sum(values):
    count = lax.axis_size("dp")
    for stride, size in ((1, 2), (2, 4), (8, count // 8)):
        if size < 2:
            continue
        parts = [lax.ppermute(values, "dp", shift_pairs(count, stride, size, step)) for step in range(1, size)]
        for part in parts:
            values = values + part
    return values


def shards(points, cluster_ids, centroids, sub_centroids):
    pts_count = points.shape[0]
    width = points.shape[1]
    dp_count = lax.axis_size("dp")
    cent_count = lax.axis_size("cent")
    group_dev = sub_centroids.shape[0]
    sub_dev = sub_centroids.shape[1]
    clusters = group_dev * dp_count
    total_cent = centroids.shape[0] * cent_count
    total_sub = sub_dev * cent_count
    scale_two = 1.0 / (width * TAU)

    gathered = lax.all_gather(sub_centroids, "dp", axis=0, tiled=True)
    inv_x = inverse_norm(points)
    ids = cluster_ids[:, 0]
    labels = lax.broadcasted_iota(jnp.int32, (pts_count, clusters), 1)
    onehot = ids[:, None] == labels
    positions = lax.broadcasted_iota(jnp.int32, (pts_count, pts_count), 0)
    earlier = (positions > positions.T).astype(jnp.bfloat16)
    before = jnp.dot(earlier, onehot.astype(jnp.bfloat16), preferred_element_type=jnp.float32)
    rank = jnp.sum(before * onehot.astype(jnp.float32), axis=1).astype(jnp.int32)
    slot = ids * CAP + rank
    source = jnp.zeros((clusters * CAP,), jnp.int32).at[slot].set(jnp.arange(pts_count, dtype=jnp.int32))
    buffer = points[source].reshape(clusters, CAP, width)
    inv_rows = inv_x[source].reshape(clusters, CAP)
    inv_u = inverse_norm(gathered)
    dots = jnp.einsum("gcd,gkd->gck", buffer, gathered, preferred_element_type=jnp.float32)
    weights = jnp.exp(dots * inv_rows[..., None] * inv_u[:, None, :] * scale_two)
    point_weights = weights.reshape(clusters * CAP, sub_dev)[slot]
    denom_part = jnp.sum(point_weights, axis=1)

    inv_c = inverse_norm(centroids)
    scores = jnp.einsum("pd,kd->pk", points, centroids, preferred_element_type=jnp.float32)
    expo = jnp.exp(scores * inv_x[:, None] * inv_c[None, :] * (1.0 / (width * TAU)))
    row_part = None
    for step in range(ITERS):
        if step == 0:
            col_part = jnp.sum(expo, axis=0)
        else:
            col_part = jnp.sum(expo * row_scale[:, None], axis=0)
        col_scale = 1.0 / dp_sum(col_part)
        row_part = jnp.sum(expo * col_scale[None, :], axis=1)
        if step + 1 < ITERS:
            row_scale = 1.0 / lax.psum(row_part, "cent")

    row_total = lax.psum(row_part, "cent")
    denominator = lax.psum(denom_part, "cent")
    row_scale = 1.0 / row_total
    assign = (expo * row_scale[:, None] * col_scale[None, :] * total_cent).astype(jnp.bfloat16)
    sub_assign = (total_sub * point_weights / denominator[:, None]).astype(jnp.bfloat16)
    return (assign, sub_assign)


def solution(mesh):
    return jax.shard_map(
        shards,
        mesh=mesh,
        in_specs=(P("dp", None), P("dp", None), P("cent", None), P("dp", "cent", None)),
        out_specs=(P("dp", "cent"), P("dp", "cent")),
        check_vma=False,
    )
```

time: 448 us -> 192 us (0.43)
  blocking collectives: 237 us -> 49.1 us
  waiting for transfers between devices: 133 us -> 23.3 us
  local copies, waits for them, and re-layouts: 15.2 us -> 42.2 us
  between operations: 0.83 us -> 14.3 us
    psum x3 -> x0, blocking collectives: 189 us -> none  [shards(): col_scale = 1.0 / lax.psum(col_part, 'dp')]
    all_to_all x2 -> x0, waiting for transfers between devices: 133 us -> none  [the longest x1 113 us: shards(): lax.all_to_all(outgoing, 'dp', split_axis=0, concat_axis=0, tiled=True)]
    gather x1 -> x3, local copies, waits for them, and re-layouts: 2.81 us -> 37.8 us  [the longest x1 18.3 us: shards(): buffer = points[source].reshape(clusters, CAP, width)]
    ppermute x0 -> x21, waiting for transfers between devices: none -> 22.6 us  [dp_sum(): lax.ppermute(values, 'dp', shift_pairs(count, stride, size, step))]
    all_to_all x2 -> x0, starting transfers between devices: 21.8 us -> none  [the longest x1 14.2 us: shards(): lax.all_to_all(weights, 'dp', split_axis=0, concat_axis=0, tiled=True)]
    ppermute x0 -> x21, starting transfers between devices: none -> 19.6 us  [dp_sum(): lax.ppermute(values, 'dp', shift_pairs(count, stride, size, step))]
    dot_general x1, matrix products: 4.78 us -> 11.3 us  [shards(): jnp.einsum('gcd,gkd->gck', buffer, gathered, preferred_element_type=jnp.f...]
    scatter x1, local copies, waits for them, and re-layouts: 10.8 us -> 4.33 us  [shards(): jnp.zeros((clusters * CAP,), jnp.int32).at[slot]]
  transfers between devices with their start and end apart: 2 -> 22, of which waited for: 2 -> 15; matrix products, arithmetic and copies ran while one was open for 2% -> 30% of each run, Pallas kernels for 0% -> 0%
where the time goes in v2:
time: 192 us; the launch traced here: 190 us
  blocking collectives  49.1 us (26%)
  local copies, waits for them, and re-layouts  42.2 us (22%)
  other arithmetic  26.5 us (14%)
  waiting for transfers between devices  23.3 us (12%)
  starting transfers between devices  19.6 us (10%)
  matrix products  14.5 us (8%)
  between operations  14.3 us (7%)
    psum x2, blocking collectives, shards(): row_scale = 1.0 / lax.psum(row_part, 'cent')  34.6 us
    ppermute x21, waiting for transfers between devices, dp_sum(): lax.ppermute(values, 'dp', shift_pairs(count, stride, size, step))  22.6 us
    ppermute x21, starting transfers between devices, dp_sum(): lax.ppermute(values, 'dp', shift_pairs(count, stride, size, step))  19.6 us
    gather x1, local copies, waits for them, and re-layouts, shards(): buffer = points[source].reshape(clusters, CAP, width)  18.3 us
    gather x1, local copies, waits for them, and re-layouts, shards(): inv_rows = inv_x[source].reshape(clusters, CAP)  16.7 us
    psum x1, blocking collectives, shards(): row_total = lax.psum(row_part, 'cent')  14.5 us
    reduce_sum x3, other arithmetic, inverse_norm(): return lax.rsqrt(jnp.mean(values * values, axis=-1) + EPS)  11.5 us
    dot_general x1, matrix products, shards(): jnp.einsum('gcd,gkd->gck', buffer, gathered, preferred_element_type=jnp.f...  11.3 us
  transfers between devices with their start and end apart: 22, of which 15 were waited for; matrix products, arithmetic and copies ran while one was open for 30% of the time, Pallas kernels for 0%

profile of v2, /device:TPU:32, one launch (start us, length us, event | category | flops | bytes accessed | tf_op | source)
XLA Modules:
  0.0 189.6 jit_solution(108511958518971730)
XLA Ops:
  7.9 2.2 %multiply_reduce_fusion.6 = f32[1024]{0:T(1024)S(1)} fusion(bf16[1024,1024]{1,0:T(8,128)(2,1)} %param.6), kind=kLoop, calls=%fused_computation.13 | loop fusion | flops 3144704 | bytes 2101248 | tf_op jit(solution)/shard_map/reduce_sum | solution.py:16
  10.1 2.1 %multiply_reduce_fusion.7 = f32[1024]{0:T(1024)S(1)} fusion(bf16[1024,1024]{1,0:T(8,128)(2,1)} %param.4), kind=kLoop, calls=%fused_computation.14 | loop fusion | flops 3144704 | bytes 2101248 | tf_op jit(solution)/shard_map/reduce_sum | solution.py:16
  12.2 2.7 %fusion.7 = (f32[1024]{0:T(1024)S(1)}, f32[1024,1024]{1,0:T(8,128)S(1)}) fusion(f32[1024]{0:T(1024)S(1)} %get-tuple-element.6, f32[1024]{0:T(1024)S(1)} %get-tuple-element.7, bf16[1024,1024]{1,0:T(8,128)(2,1)S(1)} %copy-done, bf16[1024,1024]{1,0:T(8,128)(2,1)S(1)} %copy-done.3), kind=kOutput, calls=%fused_computation.40 | convolution fusion | flops 2151676928 | bytes 8400896 | tf_op jit(solution)/shard_map/pd,kd->pk/dot_general | solution.py:70
  15.0 1.2 collective-permute-done
  16.2 3.0 %collective-permute-start.3 = (f32[1024]{0:T(1024)S(1)}, f32[1024]{0:T(1024)S(1)}, u32[]{:S(2)}, u32[]{:S(2)}) collective-permute-start(f32[1024]{0:T(1024)S(1)} %add.110), channel_id=1, source_target_pairs={{0,6},{1,7},{2,0},{3,1},{4,2},{5,3},{6,4},{7,5},{8,14},{9,15},{10,... | collective-permute-start | bytes 12296 | tf_op jit(solution)/shard_map/ppermute | solution.py:32
  20.8 3.5 %collective-permute-done.2 = f32[1024]{0:T(1024)S(1)} collective-permute-done((f32[1024]{0:T(1024)S(1)}, f32[1024]{0:T(1024)S(1)}, u32[]{:S(2)}, u32[]{:S(2)}) %collective-permute-start.2) | collective-permute-done | bytes 4128 | tf_op jit(solution)/shard_map/ppermute | solution.py:32
  24.7 2.8 %collective-permute-start.6 = (f32[1024]{0:T(1024)S(1)}, f32[1024]{0:T(1024)S(1)}, u32[]{:S(2)}, u32[]{:S(2)}) collective-permute-start(f32[1024]{0:T(1024)S(1)} %add_add_fusion.2), channel_id=1, source_target_pairs={{0,24},{1,25},{2,26},{3,27},{4,28},{5,29},{6,30},{7,31},{8,0},{9,1... | collective-permute-start | bytes 12296 | tf_op jit(solution)/shard_map/ppermute | solution.py:32
  29.1 3.6 %collective-permute-done.5 = f32[1024]{0:T(1024)S(1)} collective-permute-done((f32[1024]{0:T(1024)S(1)}, f32[1024]{0:T(1024)S(1)}, u32[]{:S(2)}, u32[]{:S(2)}) %collective-permute-start.5) | collective-permute-done | bytes 4128 | tf_op jit(solution)/shard_map/ppermute | solution.py:32
  33.4 17.9 %psum.28 = f32[1024]{0:T(1024)S(1)} all-reduce(f32[1024]{0:T(1024)S(1)} %multiply_reduce_fusion.5), channel_id=1, replica_groups=mesh['cent'=8,'dp'=32] {'cent'}, use_global_device_ids=true, to_apply=%region_4.0 | all-reduce | flops 1024 | bytes 8192 | tf_op jit(solution)/shard_map/psum | solution.py:81
  51.3 3.8 %multiply_reduce_fusion.4 = f32[1024]{0:T(1024)S(1)} fusion(f32[1024,1024]{1,0:T(8,128)} %copy-done.1, f32[1024]{0:T(1024)S(1)} %broadcast_divide_fusion.2), kind=kLoop, calls=%fused_computation.10 | loop fusion | flops 2096128 | bytes 4202496 | tf_op jit(solution)/shard_map/reduce_sum | solution.py:77
  55.2 1.2 collective-permute-done.7
  57.3 1.4 collective-permute-start.8
  58.7 1.4 collective-permute-done.10
  60.2 1.5 collective-permute-done.9
  61.7 1.2 collective-permute-done.8
  63.9 1.2 collective-permute-start.11
  66.7 1.6 collective-permute-done.12
  69.7 16.7 %psum.29 = f32[1024]{0:T(1024)S(1)} all-reduce(f32[1024]{0:T(1024)S(1)} %multiply_reduce_fusion.3), channel_id=1, replica_groups=mesh['cent'=8,'dp'=32] {'cent'}, use_global_device_ids=true, to_apply=%region_7.0 | all-reduce | flops 1024 | bytes 8192 | tf_op jit(solution)/shard_map/psum | solution.py:81
  86.4 2.7 %multiply_reduce_fusion.2 = f32[1024]{0:T(1024)S(1)} fusion(f32[1024,1024]{1,0:T(8,128)} %copy-done.1, f32[1024]{0:T(1024)S(1)} %broadcast_divide_fusion.1), kind=kLoop, calls=%fused_computation.8 | loop fusion | flops 2096128 | bytes 4202496 | tf_op jit(solution)/shard_map/reduce_sum | solution.py:77
  89.3 4.3 %scatter_custom_fusion = s32[4096]{0:T(1024)S(1)} fusion(s32[1024]{0:T(1024)S(1)} %bitcast.19, s32[1024]{0:T(1024)S(1)} %iota.18, s32[]{:T(128)} %constant.6.clone.1), kind=kCustom, calls=%fused_computation.26 | custom fusion | bytes 16388 | tf_op jit(solution)/shard_map/scatter | solution.py:60
  93.6 2.0 %collective-permute-start.17 = (f32[1024]{0:T(1024)S(1)}, f32[1024]{0:T(1024)S(1)}, u32[]{:S(2)}, u32[]{:S(2)}) collective-permute-start(f32[1024]{0:T(1024)S(1)} %add.124), channel_id=1, source_target_pairs={{0,6},{1,7},{2,0},{3,1},{4,2},{5,3},{6,4},{7,5},{8,14},{9,15},{10,... | collective-permute-start | bytes 12296 | tf_op jit(solution)/shard_map/ppermute | solution.py:32
  95.6 1.2 collective-permute-start.16
  97.3 3.4 %collective-permute-done.16 = f32[1024]{0:T(1024)S(1)} collective-permute-done((f32[1024]{0:T(1024)S(1)}, f32[1024]{0:T(1024)S(1)}, u32[]{:S(2)}, u32[]{:S(2)}) %collective-permute-start.16) | collective-permute-done | bytes 4128 | tf_op jit(solution)/shard_map/ppermute | solution.py:32
  102.2 1.2 collective-permute-start.19
  104.1 16.7 %gather_fusion.1 = f32[4096]{0:T(1024)S(1)} fusion(f32[1024]{0:T(1024)S(1)} %get-tuple-element.7, s32[4096]{0:T(1024)S(1)} %fusion.4), kind=kCustom, calls=%fused_computation.1 | custom fusion | bytes 49152 | tf_op jit(solution)/shard_map/gather | solution.py:62
  120.8 18.3 %gather_fusion = bf16[4096,1024]{1,0:T(8,128)(2,1)} fusion(bf16[1024,1024]{1,0:T(8,128)(2,1)S(1)} %copy-done, s32[4096]{0:T(1024)S(1)} %fusion.4), kind=kCustom, calls=%fused_computation | custom fusion | bytes 16793600 | tf_op jit(solution)/shard_map/gather | solution.py:61
  139.1 2.5 %multiply_reduce_fusion.1 = f32[1024]{0:T(1024)S(1)} fusion(f32[1024,1024]{1,0:T(8,128)} %copy-done.1, f32[1024]{0:T(1024)S(1)} %add_divide_fusion), kind=kLoop, calls=%fused_computation.7 | loop fusion | flops 2096128 | bytes 4202496 | tf_op jit(solution)/shard_map/reduce_sum | solution.py:79
  141.7 7.2 %multiply_reduce_fusion = f32[64,128]{1,0:T(8,128)S(1)} fusion(bf16[64,128,1024]{2,1,0:T(8,128)(2,1)} %all-gather.2.cloned.1.call-done), kind=kLoop, calls=%fused_computation.4 | loop fusion | flops 25157632 | bytes 16809984 | tf_op jit(solution)/shard_map/reduce_sum | solution.py:16
  148.9 11.3 %multiply_exponential_fusion.1 = f32[64,64,128]{2,1,0:T(8,128)S(1)} fusion(bf16[64,64,1024]{2,1,0:T(8,128)(2,1)} %bitcast.17, bf16[64,128,1024]{2,1,0:T(8,128)(2,1)} %all-gather.2.cloned.1.call-done, f32[64,128]{1,0:T(8,128)S(1)} %add_rsqrt_fusion, f32[64,64]{1,0:T(8,128)S(1)} %mul.157), kind=kOutput, calls=%fused_computation.16 | convolution fusion | flops 1075314688 | bytes 27312128 | tf_op jit(solution)/shard_map/gcd,gkd->gck/dot_general | solution.py:64
  160.2 2.8 %gather_fusion.2 = f32[1024,128]{1,0:T(8,128)S(1)} fusion(f32[4096,128]{1,0:T(8,128)S(1)} %bitcast.18, s32[1024]{0:T(1024)S(1)} %broadcast_clamp_fusion), kind=kCustom, calls=%fused_computation.2 | custom fusion | bytes 1052672 | tf_op jit(solution)/shard_map/gather | solution.py:66
  163.2 14.5 %all-reduce = (f32[1024]{0:T(1024)S(1)}, f32[1024]{0:T(1024)S(1)}) all-reduce(f32[1024]{0:T(1024)S(1)} %multiply_reduce_fusion.1, f32[1024]{0:T(1024)S(1)} %reduce_sum.109), channel_id=1, replica_groups=mesh['cent'=8,'dp'=32] {'cent'}, use_global_device_ids=true, to_apply=%region_10.0 | all-reduce | flops 2048 | bytes 16384 | tf_op jit(solution)/shard_map/psum | solution.py:83
  178.7 4.1 %multiply_convert_fusion = bf16[1024,1024]{1,0:T(8,128)(2,1)} fusion(f32[1024,1024]{1,0:T(8,128)} %copy-done.1, f32[1024]{0:T(1024)S(1)} %broadcast_divide_fusion, f32[1024]{0:T(1024)S(1)} %add_divide_fusion), kind=kLoop, calls=%fused_computation.6 | loop fusion | flops 4194304 | bytes 6299648 | tf_op jit(solution)/shard_map/convert_element_type | solution.py:86
  (64 shorter events, 14.2 us)
Async XLA Ops:
  7.2 5.1 %copy-start = (bf16[1024,1024]{1,0:T(8,128)(2,1)S(1)}, bf16[1024,1024]{1,0:T(8,128)(2,1)}, u32[]{:S(2)}) copy-start(bf16[1024,1024]{1,0:T(8,128)(2,1)} %param.4) | copy-start | bytes 6291460
  7.2 134.5 %all-gather.2.cloned.1.call-start = ((), (), s32[]{:S(2)}) async-start(), calls=%async_computation | async-start | bytes 17301504 | tf_op jit(solution)/shard_map/all_gather | solution.py:50
  7.9 4.3 %copy-start.3 = (bf16[1024,1024]{1,0:T(8,128)(2,1)S(1)}, bf16[1024,1024]{1,0:T(8,128)(2,1)}, u32[]{:S(2)}) copy-start(bf16[1024,1024]{1,0:T(8,128)(2,1)} %param.6) | copy-start | bytes 6291460
  14.9 18.1 %copy-start.1 = (f32[1024,1024]{1,0:T(8,128)}, f32[1024,1024]{1,0:T(8,128)S(1)}, u32[]{:S(2)}) copy-start(f32[1024,1024]{1,0:T(8,128)S(1)} %get-tuple-element.5) | copy-start | bytes 12582916
  14.9 1.3 collective-permute-start
  16.2 4.6 %collective-permute-start.3 = (f32[1024]{0:T(1024)S(1)}, f32[1024]{0:T(1024)S(1)}, u32[]{:S(2)}, u32[]{:S(2)}) collective-permute-start(f32[1024]{0:T(1024)S(1)} %add.110), channel_id=1, source_target_pairs={{0,6},{1,7},{2,0},{3,1},{4,2},{5,3},{6,4},{7,5},{8,14},{9,15},{10,... | collective-permute-start | bytes 12296 | tf_op jit(solution)/shard_map/ppermute | solution.py:32
  19.2 5.1 %collective-permute-start.2 = (f32[1024]{0:T(1024)S(1)}, f32[1024]{0:T(1024)S(1)}, u32[]{:S(2)}, u32[]{:S(2)}) collective-permute-start(f32[1024]{0:T(1024)S(1)} %add.110), channel_id=1, source_target_pairs={{0,4},{1,5},{2,6},{3,7},{4,0},{5,1},{6,2},{7,3},{8,12},{9,13},{10,... | collective-permute-start | bytes 12296 | tf_op jit(solution)/shard_map/ppermute | solution.py:32
  19.8 4.8 %collective-permute-start.1 = (f32[1024]{0:T(1024)S(1)}, f32[1024]{0:T(1024)S(1)}, u32[]{:S(2)}, u32[]{:S(2)}) collective-permute-start(f32[1024]{0:T(1024)S(1)} %add.110), channel_id=1, source_target_pairs={{0,2},{1,3},{2,4},{3,5},{4,6},{5,7},{6,0},{7,1},{8,10},{9,11},{10,... | collective-permute-start | bytes 12296 | tf_op jit(solution)/shard_map/ppermute | solution.py:32
  24.7 4.4 %collective-permute-start.6 = (f32[1024]{0:T(1024)S(1)}, f32[1024]{0:T(1024)S(1)}, u32[]{:S(2)}, u32[]{:S(2)}) collective-permute-start(f32[1024]{0:T(1024)S(1)} %add_add_fusion.2), channel_id=1, source_target_pairs={{0,24},{1,25},{2,26},{3,27},{4,28},{5,29},{6,30},{7,31},{8,0},{9,1... | collective-permute-start | bytes 12296 | tf_op jit(solution)/shard_map/ppermute | solution.py:32
  27.4 5.3 %collective-permute-start.5 = (f32[1024]{0:T(1024)S(1)}, f32[1024]{0:T(1024)S(1)}, u32[]{:S(2)}, u32[]{:S(2)}) collective-permute-start(f32[1024]{0:T(1024)S(1)} %add_add_fusion.2), channel_id=1, source_target_pairs={{0,16},{1,17},{2,18},{3,19},{4,20},{5,21},{6,22},{7,23},{8,24},{9,... | collective-permute-start | bytes 12296 | tf_op jit(solution)/shard_map/ppermute | solution.py:32
  28.2 4.8 %collective-permute-start.4 = (f32[1024]{0:T(1024)S(1)}, f32[1024]{0:T(1024)S(1)}, u32[]{:S(2)}, u32[]{:S(2)}) collective-permute-start(f32[1024]{0:T(1024)S(1)} %add_add_fusion.2), channel_id=1, source_target_pairs={{0,8},{1,9},{2,10},{3,11},{4,12},{5,13},{6,14},{7,15},{8,16},{9,17... | collective-permute-start | bytes 12296 | tf_op jit(solution)/shard_map/ppermute | solution.py:32
  33.0 32.0 %copy-start.4 = (s32[1024,1]{0,1:T(1,128)S(1)}, s32[1024,1]{0,1:T(1,128)}, u32[]{:S(2)}) copy-start(s32[1024,1]{0,1:T(1,128)} %param.5) | copy-start | bytes 12292
  51.3 18.1 %copy-start.2 = (f32[1024,1024]{1,0:T(8,128)S(1)}, f32[1024,1024]{1,0:T(8,128)}, u32[]{:S(2)}) copy-start(f32[1024,1024]{1,0:T(8,128)} %copy-done.1) | copy-start | bytes 12582916
  55.1 1.3 collective-permute-start.7
  56.3 3.8 %collective-permute-start.10 = (f32[1024]{0:T(1024)S(1)}, f32[1024]{0:T(1024)S(1)}, u32[]{:S(2)}, u32[]{:S(2)}) collective-permute-start(f32[1024]{0:T(1024)S(1)} %add.117), channel_id=1, source_target_pairs={{0,6},{1,7},{2,0},{3,1},{4,2},{5,3},{6,4},{7,5},{8,14},{9,15},{10,... | collective-permute-start | bytes 12296 | tf_op jit(solution)/shard_map/ppermute | solution.py:32
  56.3 5.3 %collective-permute-start.9 = (f32[1024]{0:T(1024)S(1)}, f32[1024]{0:T(1024)S(1)}, u32[]{:S(2)}, u32[]{:S(2)}) collective-permute-start(f32[1024]{0:T(1024)S(1)} %add.117), channel_id=1, source_target_pairs={{0,4},{1,5},{2,6},{3,7},{4,0},{5,1},{6,2},{7,3},{8,12},{9,13},{10,... | collective-permute-start | bytes 12296 | tf_op jit(solution)/shard_map/ppermute | solution.py:32
  57.3 5.5 %collective-permute-start.8 = (f32[1024]{0:T(1024)S(1)}, f32[1024]{0:T(1024)S(1)}, u32[]{:S(2)}, u32[]{:S(2)}) collective-permute-start(f32[1024]{0:T(1024)S(1)} %add.117), channel_id=1, source_target_pairs={{0,2},{1,3},{2,4},{3,5},{4,6},{5,7},{6,0},{7,1},{8,10},{9,11},{10,... | collective-permute-start | bytes 12296 | tf_op jit(solution)/shard_map/ppermute | solution.py:32
  62.8 3.8 %collective-permute-start.13 = (f32[1024]{0:T(1024)S(1)}, f32[1024]{0:T(1024)S(1)}, u32[]{:S(2)}, u32[]{:S(2)}) collective-permute-start(f32[1024]{0:T(1024)S(1)} %add_add_fusion.1), channel_id=1, source_target_pairs={{0,24},{1,25},{2,26},{3,27},{4,28},{5,29},{6,30},{7,31},{8,0},{9,1... | collective-permute-start | bytes 12296 | tf_op jit(solution)/shard_map/ppermute | solution.py:32
  62.8 5.4 %collective-permute-start.12 = (f32[1024]{0:T(1024)S(1)}, f32[1024]{0:T(1024)S(1)}, u32[]{:S(2)}, u32[]{:S(2)}) collective-permute-start(f32[1024]{0:T(1024)S(1)} %add_add_fusion.1), channel_id=1, source_target_pairs={{0,16},{1,17},{2,18},{3,19},{4,20},{5,21},{6,22},{7,23},{8,24},{9,... | collective-permute-start | bytes 12296 | tf_op jit(solution)/shard_map/ppermute | solution.py:32
  63.9 5.5 %collective-permute-start.11 = (f32[1024]{0:T(1024)S(1)}, f32[1024]{0:T(1024)S(1)}, u32[]{:S(2)}, u32[]{:S(2)}) collective-permute-start(f32[1024]{0:T(1024)S(1)} %add_add_fusion.1), channel_id=1, source_target_pairs={{0,8},{1,9},{2,10},{3,11},{4,12},{5,13},{6,14},{7,15},{8,16},{9,17... | collective-permute-start | bytes 12296 | tf_op jit(solution)/shard_map/ppermute | solution.py:32
  89.1 4.5 %collective-permute-start.14 = (f32[1024]{0:T(1024)S(1)}, f32[1024]{0:T(1024)S(1)}, u32[]{:S(2)}, u32[]{:S(2)}) collective-permute-start(f32[1024]{0:T(1024)S(1)} %multiply_reduce_fusion.2), channel_id=1, source_target_pairs={{0,1},{1,0},{2,3},{3,2},{4,5},{5,4},{6,7},{7,6},{8,9},{9,8},{10,11... | collective-permute-start | bytes 12296 | tf_op jit(solution)/shard_map/ppermute | solution.py:32
  93.6 3.7 %collective-permute-start.17 = (f32[1024]{0:T(1024)S(1)}, f32[1024]{0:T(1024)S(1)}, u32[]{:S(2)}, u32[]{:S(2)}) collective-permute-start(f32[1024]{0:T(1024)S(1)} %add.124), channel_id=1, source_target_pairs={{0,6},{1,7},{2,0},{3,1},{4,2},{5,3},{6,4},{7,5},{8,14},{9,15},{10,... | collective-permute-start | bytes 12296 | tf_op jit(solution)/shard_map/ppermute | solution.py:32
  95.6 5.1 %collective-permute-start.16 = (f32[1024]{0:T(1024)S(1)}, f32[1024]{0:T(1024)S(1)}, u32[]{:S(2)}, u32[]{:S(2)}) collective-permute-start(f32[1024]{0:T(1024)S(1)} %add.124), channel_id=1, source_target_pairs={{0,4},{1,5},{2,6},{3,7},{4,0},{5,1},{6,2},{7,3},{8,12},{9,13},{10,... | collective-permute-start | bytes 12296 | tf_op jit(solution)/shard_map/ppermute | solution.py:32
  96.8 4.8 %collective-permute-start.15 = (f32[1024]{0:T(1024)S(1)}, f32[1024]{0:T(1024)S(1)}, u32[]{:S(2)}, u32[]{:S(2)}) collective-permute-start(f32[1024]{0:T(1024)S(1)} %add.124), channel_id=1, source_target_pairs={{0,2},{1,3},{2,4},{3,5},{4,6},{5,7},{6,0},{7,1},{8,10},{9,11},{10,... | collective-permute-start | bytes 12296 | tf_op jit(solution)/shard_map/ppermute | solution.py:32
  101.6 37.5 %collective-permute-start.20 = (f32[1024]{0:T(1024)S(1)}, f32[1024]{0:T(1024)S(1)}, u32[]{:S(2)}, u32[]{:S(2)}) collective-permute-start(f32[1024]{0:T(1024)S(1)} %add_add_fusion), channel_id=1, source_target_pairs={{0,24},{1,25},{2,26},{3,27},{4,28},{5,29},{6,30},{7,31},{8,0},{9,1... | collective-permute-start | bytes 12296 | tf_op jit(solution)/shard_map/ppermute | solution.py:32
  102.2 36.9 %collective-permute-start.19 = (f32[1024]{0:T(1024)S(1)}, f32[1024]{0:T(1024)S(1)}, u32[]{:S(2)}, u32[]{:S(2)}) collective-permute-start(f32[1024]{0:T(1024)S(1)} %add_add_fusion), channel_id=1, source_target_pairs={{0,16},{1,17},{2,18},{3,19},{4,20},{5,21},{6,22},{7,23},{8,24},{9,... | collective-permute-start | bytes 12296 | tf_op jit(solution)/shard_map/ppermute | solution.py:32
  103.4 35.7 %collective-permute-start.18 = (f32[1024]{0:T(1024)S(1)}, f32[1024]{0:T(1024)S(1)}, u32[]{:S(2)}, u32[]{:S(2)}) collective-permute-start(f32[1024]{0:T(1024)S(1)} %add_add_fusion), channel_id=1, source_target_pairs={{0,8},{1,9},{2,10},{3,11},{4,12},{5,13},{6,14},{7,15},{8,16},{9,17... | collective-permute-start | bytes 12296 | tf_op jit(solution)/shard_map/ppermute | solution.py:32
Sparse Core Ops, SparseCore 0:
  10.5 80.3 all-gather.1

commit v3 on v2

--- a/solution.py
+++ b/solution.py
@@ -35,6 +35,15 @@
     return values
 
 
+def cent_sum(values):
+    count = lax.axis_size("cent")
+    bit = 1
+    while bit < count:
+        values = values + lax.ppermute(values, "cent", [(i, i ^ bit) for i in range(count)])
+        bit *= 2
+    return values
+
+
 def shards(points, cluster_ids, centroids, sub_centroids):
     pts_count = points.shape[0]
     width = points.shape[1]
@@ -58,8 +67,10 @@
     rank = jnp.sum(before * onehot.astype(jnp.float32), axis=1).astype(jnp.int32)
     slot = ids * CAP + rank
     source = jnp.zeros((clusters * CAP,), jnp.int32).at[slot].set(jnp.arange(pts_count, dtype=jnp.int32))
-    buffer = points[source].reshape(clusters, CAP, width)
-    inv_rows = inv_x[source].reshape(clusters, CAP)
+    pick = (source[:, None] == lax.broadcasted_iota(jnp.int32, (clusters * CAP, pts_count), 1)).astype(points.dtype)
+    buffer = jnp.dot(pick, points, preferred_element_type=jnp.float32).astype(points.dtype)
+    buffer = buffer.reshape(clusters, CAP, width)
+    inv_rows = inverse_norm(buffer)
     inv_u = inverse_norm(gathered)
     dots = jnp.einsum("gcd,gkd->gck", buffer, gathered, preferred_element_type=jnp.float32)
     weights = jnp.exp(dots * inv_rows[..., None] * inv_u[:, None, :] * scale_two)
@@ -78,10 +89,11 @@
         col_scale = 1.0 / dp_sum(col_part)
         row_part = jnp.sum(expo * col_scale[None, :], axis=1)
         if step + 1 < ITERS:
-            row_scale = 1.0 / lax.psum(row_part, "cent")
+            row_scale = 1.0 / cent_sum(row_part)
 
-    row_total = lax.psum(row_part, "cent")
-    denominator = lax.psum(denom_part, "cent")
+    totals = cent_sum(jnp.concatenate([row_part, denom_part]))
+    row_total = totals[:pts_count]
+    denominator = totals[pts_count:]
     row_scale = 1.0 / row_total
     assign = (expo * row_scale[:, None] * col_scale[None, :] * total_cent).astype(jnp.bfloat16)
     sub_assign = (total_sub * point_weights / denominator[:, None]).astype(jnp.bfloat16)

time: 192 us -> 166 us (0.86)
  blocking collectives: 49.1 us -> 0 us
  local copies, waits for them, and re-layouts: 42.2 us -> 7.24 us
  starting transfers between devices: 19.6 us -> 45.9 us
  waiting for transfers between devices: 23.3 us -> 48.1 us
  matrix products: 14.5 us -> 26.8 us
  other arithmetic: 26.5 us -> 23.1 us
    psum x3 -> x0, blocking collectives: 49.1 us -> none  [the longest x2 34.6 us: shards(): row_scale = 1.0 / lax.psum(row_part, 'cent')]
    gather x2 -> x0, local copies, waits for them, and re-layouts: 34.9 us -> none  [the longest x1 18.3 us: shards(): buffer = points[source].reshape(clusters, CAP, width)]
    ppermute x0 -> x9, starting transfers between devices: none -> 25.1 us  [cent_sum(): lax.ppermute(values, 'cent', [(i, i ^ bit) for i in range(count)])]
    ppermute x0 -> x9, waiting for transfers between devices: none -> 20.4 us  [cent_sum(): lax.ppermute(values, 'cent', [(i, i ^ bit) for i in range(count)])]
    dot_general x0 -> x1, matrix products: none -> 12.2 us  [shards(): jnp.dot(pick, points, preferred_element_type=jnp.float32)]
    ppermute x21, waiting for transfers between devices: 22.6 us -> 27 us  [dp_sum(): lax.ppermute(values, 'dp', shift_pairs(count, stride, size, step))]
    reduce_sum x2, other arithmetic: 6.48 us -> 3.06 us  [shards(): col_part = jnp.sum(expo * row_scale[:, None], axis=0)]
  transfers between devices with their start and end apart: 22 -> 31, of which waited for: 15 -> 26; matrix products, arithmetic and copies ran while one was open for 30% -> 19% of each run, Pallas kernels for 0% -> 0%
where the time goes in v3:
time: 166 us; the launch traced here: 165 us
  waiting for transfers between devices  48.1 us (29%)
  starting transfers between devices  45.9 us (28%)
  matrix products  26.8 us (16%)
  other arithmetic  23.1 us (14%)
  between operations  14.3 us (9%)
  local copies, waits for them, and re-layouts  7.24 us (4%)
    ppermute x21, waiting for transfers between devices, dp_sum(): lax.ppermute(values, 'dp', shift_pairs(count, stride, size, step))  27 us
    ppermute x9, starting transfers between devices, cent_sum(): lax.ppermute(values, 'cent', [(i, i ^ bit) for i in range(count)])  25.1 us
    ppermute x21, starting transfers between devices, dp_sum(): lax.ppermute(values, 'dp', shift_pairs(count, stride, size, step))  20.8 us
    ppermute x9, waiting for transfers between devices, cent_sum(): lax.ppermute(values, 'cent', [(i, i ^ bit) for i in range(count)])  20.4 us
    dot_general x1, matrix products, shards(): jnp.dot(pick, points, preferred_element_type=jnp.float32)  12.2 us
    reduce_sum x3, other arithmetic, inverse_norm(): return lax.rsqrt(jnp.mean(values * values, axis=-1) + EPS)  11.5 us
    dot_general x1, matrix products, shards(): jnp.einsum('gcd,gkd->gck', buffer, gathered, preferred_element_type=jnp.f...  11.3 us
    scatter x1, local copies, waits for them, and re-layouts, shards(): jnp.zeros((clusters * CAP,), jnp.int32).at[slot]  4.33 us
  transfers between devices with their start and end apart: 31, of which 26 were waited for; matrix products, arithmetic and copies ran while one was open for 19% of the time, Pallas kernels for 0%

profile of v3, /device:TPU:32, one launch (start us, length us, event | category | flops | bytes accessed | tf_op | source)
XLA Modules:
  0.0 165.5 jit_solution(16659278550976475359)
XLA Ops:
  7.9 2.2 %multiply_reduce_fusion.7 = f32[1024]{0:T(1024)S(1)} fusion(bf16[1024,1024]{1,0:T(8,128)(2,1)} %param.6), kind=kLoop, calls=%fused_computation.16 | loop fusion | flops 3144704 | bytes 2101248 | tf_op jit(solution)/shard_map/reduce_sum | solution.py:16
  10.1 2.1 %multiply_reduce_fusion.8 = f32[1024]{0:T(1024)S(1)} fusion(bf16[1024,1024]{1,0:T(8,128)(2,1)} %param.4), kind=kLoop, calls=%fused_computation.17 | loop fusion | flops 3144704 | bytes 2101248 | tf_op jit(solution)/shard_map/reduce_sum | solution.py:16
  12.2 2.7 %fusion.11 = (f32[1024]{0:T(1024)S(1)}, f32[1024,1024]{1,0:T(8,128)S(1)}) fusion(f32[1024]{0:T(1024)S(1)} %get-tuple-element.8, f32[1024]{0:T(1024)S(1)} %get-tuple-element.9, bf16[1024,1024]{1,0:T(8,128)(2,1)S(1)} %copy-done.2, bf16[1024,1024]{1,0:T(8,128)(2,1)S(1)} %copy-done.1), kind=kOutput, calls=%fused_computation.45 | convolution fusion | flops 2151676928 | bytes 8400896 | tf_op jit(solution)/shard_map/pd,kd->pk/dot_general | solution.py:81
  16.3 3.0 %collective-permute-start.3 = (f32[1024]{0:T(1024)S(1)}, f32[1024]{0:T(1024)S(1)}, u32[]{:S(2)}, u32[]{:S(2)}) collective-permute-start(f32[1024]{0:T(1024)S(1)} %add.136), channel_id=1, source_target_pairs={{0,6},{1,7},{2,0},{3,1},{4,2},{5,3},{6,4},{7,5},{8,14},{9,15},{10,... | collective-permute-start | bytes 12296 | tf_op jit(solution)/shard_map/ppermute | solution.py:32
  20.9 3.5 %collective-permute-done.2 = f32[1024]{0:T(1024)S(1)} collective-permute-done((f32[1024]{0:T(1024)S(1)}, f32[1024]{0:T(1024)S(1)}, u32[]{:S(2)}, u32[]{:S(2)}) %collective-permute-start.2) | collective-permute-done | bytes 4128 | tf_op jit(solution)/shard_map/ppermute | solution.py:32
  24.7 2.8 %collective-permute-start.6 = (f32[1024]{0:T(1024)S(1)}, f32[1024]{0:T(1024)S(1)}, u32[]{:S(2)}, u32[]{:S(2)}) collective-permute-start(f32[1024]{0:T(1024)S(1)} %add_add_fusion.2), channel_id=1, source_target_pairs={{0,24},{1,25},{2,26},{3,27},{4,28},{5,29},{6,30},{7,31},{8,0},{9,1... | collective-permute-start | bytes 12296 | tf_op jit(solution)/shard_map/ppermute | solution.py:32
  29.2 3.6 %collective-permute-done.5 = f32[1024]{0:T(1024)S(1)} collective-permute-done((f32[1024]{0:T(1024)S(1)}, f32[1024]{0:T(1024)S(1)}, u32[]{:S(2)}, u32[]{:S(2)}) %collective-permute-start.5) | collective-permute-done | bytes 4128 | tf_op jit(solution)/shard_map/ppermute | solution.py:32
  33.9 3.3 %collective-permute-done.7 = f32[1024]{0:T(1024)S(1)} collective-permute-done((f32[1024]{0:T(1024)S(1)}, f32[1024]{0:T(1024)S(1)}, u32[]{:S(2)}, u32[]{:S(2)}) %collective-permute-start.7) | collective-permute-done | bytes 4128 | tf_op jit(solution)/shard_map/ppermute | solution.py:42
  37.2 3.3 %collective-permute-start.8 = (f32[1024]{0:T(1024)S(1)}, f32[1024]{0:T(1024)S(1)}, u32[]{:S(2)}, u32[]{:S(2)}) collective-permute-start(f32[1024]{0:T(1024)S(1)} %add.143), channel_id=1, source_target_pairs={{0,64},{32,96},{64,0},{96,32},{128,192},{160,224},{192,128},{224,1... | collective-permute-start | bytes 12296 | tf_op jit(solution)/shard_map/ppermute | solution.py:42
  40.4 1.6 collective-permute-done.8
  42.0 5.9 %collective-permute-start.9 = (f32[1024]{0:T(1024)S(1)}, f32[1024]{0:T(1024)S(1)}, u32[]{:S(2)}, u32[]{:S(2)}) collective-permute-start(f32[1024]{0:T(1024)S(1)} %add.144), channel_id=1, source_target_pairs={{0,128},{32,160},{64,192},{96,224},{128,0},{160,32},{192,64},{224,... | collective-permute-start | bytes 12296 | tf_op jit(solution)/shard_map/ppermute | solution.py:42
  48.0 1.6 collective-permute-done.9
  54.8 2.4 %collective-permute-done.12 = f32[1024]{0:T(1024)S(1)} collective-permute-done((f32[1024]{0:T(1024)S(1)}, f32[1024]{0:T(1024)S(1)}, u32[]{:S(2)}, u32[]{:S(2)}) %collective-permute-start.12) | collective-permute-done | bytes 4128 | tf_op jit(solution)/shard_map/ppermute | solution.py:32
  62.0 1.7 %collective-permute-done.15 = f32[1024]{0:T(1024)S(1)} collective-permute-done((f32[1024]{0:T(1024)S(1)}, f32[1024]{0:T(1024)S(1)}, u32[]{:S(2)}, u32[]{:S(2)}) %collective-permute-start.15) | collective-permute-done | bytes 4128 | tf_op jit(solution)/shard_map/ppermute | solution.py:32
  66.2 2.6 %collective-permute-done.17 = f32[1024]{0:T(1024)S(1)} collective-permute-done((f32[1024]{0:T(1024)S(1)}, f32[1024]{0:T(1024)S(1)}, u32[]{:S(2)}, u32[]{:S(2)}) %collective-permute-start.17) | collective-permute-done | bytes 4128 | tf_op jit(solution)/shard_map/ppermute | solution.py:42
  68.8 3.0 %collective-permute-start.18 = (f32[1024]{0:T(1024)S(1)}, f32[1024]{0:T(1024)S(1)}, u32[]{:S(2)}, u32[]{:S(2)}) collective-permute-start(f32[1024]{0:T(1024)S(1)} %add.153), channel_id=1, source_target_pairs={{0,64},{32,96},{64,0},{96,32},{128,192},{160,224},{192,128},{224,1... | collective-permute-start | bytes 12296 | tf_op jit(solution)/shard_map/ppermute | solution.py:42
  73.4 5.9 %collective-permute-start.19 = (f32[1024]{0:T(1024)S(1)}, f32[1024]{0:T(1024)S(1)}, u32[]{:S(2)}, u32[]{:S(2)}) collective-permute-start(f32[1024]{0:T(1024)S(1)} %add.154), channel_id=1, source_target_pairs={{0,128},{32,160},{64,192},{96,224},{128,0},{160,32},{192,64},{224,... | collective-permute-start | bytes 12296 | tf_op jit(solution)/shard_map/ppermute | solution.py:42
  79.3 4.3 %scatter_custom_fusion = s32[4096]{0:T(1024)S(1)} fusion(s32[1024]{0:T(1024)S(1)} %bitcast.19, s32[1024]{0:T(1024)S(1)} %iota.23, s32[]{:T(128)} %constant.15.clone.1), kind=kCustom, calls=%fused_computation.29 | custom fusion | bytes 16388 | tf_op jit(solution)/shard_map/scatter | solution.py:69
  83.7 2.7 %multiply_reduce_fusion.3 = f32[1024]{0:T(1024)S(1)} fusion(f32[1024,1024]{1,0:T(8,128)} %copy-done, f32[1024]{0:T(1024)S(1)} %add_divide_fusion.1), kind=kLoop, calls=%fused_computation.11 | loop fusion | flops 2096128 | bytes 4202496 | tf_op jit(solution)/shard_map/reduce_sum | solution.py:88
  86.5 12.2 %multiply_reduce_fusion.1 = (f32[4096]{0:T(1024)S(1)}, bf16[4096,1024]{1,0:T(8,128)(2,1)}) fusion(bf16[1024,1024]{1,0:T(8,128)(2,1)S(1)} %copy-done.3, s32[4096]{0:T(1024)S(1)} %scatter_custom_fusion), kind=kOutput, calls=%fused_computation.3 | convolution fusion | flops 8610902016 | bytes 10518528 | tf_op jit(solution)/shard_map/dot_general | solution.py:71
  102.4 3.1 %collective-permute-done.22 = f32[1024]{0:T(1024)S(1)} collective-permute-done((f32[1024]{0:T(1024)S(1)}, f32[1024]{0:T(1024)S(1)}, u32[]{:S(2)}, u32[]{:S(2)}) %collective-permute-start.22) | collective-permute-done | bytes 4128 | tf_op jit(solution)/shard_map/ppermute | solution.py:32
  106.1 1.8 %collective-permute-start.26 = (f32[1024]{0:T(1024)S(1)}, f32[1024]{0:T(1024)S(1)}, u32[]{:S(2)}, u32[]{:S(2)}) collective-permute-start(f32[1024]{0:T(1024)S(1)} %add_add_fusion), channel_id=1, source_target_pairs={{0,24},{1,25},{2,26},{3,27},{4,28},{5,29},{6,30},{7,31},{8,0},{9,1... | collective-permute-start | bytes 12296 | tf_op jit(solution)/shard_map/ppermute | solution.py:32
  109.7 3.3 %collective-permute-done.25 = f32[1024]{0:T(1024)S(1)} collective-permute-done((f32[1024]{0:T(1024)S(1)}, f32[1024]{0:T(1024)S(1)}, u32[]{:S(2)}, u32[]{:S(2)}) %collective-permute-start.25) | collective-permute-done | bytes 4128 | tf_op jit(solution)/shard_map/ppermute | solution.py:32
  113.7 2.5 %multiply_reduce_fusion.2 = f32[1024]{0:T(1024)S(1)} fusion(f32[1024,1024]{1,0:T(8,128)} %copy-done, f32[1024]{0:T(1024)S(1)} %add_divide_fusion), kind=kLoop, calls=%fused_computation.10 | loop fusion | flops 2096128 | bytes 4202496 | tf_op jit(solution)/shard_map/reduce_sum | solution.py:90
  116.3 7.2 %multiply_reduce_fusion = f32[64,128]{1,0:T(8,128)S(1)} fusion(bf16[64,128,1024]{2,1,0:T(8,128)(2,1)} %all-gather.2.cloned.1.call-done), kind=kLoop, calls=%fused_computation.2 | loop fusion | flops 25157632 | bytes 16809984 | tf_op jit(solution)/shard_map/reduce_sum | solution.py:16
  123.5 11.3 %multiply_exponential_fusion.1 = f32[64,64,128]{2,1,0:T(8,128)S(1)} fusion(bf16[64,64,1024]{2,1,0:T(8,128)(2,1)} %bitcast.18, bf16[64,128,1024]{2,1,0:T(8,128)(2,1)} %all-gather.2.cloned.1.call-done, f32[64,128]{1,0:T(8,128)S(1)} %add_rsqrt_fusion, f32[64,64]{1,0:T(8,128)S(1)} %rsqrt.34), kind=kOutput, calls=%fused_computation.19 | convolution fusion | flops 1075314688 | bytes 27312128 | tf_op jit(solution)/shard_map/gcd,gkd->gck/dot_general | solution.py:75
  134.7 2.8 %gather_fusion = f32[1024,128]{1,0:T(8,128)S(1)} fusion(f32[4096,128]{1,0:T(8,128)S(1)} %bitcast.17, s32[1024]{0:T(1024)S(1)} %broadcast_clamp_fusion), kind=kCustom, calls=%fused_computation | custom fusion | bytes 1052672 | tf_op jit(solution)/shard_map/gather | solution.py:77
  138.9 2.7 %collective-permute-done.27 = f32[2048]{0:T(1024)S(1)} collective-permute-done((f32[2048]{0:T(1024)S(1)}, f32[2048]{0:T(1024)S(1)}, u32[]{:S(2)}, u32[]{:S(2)}) %collective-permute-start.27) | collective-permute-done | bytes 8224 | tf_op jit(solution)/shard_map/ppermute | solution.py:42
  142.9 3.2 %collective-permute-done.28 = f32[2048]{0:T(1024)S(1)} collective-permute-done((f32[2048]{0:T(1024)S(1)}, f32[2048]{0:T(1024)S(1)}, u32[]{:S(2)}, u32[]{:S(2)}) %collective-permute-start.28) | collective-permute-done | bytes 8224 | tf_op jit(solution)/shard_map/ppermute | solution.py:42
  146.1 3.1 %collective-permute-start.29 = (f32[2048]{0:T(1024)S(1)}, f32[2048]{0:T(1024)S(1)}, u32[]{:S(2)}, u32[]{:S(2)}) collective-permute-start(f32[2048]{0:T(1024)S(1)} %add.170), channel_id=1, source_target_pairs={{0,128},{32,160},{64,192},{96,224},{128,0},{160,32},{192,64},{224,... | collective-permute-start | bytes 24584 | tf_op jit(solution)/shard_map/ppermute | solution.py:42
  149.2 4.5 %collective-permute-done.29 = f32[2048]{0:T(1024)S(1)} collective-permute-done((f32[2048]{0:T(1024)S(1)}, f32[2048]{0:T(1024)S(1)}, u32[]{:S(2)}, u32[]{:S(2)}) %collective-permute-start.29) | collective-permute-done | bytes 8224 | tf_op jit(solution)/shard_map/ppermute | solution.py:42
  153.7 4.1 %multiply_convert_fusion = bf16[1024,1024]{1,0:T(8,128)(2,1)} fusion(f32[1024,1024]{1,0:T(8,128)} %copy-done, f32[1024]{0:T(1024)S(1)} %get-tuple-element.3, f32[1024]{0:T(1024)S(1)} %add_divide_fusion), kind=kLoop, calls=%fused_computation.9 | loop fusion | flops 4194304 | bytes 6299648 | tf_op jit(solution)/shard_map/convert_element_type | solution.py:98
  (86 shorter events, 31.3 us)
Async XLA Ops:
  7.2 109.1 %all-gather.2.cloned.1.call-start = ((), (), s32[]{:S(2)}) async-start(), calls=%async_computation | async-start | bytes 17301504 | tf_op jit(solution)/shard_map/all_gather | solution.py:59
  15.0 49.8 %copy-start = (f32[1024,1024]{1,0:T(8,128)}, f32[1024,1024]{1,0:T(8,128)S(1)}, u32[]{:S(2)}) copy-start(f32[1024,1024]{1,0:T(8,128)S(1)} %get-tuple-element.7) | copy-start | bytes 12582916
  15.0 1.3 collective-permute-start
  16.3 4.6 %collective-permute-start.3 = (f32[1024]{0:T(1024)S(1)}, f32[1024]{0:T(1024)S(1)}, u32[]{:S(2)}, u32[]{:S(2)}) collective-permute-start(f32[1024]{0:T(1024)S(1)} %add.136), channel_id=1, source_target_pairs={{0,6},{1,7},{2,0},{3,1},{4,2},{5,3},{6,4},{7,5},{8,14},{9,15},{10,... | collective-permute-start | bytes 12296 | tf_op jit(solution)/shard_map/ppermute | solution.py:32
  19.3 5.1 %collective-permute-start.2 = (f32[1024]{0:T(1024)S(1)}, f32[1024]{0:T(1024)S(1)}, u32[]{:S(2)}, u32[]{:S(2)}) collective-permute-start(f32[1024]{0:T(1024)S(1)} %add.136), channel_id=1, source_target_pairs={{0,4},{1,5},{2,6},{3,7},{4,0},{5,1},{6,2},{7,3},{8,12},{9,13},{10,... | collective-permute-start | bytes 12296 | tf_op jit(solution)/shard_map/ppermute | solution.py:32
  19.9 4.8 %collective-permute-start.1 = (f32[1024]{0:T(1024)S(1)}, f32[1024]{0:T(1024)S(1)}, u32[]{:S(2)}, u32[]{:S(2)}) collective-permute-start(f32[1024]{0:T(1024)S(1)} %add.136), channel_id=1, source_target_pairs={{0,2},{1,3},{2,4},{3,5},{4,6},{5,7},{6,0},{7,1},{8,10},{9,11},{10,... | collective-permute-start | bytes 12296 | tf_op jit(solution)/shard_map/ppermute | solution.py:32
  24.7 4.5 %collective-permute-start.6 = (f32[1024]{0:T(1024)S(1)}, f32[1024]{0:T(1024)S(1)}, u32[]{:S(2)}, u32[]{:S(2)}) collective-permute-start(f32[1024]{0:T(1024)S(1)} %add_add_fusion.2), channel_id=1, source_target_pairs={{0,24},{1,25},{2,26},{3,27},{4,28},{5,29},{6,30},{7,31},{8,0},{9,1... | collective-permute-start | bytes 12296 | tf_op jit(solution)/shard_map/ppermute | solution.py:32
  27.5 5.3 %collective-permute-start.5 = (f32[1024]{0:T(1024)S(1)}, f32[1024]{0:T(1024)S(1)}, u32[]{:S(2)}, u32[]{:S(2)}) collective-permute-start(f32[1024]{0:T(1024)S(1)} %add_add_fusion.2), channel_id=1, source_target_pairs={{0,16},{1,17},{2,18},{3,19},{4,20},{5,21},{6,22},{7,23},{8,24},{9,... | collective-permute-start | bytes 12296 | tf_op jit(solution)/shard_map/ppermute | solution.py:32
  28.3 4.8 %collective-permute-start.4 = (f32[1024]{0:T(1024)S(1)}, f32[1024]{0:T(1024)S(1)}, u32[]{:S(2)}, u32[]{:S(2)}) collective-permute-start(f32[1024]{0:T(1024)S(1)} %add_add_fusion.2), channel_id=1, source_target_pairs={{0,8},{1,9},{2,10},{3,11},{4,12},{5,13},{6,14},{7,15},{8,16},{9,17... | collective-permute-start | bytes 12296 | tf_op jit(solution)/shard_map/ppermute | solution.py:32
  33.5 3.7 %collective-permute-start.7 = (f32[1024]{0:T(1024)S(1)}, f32[1024]{0:T(1024)S(1)}, u32[]{:S(2)}, u32[]{:S(2)}) collective-permute-start(f32[1024]{0:T(1024)S(1)} %multiply_reduce_fusion.6), channel_id=1, source_target_pairs={{0,32},{32,0},{64,96},{96,64},{128,160},{160,128},{192,224},{224,1... | collective-permute-start | bytes 12296 | tf_op jit(solution)/shard_map/ppermute | solution.py:42
  37.2 4.9 %collective-permute-start.8 = (f32[1024]{0:T(1024)S(1)}, f32[1024]{0:T(1024)S(1)}, u32[]{:S(2)}, u32[]{:S(2)}) collective-permute-start(f32[1024]{0:T(1024)S(1)} %add.143), channel_id=1, source_target_pairs={{0,64},{32,96},{64,0},{96,32},{128,192},{160,224},{192,128},{224,1... | collective-permute-start | bytes 12296 | tf_op jit(solution)/shard_map/ppermute | solution.py:42
  42.0 7.5 %collective-permute-start.9 = (f32[1024]{0:T(1024)S(1)}, f32[1024]{0:T(1024)S(1)}, u32[]{:S(2)}, u32[]{:S(2)}) collective-permute-start(f32[1024]{0:T(1024)S(1)} %add.144), channel_id=1, source_target_pairs={{0,128},{32,160},{64,192},{96,224},{128,0},{160,32},{192,64},{224,... | collective-permute-start | bytes 12296 | tf_op jit(solution)/shard_map/ppermute | solution.py:42
  49.9 1.3 collective-permute-start.10
  51.2 3.6 %collective-permute-start.13 = (f32[1024]{0:T(1024)S(1)}, f32[1024]{0:T(1024)S(1)}, u32[]{:S(2)}, u32[]{:S(2)}) collective-permute-start(f32[1024]{0:T(1024)S(1)} %add.146), channel_id=1, source_target_pairs={{0,6},{1,7},{2,0},{3,1},{4,2},{5,3},{6,4},{7,5},{8,14},{9,15},{10,... | collective-permute-start | bytes 12296 | tf_op jit(solution)/shard_map/ppermute | solution.py:32
  51.9 5.3 %collective-permute-start.12 = (f32[1024]{0:T(1024)S(1)}, f32[1024]{0:T(1024)S(1)}, u32[]{:S(2)}, u32[]{:S(2)}) collective-permute-start(f32[1024]{0:T(1024)S(1)} %add.146), channel_id=1, source_target_pairs={{0,4},{1,5},{2,6},{3,7},{4,0},{5,1},{6,2},{7,3},{8,12},{9,13},{10,... | collective-permute-start | bytes 12296 | tf_op jit(solution)/shard_map/ppermute | solution.py:32
  53.2 5.0 %collective-permute-start.11 = (f32[1024]{0:T(1024)S(1)}, f32[1024]{0:T(1024)S(1)}, u32[]{:S(2)}, u32[]{:S(2)}) collective-permute-start(f32[1024]{0:T(1024)S(1)} %add.146), channel_id=1, source_target_pairs={{0,2},{1,3},{2,4},{3,5},{4,6},{5,7},{6,0},{7,1},{8,10},{9,11},{10,... | collective-permute-start | bytes 12296 | tf_op jit(solution)/shard_map/ppermute | solution.py:32
  58.2 3.8 %collective-permute-start.16 = (f32[1024]{0:T(1024)S(1)}, f32[1024]{0:T(1024)S(1)}, u32[]{:S(2)}, u32[]{:S(2)}) collective-permute-start(f32[1024]{0:T(1024)S(1)} %add_add_fusion.1), channel_id=1, source_target_pairs={{0,24},{1,25},{2,26},{3,27},{4,28},{5,29},{6,30},{7,31},{8,0},{9,1... | collective-permute-start | bytes 12296 | tf_op jit(solution)/shard_map/ppermute | solution.py:32
  58.3 5.4 %collective-permute-start.15 = (f32[1024]{0:T(1024)S(1)}, f32[1024]{0:T(1024)S(1)}, u32[]{:S(2)}, u32[]{:S(2)}) collective-permute-start(f32[1024]{0:T(1024)S(1)} %add_add_fusion.1), channel_id=1, source_target_pairs={{0,16},{1,17},{2,18},{3,19},{4,20},{5,21},{6,22},{7,23},{8,24},{9,... | collective-permute-start | bytes 12296 | tf_op jit(solution)/shard_map/ppermute | solution.py:32
  59.8 5.0 %collective-permute-start.14 = (f32[1024]{0:T(1024)S(1)}, f32[1024]{0:T(1024)S(1)}, u32[]{:S(2)}, u32[]{:S(2)}) collective-permute-start(f32[1024]{0:T(1024)S(1)} %add_add_fusion.1), channel_id=1, source_target_pairs={{0,8},{1,9},{2,10},{3,11},{4,12},{5,13},{6,14},{7,15},{8,16},{9,17... | collective-permute-start | bytes 12296 | tf_op jit(solution)/shard_map/ppermute | solution.py:32
  65.2 3.7 %collective-permute-start.17 = (f32[1024]{0:T(1024)S(1)}, f32[1024]{0:T(1024)S(1)}, u32[]{:S(2)}, u32[]{:S(2)}) collective-permute-start(f32[1024]{0:T(1024)S(1)} %multiply_reduce_fusion.4), channel_id=1, source_target_pairs={{0,32},{32,0},{64,96},{96,64},{128,160},{160,128},{192,224},{224,1... | collective-permute-start | bytes 12296 | tf_op jit(solution)/shard_map/ppermute | solution.py:42
  68.8 4.6 %collective-permute-start.18 = (f32[1024]{0:T(1024)S(1)}, f32[1024]{0:T(1024)S(1)}, u32[]{:S(2)}, u32[]{:S(2)}) collective-permute-start(f32[1024]{0:T(1024)S(1)} %add.153), channel_id=1, source_target_pairs={{0,64},{32,96},{64,0},{96,32},{128,192},{160,224},{192,128},{224,1... | collective-permute-start | bytes 12296 | tf_op jit(solution)/shard_map/ppermute | solution.py:42
  73.4 10.2 %collective-permute-start.19 = (f32[1024]{0:T(1024)S(1)}, f32[1024]{0:T(1024)S(1)}, u32[]{:S(2)}, u32[]{:S(2)}) collective-permute-start(f32[1024]{0:T(1024)S(1)} %add.154), channel_id=1, source_target_pairs={{0,128},{32,160},{64,192},{96,224},{128,0},{160,32},{192,64},{224,... | collective-permute-start | bytes 12296 | tf_op jit(solution)/shard_map/ppermute | solution.py:42
  86.4 12.3 %collective-permute-start.20 = (f32[1024]{0:T(1024)S(1)}, f32[1024]{0:T(1024)S(1)}, u32[]{:S(2)}, u32[]{:S(2)}) collective-permute-start(f32[1024]{0:T(1024)S(1)} %multiply_reduce_fusion.3), channel_id=1, source_target_pairs={{0,1},{1,0},{2,3},{3,2},{4,5},{5,4},{6,7},{7,6},{8,9},{9,8},{10,11... | collective-permute-start | bytes 12296 | tf_op jit(solution)/shard_map/ppermute | solution.py:32
  98.8 3.6 %collective-permute-start.23 = (f32[1024]{0:T(1024)S(1)}, f32[1024]{0:T(1024)S(1)}, u32[]{:S(2)}, u32[]{:S(2)}) collective-permute-start(f32[1024]{0:T(1024)S(1)} %add.156), channel_id=1, source_target_pairs={{0,6},{1,7},{2,0},{3,1},{4,2},{5,3},{6,4},{7,5},{8,14},{9,15},{10,... | collective-permute-start | bytes 12296 | tf_op jit(solution)/shard_map/ppermute | solution.py:32
  100.3 5.2 %collective-permute-start.22 = (f32[1024]{0:T(1024)S(1)}, f32[1024]{0:T(1024)S(1)}, u32[]{:S(2)}, u32[]{:S(2)}) collective-permute-start(f32[1024]{0:T(1024)S(1)} %add.156), channel_id=1, source_target_pairs={{0,4},{1,5},{2,6},{3,7},{4,0},{5,1},{6,2},{7,3},{8,12},{9,13},{10,... | collective-permute-start | bytes 12296 | tf_op jit(solution)/shard_map/ppermute | solution.py:32
  101.3 4.8 %collective-permute-start.21 = (f32[1024]{0:T(1024)S(1)}, f32[1024]{0:T(1024)S(1)}, u32[]{:S(2)}, u32[]{:S(2)}) collective-permute-start(f32[1024]{0:T(1024)S(1)} %add.156), channel_id=1, source_target_pairs={{0,2},{1,3},{2,4},{3,5},{4,6},{5,7},{6,0},{7,1},{8,10},{9,11},{10,... | collective-permute-start | bytes 12296 | tf_op jit(solution)/shard_map/ppermute | solution.py:32
  106.1 3.6 %collective-permute-start.26 = (f32[1024]{0:T(1024)S(1)}, f32[1024]{0:T(1024)S(1)}, u32[]{:S(2)}, u32[]{:S(2)}) collective-permute-start(f32[1024]{0:T(1024)S(1)} %add_add_fusion), channel_id=1, source_target_pairs={{0,24},{1,25},{2,26},{3,27},{4,28},{5,29},{6,30},{7,31},{8,0},{9,1... | collective-permute-start | bytes 12296 | tf_op jit(solution)/shard_map/ppermute | solution.py:32
  107.9 5.1 %collective-permute-start.25 = (f32[1024]{0:T(1024)S(1)}, f32[1024]{0:T(1024)S(1)}, u32[]{:S(2)}, u32[]{:S(2)}) collective-permute-start(f32[1024]{0:T(1024)S(1)} %add_add_fusion), channel_id=1, source_target_pairs={{0,16},{1,17},{2,18},{3,19},{4,20},{5,21},{6,22},{7,23},{8,24},{9,... | collective-permute-start | bytes 12296 | tf_op jit(solution)/shard_map/ppermute | solution.py:32
  108.9 4.8 %collective-permute-start.24 = (f32[1024]{0:T(1024)S(1)}, f32[1024]{0:T(1024)S(1)}, u32[]{:S(2)}, u32[]{:S(2)}) collective-permute-start(f32[1024]{0:T(1024)S(1)} %add_add_fusion), channel_id=1, source_target_pairs={{0,8},{1,9},{2,10},{3,11},{4,12},{5,13},{6,14},{7,15},{8,16},{9,17... | collective-permute-start | bytes 12296 | tf_op jit(solution)/shard_map/ppermute | solution.py:32
  137.8 3.7 %collective-permute-start.27 = (f32[2048]{0:T(1024)S(1)}, f32[2048]{0:T(1024)S(1)}, u32[]{:S(2)}, u32[]{:S(2)}) collective-permute-start(f32[2048]{0:T(1024)S(1)} %pad_maximum_fusion), channel_id=1, source_target_pairs={{0,32},{32,0},{64,96},{96,64},{128,160},{160,128},{192,224},{224,1... | collective-permute-start | bytes 24584 | tf_op jit(solution)/shard_map/ppermute | solution.py:42
  141.5 4.6 %collective-permute-start.28 = (f32[2048]{0:T(1024)S(1)}, f32[2048]{0:T(1024)S(1)}, u32[]{:S(2)}, u32[]{:S(2)}) collective-permute-start(f32[2048]{0:T(1024)S(1)} %fusion.9), channel_id=1, source_target_pairs={{0,64},{32,96},{64,0},{96,32},{128,192},{160,224},{192,128},{224,1... | collective-permute-start | bytes 24584 | tf_op jit(solution)/shard_map/ppermute | solution.py:42
  146.1 7.6 %collective-permute-start.29 = (f32[2048]{0:T(1024)S(1)}, f32[2048]{0:T(1024)S(1)}, u32[]{:S(2)}, u32[]{:S(2)}) collective-permute-start(f32[2048]{0:T(1024)S(1)} %add.170), channel_id=1, source_target_pairs={{0,128},{32,160},{64,192},{96,224},{128,0},{160,32},{192,64},{224,... | collective-permute-start | bytes 24584 | tf_op jit(solution)/shard_map/ppermute | solution.py:42
  (4 other events, 53.4 us)
Sparse Core Ops, SparseCore 0:
  10.5 80.3 all-gather.1

commit v4 on v3

--- a/solution.py
+++ b/solution.py
@@ -91,9 +91,8 @@
         if step + 1 < ITERS:
             row_scale = 1.0 / cent_sum(row_part)
 
-    totals = cent_sum(jnp.concatenate([row_part, denom_part]))
-    row_total = totals[:pts_count]
-    denominator = totals[pts_count:]
+    row_total = cent_sum(row_part)
+    denominator = cent_sum(denom_part)
     row_scale = 1.0 / row_total
     assign = (expo * row_scale[:, None] * col_scale[None, :] * total_cent).astype(jnp.bfloat16)
     sub_assign = (total_sub * point_weights / denominator[:, None]).astype(jnp.bfloat16)

time: 166 us -> 164 us (0.988)
  starting transfers between devices: 45.9 us -> 54.7 us
  waiting for transfers between devices: 48.1 us -> 40.6 us
  other arithmetic: 23.1 us -> 18.5 us
    ppermute x9 -> x12, starting transfers between devices: 25.1 us -> 33.7 us  [cent_sum(): lax.ppermute(values, 'cent', [(i, i ^ bit) for i in range(count)])]
    ppermute x21, waiting for transfers between devices: 27 us -> 22.3 us  [dp_sum(): lax.ppermute(values, 'dp', shift_pairs(count, stride, size, step))]
    ppermute x9 -> x12, waiting for transfers between devices: 20.4 us -> 17.7 us  [cent_sum(): lax.ppermute(values, 'cent', [(i, i ^ bit) for i in range(count)])]
    reduce_sum x2, other arithmetic: 3.06 us -> 0.7 us  [shards(): col_part = jnp.sum(expo * row_scale[:, None], axis=0)]
    reduce_sum x3, other arithmetic: 3.24 us -> 1.06 us  [shards(): row_part = jnp.sum(expo * col_scale[None, :], axis=1)]
  transfers between devices with their start and end apart: 31 -> 34, of which waited for: 26 -> 25; matrix products, arithmetic and copies ran while one was open for 19% -> 32% of each run, Pallas kernels for 0% -> 0%
where the time goes in v4:
time: 164 us; the launch traced here: 162 us
  starting transfers between devices  54.7 us (33%)
  waiting for transfers between devices  40.6 us (25%)
  matrix products  26.8 us (16%)
  other arithmetic  18.5 us (11%)
  between operations  14.3 us (9%)
  local copies, waits for them, and re-layouts  7.24 us (4%)
    ppermute x12, starting transfers between devices, cent_sum(): lax.ppermute(values, 'cent', [(i, i ^ bit) for i in range(count)])  33.7 us
    ppermute x21, waiting for transfers between devices, dp_sum(): lax.ppermute(values, 'dp', shift_pairs(count, stride, size, step))  22.3 us
    ppermute x21, starting transfers between devices, dp_sum(): lax.ppermute(values, 'dp', shift_pairs(count, stride, size, step))  21 us
    ppermute x12, waiting for transfers between devices, cent_sum(): lax.ppermute(values, 'cent', [(i, i ^ bit) for i in range(count)])  17.7 us
    dot_general x1, matrix products, shards(): jnp.dot(pick, points, preferred_element_type=jnp.float32)  12.2 us
    reduce_sum x3, other arithmetic, inverse_norm(): return lax.rsqrt(jnp.mean(values * values, axis=-1) + EPS)  11.5 us
    dot_general x1, matrix products, shards(): jnp.einsum('gcd,gkd->gck', buffer, gathered, preferred_element_type=jnp.f...  11.3 us
    scatter x1, local copies, waits for them, and re-layouts, shards(): jnp.zeros((clusters * CAP,), jnp.int32).at[slot]  4.33 us
  transfers between devices with their start and end apart: 34, of which 25 were waited for; matrix products, arithmetic and copies ran while one was open for 32% of the time, Pallas kernels for 0%

profile of v4, /device:TPU:32, one launch (start us, length us, event | category | flops | bytes accessed | tf_op | source)
XLA Modules:
  0.0 162.2 jit_solution(3775461975852737764)
XLA Ops:
  7.9 2.2 %multiply_reduce_fusion.7 = f32[1024]{0:T(1024)S(1)} fusion(bf16[1024,1024]{1,0:T(8,128)(2,1)} %param.6), kind=kLoop, calls=%fused_computation.16 | loop fusion | flops 3144704 | bytes 2101248 | tf_op jit(solution)/shard_map/reduce_sum | solution.py:16
  10.1 2.1 %multiply_reduce_fusion.8 = f32[1024]{0:T(1024)S(1)} fusion(bf16[1024,1024]{1,0:T(8,128)(2,1)} %param.4), kind=kLoop, calls=%fused_computation.17 | loop fusion | flops 3144704 | bytes 2101248 | tf_op jit(solution)/shard_map/reduce_sum | solution.py:16
  12.2 2.7 %fusion.9 = (f32[1024]{0:T(1024)S(1)}, f32[1024,1024]{1,0:T(8,128)S(1)}) fusion(f32[1024]{0:T(1024)S(1)} %get-tuple-element.6, f32[1024]{0:T(1024)S(1)} %get-tuple-element.7, bf16[1024,1024]{1,0:T(8,128)(2,1)S(1)} %copy-done.3, bf16[1024,1024]{1,0:T(8,128)(2,1)S(1)} %copy-done.2), kind=kOutput, calls=%fused_computation.42 | convolution fusion | flops 2151676928 | bytes 8400896 | tf_op jit(solution)/shard_map/pd,kd->pk/dot_general | solution.py:81
  16.3 3.0 %collective-permute-start.3 = (f32[1024]{0:T(1024)S(1)}, f32[1024]{0:T(1024)S(1)}, u32[]{:S(2)}, u32[]{:S(2)}) collective-permute-start(f32[1024]{0:T(1024)S(1)} %add.145), channel_id=1, source_target_pairs={{0,6},{1,7},{2,0},{3,1},{4,2},{5,3},{6,4},{7,5},{8,14},{9,15},{10,... | collective-permute-start | bytes 12296 | tf_op jit(solution)/shard_map/ppermute | solution.py:32
  20.9 3.5 %collective-permute-done.2 = f32[1024]{0:T(1024)S(1)} collective-permute-done((f32[1024]{0:T(1024)S(1)}, f32[1024]{0:T(1024)S(1)}, u32[]{:S(2)}, u32[]{:S(2)}) %collective-permute-start.2) | collective-permute-done | bytes 4128 | tf_op jit(solution)/shard_map/ppermute | solution.py:32
  24.7 2.8 %collective-permute-start.6 = (f32[1024]{0:T(1024)S(1)}, f32[1024]{0:T(1024)S(1)}, u32[]{:S(2)}, u32[]{:S(2)}) collective-permute-start(f32[1024]{0:T(1024)S(1)} %add_add_fusion.2), channel_id=1, source_target_pairs={{0,24},{1,25},{2,26},{3,27},{4,28},{5,29},{6,30},{7,31},{8,0},{9,1... | collective-permute-start | bytes 12296 | tf_op jit(solution)/shard_map/ppermute | solution.py:32
  29.2 3.6 %collective-permute-done.5 = f32[1024]{0:T(1024)S(1)} collective-permute-done((f32[1024]{0:T(1024)S(1)}, f32[1024]{0:T(1024)S(1)}, u32[]{:S(2)}, u32[]{:S(2)}) %collective-permute-start.5) | collective-permute-done | bytes 4128 | tf_op jit(solution)/shard_map/ppermute | solution.py:32
  33.9 3.3 %collective-permute-done.7 = f32[1024]{0:T(1024)S(1)} collective-permute-done((f32[1024]{0:T(1024)S(1)}, f32[1024]{0:T(1024)S(1)}, u32[]{:S(2)}, u32[]{:S(2)}) %collective-permute-start.7) | collective-permute-done | bytes 4128 | tf_op jit(solution)/shard_map/ppermute | solution.py:42
  37.2 3.3 %collective-permute-start.8 = (f32[1024]{0:T(1024)S(1)}, f32[1024]{0:T(1024)S(1)}, u32[]{:S(2)}, u32[]{:S(2)}) collective-permute-start(f32[1024]{0:T(1024)S(1)} %add.152), channel_id=1, source_target_pairs={{0,64},{32,96},{64,0},{96,32},{128,192},{160,224},{192,128},{224,1... | collective-permute-start | bytes 12296 | tf_op jit(solution)/shard_map/ppermute | solution.py:42
  40.4 1.6 collective-permute-done.8
  42.0 5.9 %collective-permute-start.9 = (f32[1024]{0:T(1024)S(1)}, f32[1024]{0:T(1024)S(1)}, u32[]{:S(2)}, u32[]{:S(2)}) collective-permute-start(f32[1024]{0:T(1024)S(1)} %add.153), channel_id=1, source_target_pairs={{0,128},{32,160},{64,192},{96,224},{128,0},{160,32},{192,64},{224,... | collective-permute-start | bytes 12296 | tf_op jit(solution)/shard_map/ppermute | solution.py:42
  48.0 1.6 collective-permute-done.9
  54.8 2.4 %collective-permute-done.12 = f32[1024]{0:T(1024)S(1)} collective-permute-done((f32[1024]{0:T(1024)S(1)}, f32[1024]{0:T(1024)S(1)}, u32[]{:S(2)}, u32[]{:S(2)}) %collective-permute-start.12) | collective-permute-done | bytes 4128 | tf_op jit(solution)/shard_map/ppermute | solution.py:32
  62.0 1.7 %collective-permute-done.15 = f32[1024]{0:T(1024)S(1)} collective-permute-done((f32[1024]{0:T(1024)S(1)}, f32[1024]{0:T(1024)S(1)}, u32[]{:S(2)}, u32[]{:S(2)}) %collective-permute-start.15) | collective-permute-done | bytes 4128 | tf_op jit(solution)/shard_map/ppermute | solution.py:32
  66.2 2.6 %collective-permute-done.17 = f32[1024]{0:T(1024)S(1)} collective-permute-done((f32[1024]{0:T(1024)S(1)}, f32[1024]{0:T(1024)S(1)}, u32[]{:S(2)}, u32[]{:S(2)}) %collective-permute-start.17) | collective-permute-done | bytes 4128 | tf_op jit(solution)/shard_map/ppermute | solution.py:42
  68.8 3.0 %collective-permute-start.18 = (f32[1024]{0:T(1024)S(1)}, f32[1024]{0:T(1024)S(1)}, u32[]{:S(2)}, u32[]{:S(2)}) collective-permute-start(f32[1024]{0:T(1024)S(1)} %add.162), channel_id=1, source_target_pairs={{0,64},{32,96},{64,0},{96,32},{128,192},{160,224},{192,128},{224,1... | collective-permute-start | bytes 12296 | tf_op jit(solution)/shard_map/ppermute | solution.py:42
  71.8 1.6 collective-permute-done.18
  73.4 5.9 %collective-permute-start.19 = (f32[1024]{0:T(1024)S(1)}, f32[1024]{0:T(1024)S(1)}, u32[]{:S(2)}, u32[]{:S(2)}) collective-permute-start(f32[1024]{0:T(1024)S(1)} %add.163), channel_id=1, source_target_pairs={{0,128},{32,160},{64,192},{96,224},{128,0},{160,32},{192,64},{224,... | collective-permute-start | bytes 12296 | tf_op jit(solution)/shard_map/ppermute | solution.py:42
  81.4 4.3 %scatter_custom_fusion = s32[4096]{0:T(1024)S(1)} fusion(s32[1024]{0:T(1024)S(1)} %bitcast.20, s32[1024]{0:T(1024)S(1)} %iota.23, s32[]{:T(128)} %constant.5.clone.1), kind=kCustom, calls=%fused_computation.28 | custom fusion | bytes 16388 | tf_op jit(solution)/shard_map/scatter | solution.py:69
  85.8 1.7 %collective-permute-start.23 = (f32[1024]{0:T(1024)S(1)}, f32[1024]{0:T(1024)S(1)}, u32[]{:S(2)}, u32[]{:S(2)}) collective-permute-start(f32[1024]{0:T(1024)S(1)} %add.165), channel_id=1, source_target_pairs={{0,6},{1,7},{2,0},{3,1},{4,2},{5,3},{6,4},{7,5},{8,14},{9,15},{10,... | collective-permute-start | bytes 12296 | tf_op jit(solution)/shard_map/ppermute | solution.py:32
  88.5 12.2 %multiply_reduce_fusion.1 = (f32[4096]{0:T(1024)S(1)}, bf16[4096,1024]{1,0:T(8,128)(2,1)}) fusion(bf16[1024,1024]{1,0:T(8,128)(2,1)S(1)} %copy-done.4, s32[4096]{0:T(1024)S(1)} %scatter_custom_fusion), kind=kOutput, calls=%fused_computation.3 | convolution fusion | flops 8610902016 | bytes 10518528 | tf_op jit(solution)/shard_map/dot_general | solution.py:71
  100.7 1.8 %collective-permute-start.26 = (f32[1024]{0:T(1024)S(1)}, f32[1024]{0:T(1024)S(1)}, u32[]{:S(2)}, u32[]{:S(2)}) collective-permute-start(f32[1024]{0:T(1024)S(1)} %add_add_fusion), channel_id=1, source_target_pairs={{0,24},{1,25},{2,26},{3,27},{4,28},{5,29},{6,30},{7,31},{8,0},{9,1... | collective-permute-start | bytes 12296 | tf_op jit(solution)/shard_map/ppermute | solution.py:32
  104.4 3.3 %collective-permute-done.25 = f32[1024]{0:T(1024)S(1)} collective-permute-done((f32[1024]{0:T(1024)S(1)}, f32[1024]{0:T(1024)S(1)}, u32[]{:S(2)}, u32[]{:S(2)}) %collective-permute-start.25) | collective-permute-done | bytes 4128 | tf_op jit(solution)/shard_map/ppermute | solution.py:32
  109.8 2.5 %collective-permute-done.27 = f32[1024]{0:T(1024)S(1)} collective-permute-done((f32[1024]{0:T(1024)S(1)}, f32[1024]{0:T(1024)S(1)}, u32[]{:S(2)}, u32[]{:S(2)}) %collective-permute-start.27) | collective-permute-done | bytes 4128 | tf_op jit(solution)/shard_map/ppermute | solution.py:42
  112.4 2.9 %collective-permute-start.28 = (f32[1024]{0:T(1024)S(1)}, f32[1024]{0:T(1024)S(1)}, u32[]{:S(2)}, u32[]{:S(2)}) collective-permute-start(f32[1024]{0:T(1024)S(1)} %add.172), channel_id=1, source_target_pairs={{0,64},{32,96},{64,0},{96,32},{128,192},{160,224},{192,128},{224,1... | collective-permute-start | bytes 12296 | tf_op jit(solution)/shard_map/ppermute | solution.py:42
  115.3 7.2 %multiply_reduce_fusion = f32[64,128]{1,0:T(8,128)S(1)} fusion(bf16[64,128,1024]{2,1,0:T(8,128)(2,1)} %all-gather.2.cloned.1.call-done), kind=kLoop, calls=%fused_computation.2 | loop fusion | flops 25157632 | bytes 16809984 | tf_op jit(solution)/shard_map/reduce_sum | solution.py:16
  122.5 11.3 %multiply_exponential_fusion.1 = f32[64,64,128]{2,1,0:T(8,128)S(1)} fusion(bf16[64,64,1024]{2,1,0:T(8,128)(2,1)} %bitcast.19, bf16[64,128,1024]{2,1,0:T(8,128)(2,1)} %all-gather.2.cloned.1.call-done, f32[64,128]{1,0:T(8,128)S(1)} %add_rsqrt_fusion, f32[64,64]{1,0:T(8,128)S(1)} %rsqrt.34), kind=kOutput, calls=%fused_computation.19 | convolution fusion | flops 1075314688 | bytes 27312128 | tf_op jit(solution)/shard_map/gcd,gkd->gck/dot_general | solution.py:75
  133.8 2.8 %gather_fusion = f32[1024,128]{1,0:T(8,128)S(1)} fusion(f32[4096,128]{1,0:T(8,128)S(1)} %bitcast.18, s32[1024]{0:T(1024)S(1)} %broadcast_clamp_fusion), kind=kCustom, calls=%fused_computation | custom fusion | bytes 1052672 | tf_op jit(solution)/shard_map/gather | solution.py:77
  137.0 5.4 %collective-permute-start.29 = (f32[1024]{0:T(1024)S(1)}, f32[1024]{0:T(1024)S(1)}, u32[]{:S(2)}, u32[]{:S(2)}) collective-permute-start(f32[1024]{0:T(1024)S(1)} %add.173), channel_id=1, source_target_pairs={{0,128},{32,160},{64,192},{96,224},{128,0},{160,32},{192,64},{224,... | collective-permute-start | bytes 12296 | tf_op jit(solution)/shard_map/ppermute | solution.py:42
  144.5 2.4 %collective-permute-done.31 = f32[1024]{0:T(1024)S(1)} collective-permute-done((f32[1024]{0:T(1024)S(1)}, f32[1024]{0:T(1024)S(1)}, u32[]{:S(2)}, u32[]{:S(2)}) %collective-permute-start.31) | collective-permute-done | bytes 4128 | tf_op jit(solution)/shard_map/ppermute | solution.py:42
  146.9 3.1 %collective-permute-start.32 = (f32[1024]{0:T(1024)S(1)}, f32[1024]{0:T(1024)S(1)}, u32[]{:S(2)}, u32[]{:S(2)}) collective-permute-start(f32[1024]{0:T(1024)S(1)} %add.182), channel_id=1, source_target_pairs={{0,128},{32,160},{64,192},{96,224},{128,0},{160,32},{192,64},{224,... | collective-permute-start | bytes 12296 | tf_op jit(solution)/shard_map/ppermute | solution.py:42
  150.0 4.0 %multiply_convert_fusion = bf16[1024,1024]{1,0:T(8,128)(2,1)} fusion(f32[1024,1024]{1,0:T(8,128)} %copy-done, f32[1024]{0:T(1024)S(1)} %add_divide_fusion, f32[1024]{0:T(1024)S(1)} %add_divide_fusion.1), kind=kLoop, calls=%fused_computation.9 | loop fusion | flops 4194304 | bytes 6299648 | tf_op jit(solution)/shard_map/convert_element_type | solution.py:97
  (95 shorter events, 30.2 us)
Async XLA Ops:
  7.2 108.1 %all-gather.2.cloned.1.call-start = ((), (), s32[]{:S(2)}) async-start(), calls=%async_computation | async-start | bytes 17301504 | tf_op jit(solution)/shard_map/all_gather | solution.py:59
  16.3 4.6 %collective-permute-start.3 = (f32[1024]{0:T(1024)S(1)}, f32[1024]{0:T(1024)S(1)}, u32[]{:S(2)}, u32[]{:S(2)}) collective-permute-start(f32[1024]{0:T(1024)S(1)} %add.145), channel_id=1, source_target_pairs={{0,6},{1,7},{2,0},{3,1},{4,2},{5,3},{6,4},{7,5},{8,14},{9,15},{10,... | collective-permute-start | bytes 12296 | tf_op jit(solution)/shard_map/ppermute | solution.py:32
  19.3 5.1 %collective-permute-start.2 = (f32[1024]{0:T(1024)S(1)}, f32[1024]{0:T(1024)S(1)}, u32[]{:S(2)}, u32[]{:S(2)}) collective-permute-start(f32[1024]{0:T(1024)S(1)} %add.145), channel_id=1, source_target_pairs={{0,4},{1,5},{2,6},{3,7},{4,0},{5,1},{6,2},{7,3},{8,12},{9,13},{10,... | collective-permute-start | bytes 12296 | tf_op jit(solution)/shard_map/ppermute | solution.py:32
  19.9 4.8 %collective-permute-start.1 = (f32[1024]{0:T(1024)S(1)}, f32[1024]{0:T(1024)S(1)}, u32[]{:S(2)}, u32[]{:S(2)}) collective-permute-start(f32[1024]{0:T(1024)S(1)} %add.145), channel_id=1, source_target_pairs={{0,2},{1,3},{2,4},{3,5},{4,6},{5,7},{6,0},{7,1},{8,10},{9,11},{10,... | collective-permute-start | bytes 12296 | tf_op jit(solution)/shard_map/ppermute | solution.py:32
  24.7 4.5 %collective-permute-start.6 = (f32[1024]{0:T(1024)S(1)}, f32[1024]{0:T(1024)S(1)}, u32[]{:S(2)}, u32[]{:S(2)}) collective-permute-start(f32[1024]{0:T(1024)S(1)} %add_add_fusion.2), channel_id=1, source_target_pairs={{0,24},{1,25},{2,26},{3,27},{4,28},{5,29},{6,30},{7,31},{8,0},{9,1... | collective-permute-start | bytes 12296 | tf_op jit(solution)/shard_map/ppermute | solution.py:32
  27.5 5.3 %collective-permute-start.5 = (f32[1024]{0:T(1024)S(1)}, f32[1024]{0:T(1024)S(1)}, u32[]{:S(2)}, u32[]{:S(2)}) collective-permute-start(f32[1024]{0:T(1024)S(1)} %add_add_fusion.2), channel_id=1, source_target_pairs={{0,16},{1,17},{2,18},{3,19},{4,20},{5,21},{6,22},{7,23},{8,24},{9,... | collective-permute-start | bytes 12296 | tf_op jit(solution)/shard_map/ppermute | solution.py:32
  28.3 4.8 %collective-permute-start.4 = (f32[1024]{0:T(1024)S(1)}, f32[1024]{0:T(1024)S(1)}, u32[]{:S(2)}, u32[]{:S(2)}) collective-permute-start(f32[1024]{0:T(1024)S(1)} %add_add_fusion.2), channel_id=1, source_target_pairs={{0,8},{1,9},{2,10},{3,11},{4,12},{5,13},{6,14},{7,15},{8,16},{9,17... | collective-permute-start | bytes 12296 | tf_op jit(solution)/shard_map/ppermute | solution.py:32
  33.5 3.7 %collective-permute-start.7 = (f32[1024]{0:T(1024)S(1)}, f32[1024]{0:T(1024)S(1)}, u32[]{:S(2)}, u32[]{:S(2)}) collective-permute-start(f32[1024]{0:T(1024)S(1)} %multiply_reduce_fusion.6), channel_id=1, source_target_pairs={{0,32},{32,0},{64,96},{96,64},{128,160},{160,128},{192,224},{224,1... | collective-permute-start | bytes 12296 | tf_op jit(solution)/shard_map/ppermute | solution.py:42
  37.2 4.9 %collective-permute-start.8 = (f32[1024]{0:T(1024)S(1)}, f32[1024]{0:T(1024)S(1)}, u32[]{:S(2)}, u32[]{:S(2)}) collective-permute-start(f32[1024]{0:T(1024)S(1)} %add.152), channel_id=1, source_target_pairs={{0,64},{32,96},{64,0},{96,32},{128,192},{160,224},{192,128},{224,1... | collective-permute-start | bytes 12296 | tf_op jit(solution)/shard_map/ppermute | solution.py:42
  42.0 7.5 %collective-permute-start.9 = (f32[1024]{0:T(1024)S(1)}, f32[1024]{0:T(1024)S(1)}, u32[]{:S(2)}, u32[]{:S(2)}) collective-permute-start(f32[1024]{0:T(1024)S(1)} %add.153), channel_id=1, source_target_pairs={{0,128},{32,160},{64,192},{96,224},{128,0},{160,32},{192,64},{224,... | collective-permute-start | bytes 12296 | tf_op jit(solution)/shard_map/ppermute | solution.py:42
  51.2 3.6 %collective-permute-start.13 = (f32[1024]{0:T(1024)S(1)}, f32[1024]{0:T(1024)S(1)}, u32[]{:S(2)}, u32[]{:S(2)}) collective-permute-start(f32[1024]{0:T(1024)S(1)} %add.155), channel_id=1, source_target_pairs={{0,6},{1,7},{2,0},{3,1},{4,2},{5,3},{6,4},{7,5},{8,14},{9,15},{10,... | collective-permute-start | bytes 12296 | tf_op jit(solution)/shard_map/ppermute | solution.py:32
  51.9 5.3 %collective-permute-start.12 = (f32[1024]{0:T(1024)S(1)}, f32[1024]{0:T(1024)S(1)}, u32[]{:S(2)}, u32[]{:S(2)}) collective-permute-start(f32[1024]{0:T(1024)S(1)} %add.155), channel_id=1, source_target_pairs={{0,4},{1,5},{2,6},{3,7},{4,0},{5,1},{6,2},{7,3},{8,12},{9,13},{10,... | collective-permute-start | bytes 12296 | tf_op jit(solution)/shard_map/ppermute | solution.py:32
  53.2 5.0 %collective-permute-start.11 = (f32[1024]{0:T(1024)S(1)}, f32[1024]{0:T(1024)S(1)}, u32[]{:S(2)}, u32[]{:S(2)}) collective-permute-start(f32[1024]{0:T(1024)S(1)} %add.155), channel_id=1, source_target_pairs={{0,2},{1,3},{2,4},{3,5},{4,6},{5,7},{6,0},{7,1},{8,10},{9,11},{10,... | collective-permute-start | bytes 12296 | tf_op jit(solution)/shard_map/ppermute | solution.py:32
  58.2 3.8 %collective-permute-start.16 = (f32[1024]{0:T(1024)S(1)}, f32[1024]{0:T(1024)S(1)}, u32[]{:S(2)}, u32[]{:S(2)}) collective-permute-start(f32[1024]{0:T(1024)S(1)} %add_add_fusion.1), channel_id=1, source_target_pairs={{0,24},{1,25},{2,26},{3,27},{4,28},{5,29},{6,30},{7,31},{8,0},{9,1... | collective-permute-start | bytes 12296 | tf_op jit(solution)/shard_map/ppermute | solution.py:32
  58.3 5.4 %collective-permute-start.15 = (f32[1024]{0:T(1024)S(1)}, f32[1024]{0:T(1024)S(1)}, u32[]{:S(2)}, u32[]{:S(2)}) collective-permute-start(f32[1024]{0:T(1024)S(1)} %add_add_fusion.1), channel_id=1, source_target_pairs={{0,16},{1,17},{2,18},{3,19},{4,20},{5,21},{6,22},{7,23},{8,24},{9,... | collective-permute-start | bytes 12296 | tf_op jit(solution)/shard_map/ppermute | solution.py:32
  59.8 5.0 %collective-permute-start.14 = (f32[1024]{0:T(1024)S(1)}, f32[1024]{0:T(1024)S(1)}, u32[]{:S(2)}, u32[]{:S(2)}) collective-permute-start(f32[1024]{0:T(1024)S(1)} %add_add_fusion.1), channel_id=1, source_target_pairs={{0,8},{1,9},{2,10},{3,11},{4,12},{5,13},{6,14},{7,15},{8,16},{9,17... | collective-permute-start | bytes 12296 | tf_op jit(solution)/shard_map/ppermute | solution.py:32
  65.1 3.7 %collective-permute-start.17 = (f32[1024]{0:T(1024)S(1)}, f32[1024]{0:T(1024)S(1)}, u32[]{:S(2)}, u32[]{:S(2)}) collective-permute-start(f32[1024]{0:T(1024)S(1)} %multiply_reduce_fusion.4), channel_id=1, source_target_pairs={{0,32},{32,0},{64,96},{96,64},{128,160},{160,128},{192,224},{224,1... | collective-permute-start | bytes 12296 | tf_op jit(solution)/shard_map/ppermute | solution.py:42
  68.8 4.6 %collective-permute-start.18 = (f32[1024]{0:T(1024)S(1)}, f32[1024]{0:T(1024)S(1)}, u32[]{:S(2)}, u32[]{:S(2)}) collective-permute-start(f32[1024]{0:T(1024)S(1)} %add.162), channel_id=1, source_target_pairs={{0,64},{32,96},{64,0},{96,32},{128,192},{160,224},{192,128},{224,1... | collective-permute-start | bytes 12296 | tf_op jit(solution)/shard_map/ppermute | solution.py:42
  73.4 7.5 %collective-permute-start.19 = (f32[1024]{0:T(1024)S(1)}, f32[1024]{0:T(1024)S(1)}, u32[]{:S(2)}, u32[]{:S(2)}) collective-permute-start(f32[1024]{0:T(1024)S(1)} %add.163), channel_id=1, source_target_pairs={{0,128},{32,160},{64,192},{96,224},{128,0},{160,32},{192,64},{224,... | collective-permute-start | bytes 12296 | tf_op jit(solution)/shard_map/ppermute | solution.py:42
  81.3 4.5 %collective-permute-start.20 = (f32[1024]{0:T(1024)S(1)}, f32[1024]{0:T(1024)S(1)}, u32[]{:S(2)}, u32[]{:S(2)}) collective-permute-start(f32[1024]{0:T(1024)S(1)} %multiply_reduce_fusion.3), channel_id=1, source_target_pairs={{0,1},{1,0},{2,3},{3,2},{4,5},{5,4},{6,7},{7,6},{8,9},{9,8},{10,11... | collective-permute-start | bytes 12296 | tf_op jit(solution)/shard_map/ppermute | solution.py:32
  85.8 14.9 %collective-permute-start.23 = (f32[1024]{0:T(1024)S(1)}, f32[1024]{0:T(1024)S(1)}, u32[]{:S(2)}, u32[]{:S(2)}) collective-permute-start(f32[1024]{0:T(1024)S(1)} %add.165), channel_id=1, source_target_pairs={{0,6},{1,7},{2,0},{3,1},{4,2},{5,3},{6,4},{7,5},{8,14},{9,15},{10,... | collective-permute-start | bytes 12296 | tf_op jit(solution)/shard_map/ppermute | solution.py:32
  87.5 13.2 %collective-permute-start.22 = (f32[1024]{0:T(1024)S(1)}, f32[1024]{0:T(1024)S(1)}, u32[]{:S(2)}, u32[]{:S(2)}) collective-permute-start(f32[1024]{0:T(1024)S(1)} %add.165), channel_id=1, source_target_pairs={{0,4},{1,5},{2,6},{3,7},{4,0},{5,1},{6,2},{7,3},{8,12},{9,13},{10,... | collective-permute-start | bytes 12296 | tf_op jit(solution)/shard_map/ppermute | solution.py:32
  88.5 12.3 %collective-permute-start.21 = (f32[1024]{0:T(1024)S(1)}, f32[1024]{0:T(1024)S(1)}, u32[]{:S(2)}, u32[]{:S(2)}) collective-permute-start(f32[1024]{0:T(1024)S(1)} %add.165), channel_id=1, source_target_pairs={{0,2},{1,3},{2,4},{3,5},{4,6},{5,7},{6,0},{7,1},{8,10},{9,11},{10,... | collective-permute-start | bytes 12296 | tf_op jit(solution)/shard_map/ppermute | solution.py:32
  100.7 3.7 %collective-permute-start.26 = (f32[1024]{0:T(1024)S(1)}, f32[1024]{0:T(1024)S(1)}, u32[]{:S(2)}, u32[]{:S(2)}) collective-permute-start(f32[1024]{0:T(1024)S(1)} %add_add_fusion), channel_id=1, source_target_pairs={{0,24},{1,25},{2,26},{3,27},{4,28},{5,29},{6,30},{7,31},{8,0},{9,1... | collective-permute-start | bytes 12296 | tf_op jit(solution)/shard_map/ppermute | solution.py:32
  102.6 5.1 %collective-permute-start.25 = (f32[1024]{0:T(1024)S(1)}, f32[1024]{0:T(1024)S(1)}, u32[]{:S(2)}, u32[]{:S(2)}) collective-permute-start(f32[1024]{0:T(1024)S(1)} %add_add_fusion), channel_id=1, source_target_pairs={{0,16},{1,17},{2,18},{3,19},{4,20},{5,21},{6,22},{7,23},{8,24},{9,... | collective-permute-start | bytes 12296 | tf_op jit(solution)/shard_map/ppermute | solution.py:32
  103.5 4.8 %collective-permute-start.24 = (f32[1024]{0:T(1024)S(1)}, f32[1024]{0:T(1024)S(1)}, u32[]{:S(2)}, u32[]{:S(2)}) collective-permute-start(f32[1024]{0:T(1024)S(1)} %add_add_fusion), channel_id=1, source_target_pairs={{0,8},{1,9},{2,10},{3,11},{4,12},{5,13},{6,14},{7,15},{8,16},{9,17... | collective-permute-start | bytes 12296 | tf_op jit(solution)/shard_map/ppermute | solution.py:32
  108.7 3.7 %collective-permute-start.27 = (f32[1024]{0:T(1024)S(1)}, f32[1024]{0:T(1024)S(1)}, u32[]{:S(2)}, u32[]{:S(2)}) collective-permute-start(f32[1024]{0:T(1024)S(1)} %multiply_reduce_fusion.2), channel_id=1, source_target_pairs={{0,32},{32,0},{64,96},{96,64},{128,160},{160,128},{192,224},{224,1... | collective-permute-start | bytes 12296 | tf_op jit(solution)/shard_map/ppermute | solution.py:42
  112.4 24.6 %collective-permute-start.28 = (f32[1024]{0:T(1024)S(1)}, f32[1024]{0:T(1024)S(1)}, u32[]{:S(2)}, u32[]{:S(2)}) collective-permute-start(f32[1024]{0:T(1024)S(1)} %add.172), channel_id=1, source_target_pairs={{0,64},{32,96},{64,0},{96,32},{128,192},{160,224},{192,128},{224,1... | collective-permute-start | bytes 12296 | tf_op jit(solution)/shard_map/ppermute | solution.py:42
  136.8 5.6 %collective-permute-start.30 = (f32[1024]{0:T(1024)S(1)}, f32[1024]{0:T(1024)S(1)}, u32[]{:S(2)}, u32[]{:S(2)}) collective-permute-start(f32[1024]{0:T(1024)S(1)} %reduce_sum.119), channel_id=1, source_target_pairs={{0,32},{32,0},{64,96},{96,64},{128,160},{160,128},{192,224},{224,1... | collective-permute-start | bytes 12296 | tf_op jit(solution)/shard_map/ppermute | solution.py:42
  137.0 7.5 %collective-permute-start.29 = (f32[1024]{0:T(1024)S(1)}, f32[1024]{0:T(1024)S(1)}, u32[]{:S(2)}, u32[]{:S(2)}) collective-permute-start(f32[1024]{0:T(1024)S(1)} %add.173), channel_id=1, source_target_pairs={{0,128},{32,160},{64,192},{96,224},{128,0},{160,32},{192,64},{224,... | collective-permute-start | bytes 12296 | tf_op jit(solution)/shard_map/ppermute | solution.py:42
  142.4 4.5 %collective-permute-start.31 = (f32[1024]{0:T(1024)S(1)}, f32[1024]{0:T(1024)S(1)}, u32[]{:S(2)}, u32[]{:S(2)}) collective-permute-start(f32[1024]{0:T(1024)S(1)} %add.181), channel_id=1, source_target_pairs={{0,64},{32,96},{64,0},{96,32},{128,192},{160,224},{192,128},{224,1... | collective-permute-start | bytes 12296 | tf_op jit(solution)/shard_map/ppermute | solution.py:42
  146.9 7.5 %collective-permute-start.32 = (f32[1024]{0:T(1024)S(1)}, f32[1024]{0:T(1024)S(1)}, u32[]{:S(2)}, u32[]{:S(2)}) collective-permute-start(f32[1024]{0:T(1024)S(1)} %add.182), channel_id=1, source_target_pairs={{0,128},{32,160},{64,192},{96,224},{128,0},{160,32},{192,64},{224,... | collective-permute-start | bytes 12296 | tf_op jit(solution)/shard_map/ppermute | solution.py:42
  (8 other events, 153.8 us)
Sparse Core Ops, SparseCore 0:
  10.5 80.3 all-gather.1

commit v5 on v4

--- a/solution.py
+++ b/solution.py
@@ -1,6 +1,7 @@
 import jax
 import jax.numpy as jnp
 from jax import lax
+from jax.experimental import pallas as pl
 from jax.sharding import PartitionSpec as P
 
 CAP = 64
@@ -9,6 +10,39 @@
 
 EPS = 1e-06
 TAU = 0.05
+BLOCK = 8
+
+
+def level_two_kernel(rows_ref, subs_ref, out_ref):
+    width = rows_ref.shape[-1]
+    scale = 1.0 / (width * TAU)
+    ones = jnp.ones((8, width), jnp.bfloat16)
+    nt = (((1,), (1,)), ((), ()))
+    for g in range(rows_ref.shape[0]):
+        rows = rows_ref[g]
+        subs = subs_ref[g]
+        wide = rows.astype(jnp.float32)
+        inv_rows = lax.rsqrt(jnp.sum(wide * wide, axis=-1, keepdims=True) / width + EPS)
+        square = subs.astype(jnp.float32) * subs.astype(jnp.float32)
+        high = square.astype(jnp.bfloat16)
+        low = (square - high.astype(jnp.float32)).astype(jnp.bfloat16)
+        total = lax.dot_general(ones, high, nt, preferred_element_type=jnp.float32)
+        total = total + lax.dot_general(ones, low, nt, preferred_element_type=jnp.float32)
+        inv_u = lax.rsqrt(total[0:1, :] / width + EPS)
+        dots = lax.dot_general(rows, subs, nt, preferred_element_type=jnp.float32)
+        out_ref[g] = jnp.exp(dots * inv_rows * inv_u * scale)
+
+def level_two(rows, subs):
+    groups, cap, width = rows.shape
+    count = subs.shape[1]
+    return pl.pallas_call(
+        level_two_kernel,
+        grid=(groups // BLOCK,),
+        in_specs=[pl.BlockSpec((BLOCK, cap, width), lambda i: (i, 0, 0)),
+                  pl.BlockSpec((BLOCK, count, width), lambda i: (i, 0, 0))],
+        out_specs=pl.BlockSpec((BLOCK, cap, count), lambda i: (i, 0, 0)),
+        out_shape=jax.ShapeDtypeStruct((groups, cap, count), jnp.float32),
+    )(rows, subs)
 
 
 def inverse_norm(rows):
@@ -70,10 +104,7 @@
     pick = (source[:, None] == lax.broadcasted_iota(jnp.int32, (clusters * CAP, pts_count), 1)).astype(points.dtype)
     buffer = jnp.dot(pick, points, preferred_element_type=jnp.float32).astype(points.dtype)
     buffer = buffer.reshape(clusters, CAP, width)
-    inv_rows = inverse_norm(buffer)
-    inv_u = inverse_norm(gathered)
-    dots = jnp.einsum("gcd,gkd->gck", buffer, gathered, preferred_element_type=jnp.float32)
-    weights = jnp.exp(dots * inv_rows[..., None] * inv_u[:, None, :] * scale_two)
+    weights = level_two(buffer, gathered)
     point_weights = weights.reshape(clusters * CAP, sub_dev)[slot]
     denom_part = jnp.sum(point_weights, axis=1)
 

time: 164 us -> 166 us (1.012)
  Pallas kernels: 0 us -> 18.2 us
  matrix products: 26.8 us -> 14.8 us
  other arithmetic: 18.5 us -> 13.5 us
    pallas_call x0 -> x1, Pallas kernels: none -> 18.2 us  [level_two(): pl.pallas_call(level_two_kernel, grid=(groups // BLOCK,), in_specs=[pl.Bl...]
    dot_general x1 -> x0, matrix products: 11.3 us -> none  [shards(): jnp.einsum('gcd,gkd->gck', buffer, gathered, preferred_element_type=jnp.f...]
    reduce_sum x3 -> x2, other arithmetic: 11.5 us -> 4.29 us  [inverse_norm(): return lax.rsqrt(jnp.mean(values * values, axis=-1) + EPS)]
    reduce_sum x3, other arithmetic: 1.06 us -> 3.24 us  [shards(): row_part = jnp.sum(expo * col_scale[None, :], axis=1)]
    ppermute x12, waiting for transfers between devices: 17.7 us -> 15.7 us  [cent_sum(): lax.ppermute(values, 'cent', [(i, i ^ bit) for i in range(count)])]
  transfers between devices with their start and end apart: 34 -> 34, of which waited for: 25 -> 26; matrix products, arithmetic and copies ran while one was open for 32% -> 22% of each run, Pallas kernels for 0% -> 11%
where the time goes in v5:
time: 166 us; the launch traced here: 164 us
  starting transfers between devices  54.8 us (33%)
  waiting for transfers between devices  39.7 us (24%)
  Pallas kernels  18.2 us (11%)
  matrix products  14.8 us (9%)
  between operations  14.2 us (9%)
  other arithmetic  13.5 us (8%)
  local copies, waits for them, and re-layouts  8.75 us (5%)
    ppermute x12, starting transfers between devices, cent_sum(): lax.ppermute(values, 'cent', [(i, i ^ bit) for i in range(count)])  33.9 us
    ppermute x21, waiting for transfers between devices, dp_sum(): lax.ppermute(values, 'dp', shift_pairs(count, stride, size, step))  23.3 us
    ppermute x21, starting transfers between devices, dp_sum(): lax.ppermute(values, 'dp', shift_pairs(count, stride, size, step))  20.8 us
    pallas_call x1, Pallas kernels, level_two(): pl.pallas_call(level_two_kernel, grid=(groups // BLOCK,), in_specs=[pl.Bl...  18.2 us
    ppermute x12, waiting for transfers between devices, cent_sum(): lax.ppermute(values, 'cent', [(i, i ^ bit) for i in range(count)])  15.7 us
    dot_general x1, matrix products, shards(): jnp.dot(pick, points, preferred_element_type=jnp.float32)  11.5 us
    gather x1, local copies, waits for them, and re-layouts, shards(): point_weights = weights.reshape(clusters * CAP, sub_dev)[slot]  4.4 us
    scatter x1, local copies, waits for them, and re-layouts, shards(): jnp.zeros((clusters * CAP,), jnp.int32).at[slot]  4.33 us
  transfers between devices with their start and end apart: 34, of which 26 were waited for; matrix products, arithmetic and copies ran while one was open for 22% of the time, Pallas kernels for 11%

profile of v5, /device:TPU:32, one launch (start us, length us, event | category | flops | bytes accessed | tf_op | source)
XLA Modules:
  0.0 164.0 jit_solution(9691304619843629964)
XLA Ops:
  7.9 2.2 %multiply_reduce_fusion.5 = f32[1024]{0:T(1024)S(1)} fusion(bf16[1024,1024]{1,0:T(8,128)(2,1)} %param.6), kind=kLoop, calls=%fused_computation.14 | loop fusion | flops 3144704 | bytes 2101248 | tf_op jit(solution)/shard_map/reduce_sum | solution.py:50
  10.1 2.1 %multiply_reduce_fusion.6 = f32[1024]{0:T(1024)S(1)} fusion(bf16[1024,1024]{1,0:T(8,128)(2,1)} %param.4), kind=kLoop, calls=%fused_computation.15 | loop fusion | flops 3144704 | bytes 2101248 | tf_op jit(solution)/shard_map/reduce_sum | solution.py:50
  12.2 2.7 %fusion.9 = (f32[1024]{0:T(1024)S(1)}, f32[1024,1024]{1,0:T(8,128)S(1)}) fusion(f32[1024]{0:T(1024)S(1)} %get-tuple-element.4, f32[1024]{0:T(1024)S(1)} %get-tuple-element.5, bf16[1024,1024]{1,0:T(8,128)(2,1)S(1)} %copy-done.2, bf16[1024,1024]{1,0:T(8,128)(2,1)S(1)} %copy-done.1), kind=kOutput, calls=%fused_computation.37 | convolution fusion | flops 2151676928 | bytes 8400896 | tf_op jit(solution)/shard_map/pd,kd->pk/dot_general | solution.py:112
  16.3 3.0 %collective-permute-start.3 = (f32[1024]{0:T(1024)S(1)}, f32[1024]{0:T(1024)S(1)}, u32[]{:S(2)}, u32[]{:S(2)}) collective-permute-start(f32[1024]{0:T(1024)S(1)} %add.124), channel_id=1, source_target_pairs={{0,6},{1,7},{2,0},{3,1},{4,2},{5,3},{6,4},{7,5},{8,14},{9,15},{10,... | collective-permute-start | bytes 12296 | tf_op jit(solution)/shard_map/ppermute | solution.py:66
  20.9 3.5 %collective-permute-done.2 = f32[1024]{0:T(1024)S(1)} collective-permute-done((f32[1024]{0:T(1024)S(1)}, f32[1024]{0:T(1024)S(1)}, u32[]{:S(2)}, u32[]{:S(2)}) %collective-permute-start.2) | collective-permute-done | bytes 4128 | tf_op jit(solution)/shard_map/ppermute | solution.py:66
  24.7 2.8 %collective-permute-start.6 = (f32[1024]{0:T(1024)S(1)}, f32[1024]{0:T(1024)S(1)}, u32[]{:S(2)}, u32[]{:S(2)}) collective-permute-start(f32[1024]{0:T(1024)S(1)} %add_add_fusion.2), channel_id=1, source_target_pairs={{0,24},{1,25},{2,26},{3,27},{4,28},{5,29},{6,30},{7,31},{8,0},{9,1... | collective-permute-start | bytes 12296 | tf_op jit(solution)/shard_map/ppermute | solution.py:66
  29.2 3.6 %collective-permute-done.5 = f32[1024]{0:T(1024)S(1)} collective-permute-done((f32[1024]{0:T(1024)S(1)}, f32[1024]{0:T(1024)S(1)}, u32[]{:S(2)}, u32[]{:S(2)}) %collective-permute-start.5) | collective-permute-done | bytes 4128 | tf_op jit(solution)/shard_map/ppermute | solution.py:66
  33.9 3.3 %collective-permute-done.7 = f32[1024]{0:T(1024)S(1)} collective-permute-done((f32[1024]{0:T(1024)S(1)}, f32[1024]{0:T(1024)S(1)}, u32[]{:S(2)}, u32[]{:S(2)}) %collective-permute-start.7) | collective-permute-done | bytes 4128 | tf_op jit(solution)/shard_map/ppermute | solution.py:76
  37.2 3.3 %collective-permute-start.8 = (f32[1024]{0:T(1024)S(1)}, f32[1024]{0:T(1024)S(1)}, u32[]{:S(2)}, u32[]{:S(2)}) collective-permute-start(f32[1024]{0:T(1024)S(1)} %add.131), channel_id=1, source_target_pairs={{0,64},{32,96},{64,0},{96,32},{128,192},{160,224},{192,128},{224,1... | collective-permute-start | bytes 12296 | tf_op jit(solution)/shard_map/ppermute | solution.py:76
  40.4 1.6 collective-permute-done.8
  42.0 5.9 %collective-permute-start.9 = (f32[1024]{0:T(1024)S(1)}, f32[1024]{0:T(1024)S(1)}, u32[]{:S(2)}, u32[]{:S(2)}) collective-permute-start(f32[1024]{0:T(1024)S(1)} %add.132), channel_id=1, source_target_pairs={{0,128},{32,160},{64,192},{96,224},{128,0},{160,32},{192,64},{224,... | collective-permute-start | bytes 12296 | tf_op jit(solution)/shard_map/ppermute | solution.py:76
  48.0 1.6 collective-permute-done.9
  54.8 2.4 %collective-permute-done.12 = f32[1024]{0:T(1024)S(1)} collective-permute-done((f32[1024]{0:T(1024)S(1)}, f32[1024]{0:T(1024)S(1)}, u32[]{:S(2)}, u32[]{:S(2)}) %collective-permute-start.12) | collective-permute-done | bytes 4128 | tf_op jit(solution)/shard_map/ppermute | solution.py:66
  62.0 1.7 %collective-permute-done.15 = f32[1024]{0:T(1024)S(1)} collective-permute-done((f32[1024]{0:T(1024)S(1)}, f32[1024]{0:T(1024)S(1)}, u32[]{:S(2)}, u32[]{:S(2)}) %collective-permute-start.15) | collective-permute-done | bytes 4128 | tf_op jit(solution)/shard_map/ppermute | solution.py:66
  66.2 2.6 %collective-permute-done.17 = f32[1024]{0:T(1024)S(1)} collective-permute-done((f32[1024]{0:T(1024)S(1)}, f32[1024]{0:T(1024)S(1)}, u32[]{:S(2)}, u32[]{:S(2)}) %collective-permute-start.17) | collective-permute-done | bytes 4128 | tf_op jit(solution)/shard_map/ppermute | solution.py:76
  68.8 3.0 %collective-permute-start.18 = (f32[1024]{0:T(1024)S(1)}, f32[1024]{0:T(1024)S(1)}, u32[]{:S(2)}, u32[]{:S(2)}) collective-permute-start(f32[1024]{0:T(1024)S(1)} %add.141), channel_id=1, source_target_pairs={{0,64},{32,96},{64,0},{96,32},{128,192},{160,224},{192,128},{224,1... | collective-permute-start | bytes 12296 | tf_op jit(solution)/shard_map/ppermute | solution.py:76
  71.8 1.6 collective-permute-done.18
  73.4 5.9 %collective-permute-start.19 = (f32[1024]{0:T(1024)S(1)}, f32[1024]{0:T(1024)S(1)}, u32[]{:S(2)}, u32[]{:S(2)}) collective-permute-start(f32[1024]{0:T(1024)S(1)} %add.142), channel_id=1, source_target_pairs={{0,128},{32,160},{64,192},{96,224},{128,0},{160,32},{192,64},{224,... | collective-permute-start | bytes 12296 | tf_op jit(solution)/shard_map/ppermute | solution.py:76
  79.3 1.6 collective-permute-done.19
  82.6 1.6 collective-permute-start.23
  86.4 2.9 %collective-permute-done.22 = f32[1024]{0:T(1024)S(1)} collective-permute-done((f32[1024]{0:T(1024)S(1)}, f32[1024]{0:T(1024)S(1)}, u32[]{:S(2)}, u32[]{:S(2)}) %collective-permute-start.22) | collective-permute-done | bytes 4128 | tf_op jit(solution)/shard_map/ppermute | solution.py:66
  90.0 1.8 %collective-permute-start.26 = (f32[1024]{0:T(1024)S(1)}, f32[1024]{0:T(1024)S(1)}, u32[]{:S(2)}, u32[]{:S(2)}) collective-permute-start(f32[1024]{0:T(1024)S(1)} %add_add_fusion), channel_id=1, source_target_pairs={{0,24},{1,25},{2,26},{3,27},{4,28},{5,29},{6,30},{7,31},{8,0},{9,1... | collective-permute-start | bytes 12296 | tf_op jit(solution)/shard_map/ppermute | solution.py:66
  92.7 4.3 %scatter_custom_fusion = s32[4096]{0:T(1024)S(1)} fusion(s32[1024]{0:T(1024)S(1)} %bitcast.18, s32[1024]{0:T(1024)S(1)} %iota.23, s32[]{:T(128)} %constant.8.clone.1), kind=kCustom, calls=%fused_computation.23 | custom fusion | bytes 16388 | tf_op jit(solution)/shard_map/scatter | solution.py:103
  97.5 2.5 %multiply_reduce_fusion = f32[1024]{0:T(1024)S(1)} fusion(f32[1024,1024]{1,0:T(8,128)} %copy-done, f32[1024]{0:T(1024)S(1)} %add_divide_fusion.1), kind=kLoop, calls=%fused_computation.8 | loop fusion | flops 2096128 | bytes 4202496 | tf_op jit(solution)/shard_map/reduce_sum | solution.py:121
  101.3 11.5 %fusion.2 = bf16[4096,1024]{1,0:T(8,128)(2,1)} fusion(bf16[1024,1024]{1,0:T(8,128)(2,1)S(1)} %copy-done.3, s32[4096]{0:T(1024)S(1)} %scatter_custom_fusion), kind=kOutput, calls=%fused_computation.5 | convolution fusion | flops 8598323200 | bytes 10502144 | tf_op jit(solution)/shard_map/dot_general | solution.py:105
  112.8 2.0 %collective-permute-start.28 = (f32[1024]{0:T(1024)S(1)}, f32[1024]{0:T(1024)S(1)}, u32[]{:S(2)}, u32[]{:S(2)}) collective-permute-start(f32[1024]{0:T(1024)S(1)} %add.151), channel_id=1, source_target_pairs={{0,64},{32,96},{64,0},{96,32},{128,192},{160,224},{192,128},{224,1... | collective-permute-start | bytes 12296 | tf_op jit(solution)/shard_map/ppermute | solution.py:76
  114.9 18.2 %shard_map.59 = f32[64,64,128]{2,1,0:T(8,128)} custom-call(bf16[64,64,1024]{2,1,0:T(8,128)(2,1)} %bitcast.17, bf16[64,128,1024]{2,1,0:T(8,128)(2,1)} %all-gather.2.cloned.1.call-done.subs_ref), custom_call_target="tpu_custom_call" | custom-call | tf_op jit(solution)/shard_map/pallas_call | solution.py:38
  133.1 4.4 %gather_fusion = f32[1024,128]{1,0:T(8,128)S(1)} fusion(f32[4096,128]{1,0:T(8,128)} %bitcast.16, s32[1024]{0:T(1024)S(1)} %broadcast_clamp_fusion), kind=kCustom, calls=%fused_computation | custom fusion | bytes 1052672 | tf_op jit(solution)/shard_map/gather | solution.py:108
  137.7 2.0 %collective-permute-start.30 = (f32[1024]{0:T(1024)S(1)}, f32[1024]{0:T(1024)S(1)}, u32[]{:S(2)}, u32[]{:S(2)}) collective-permute-start(f32[1024]{0:T(1024)S(1)} %reduce_sum.99), channel_id=1, source_target_pairs={{0,32},{32,0},{64,96},{96,64},{128,160},{160,128},{192,224},{224,1... | collective-permute-start | bytes 12296 | tf_op jit(solution)/shard_map/ppermute | solution.py:76
  139.7 4.5 %collective-permute-start.29 = (f32[1024]{0:T(1024)S(1)}, f32[1024]{0:T(1024)S(1)}, u32[]{:S(2)}, u32[]{:S(2)}) collective-permute-start(f32[1024]{0:T(1024)S(1)} %add.152), channel_id=1, source_target_pairs={{0,128},{32,160},{64,192},{96,224},{128,0},{160,32},{192,64},{224,... | collective-permute-start | bytes 12296 | tf_op jit(solution)/shard_map/ppermute | solution.py:76
  148.7 3.1 %collective-permute-start.32 = (f32[1024]{0:T(1024)S(1)}, f32[1024]{0:T(1024)S(1)}, u32[]{:S(2)}, u32[]{:S(2)}) collective-permute-start(f32[1024]{0:T(1024)S(1)} %add.157), channel_id=1, source_target_pairs={{0,128},{32,160},{64,192},{96,224},{128,0},{160,32},{192,64},{224,... | collective-permute-start | bytes 12296 | tf_op jit(solution)/shard_map/ppermute | solution.py:76
  151.8 4.0 %multiply_convert_fusion = bf16[1024,1024]{1,0:T(8,128)(2,1)} fusion(f32[1024,1024]{1,0:T(8,128)} %copy-done, f32[1024]{0:T(1024)S(1)} %add_divide_fusion, f32[1024]{0:T(1024)S(1)} %add_divide_fusion.1), kind=kLoop, calls=%fused_computation.7 | loop fusion | flops 4194304 | bytes 6299648 | tf_op jit(solution)/shard_map/convert_element_type | solution.py:128
  (89 shorter events, 32.5 us)
Async XLA Ops:
  7.2 107.7 %all-gather.2.cloned.1.call-start = ((), (), s32[]{:S(2)}) async-start(), calls=%async_computation | async-start | bytes 17301504 | tf_op jit(solution)/shard_map/all_gather | solution.py:93
  15.0 1.3 collective-permute-start
  16.3 4.6 %collective-permute-start.3 = (f32[1024]{0:T(1024)S(1)}, f32[1024]{0:T(1024)S(1)}, u32[]{:S(2)}, u32[]{:S(2)}) collective-permute-start(f32[1024]{0:T(1024)S(1)} %add.124), channel_id=1, source_target_pairs={{0,6},{1,7},{2,0},{3,1},{4,2},{5,3},{6,4},{7,5},{8,14},{9,15},{10,... | collective-permute-start | bytes 12296 | tf_op jit(solution)/shard_map/ppermute | solution.py:66
  19.3 5.1 %collective-permute-start.2 = (f32[1024]{0:T(1024)S(1)}, f32[1024]{0:T(1024)S(1)}, u32[]{:S(2)}, u32[]{:S(2)}) collective-permute-start(f32[1024]{0:T(1024)S(1)} %add.124), channel_id=1, source_target_pairs={{0,4},{1,5},{2,6},{3,7},{4,0},{5,1},{6,2},{7,3},{8,12},{9,13},{10,... | collective-permute-start | bytes 12296 | tf_op jit(solution)/shard_map/ppermute | solution.py:66
  19.9 4.8 %collective-permute-start.1 = (f32[1024]{0:T(1024)S(1)}, f32[1024]{0:T(1024)S(1)}, u32[]{:S(2)}, u32[]{:S(2)}) collective-permute-start(f32[1024]{0:T(1024)S(1)} %add.124), channel_id=1, source_target_pairs={{0,2},{1,3},{2,4},{3,5},{4,6},{5,7},{6,0},{7,1},{8,10},{9,11},{10,... | collective-permute-start | bytes 12296 | tf_op jit(solution)/shard_map/ppermute | solution.py:66
  24.7 4.5 %collective-permute-start.6 = (f32[1024]{0:T(1024)S(1)}, f32[1024]{0:T(1024)S(1)}, u32[]{:S(2)}, u32[]{:S(2)}) collective-permute-start(f32[1024]{0:T(1024)S(1)} %add_add_fusion.2), channel_id=1, source_target_pairs={{0,24},{1,25},{2,26},{3,27},{4,28},{5,29},{6,30},{7,31},{8,0},{9,1... | collective-permute-start | bytes 12296 | tf_op jit(solution)/shard_map/ppermute | solution.py:66
  27.5 5.3 %collective-permute-start.5 = (f32[1024]{0:T(1024)S(1)}, f32[1024]{0:T(1024)S(1)}, u32[]{:S(2)}, u32[]{:S(2)}) collective-permute-start(f32[1024]{0:T(1024)S(1)} %add_add_fusion.2), channel_id=1, source_target_pairs={{0,16},{1,17},{2,18},{3,19},{4,20},{5,21},{6,22},{7,23},{8,24},{9,... | collective-permute-start | bytes 12296 | tf_op jit(solution)/shard_map/ppermute | solution.py:66
  28.3 4.8 %collective-permute-start.4 = (f32[1024]{0:T(1024)S(1)}, f32[1024]{0:T(1024)S(1)}, u32[]{:S(2)}, u32[]{:S(2)}) collective-permute-start(f32[1024]{0:T(1024)S(1)} %add_add_fusion.2), channel_id=1, source_target_pairs={{0,8},{1,9},{2,10},{3,11},{4,12},{5,13},{6,14},{7,15},{8,16},{9,17... | collective-permute-start | bytes 12296 | tf_op jit(solution)/shard_map/ppermute | solution.py:66
  33.5 3.7 %collective-permute-start.7 = (f32[1024]{0:T(1024)S(1)}, f32[1024]{0:T(1024)S(1)}, u32[]{:S(2)}, u32[]{:S(2)}) collective-permute-start(f32[1024]{0:T(1024)S(1)} %multiply_reduce_fusion.4), channel_id=1, source_target_pairs={{0,32},{32,0},{64,96},{96,64},{128,160},{160,128},{192,224},{224,1... | collective-permute-start | bytes 12296 | tf_op jit(solution)/shard_map/ppermute | solution.py:76
  37.2 4.9 %collective-permute-start.8 = (f32[1024]{0:T(1024)S(1)}, f32[1024]{0:T(1024)S(1)}, u32[]{:S(2)}, u32[]{:S(2)}) collective-permute-start(f32[1024]{0:T(1024)S(1)} %add.131), channel_id=1, source_target_pairs={{0,64},{32,96},{64,0},{96,32},{128,192},{160,224},{192,128},{224,1... | collective-permute-start | bytes 12296 | tf_op jit(solution)/shard_map/ppermute | solution.py:76
  42.0 7.5 %collective-permute-start.9 = (f32[1024]{0:T(1024)S(1)}, f32[1024]{0:T(1024)S(1)}, u32[]{:S(2)}, u32[]{:S(2)}) collective-permute-start(f32[1024]{0:T(1024)S(1)} %add.132), channel_id=1, source_target_pairs={{0,128},{32,160},{64,192},{96,224},{128,0},{160,32},{192,64},{224,... | collective-permute-start | bytes 12296 | tf_op jit(solution)/shard_map/ppermute | solution.py:76
  51.2 3.6 %collective-permute-start.13 = (f32[1024]{0:T(1024)S(1)}, f32[1024]{0:T(1024)S(1)}, u32[]{:S(2)}, u32[]{:S(2)}) collective-permute-start(f32[1024]{0:T(1024)S(1)} %add.134), channel_id=1, source_target_pairs={{0,6},{1,7},{2,0},{3,1},{4,2},{5,3},{6,4},{7,5},{8,14},{9,15},{10,... | collective-permute-start | bytes 12296 | tf_op jit(solution)/shard_map/ppermute | solution.py:66
  51.9 5.3 %collective-permute-start.12 = (f32[1024]{0:T(1024)S(1)}, f32[1024]{0:T(1024)S(1)}, u32[]{:S(2)}, u32[]{:S(2)}) collective-permute-start(f32[1024]{0:T(1024)S(1)} %add.134), channel_id=1, source_target_pairs={{0,4},{1,5},{2,6},{3,7},{4,0},{5,1},{6,2},{7,3},{8,12},{9,13},{10,... | collective-permute-start | bytes 12296 | tf_op jit(solution)/shard_map/ppermute | solution.py:66
  53.2 5.0 %collective-permute-start.11 = (f32[1024]{0:T(1024)S(1)}, f32[1024]{0:T(1024)S(1)}, u32[]{:S(2)}, u32[]{:S(2)}) collective-permute-start(f32[1024]{0:T(1024)S(1)} %add.134), channel_id=1, source_target_pairs={{0,2},{1,3},{2,4},{3,5},{4,6},{5,7},{6,0},{7,1},{8,10},{9,11},{10,... | collective-permute-start | bytes 12296 | tf_op jit(solution)/shard_map/ppermute | solution.py:66
  58.2 3.8 %collective-permute-start.16 = (f32[1024]{0:T(1024)S(1)}, f32[1024]{0:T(1024)S(1)}, u32[]{:S(2)}, u32[]{:S(2)}) collective-permute-start(f32[1024]{0:T(1024)S(1)} %add_add_fusion.1), channel_id=1, source_target_pairs={{0,24},{1,25},{2,26},{3,27},{4,28},{5,29},{6,30},{7,31},{8,0},{9,1... | collective-permute-start | bytes 12296 | tf_op jit(solution)/shard_map/ppermute | solution.py:66
  58.3 5.4 %collective-permute-start.15 = (f32[1024]{0:T(1024)S(1)}, f32[1024]{0:T(1024)S(1)}, u32[]{:S(2)}, u32[]{:S(2)}) collective-permute-start(f32[1024]{0:T(1024)S(1)} %add_add_fusion.1), channel_id=1, source_target_pairs={{0,16},{1,17},{2,18},{3,19},{4,20},{5,21},{6,22},{7,23},{8,24},{9,... | collective-permute-start | bytes 12296 | tf_op jit(solution)/shard_map/ppermute | solution.py:66
  59.8 5.0 %collective-permute-start.14 = (f32[1024]{0:T(1024)S(1)}, f32[1024]{0:T(1024)S(1)}, u32[]{:S(2)}, u32[]{:S(2)}) collective-permute-start(f32[1024]{0:T(1024)S(1)} %add_add_fusion.1), channel_id=1, source_target_pairs={{0,8},{1,9},{2,10},{3,11},{4,12},{5,13},{6,14},{7,15},{8,16},{9,17... | collective-permute-start | bytes 12296 | tf_op jit(solution)/shard_map/ppermute | solution.py:66
  65.1 3.7 %collective-permute-start.17 = (f32[1024]{0:T(1024)S(1)}, f32[1024]{0:T(1024)S(1)}, u32[]{:S(2)}, u32[]{:S(2)}) collective-permute-start(f32[1024]{0:T(1024)S(1)} %multiply_reduce_fusion.2), channel_id=1, source_target_pairs={{0,32},{32,0},{64,96},{96,64},{128,160},{160,128},{192,224},{224,1... | collective-permute-start | bytes 12296 | tf_op jit(solution)/shard_map/ppermute | solution.py:76
  68.8 4.6 %collective-permute-start.18 = (f32[1024]{0:T(1024)S(1)}, f32[1024]{0:T(1024)S(1)}, u32[]{:S(2)}, u32[]{:S(2)}) collective-permute-start(f32[1024]{0:T(1024)S(1)} %add.141), channel_id=1, source_target_pairs={{0,64},{32,96},{64,0},{96,32},{128,192},{160,224},{192,128},{224,1... | collective-permute-start | bytes 12296 | tf_op jit(solution)/shard_map/ppermute | solution.py:76
  73.4 7.5 %collective-permute-start.19 = (f32[1024]{0:T(1024)S(1)}, f32[1024]{0:T(1024)S(1)}, u32[]{:S(2)}, u32[]{:S(2)}) collective-permute-start(f32[1024]{0:T(1024)S(1)} %add.142), channel_id=1, source_target_pairs={{0,128},{32,160},{64,192},{96,224},{128,0},{160,32},{192,64},{224,... | collective-permute-start | bytes 12296 | tf_op jit(solution)/shard_map/ppermute | solution.py:76
  82.6 3.8 %collective-permute-start.23 = (f32[1024]{0:T(1024)S(1)}, f32[1024]{0:T(1024)S(1)}, u32[]{:S(2)}, u32[]{:S(2)}) collective-permute-start(f32[1024]{0:T(1024)S(1)} %add.144), channel_id=1, source_target_pairs={{0,6},{1,7},{2,0},{3,1},{4,2},{5,3},{6,4},{7,5},{8,14},{9,15},{10,... | collective-permute-start | bytes 12296 | tf_op jit(solution)/shard_map/ppermute | solution.py:66
  84.2 5.1 %collective-permute-start.22 = (f32[1024]{0:T(1024)S(1)}, f32[1024]{0:T(1024)S(1)}, u32[]{:S(2)}, u32[]{:S(2)}) collective-permute-start(f32[1024]{0:T(1024)S(1)} %add.144), channel_id=1, source_target_pairs={{0,4},{1,5},{2,6},{3,7},{4,0},{5,1},{6,2},{7,3},{8,12},{9,13},{10,... | collective-permute-start | bytes 12296 | tf_op jit(solution)/shard_map/ppermute | solution.py:66
  85.2 4.8 %collective-permute-start.21 = (f32[1024]{0:T(1024)S(1)}, f32[1024]{0:T(1024)S(1)}, u32[]{:S(2)}, u32[]{:S(2)}) collective-permute-start(f32[1024]{0:T(1024)S(1)} %add.144), channel_id=1, source_target_pairs={{0,2},{1,3},{2,4},{3,5},{4,6},{5,7},{6,0},{7,1},{8,10},{9,11},{10,... | collective-permute-start | bytes 12296 | tf_op jit(solution)/shard_map/ppermute | solution.py:66
  90.0 7.1 %collective-permute-start.26 = (f32[1024]{0:T(1024)S(1)}, f32[1024]{0:T(1024)S(1)}, u32[]{:S(2)}, u32[]{:S(2)}) collective-permute-start(f32[1024]{0:T(1024)S(1)} %add_add_fusion), channel_id=1, source_target_pairs={{0,24},{1,25},{2,26},{3,27},{4,28},{5,29},{6,30},{7,31},{8,0},{9,1... | collective-permute-start | bytes 12296 | tf_op jit(solution)/shard_map/ppermute | solution.py:66
  91.8 5.3 %collective-permute-start.25 = (f32[1024]{0:T(1024)S(1)}, f32[1024]{0:T(1024)S(1)}, u32[]{:S(2)}, u32[]{:S(2)}) collective-permute-start(f32[1024]{0:T(1024)S(1)} %add_add_fusion), channel_id=1, source_target_pairs={{0,16},{1,17},{2,18},{3,19},{4,20},{5,21},{6,22},{7,23},{8,24},{9,... | collective-permute-start | bytes 12296 | tf_op jit(solution)/shard_map/ppermute | solution.py:66
  92.7 4.8 %collective-permute-start.24 = (f32[1024]{0:T(1024)S(1)}, f32[1024]{0:T(1024)S(1)}, u32[]{:S(2)}, u32[]{:S(2)}) collective-permute-start(f32[1024]{0:T(1024)S(1)} %add_add_fusion), channel_id=1, source_target_pairs={{0,8},{1,9},{2,10},{3,11},{4,12},{5,13},{6,14},{7,15},{8,16},{9,17... | collective-permute-start | bytes 12296 | tf_op jit(solution)/shard_map/ppermute | solution.py:66
  100.0 12.8 %collective-permute-start.27 = (f32[1024]{0:T(1024)S(1)}, f32[1024]{0:T(1024)S(1)}, u32[]{:S(2)}, u32[]{:S(2)}) collective-permute-start(f32[1024]{0:T(1024)S(1)} %multiply_reduce_fusion), channel_id=1, source_target_pairs={{0,32},{32,0},{64,96},{96,64},{128,160},{160,128},{192,224},{224,1... | collective-permute-start | bytes 12296 | tf_op jit(solution)/shard_map/ppermute | solution.py:76
  112.8 26.8 %collective-permute-start.28 = (f32[1024]{0:T(1024)S(1)}, f32[1024]{0:T(1024)S(1)}, u32[]{:S(2)}, u32[]{:S(2)}) collective-permute-start(f32[1024]{0:T(1024)S(1)} %add.151), channel_id=1, source_target_pairs={{0,64},{32,96},{64,0},{96,32},{128,192},{160,224},{192,128},{224,1... | collective-permute-start | bytes 12296 | tf_op jit(solution)/shard_map/ppermute | solution.py:76
  137.7 6.5 %collective-permute-start.30 = (f32[1024]{0:T(1024)S(1)}, f32[1024]{0:T(1024)S(1)}, u32[]{:S(2)}, u32[]{:S(2)}) collective-permute-start(f32[1024]{0:T(1024)S(1)} %reduce_sum.99), channel_id=1, source_target_pairs={{0,32},{32,0},{64,96},{96,64},{128,160},{160,128},{192,224},{224,1... | collective-permute-start | bytes 12296 | tf_op jit(solution)/shard_map/ppermute | solution.py:76
  139.7 7.5 %collective-permute-start.29 = (f32[1024]{0:T(1024)S(1)}, f32[1024]{0:T(1024)S(1)}, u32[]{:S(2)}, u32[]{:S(2)}) collective-permute-start(f32[1024]{0:T(1024)S(1)} %add.152), channel_id=1, source_target_pairs={{0,128},{32,160},{64,192},{96,224},{128,0},{160,32},{192,64},{224,... | collective-permute-start | bytes 12296 | tf_op jit(solution)/shard_map/ppermute | solution.py:76
  144.2 4.5 %collective-permute-start.31 = (f32[1024]{0:T(1024)S(1)}, f32[1024]{0:T(1024)S(1)}, u32[]{:S(2)}, u32[]{:S(2)}) collective-permute-start(f32[1024]{0:T(1024)S(1)} %add.156), channel_id=1, source_target_pairs={{0,64},{32,96},{64,0},{96,32},{128,192},{160,224},{192,128},{224,1... | collective-permute-start | bytes 12296 | tf_op jit(solution)/shard_map/ppermute | solution.py:76
  148.7 7.5 %collective-permute-start.32 = (f32[1024]{0:T(1024)S(1)}, f32[1024]{0:T(1024)S(1)}, u32[]{:S(2)}, u32[]{:S(2)}) collective-permute-start(f32[1024]{0:T(1024)S(1)} %add.157), channel_id=1, source_target_pairs={{0,128},{32,160},{64,192},{96,224},{128,0},{160,32},{192,64},{224,... | collective-permute-start | bytes 12296 | tf_op jit(solution)/shard_map/ppermute | solution.py:76
  (7 other events, 118.6 us)
Sparse Core Ops, SparseCore 0:
  10.5 80.4 all-gather.1

commit v6 on v4

--- a/solution.py
+++ b/solution.py
@@ -56,7 +56,22 @@
     total_sub = sub_dev * cent_count
     scale_two = 1.0 / (width * TAU)
 
-    gathered = lax.all_gather(sub_centroids, "dp", axis=0, tiled=True)
+    own_inv = inverse_norm(sub_centroids)
+    spread = own_inv * 65537.0
+    high = spread - (spread - own_inv)
+    rest = own_inv - high
+    spread = rest * 65537.0
+    mid = spread - (spread - rest)
+    low = (rest - mid).astype(jnp.bfloat16)
+    high = high.astype(jnp.bfloat16)
+    mid = mid.astype(jnp.bfloat16)
+    extra = jnp.concatenate([high, mid, low, jnp.zeros((group_dev, width - 3 * sub_dev), jnp.bfloat16)], axis=1)
+    pad = jnp.zeros((group_dev, 7, width), jnp.bfloat16)
+    packed = jnp.concatenate([sub_centroids, extra[:, None, :], pad], axis=1)
+    arrived = lax.all_gather(packed, "dp", axis=0, tiled=True)
+    gathered = arrived[:, :sub_dev, :]
+    parts = arrived[:, sub_dev, : 3 * sub_dev].astype(jnp.float32)
+    inv_u = (parts[:, :sub_dev] + parts[:, sub_dev : 2 * sub_dev]) + parts[:, 2 * sub_dev :]
     inv_x = inverse_norm(points)
     ids = cluster_ids[:, 0]
     labels = lax.broadcasted_iota(jnp.int32, (pts_count, clusters), 1)
@@ -71,7 +86,6 @@
     buffer = jnp.dot(pick, points, preferred_element_type=jnp.float32).astype(points.dtype)
     buffer = buffer.reshape(clusters, CAP, width)
     inv_rows = inverse_norm(buffer)
-    inv_u = inverse_norm(gathered)
     dots = jnp.einsum("gcd,gkd->gck", buffer, gathered, preferred_element_type=jnp.float32)
     weights = jnp.exp(dots * inv_rows[..., None] * inv_u[:, None, :] * scale_two)
     point_weights = weights.reshape(clusters * CAP, sub_dev)[slot]

time: 164 us -> 162 us (0.988)
  starting transfers between devices: 54.7 us -> 62.2 us
  waiting for transfers between devices: 40.6 us -> 34.1 us
  other arithmetic: 18.5 us -> 15.8 us
    ppermute x21, starting transfers between devices: 21 us -> 28.7 us  [dp_sum(): lax.ppermute(values, 'dp', shift_pairs(count, stride, size, step))]
    ppermute x21, waiting for transfers between devices: 22.3 us -> 16.4 us  [dp_sum(): lax.ppermute(values, 'dp', shift_pairs(count, stride, size, step))]
    reduce_sum x3, other arithmetic: 11.5 us -> 5.65 us  [inverse_norm(): return lax.rsqrt(jnp.mean(values * values, axis=-1) + EPS)]
    concatenate x0 -> x1, other arithmetic: none -> 2 us  [shards(): packed = jnp.concatenate([sub_centroids, extra[:, None, :], pad], axis=1)]
  transfers between devices with their start and end apart: 34 -> 34, of which waited for: 25 -> 25; matrix products, arithmetic and copies ran while one was open for 32% -> 28% of each run, Pallas kernels for 0% -> 0%
where the time goes in v6:
time: 162 us; the launch traced here: 161 us
  starting transfers between devices  62.2 us (38%)
  waiting for transfers between devices  34.1 us (21%)
  matrix products  26.9 us (17%)
  other arithmetic  15.8 us (10%)
  between operations  14.3 us (9%)
  local copies, waits for them, and re-layouts  7.35 us (5%)
    ppermute x12, starting transfers between devices, cent_sum(): lax.ppermute(values, 'cent', [(i, i ^ bit) for i in range(count)])  33.5 us
    ppermute x21, starting transfers between devices, dp_sum(): lax.ppermute(values, 'dp', shift_pairs(count, stride, size, step))  28.7 us
    ppermute x12, waiting for transfers between devices, cent_sum(): lax.ppermute(values, 'cent', [(i, i ^ bit) for i in range(count)])  17.7 us
    ppermute x21, waiting for transfers between devices, dp_sum(): lax.ppermute(values, 'dp', shift_pairs(count, stride, size, step))  16.4 us
    dot_general x1, matrix products, shards(): jnp.dot(pick, points, preferred_element_type=jnp.float32)  12.3 us
    dot_general x1, matrix products, shards(): jnp.einsum('gcd,gkd->gck', buffer, gathered, preferred_element_type=jnp.f...  11.3 us
    reduce_sum x3, other arithmetic, inverse_norm(): return lax.rsqrt(jnp.mean(values * values, axis=-1) + EPS)  5.65 us
    scatter x1, local copies, waits for them, and re-layouts, shards(): jnp.zeros((clusters * CAP,), jnp.int32).at[slot]  4.33 us
  transfers between devices with their start and end apart: 34, of which 25 were waited for; matrix products, arithmetic and copies ran while one was open for 28% of the time, Pallas kernels for 0%

profile of v6, /device:TPU:32, one launch (start us, length us, event | category | flops | bytes accessed | tf_op | source)
XLA Modules:
  0.0 160.7 jit_solution(347990854329160626)
XLA Ops:
  8.7 2.0 %maximum_maximum_fusion = bf16[2,136,1024]{2,1,0:T(8,128)(2,1)} fusion(bf16[2,1,1024]{2,1,0:T(2,128)(2,1)S(1)} %copy.7, bf16[2,128,1024]{2,1,0:T(8,128)(2,1)} %param.7, bf16[136]{0:T(256)(128)(2,1)S(1)} %pad.2.clone), kind=kLoop, calls=%fused_computation.24 | loop fusion | flops 1671168 | bytes 1085712 | tf_op jit(solution)/shard_map/concatenate | solution.py:70
  10.8 2.2 %multiply_reduce_fusion.6 = f32[1024]{0:T(1024)S(1)} fusion(bf16[1024,1024]{1,0:T(8,128)(2,1)} %param.6), kind=kLoop, calls=%fused_computation.17 | loop fusion | flops 3144704 | bytes 2101248 | tf_op jit(solution)/shard_map/reduce_sum | solution.py:16
  13.0 2.1 %multiply_reduce_fusion.7 = f32[1024]{0:T(1024)S(1)} fusion(bf16[1024,1024]{1,0:T(8,128)(2,1)} %param.4), kind=kLoop, calls=%fused_computation.18 | loop fusion | flops 3144704 | bytes 2101248 | tf_op jit(solution)/shard_map/reduce_sum | solution.py:16
  15.1 2.7 %fusion.16 = (f32[1024]{0:T(1024)S(1)}, f32[1024,1024]{1,0:T(8,128)S(1)}) fusion(f32[1024]{0:T(1024)S(1)} %get-tuple-element.9, f32[1024]{0:T(1024)S(1)} %get-tuple-element.10, bf16[1024,1024]{1,0:T(8,128)(2,1)S(1)} %copy-done.3, bf16[1024,1024]{1,0:T(8,128)(2,1)S(1)} %copy-done.2), kind=kOutput, calls=%fused_computation.56 | convolution fusion | flops 2151676928 | bytes 8400896 | tf_op jit(solution)/shard_map/pd,kd->pk/dot_general | solution.py:95
  19.1 1.6 collective-permute-start.1
  20.7 2.9 %collective-permute-start.2 = (f32[1024]{0:T(1024)S(1)}, f32[1024]{0:T(1024)S(1)}, u32[]{:S(2)}, u32[]{:S(2)}) collective-permute-start(f32[1024]{0:T(1024)S(1)} %add.147), channel_id=1, source_target_pairs={{0,4},{1,5},{2,6},{3,7},{4,0},{5,1},{6,2},{7,3},{8,12},{9,13},{10,... | collective-permute-start | bytes 12296 | tf_op jit(solution)/shard_map/ppermute | solution.py:32
  28.7 2.7 %collective-permute-start.5 = (f32[1024]{0:T(1024)S(1)}, f32[1024]{0:T(1024)S(1)}, u32[]{:S(2)}, u32[]{:S(2)}) collective-permute-start(f32[1024]{0:T(1024)S(1)} %add_add_fusion.2), channel_id=1, source_target_pairs={{0,16},{1,17},{2,18},{3,19},{4,20},{5,21},{6,22},{7,23},{8,24},{9,... | collective-permute-start | bytes 12296 | tf_op jit(solution)/shard_map/ppermute | solution.py:32
  35.6 3.5 %collective-permute-done.7 = f32[1024]{0:T(1024)S(1)} collective-permute-done((f32[1024]{0:T(1024)S(1)}, f32[1024]{0:T(1024)S(1)}, u32[]{:S(2)}, u32[]{:S(2)}) %collective-permute-start.7) | collective-permute-done | bytes 4128 | tf_op jit(solution)/shard_map/ppermute | solution.py:42
  39.1 3.3 %collective-permute-start.8 = (f32[1024]{0:T(1024)S(1)}, f32[1024]{0:T(1024)S(1)}, u32[]{:S(2)}, u32[]{:S(2)}) collective-permute-start(f32[1024]{0:T(1024)S(1)} %add.154), channel_id=1, source_target_pairs={{0,64},{32,96},{64,0},{96,32},{128,192},{160,224},{192,128},{224,1... | collective-permute-start | bytes 12296 | tf_op jit(solution)/shard_map/ppermute | solution.py:42
  42.4 1.6 collective-permute-done.8
  44.0 6.0 %collective-permute-start.9 = (f32[1024]{0:T(1024)S(1)}, f32[1024]{0:T(1024)S(1)}, u32[]{:S(2)}, u32[]{:S(2)}) collective-permute-start(f32[1024]{0:T(1024)S(1)} %add.155), channel_id=1, source_target_pairs={{0,128},{32,160},{64,192},{96,224},{128,0},{160,32},{192,64},{224,... | collective-permute-start | bytes 12296 | tf_op jit(solution)/shard_map/ppermute | solution.py:42
  50.0 1.6 collective-permute-done.9
  53.4 3.8 %collective-permute-start.12 = (f32[1024]{0:T(1024)S(1)}, f32[1024]{0:T(1024)S(1)}, u32[]{:S(2)}, u32[]{:S(2)}) collective-permute-start(f32[1024]{0:T(1024)S(1)} %add.157), channel_id=1, source_target_pairs={{0,4},{1,5},{2,6},{3,7},{4,0},{5,1},{6,2},{7,3},{8,12},{9,13},{10,... | collective-permute-start | bytes 12296 | tf_op jit(solution)/shard_map/ppermute | solution.py:32
  59.1 1.9 %collective-permute-done.13 = f32[1024]{0:T(1024)S(1)} collective-permute-done((f32[1024]{0:T(1024)S(1)}, f32[1024]{0:T(1024)S(1)}, u32[]{:S(2)}, u32[]{:S(2)}) %collective-permute-start.13) | collective-permute-done | bytes 4128 | tf_op jit(solution)/shard_map/ppermute | solution.py:32
  61.4 3.7 %collective-permute-start.15 = (f32[1024]{0:T(1024)S(1)}, f32[1024]{0:T(1024)S(1)}, u32[]{:S(2)}, u32[]{:S(2)}) collective-permute-start(f32[1024]{0:T(1024)S(1)} %add_add_fusion.1), channel_id=1, source_target_pairs={{0,16},{1,17},{2,18},{3,19},{4,20},{5,21},{6,22},{7,23},{8,24},{9,... | collective-permute-start | bytes 12296 | tf_op jit(solution)/shard_map/ppermute | solution.py:32
  67.0 1.9 %collective-permute-done.16 = f32[1024]{0:T(1024)S(1)} collective-permute-done((f32[1024]{0:T(1024)S(1)}, f32[1024]{0:T(1024)S(1)}, u32[]{:S(2)}, u32[]{:S(2)}) %collective-permute-start.16) | collective-permute-done | bytes 4128 | tf_op jit(solution)/shard_map/ppermute | solution.py:32
  70.4 2.6 %collective-permute-done.17 = f32[1024]{0:T(1024)S(1)} collective-permute-done((f32[1024]{0:T(1024)S(1)}, f32[1024]{0:T(1024)S(1)}, u32[]{:S(2)}, u32[]{:S(2)}) %collective-permute-start.17) | collective-permute-done | bytes 4128 | tf_op jit(solution)/shard_map/ppermute | solution.py:42
  73.0 2.9 %collective-permute-start.18 = (f32[1024]{0:T(1024)S(1)}, f32[1024]{0:T(1024)S(1)}, u32[]{:S(2)}, u32[]{:S(2)}) collective-permute-start(f32[1024]{0:T(1024)S(1)} %add.164), channel_id=1, source_target_pairs={{0,64},{32,96},{64,0},{96,32},{128,192},{160,224},{192,128},{224,1... | collective-permute-start | bytes 12296 | tf_op jit(solution)/shard_map/ppermute | solution.py:42
  75.9 1.6 collective-permute-done.18
  77.5 5.9 %collective-permute-start.19 = (f32[1024]{0:T(1024)S(1)}, f32[1024]{0:T(1024)S(1)}, u32[]{:S(2)}, u32[]{:S(2)}) collective-permute-start(f32[1024]{0:T(1024)S(1)} %add.165), channel_id=1, source_target_pairs={{0,128},{32,160},{64,192},{96,224},{128,0},{160,32},{192,64},{224,... | collective-permute-start | bytes 12296 | tf_op jit(solution)/shard_map/ppermute | solution.py:42
  85.5 4.3 %scatter_custom_fusion = s32[4096]{0:T(1024)S(1)} fusion(s32[1024]{0:T(1024)S(1)} %bitcast.23, s32[1024]{0:T(1024)S(1)} %iota.23, s32[]{:T(128)} %constant.18.clone.1), kind=kCustom, calls=%fused_computation.34 | custom fusion | bytes 16388 | tf_op jit(solution)/shard_map/scatter | solution.py:84
  90.0 2.8 %collective-permute-start.22 = (f32[1024]{0:T(1024)S(1)}, f32[1024]{0:T(1024)S(1)}, u32[]{:S(2)}, u32[]{:S(2)}) collective-permute-start(f32[1024]{0:T(1024)S(1)} %add.167), channel_id=1, source_target_pairs={{0,4},{1,5},{2,6},{3,7},{4,0},{5,1},{6,2},{7,3},{8,12},{9,13},{10,... | collective-permute-start | bytes 12296 | tf_op jit(solution)/shard_map/ppermute | solution.py:32
  94.2 12.3 %multiply_reduce_fusion = (f32[4096]{0:T(1024)S(1)}, bf16[4096,1024]{1,0:T(8,128)(2,1)}) fusion(bf16[1024,1024]{1,0:T(8,128)(2,1)S(1)} %copy-done.4, s32[4096]{0:T(1024)S(1)} %scatter_custom_fusion), kind=kOutput, calls=%fused_computation.4 | convolution fusion | flops 8610902016 | bytes 10518528 | tf_op jit(solution)/shard_map/dot_general | solution.py:86
  106.6 2.8 %collective-permute-start.25 = (f32[1024]{0:T(1024)S(1)}, f32[1024]{0:T(1024)S(1)}, u32[]{:S(2)}, u32[]{:S(2)}) collective-permute-start(f32[1024]{0:T(1024)S(1)} %add_add_fusion), channel_id=1, source_target_pairs={{0,16},{1,17},{2,18},{3,19},{4,20},{5,21},{6,22},{7,23},{8,24},{9,... | collective-permute-start | bytes 12296 | tf_op jit(solution)/shard_map/ppermute | solution.py:32
  114.5 2.5 %collective-permute-done.27 = f32[1024]{0:T(1024)S(1)} collective-permute-done((f32[1024]{0:T(1024)S(1)}, f32[1024]{0:T(1024)S(1)}, u32[]{:S(2)}, u32[]{:S(2)}) %collective-permute-start.27) | collective-permute-done | bytes 4128 | tf_op jit(solution)/shard_map/ppermute | solution.py:42
  117.0 2.8 %collective-permute-start.28 = (f32[1024]{0:T(1024)S(1)}, f32[1024]{0:T(1024)S(1)}, u32[]{:S(2)}, u32[]{:S(2)}) collective-permute-start(f32[1024]{0:T(1024)S(1)} %add.174), channel_id=1, source_target_pairs={{0,64},{32,96},{64,0},{96,32},{128,192},{160,224},{192,128},{224,1... | collective-permute-start | bytes 12296 | tf_op jit(solution)/shard_map/ppermute | solution.py:42
  120.9 11.3 %multiply_exponential_fusion.1 = f32[64,64,128]{2,1,0:T(8,128)S(1)} fusion(bf16[64,64,1024]{2,1,0:T(8,128)(2,1)} %bitcast.27, bf16[64,136,1024]{2,1,0:T(8,128)(2,1)} %all-gather.2.cloned.1.call-done, f32[64,128]{1,0:T(8,128)S(1)} %slice_add_fusion, f32[64,64]{1,0:T(8,128)S(1)} %rsqrt.31), kind=kOutput, calls=%fused_computation.20 | convolution fusion | flops 1075314688 | bytes 27312128 | tf_op jit(solution)/shard_map/gcd,gkd->gck/dot_general | solution.py:89
  132.2 2.8 %gather_fusion = f32[1024,128]{1,0:T(8,128)S(1)} fusion(f32[4096,128]{1,0:T(8,128)S(1)} %bitcast.21, s32[1024]{0:T(1024)S(1)} %broadcast_clamp_fusion), kind=kCustom, calls=%fused_computation | custom fusion | bytes 1052672 | tf_op jit(solution)/shard_map/gather | solution.py:91
  135.5 5.4 %collective-permute-start.29 = (f32[1024]{0:T(1024)S(1)}, f32[1024]{0:T(1024)S(1)}, u32[]{:S(2)}, u32[]{:S(2)}) collective-permute-start(f32[1024]{0:T(1024)S(1)} %add.175), channel_id=1, source_target_pairs={{0,128},{32,160},{64,192},{96,224},{128,0},{160,32},{192,64},{224,... | collective-permute-start | bytes 12296 | tf_op jit(solution)/shard_map/ppermute | solution.py:42
  143.0 2.3 %collective-permute-done.31 = f32[1024]{0:T(1024)S(1)} collective-permute-done((f32[1024]{0:T(1024)S(1)}, f32[1024]{0:T(1024)S(1)}, u32[]{:S(2)}, u32[]{:S(2)}) %collective-permute-start.31) | collective-permute-done | bytes 4128 | tf_op jit(solution)/shard_map/ppermute | solution.py:42
  145.4 3.1 %collective-permute-start.32 = (f32[1024]{0:T(1024)S(1)}, f32[1024]{0:T(1024)S(1)}, u32[]{:S(2)}, u32[]{:S(2)}) collective-permute-start(f32[1024]{0:T(1024)S(1)} %add.186), channel_id=1, source_target_pairs={{0,128},{32,160},{64,192},{96,224},{128,0},{160,32},{192,64},{224,... | collective-permute-start | bytes 12296 | tf_op jit(solution)/shard_map/ppermute | solution.py:42
  148.5 4.0 %multiply_convert_fusion = bf16[1024,1024]{1,0:T(8,128)(2,1)} fusion(f32[1024,1024]{1,0:T(8,128)} %copy-done, f32[1024]{0:T(1024)S(1)} %add_divide_fusion, f32[1024]{0:T(1024)S(1)} %add_divide_fusion.1), kind=kLoop, calls=%fused_computation.10 | loop fusion | flops 4194304 | bytes 6299648 | tf_op jit(solution)/shard_map/convert_element_type | solution.py:111
  (105 shorter events, 33.4 us)
Async XLA Ops:
  7.2 112.6 %all-gather.2.cloned.1.call-start = ((), (), s32[]{:S(2)}) async-start(), calls=%async_computation | async-start | bytes 18382848 | tf_op jit(solution)/shard_map/all_gather | solution.py:71
  19.1 5.8 %collective-permute-start.1 = (f32[1024]{0:T(1024)S(1)}, f32[1024]{0:T(1024)S(1)}, u32[]{:S(2)}, u32[]{:S(2)}) collective-permute-start(f32[1024]{0:T(1024)S(1)} %add.147), channel_id=1, source_target_pairs={{0,2},{1,3},{2,4},{3,5},{4,6},{5,7},{6,0},{7,1},{8,10},{9,11},{10,... | collective-permute-start | bytes 12296 | tf_op jit(solution)/shard_map/ppermute | solution.py:32
  20.7 5.1 %collective-permute-start.2 = (f32[1024]{0:T(1024)S(1)}, f32[1024]{0:T(1024)S(1)}, u32[]{:S(2)}, u32[]{:S(2)}) collective-permute-start(f32[1024]{0:T(1024)S(1)} %add.147), channel_id=1, source_target_pairs={{0,4},{1,5},{2,6},{3,7},{4,0},{5,1},{6,2},{7,3},{8,12},{9,13},{10,... | collective-permute-start | bytes 12296 | tf_op jit(solution)/shard_map/ppermute | solution.py:32
  23.6 3.6 %collective-permute-start.3 = (f32[1024]{0:T(1024)S(1)}, f32[1024]{0:T(1024)S(1)}, u32[]{:S(2)}, u32[]{:S(2)}) collective-permute-start(f32[1024]{0:T(1024)S(1)} %add.147), channel_id=1, source_target_pairs={{0,6},{1,7},{2,0},{3,1},{4,2},{5,3},{6,4},{7,5},{8,14},{9,15},{10,... | collective-permute-start | bytes 12296 | tf_op jit(solution)/shard_map/ppermute | solution.py:32
  27.2 5.7 %collective-permute-start.4 = (f32[1024]{0:T(1024)S(1)}, f32[1024]{0:T(1024)S(1)}, u32[]{:S(2)}, u32[]{:S(2)}) collective-permute-start(f32[1024]{0:T(1024)S(1)} %add_add_fusion.2), channel_id=1, source_target_pairs={{0,8},{1,9},{2,10},{3,11},{4,12},{5,13},{6,14},{7,15},{8,16},{9,17... | collective-permute-start | bytes 12296 | tf_op jit(solution)/shard_map/ppermute | solution.py:32
  28.7 5.3 %collective-permute-start.5 = (f32[1024]{0:T(1024)S(1)}, f32[1024]{0:T(1024)S(1)}, u32[]{:S(2)}, u32[]{:S(2)}) collective-permute-start(f32[1024]{0:T(1024)S(1)} %add_add_fusion.2), channel_id=1, source_target_pairs={{0,16},{1,17},{2,18},{3,19},{4,20},{5,21},{6,22},{7,23},{8,24},{9,... | collective-permute-start | bytes 12296 | tf_op jit(solution)/shard_map/ppermute | solution.py:32
  31.4 3.6 %collective-permute-start.6 = (f32[1024]{0:T(1024)S(1)}, f32[1024]{0:T(1024)S(1)}, u32[]{:S(2)}, u32[]{:S(2)}) collective-permute-start(f32[1024]{0:T(1024)S(1)} %add_add_fusion.2), channel_id=1, source_target_pairs={{0,24},{1,25},{2,26},{3,27},{4,28},{5,29},{6,30},{7,31},{8,0},{9,1... | collective-permute-start | bytes 12296 | tf_op jit(solution)/shard_map/ppermute | solution.py:32
  35.4 3.7 %collective-permute-start.7 = (f32[1024]{0:T(1024)S(1)}, f32[1024]{0:T(1024)S(1)}, u32[]{:S(2)}, u32[]{:S(2)}) collective-permute-start(f32[1024]{0:T(1024)S(1)} %multiply_reduce_fusion.5), channel_id=1, source_target_pairs={{0,32},{32,0},{64,96},{96,64},{128,160},{160,128},{192,224},{224,1... | collective-permute-start | bytes 12296 | tf_op jit(solution)/shard_map/ppermute | solution.py:42
  39.1 4.9 %collective-permute-start.8 = (f32[1024]{0:T(1024)S(1)}, f32[1024]{0:T(1024)S(1)}, u32[]{:S(2)}, u32[]{:S(2)}) collective-permute-start(f32[1024]{0:T(1024)S(1)} %add.154), channel_id=1, source_target_pairs={{0,64},{32,96},{64,0},{96,32},{128,192},{160,224},{192,128},{224,1... | collective-permute-start | bytes 12296 | tf_op jit(solution)/shard_map/ppermute | solution.py:42
  44.0 7.5 %collective-permute-start.9 = (f32[1024]{0:T(1024)S(1)}, f32[1024]{0:T(1024)S(1)}, u32[]{:S(2)}, u32[]{:S(2)}) collective-permute-start(f32[1024]{0:T(1024)S(1)} %add.155), channel_id=1, source_target_pairs={{0,128},{32,160},{64,192},{96,224},{128,0},{160,32},{192,64},{224,... | collective-permute-start | bytes 12296 | tf_op jit(solution)/shard_map/ppermute | solution.py:42
  53.2 5.1 %collective-permute-start.11 = (f32[1024]{0:T(1024)S(1)}, f32[1024]{0:T(1024)S(1)}, u32[]{:S(2)}, u32[]{:S(2)}) collective-permute-start(f32[1024]{0:T(1024)S(1)} %add.157), channel_id=1, source_target_pairs={{0,2},{1,3},{2,4},{3,5},{4,6},{5,7},{6,0},{7,1},{8,10},{9,11},{10,... | collective-permute-start | bytes 12296 | tf_op jit(solution)/shard_map/ppermute | solution.py:32
  53.4 5.7 %collective-permute-start.12 = (f32[1024]{0:T(1024)S(1)}, f32[1024]{0:T(1024)S(1)}, u32[]{:S(2)}, u32[]{:S(2)}) collective-permute-start(f32[1024]{0:T(1024)S(1)} %add.157), channel_id=1, source_target_pairs={{0,4},{1,5},{2,6},{3,7},{4,0},{5,1},{6,2},{7,3},{8,12},{9,13},{10,... | collective-permute-start | bytes 12296 | tf_op jit(solution)/shard_map/ppermute | solution.py:32
  57.2 3.8 %collective-permute-start.13 = (f32[1024]{0:T(1024)S(1)}, f32[1024]{0:T(1024)S(1)}, u32[]{:S(2)}, u32[]{:S(2)}) collective-permute-start(f32[1024]{0:T(1024)S(1)} %add.157), channel_id=1, source_target_pairs={{0,6},{1,7},{2,0},{3,1},{4,2},{5,3},{6,4},{7,5},{8,14},{9,15},{10,... | collective-permute-start | bytes 12296 | tf_op jit(solution)/shard_map/ppermute | solution.py:32
  61.0 5.0 %collective-permute-start.14 = (f32[1024]{0:T(1024)S(1)}, f32[1024]{0:T(1024)S(1)}, u32[]{:S(2)}, u32[]{:S(2)}) collective-permute-start(f32[1024]{0:T(1024)S(1)} %add_add_fusion.1), channel_id=1, source_target_pairs={{0,8},{1,9},{2,10},{3,11},{4,12},{5,13},{6,14},{7,15},{8,16},{9,17... | collective-permute-start | bytes 12296 | tf_op jit(solution)/shard_map/ppermute | solution.py:32
  61.4 5.7 %collective-permute-start.15 = (f32[1024]{0:T(1024)S(1)}, f32[1024]{0:T(1024)S(1)}, u32[]{:S(2)}, u32[]{:S(2)}) collective-permute-start(f32[1024]{0:T(1024)S(1)} %add_add_fusion.1), channel_id=1, source_target_pairs={{0,16},{1,17},{2,18},{3,19},{4,20},{5,21},{6,22},{7,23},{8,24},{9,... | collective-permute-start | bytes 12296 | tf_op jit(solution)/shard_map/ppermute | solution.py:32
  65.1 3.8 %collective-permute-start.16 = (f32[1024]{0:T(1024)S(1)}, f32[1024]{0:T(1024)S(1)}, u32[]{:S(2)}, u32[]{:S(2)}) collective-permute-start(f32[1024]{0:T(1024)S(1)} %add_add_fusion.1), channel_id=1, source_target_pairs={{0,24},{1,25},{2,26},{3,27},{4,28},{5,29},{6,30},{7,31},{8,0},{9,1... | collective-permute-start | bytes 12296 | tf_op jit(solution)/shard_map/ppermute | solution.py:32
  69.3 3.7 %collective-permute-start.17 = (f32[1024]{0:T(1024)S(1)}, f32[1024]{0:T(1024)S(1)}, u32[]{:S(2)}, u32[]{:S(2)}) collective-permute-start(f32[1024]{0:T(1024)S(1)} %multiply_reduce_fusion.3), channel_id=1, source_target_pairs={{0,32},{32,0},{64,96},{96,64},{128,160},{160,128},{192,224},{224,1... | collective-permute-start | bytes 12296 | tf_op jit(solution)/shard_map/ppermute | solution.py:42
  73.0 4.5 %collective-permute-start.18 = (f32[1024]{0:T(1024)S(1)}, f32[1024]{0:T(1024)S(1)}, u32[]{:S(2)}, u32[]{:S(2)}) collective-permute-start(f32[1024]{0:T(1024)S(1)} %add.164), channel_id=1, source_target_pairs={{0,64},{32,96},{64,0},{96,32},{128,192},{160,224},{192,128},{224,1... | collective-permute-start | bytes 12296 | tf_op jit(solution)/shard_map/ppermute | solution.py:42
  77.5 7.5 %collective-permute-start.19 = (f32[1024]{0:T(1024)S(1)}, f32[1024]{0:T(1024)S(1)}, u32[]{:S(2)}, u32[]{:S(2)}) collective-permute-start(f32[1024]{0:T(1024)S(1)} %add.165), channel_id=1, source_target_pairs={{0,128},{32,160},{64,192},{96,224},{128,0},{160,32},{192,64},{224,... | collective-permute-start | bytes 12296 | tf_op jit(solution)/shard_map/ppermute | solution.py:42
  85.4 4.5 %collective-permute-start.20 = (f32[1024]{0:T(1024)S(1)}, f32[1024]{0:T(1024)S(1)}, u32[]{:S(2)}, u32[]{:S(2)}) collective-permute-start(f32[1024]{0:T(1024)S(1)} %multiply_reduce_fusion.2), channel_id=1, source_target_pairs={{0,1},{1,0},{2,3},{3,2},{4,5},{5,4},{6,7},{7,6},{8,9},{9,8},{10,11... | collective-permute-start | bytes 12296 | tf_op jit(solution)/shard_map/ppermute | solution.py:32
  89.9 16.6 %collective-permute-start.21 = (f32[1024]{0:T(1024)S(1)}, f32[1024]{0:T(1024)S(1)}, u32[]{:S(2)}, u32[]{:S(2)}) collective-permute-start(f32[1024]{0:T(1024)S(1)} %add.167), channel_id=1, source_target_pairs={{0,2},{1,3},{2,4},{3,5},{4,6},{5,7},{6,0},{7,1},{8,10},{9,11},{10,... | collective-permute-start | bytes 12296 | tf_op jit(solution)/shard_map/ppermute | solution.py:32
  90.0 16.4 %collective-permute-start.22 = (f32[1024]{0:T(1024)S(1)}, f32[1024]{0:T(1024)S(1)}, u32[]{:S(2)}, u32[]{:S(2)}) collective-permute-start(f32[1024]{0:T(1024)S(1)} %add.167), channel_id=1, source_target_pairs={{0,4},{1,5},{2,6},{3,7},{4,0},{5,1},{6,2},{7,3},{8,12},{9,13},{10,... | collective-permute-start | bytes 12296 | tf_op jit(solution)/shard_map/ppermute | solution.py:32
  92.8 13.6 %collective-permute-start.23 = (f32[1024]{0:T(1024)S(1)}, f32[1024]{0:T(1024)S(1)}, u32[]{:S(2)}, u32[]{:S(2)}) collective-permute-start(f32[1024]{0:T(1024)S(1)} %add.167), channel_id=1, source_target_pairs={{0,6},{1,7},{2,0},{3,1},{4,2},{5,3},{6,4},{7,5},{8,14},{9,15},{10,... | collective-permute-start | bytes 12296 | tf_op jit(solution)/shard_map/ppermute | solution.py:32
  106.5 4.9 %collective-permute-start.24 = (f32[1024]{0:T(1024)S(1)}, f32[1024]{0:T(1024)S(1)}, u32[]{:S(2)}, u32[]{:S(2)}) collective-permute-start(f32[1024]{0:T(1024)S(1)} %add_add_fusion), channel_id=1, source_target_pairs={{0,8},{1,9},{2,10},{3,11},{4,12},{5,13},{6,14},{7,15},{8,16},{9,17... | collective-permute-start | bytes 12296 | tf_op jit(solution)/shard_map/ppermute | solution.py:32
  106.6 5.2 %collective-permute-start.25 = (f32[1024]{0:T(1024)S(1)}, f32[1024]{0:T(1024)S(1)}, u32[]{:S(2)}, u32[]{:S(2)}) collective-permute-start(f32[1024]{0:T(1024)S(1)} %add_add_fusion), channel_id=1, source_target_pairs={{0,16},{1,17},{2,18},{3,19},{4,20},{5,21},{6,22},{7,23},{8,24},{9,... | collective-permute-start | bytes 12296 | tf_op jit(solution)/shard_map/ppermute | solution.py:32
  109.3 3.6 %collective-permute-start.26 = (f32[1024]{0:T(1024)S(1)}, f32[1024]{0:T(1024)S(1)}, u32[]{:S(2)}, u32[]{:S(2)}) collective-permute-start(f32[1024]{0:T(1024)S(1)} %add_add_fusion), channel_id=1, source_target_pairs={{0,24},{1,25},{2,26},{3,27},{4,28},{5,29},{6,30},{7,31},{8,0},{9,1... | collective-permute-start | bytes 12296 | tf_op jit(solution)/shard_map/ppermute | solution.py:32
  113.3 3.7 %collective-permute-start.27 = (f32[1024]{0:T(1024)S(1)}, f32[1024]{0:T(1024)S(1)}, u32[]{:S(2)}, u32[]{:S(2)}) collective-permute-start(f32[1024]{0:T(1024)S(1)} %multiply_reduce_fusion.1), channel_id=1, source_target_pairs={{0,32},{32,0},{64,96},{96,64},{128,160},{160,128},{192,224},{224,1... | collective-permute-start | bytes 12296 | tf_op jit(solution)/shard_map/ppermute | solution.py:42
  117.0 18.5 %collective-permute-start.28 = (f32[1024]{0:T(1024)S(1)}, f32[1024]{0:T(1024)S(1)}, u32[]{:S(2)}, u32[]{:S(2)}) collective-permute-start(f32[1024]{0:T(1024)S(1)} %add.174), channel_id=1, source_target_pairs={{0,64},{32,96},{64,0},{96,32},{128,192},{160,224},{192,128},{224,1... | collective-permute-start | bytes 12296 | tf_op jit(solution)/shard_map/ppermute | solution.py:42
  135.2 5.6 %collective-permute-start.30 = (f32[1024]{0:T(1024)S(1)}, f32[1024]{0:T(1024)S(1)}, u32[]{:S(2)}, u32[]{:S(2)}) collective-permute-start(f32[1024]{0:T(1024)S(1)} %reduce_sum.119), channel_id=1, source_target_pairs={{0,32},{32,0},{64,96},{96,64},{128,160},{160,128},{192,224},{224,1... | collective-permute-start | bytes 12296 | tf_op jit(solution)/shard_map/ppermute | solution.py:42
  135.5 7.5 %collective-permute-start.29 = (f32[1024]{0:T(1024)S(1)}, f32[1024]{0:T(1024)S(1)}, u32[]{:S(2)}, u32[]{:S(2)}) collective-permute-start(f32[1024]{0:T(1024)S(1)} %add.175), channel_id=1, source_target_pairs={{0,128},{32,160},{64,192},{96,224},{128,0},{160,32},{192,64},{224,... | collective-permute-start | bytes 12296 | tf_op jit(solution)/shard_map/ppermute | solution.py:42
  140.9 4.5 %collective-permute-start.31 = (f32[1024]{0:T(1024)S(1)}, f32[1024]{0:T(1024)S(1)}, u32[]{:S(2)}, u32[]{:S(2)}) collective-permute-start(f32[1024]{0:T(1024)S(1)} %add.185), channel_id=1, source_target_pairs={{0,64},{32,96},{64,0},{96,32},{128,192},{160,224},{192,128},{224,1... | collective-permute-start | bytes 12296 | tf_op jit(solution)/shard_map/ppermute | solution.py:42
  145.4 7.5 %collective-permute-start.32 = (f32[1024]{0:T(1024)S(1)}, f32[1024]{0:T(1024)S(1)}, u32[]{:S(2)}, u32[]{:S(2)}) collective-permute-start(f32[1024]{0:T(1024)S(1)} %add.186), channel_id=1, source_target_pairs={{0,128},{32,160},{64,192},{96,224},{128,0},{160,32},{192,64},{224,... | collective-permute-start | bytes 12296 | tf_op jit(solution)/shard_map/ppermute | solution.py:42
  (8 other events, 162.2 us)
Sparse Core Ops, SparseCore 0:
  11.1 82.7 all-gather.1

commit v7 on v6

--- a/solution.py
+++ b/solution.py
@@ -26,12 +26,10 @@
 
 def dp_sum(values):
     count = lax.axis_size("dp")
-    for stride, size in ((1, 2), (2, 4), (8, count // 8)):
-        if size < 2:
-            continue
-        parts = [lax.ppermute(values, "dp", shift_pairs(count, stride, size, step)) for step in range(1, size)]
-        for part in parts:
-            values = values + part
+    bit = 1
+    while bit < count:
+        values = values + lax.ppermute(values, "dp", [(i, i ^ bit) for i in range(count)])
+        bit *= 2
     return values
 
 

time: 162 us -> 170 us (1.049)
  waiting for transfers between devices: 34.1 us -> 40.8 us
    ppermute x21 -> x15, waiting for transfers between devices: 16.4 us -> 24.3 us  [dp_sum(): lax.ppermute(values, 'dp', [(i, i ^ bit) for i in range(count)])]
    ppermute x12, starting transfers between devices: 33.5 us -> 35.4 us  [cent_sum(): lax.ppermute(values, 'cent', [(i, i ^ bit) for i in range(count)])]
    ppermute x21 -> x15, starting transfers between devices: 28.7 us -> 28.4 us  [dp_sum(): lax.ppermute(values, 'dp', [(i, i ^ bit) for i in range(count)])]
  transfers between devices with their start and end apart: 34 -> 28, of which waited for: 25 -> 23; matrix products, arithmetic and copies ran while one was open for 28% -> 27% of each run, Pallas kernels for 0% -> 0%
where the time goes in v7:
time: 170 us; the launch traced here: 169 us
  starting transfers between devices  63.8 us (38%)
  waiting for transfers between devices  40.8 us (24%)
  matrix products  26.9 us (16%)
  other arithmetic  15.8 us (9%)
  between operations  14.3 us (8%)
  local copies, waits for them, and re-layouts  7.35 us (4%)
    ppermute x12, starting transfers between devices, cent_sum(): lax.ppermute(values, 'cent', [(i, i ^ bit) for i in range(count)])  35.4 us
    ppermute x15, starting transfers between devices, dp_sum(): lax.ppermute(values, 'dp', [(i, i ^ bit) for i in range(count)])  28.4 us
    ppermute x15, waiting for transfers between devices, dp_sum(): lax.ppermute(values, 'dp', [(i, i ^ bit) for i in range(count)])  24.3 us
    ppermute x12, waiting for transfers between devices, cent_sum(): lax.ppermute(values, 'cent', [(i, i ^ bit) for i in range(count)])  16.5 us
    dot_general x1, matrix products, shards(): jnp.dot(pick, points, preferred_element_type=jnp.float32)  12.3 us
    dot_general x1, matrix products, shards(): jnp.einsum('gcd,gkd->gck', buffer, gathered, preferred_element_type=jnp.f...  11.3 us
    reduce_sum x3, other arithmetic, inverse_norm(): return lax.rsqrt(jnp.mean(values * values, axis=-1) + EPS)  5.65 us
    scatter x1, local copies, waits for them, and re-layouts, shards(): jnp.zeros((clusters * CAP,), jnp.int32).at[slot]  4.33 us
  transfers between devices with their start and end apart: 28, of which 23 were waited for; matrix products, arithmetic and copies ran while one was open for 27% of the time, Pallas kernels for 0%

profile of v7, /device:TPU:32, one launch (start us, length us, event | category | flops | bytes accessed | tf_op | source)
XLA Modules:
  0.0 169.0 jit_solution(11659711763395220392)
XLA Ops:
  8.7 2.0 %maximum_maximum_fusion = bf16[2,136,1024]{2,1,0:T(8,128)(2,1)} fusion(bf16[2,1,1024]{2,1,0:T(2,128)(2,1)S(1)} %copy.7, bf16[2,128,1024]{2,1,0:T(8,128)(2,1)} %param.7, bf16[136]{0:T(256)(128)(2,1)S(1)} %pad.2.clone), kind=kLoop, calls=%fused_computation.24 | loop fusion | flops 1671168 | bytes 1085712 | tf_op jit(solution)/shard_map/concatenate | solution.py:68
  10.8 2.2 %multiply_reduce_fusion.6 = f32[1024]{0:T(1024)S(1)} fusion(bf16[1024,1024]{1,0:T(8,128)(2,1)} %param.6), kind=kLoop, calls=%fused_computation.17 | loop fusion | flops 3144704 | bytes 2101248 | tf_op jit(solution)/shard_map/reduce_sum | solution.py:16
  13.0 2.1 %multiply_reduce_fusion.7 = f32[1024]{0:T(1024)S(1)} fusion(bf16[1024,1024]{1,0:T(8,128)(2,1)} %param.4), kind=kLoop, calls=%fused_computation.18 | loop fusion | flops 3144704 | bytes 2101248 | tf_op jit(solution)/shard_map/reduce_sum | solution.py:16
  15.1 2.7 %fusion.16 = (f32[1024]{0:T(1024)S(1)}, f32[1024,1024]{1,0:T(8,128)S(1)}) fusion(f32[1024]{0:T(1024)S(1)} %get-tuple-element.9, f32[1024]{0:T(1024)S(1)} %get-tuple-element.10, bf16[1024,1024]{1,0:T(8,128)(2,1)S(1)} %copy-done.3, bf16[1024,1024]{1,0:T(8,128)(2,1)S(1)} %copy-done.2), kind=kOutput, calls=%fused_computation.53 | convolution fusion | flops 2151676928 | bytes 8400896 | tf_op jit(solution)/shard_map/pd,kd->pk/dot_general | solution.py:93
  20.7 2.0 %collective-permute-done.1 = f32[1024]{0:T(1024)S(1)} collective-permute-done((f32[1024]{0:T(1024)S(1)}, f32[1024]{0:T(1024)S(1)}, u32[]{:S(2)}, u32[]{:S(2)}) %collective-permute-start.1) | collective-permute-done | bytes 4128 | tf_op jit(solution)/shard_map/ppermute | solution.py:31
  22.7 3.2 %collective-permute-start.2 = (f32[1024]{0:T(1024)S(1)}, f32[1024]{0:T(1024)S(1)}, u32[]{:S(2)}, u32[]{:S(2)}) collective-permute-start(f32[1024]{0:T(1024)S(1)} %add.130), channel_id=1, source_target_pairs={{0,4},{1,5},{2,6},{3,7},{4,0},{5,1},{6,2},{7,3},{8,12},{9,13},{10,... | collective-permute-start | bytes 12296 | tf_op jit(solution)/shard_map/ppermute | solution.py:31
  29.3 2.3 %collective-permute-done.3 = f32[1024]{0:T(1024)S(1)} collective-permute-done((f32[1024]{0:T(1024)S(1)}, f32[1024]{0:T(1024)S(1)}, u32[]{:S(2)}, u32[]{:S(2)}) %collective-permute-start.3) | collective-permute-done | bytes 4128 | tf_op jit(solution)/shard_map/ppermute | solution.py:31
  31.7 3.0 %collective-permute-start.4 = (f32[1024]{0:T(1024)S(1)}, f32[1024]{0:T(1024)S(1)}, u32[]{:S(2)}, u32[]{:S(2)}) collective-permute-start(f32[1024]{0:T(1024)S(1)} %add.132), channel_id=1, source_target_pairs={{0,16},{1,17},{2,18},{3,19},{4,20},{5,21},{6,22},{7,23},{8,24},{9,... | collective-permute-start | bytes 12296 | tf_op jit(solution)/shard_map/ppermute | solution.py:31
  34.7 2.1 %collective-permute-done.4 = f32[1024]{0:T(1024)S(1)} collective-permute-done((f32[1024]{0:T(1024)S(1)}, f32[1024]{0:T(1024)S(1)}, u32[]{:S(2)}, u32[]{:S(2)}) %collective-permute-start.4) | collective-permute-done | bytes 4128 | tf_op jit(solution)/shard_map/ppermute | solution.py:31
  40.9 3.1 %collective-permute-start.6 = (f32[1024]{0:T(1024)S(1)}, f32[1024]{0:T(1024)S(1)}, u32[]{:S(2)}, u32[]{:S(2)}) collective-permute-start(f32[1024]{0:T(1024)S(1)} %add.134), channel_id=1, source_target_pairs={{0,64},{32,96},{64,0},{96,32},{128,192},{160,224},{192,128},{224,1... | collective-permute-start | bytes 12296 | tf_op jit(solution)/shard_map/ppermute | solution.py:40
  45.6 5.9 %collective-permute-start.7 = (f32[1024]{0:T(1024)S(1)}, f32[1024]{0:T(1024)S(1)}, u32[]{:S(2)}, u32[]{:S(2)}) collective-permute-start(f32[1024]{0:T(1024)S(1)} %add.135), channel_id=1, source_target_pairs={{0,128},{32,160},{64,192},{96,224},{128,0},{160,32},{192,64},{224,... | collective-permute-start | bytes 12296 | tf_op jit(solution)/shard_map/ppermute | solution.py:40
  56.4 2.2 %collective-permute-done.9 = f32[1024]{0:T(1024)S(1)} collective-permute-done((f32[1024]{0:T(1024)S(1)}, f32[1024]{0:T(1024)S(1)}, u32[]{:S(2)}, u32[]{:S(2)}) %collective-permute-start.9) | collective-permute-done | bytes 4128 | tf_op jit(solution)/shard_map/ppermute | solution.py:31
  58.6 3.4 %collective-permute-start.10 = (f32[1024]{0:T(1024)S(1)}, f32[1024]{0:T(1024)S(1)}, u32[]{:S(2)}, u32[]{:S(2)}) collective-permute-start(f32[1024]{0:T(1024)S(1)} %add.138), channel_id=1, source_target_pairs={{0,4},{1,5},{2,6},{3,7},{4,0},{5,1},{6,2},{7,3},{8,12},{9,13},{10,... | collective-permute-start | bytes 12296 | tf_op jit(solution)/shard_map/ppermute | solution.py:31
  65.4 2.3 %collective-permute-done.11 = f32[1024]{0:T(1024)S(1)} collective-permute-done((f32[1024]{0:T(1024)S(1)}, f32[1024]{0:T(1024)S(1)}, u32[]{:S(2)}, u32[]{:S(2)}) %collective-permute-start.11) | collective-permute-done | bytes 4128 | tf_op jit(solution)/shard_map/ppermute | solution.py:31
  67.7 3.1 %collective-permute-start.12 = (f32[1024]{0:T(1024)S(1)}, f32[1024]{0:T(1024)S(1)}, u32[]{:S(2)}, u32[]{:S(2)}) collective-permute-start(f32[1024]{0:T(1024)S(1)} %add.140), channel_id=1, source_target_pairs={{0,16},{1,17},{2,18},{3,19},{4,20},{5,21},{6,22},{7,23},{8,24},{9,... | collective-permute-start | bytes 12296 | tf_op jit(solution)/shard_map/ppermute | solution.py:31
  70.8 2.2 %collective-permute-done.12 = f32[1024]{0:T(1024)S(1)} collective-permute-done((f32[1024]{0:T(1024)S(1)}, f32[1024]{0:T(1024)S(1)}, u32[]{:S(2)}, u32[]{:S(2)}) %collective-permute-start.12) | collective-permute-done | bytes 4128 | tf_op jit(solution)/shard_map/ppermute | solution.py:31
  75.2 2.1 %collective-permute-done.13 = f32[1024]{0:T(1024)S(1)} collective-permute-done((f32[1024]{0:T(1024)S(1)}, f32[1024]{0:T(1024)S(1)}, u32[]{:S(2)}, u32[]{:S(2)}) %collective-permute-start.13) | collective-permute-done | bytes 4128 | tf_op jit(solution)/shard_map/ppermute | solution.py:40
  77.3 2.9 %collective-permute-start.14 = (f32[1024]{0:T(1024)S(1)}, f32[1024]{0:T(1024)S(1)}, u32[]{:S(2)}, u32[]{:S(2)}) collective-permute-start(f32[1024]{0:T(1024)S(1)} %add.142), channel_id=1, source_target_pairs={{0,64},{32,96},{64,0},{96,32},{128,192},{160,224},{192,128},{224,1... | collective-permute-start | bytes 12296 | tf_op jit(solution)/shard_map/ppermute | solution.py:40
  81.8 5.9 %collective-permute-start.15 = (f32[1024]{0:T(1024)S(1)}, f32[1024]{0:T(1024)S(1)}, u32[]{:S(2)}, u32[]{:S(2)}) collective-permute-start(f32[1024]{0:T(1024)S(1)} %add.143), channel_id=1, source_target_pairs={{0,128},{32,160},{64,192},{96,224},{128,0},{160,32},{192,64},{224,... | collective-permute-start | bytes 12296 | tf_op jit(solution)/shard_map/ppermute | solution.py:40
  94.5 3.3 %collective-permute-start.18 = (f32[1024]{0:T(1024)S(1)}, f32[1024]{0:T(1024)S(1)}, u32[]{:S(2)}, u32[]{:S(2)}) collective-permute-start(f32[1024]{0:T(1024)S(1)} %add.146), channel_id=1, source_target_pairs={{0,4},{1,5},{2,6},{3,7},{4,0},{5,1},{6,2},{7,3},{8,12},{9,13},{10,... | collective-permute-start | bytes 12296 | tf_op jit(solution)/shard_map/ppermute | solution.py:31
  97.9 4.3 %scatter_custom_fusion = s32[4096]{0:T(1024)S(1)} fusion(s32[1024]{0:T(1024)S(1)} %bitcast.23, s32[1024]{0:T(1024)S(1)} %iota.23, s32[]{:T(128)} %constant.18.clone.1), kind=kCustom, calls=%fused_computation.34 | custom fusion | bytes 16388 | tf_op jit(solution)/shard_map/scatter | solution.py:82
  103.8 12.3 %multiply_reduce_fusion = (f32[4096]{0:T(1024)S(1)}, bf16[4096,1024]{1,0:T(8,128)(2,1)}) fusion(bf16[1024,1024]{1,0:T(8,128)(2,1)S(1)} %copy-done.4, s32[4096]{0:T(1024)S(1)} %scatter_custom_fusion), kind=kOutput, calls=%fused_computation.4 | convolution fusion | flops 8610902016 | bytes 10518528 | tf_op jit(solution)/shard_map/dot_general | solution.py:84
  116.1 2.8 %collective-permute-start.20 = (f32[1024]{0:T(1024)S(1)}, f32[1024]{0:T(1024)S(1)}, u32[]{:S(2)}, u32[]{:S(2)}) collective-permute-start(f32[1024]{0:T(1024)S(1)} %add.148), channel_id=1, source_target_pairs={{0,16},{1,17},{2,18},{3,19},{4,20},{5,21},{6,22},{7,23},{8,24},{9,... | collective-permute-start | bytes 12296 | tf_op jit(solution)/shard_map/ppermute | solution.py:31
  118.9 2.3 %collective-permute-done.20 = f32[1024]{0:T(1024)S(1)} collective-permute-done((f32[1024]{0:T(1024)S(1)}, f32[1024]{0:T(1024)S(1)}, u32[]{:S(2)}, u32[]{:S(2)}) %collective-permute-start.20) | collective-permute-done | bytes 4128 | tf_op jit(solution)/shard_map/ppermute | solution.py:31
  122.7 2.5 %collective-permute-done.21 = f32[1024]{0:T(1024)S(1)} collective-permute-done((f32[1024]{0:T(1024)S(1)}, f32[1024]{0:T(1024)S(1)}, u32[]{:S(2)}, u32[]{:S(2)}) %collective-permute-start.21) | collective-permute-done | bytes 4128 | tf_op jit(solution)/shard_map/ppermute | solution.py:40
  125.3 2.9 %collective-permute-start.22 = (f32[1024]{0:T(1024)S(1)}, f32[1024]{0:T(1024)S(1)}, u32[]{:S(2)}, u32[]{:S(2)}) collective-permute-start(f32[1024]{0:T(1024)S(1)} %add.150), channel_id=1, source_target_pairs={{0,64},{32,96},{64,0},{96,32},{128,192},{160,224},{192,128},{224,1... | collective-permute-start | bytes 12296 | tf_op jit(solution)/shard_map/ppermute | solution.py:40
  129.3 11.3 %multiply_exponential_fusion.1 = f32[64,64,128]{2,1,0:T(8,128)S(1)} fusion(bf16[64,64,1024]{2,1,0:T(8,128)(2,1)} %bitcast.27, bf16[64,136,1024]{2,1,0:T(8,128)(2,1)} %all-gather.2.cloned.1.call-done, f32[64,128]{1,0:T(8,128)S(1)} %slice_add_fusion, f32[64,64]{1,0:T(8,128)S(1)} %rsqrt.31), kind=kOutput, calls=%fused_computation.20 | convolution fusion | flops 1075314688 | bytes 27312128 | tf_op jit(solution)/shard_map/gcd,gkd->gck/dot_general | solution.py:87
  140.6 2.8 %gather_fusion = f32[1024,128]{1,0:T(8,128)S(1)} fusion(f32[4096,128]{1,0:T(8,128)S(1)} %bitcast.21, s32[1024]{0:T(1024)S(1)} %broadcast_clamp_fusion), kind=kCustom, calls=%fused_computation | custom fusion | bytes 1052672 | tf_op jit(solution)/shard_map/gather | solution.py:89
  143.8 5.3 %collective-permute-start.23 = (f32[1024]{0:T(1024)S(1)}, f32[1024]{0:T(1024)S(1)}, u32[]{:S(2)}, u32[]{:S(2)}) collective-permute-start(f32[1024]{0:T(1024)S(1)} %add.151), channel_id=1, source_target_pairs={{0,128},{32,160},{64,192},{96,224},{128,0},{160,32},{192,64},{224,... | collective-permute-start | bytes 12296 | tf_op jit(solution)/shard_map/ppermute | solution.py:40
  151.4 2.3 %collective-permute-done.25 = f32[1024]{0:T(1024)S(1)} collective-permute-done((f32[1024]{0:T(1024)S(1)}, f32[1024]{0:T(1024)S(1)}, u32[]{:S(2)}, u32[]{:S(2)}) %collective-permute-start.25) | collective-permute-done | bytes 4128 | tf_op jit(solution)/shard_map/ppermute | solution.py:40
  153.7 3.1 %collective-permute-start.26 = (f32[1024]{0:T(1024)S(1)}, f32[1024]{0:T(1024)S(1)}, u32[]{:S(2)}, u32[]{:S(2)}) collective-permute-start(f32[1024]{0:T(1024)S(1)} %add.162), channel_id=1, source_target_pairs={{0,128},{32,160},{64,192},{96,224},{128,0},{160,32},{192,64},{224,... | collective-permute-start | bytes 12296 | tf_op jit(solution)/shard_map/ppermute | solution.py:40
  156.8 4.0 %multiply_convert_fusion = bf16[1024,1024]{1,0:T(8,128)(2,1)} fusion(f32[1024,1024]{1,0:T(8,128)} %copy-done, f32[1024]{0:T(1024)S(1)} %add_divide_fusion, f32[1024]{0:T(1024)S(1)} %add_divide_fusion.1), kind=kLoop, calls=%fused_computation.10 | loop fusion | flops 4194304 | bytes 6299648 | tf_op jit(solution)/shard_map/convert_element_type | solution.py:109
  (99 shorter events, 40.5 us)
Async XLA Ops:
  7.2 121.0 %all-gather.2.cloned.1.call-start = ((), (), s32[]{:S(2)}) async-start(), calls=%async_computation | async-start | bytes 18382848 | tf_op jit(solution)/shard_map/all_gather | solution.py:69
  17.8 71.5 %copy-start = (f32[1024,1024]{1,0:T(8,128)}, f32[1024,1024]{1,0:T(8,128)S(1)}, u32[]{:S(2)}) copy-start(f32[1024,1024]{1,0:T(8,128)S(1)} %get-tuple-element.6) | copy-start | bytes 12582916
  17.9 1.3 collective-permute-start
  19.1 3.6 %collective-permute-start.1 = (f32[1024]{0:T(1024)S(1)}, f32[1024]{0:T(1024)S(1)}, u32[]{:S(2)}, u32[]{:S(2)}) collective-permute-start(f32[1024]{0:T(1024)S(1)} %add.129), channel_id=1, source_target_pairs={{0,2},{1,3},{2,0},{3,1},{4,6},{5,7},{6,4},{7,5},{8,10},{9,11},{10,... | collective-permute-start | bytes 12296 | tf_op jit(solution)/shard_map/ppermute | solution.py:31
  22.7 5.1 %collective-permute-start.2 = (f32[1024]{0:T(1024)S(1)}, f32[1024]{0:T(1024)S(1)}, u32[]{:S(2)}, u32[]{:S(2)}) collective-permute-start(f32[1024]{0:T(1024)S(1)} %add.130), channel_id=1, source_target_pairs={{0,4},{1,5},{2,6},{3,7},{4,0},{5,1},{6,2},{7,3},{8,12},{9,13},{10,... | collective-permute-start | bytes 12296 | tf_op jit(solution)/shard_map/ppermute | solution.py:31
  27.8 3.8 %collective-permute-start.3 = (f32[1024]{0:T(1024)S(1)}, f32[1024]{0:T(1024)S(1)}, u32[]{:S(2)}, u32[]{:S(2)}) collective-permute-start(f32[1024]{0:T(1024)S(1)} %add.131), channel_id=1, source_target_pairs={{0,8},{1,9},{2,10},{3,11},{4,12},{5,13},{6,14},{7,15},{8,0},{9,1},... | collective-permute-start | bytes 12296 | tf_op jit(solution)/shard_map/ppermute | solution.py:31
  31.7 5.2 %collective-permute-start.4 = (f32[1024]{0:T(1024)S(1)}, f32[1024]{0:T(1024)S(1)}, u32[]{:S(2)}, u32[]{:S(2)}) collective-permute-start(f32[1024]{0:T(1024)S(1)} %add.132), channel_id=1, source_target_pairs={{0,16},{1,17},{2,18},{3,19},{4,20},{5,21},{6,22},{7,23},{8,24},{9,... | collective-permute-start | bytes 12296 | tf_op jit(solution)/shard_map/ppermute | solution.py:31
  37.2 3.7 %collective-permute-start.5 = (f32[1024]{0:T(1024)S(1)}, f32[1024]{0:T(1024)S(1)}, u32[]{:S(2)}, u32[]{:S(2)}) collective-permute-start(f32[1024]{0:T(1024)S(1)} %multiply_reduce_fusion.5), channel_id=1, source_target_pairs={{0,32},{32,0},{64,96},{96,64},{128,160},{160,128},{192,224},{224,1... | collective-permute-start | bytes 12296 | tf_op jit(solution)/shard_map/ppermute | solution.py:40
  40.9 4.7 %collective-permute-start.6 = (f32[1024]{0:T(1024)S(1)}, f32[1024]{0:T(1024)S(1)}, u32[]{:S(2)}, u32[]{:S(2)}) collective-permute-start(f32[1024]{0:T(1024)S(1)} %add.134), channel_id=1, source_target_pairs={{0,64},{32,96},{64,0},{96,32},{128,192},{160,224},{192,128},{224,1... | collective-permute-start | bytes 12296 | tf_op jit(solution)/shard_map/ppermute | solution.py:40
  45.6 7.5 %collective-permute-start.7 = (f32[1024]{0:T(1024)S(1)}, f32[1024]{0:T(1024)S(1)}, u32[]{:S(2)}, u32[]{:S(2)}) collective-permute-start(f32[1024]{0:T(1024)S(1)} %add.135), channel_id=1, source_target_pairs={{0,128},{32,160},{64,192},{96,224},{128,0},{160,32},{192,64},{224,... | collective-permute-start | bytes 12296 | tf_op jit(solution)/shard_map/ppermute | solution.py:40
  53.5 1.3 collective-permute-start.8
  54.7 3.8 %collective-permute-start.9 = (f32[1024]{0:T(1024)S(1)}, f32[1024]{0:T(1024)S(1)}, u32[]{:S(2)}, u32[]{:S(2)}) collective-permute-start(f32[1024]{0:T(1024)S(1)} %add.137), channel_id=1, source_target_pairs={{0,2},{1,3},{2,0},{3,1},{4,6},{5,7},{6,4},{7,5},{8,10},{9,11},{10,... | collective-permute-start | bytes 12296 | tf_op jit(solution)/shard_map/ppermute | solution.py:31
  58.6 5.3 %collective-permute-start.10 = (f32[1024]{0:T(1024)S(1)}, f32[1024]{0:T(1024)S(1)}, u32[]{:S(2)}, u32[]{:S(2)}) collective-permute-start(f32[1024]{0:T(1024)S(1)} %add.138), channel_id=1, source_target_pairs={{0,4},{1,5},{2,6},{3,7},{4,0},{5,1},{6,2},{7,3},{8,12},{9,13},{10,... | collective-permute-start | bytes 12296 | tf_op jit(solution)/shard_map/ppermute | solution.py:31
  63.9 3.8 %collective-permute-start.11 = (f32[1024]{0:T(1024)S(1)}, f32[1024]{0:T(1024)S(1)}, u32[]{:S(2)}, u32[]{:S(2)}) collective-permute-start(f32[1024]{0:T(1024)S(1)} %add.139), channel_id=1, source_target_pairs={{0,8},{1,9},{2,10},{3,11},{4,12},{5,13},{6,14},{7,15},{8,0},{9,1},... | collective-permute-start | bytes 12296 | tf_op jit(solution)/shard_map/ppermute | solution.py:31
  67.7 5.3 %collective-permute-start.12 = (f32[1024]{0:T(1024)S(1)}, f32[1024]{0:T(1024)S(1)}, u32[]{:S(2)}, u32[]{:S(2)}) collective-permute-start(f32[1024]{0:T(1024)S(1)} %add.140), channel_id=1, source_target_pairs={{0,16},{1,17},{2,18},{3,19},{4,20},{5,21},{6,22},{7,23},{8,24},{9,... | collective-permute-start | bytes 12296 | tf_op jit(solution)/shard_map/ppermute | solution.py:31
  73.1 19.5 %copy-start.5 = (s32[1024,1]{0,1:T(1,128)S(1)}, s32[1024,1]{0,1:T(1,128)}, u32[]{:S(2)}) copy-start(s32[1024,1]{0,1:T(1,128)} %param.5) | copy-start | bytes 12292
  73.1 30.8 %copy-start.4 = (bf16[1024,1024]{1,0:T(8,128)(2,1)S(1)}, bf16[1024,1024]{1,0:T(8,128)(2,1)}, u32[]{:S(2)}) copy-start(bf16[1024,1024]{1,0:T(8,128)(2,1)} %param.4) | copy-start | bytes 6291460
  73.4 3.9 %collective-permute-start.13 = (f32[1024]{0:T(1024)S(1)}, f32[1024]{0:T(1024)S(1)}, u32[]{:S(2)}, u32[]{:S(2)}) collective-permute-start(f32[1024]{0:T(1024)S(1)} %multiply_reduce_fusion.3), channel_id=1, source_target_pairs={{0,32},{32,0},{64,96},{96,64},{128,160},{160,128},{192,224},{224,1... | collective-permute-start | bytes 12296 | tf_op jit(solution)/shard_map/ppermute | solution.py:40
  77.3 4.5 %collective-permute-start.14 = (f32[1024]{0:T(1024)S(1)}, f32[1024]{0:T(1024)S(1)}, u32[]{:S(2)}, u32[]{:S(2)}) collective-permute-start(f32[1024]{0:T(1024)S(1)} %add.142), channel_id=1, source_target_pairs={{0,64},{32,96},{64,0},{96,32},{128,192},{160,224},{192,128},{224,1... | collective-permute-start | bytes 12296 | tf_op jit(solution)/shard_map/ppermute | solution.py:40
  81.8 7.5 %collective-permute-start.15 = (f32[1024]{0:T(1024)S(1)}, f32[1024]{0:T(1024)S(1)}, u32[]{:S(2)}, u32[]{:S(2)}) collective-permute-start(f32[1024]{0:T(1024)S(1)} %add.143), channel_id=1, source_target_pairs={{0,128},{32,160},{64,192},{96,224},{128,0},{160,32},{192,64},{224,... | collective-permute-start | bytes 12296 | tf_op jit(solution)/shard_map/ppermute | solution.py:40
  89.7 1.3 collective-permute-start.16
  90.9 3.6 %collective-permute-start.17 = (f32[1024]{0:T(1024)S(1)}, f32[1024]{0:T(1024)S(1)}, u32[]{:S(2)}, u32[]{:S(2)}) collective-permute-start(f32[1024]{0:T(1024)S(1)} %add.145), channel_id=1, source_target_pairs={{0,2},{1,3},{2,0},{3,1},{4,6},{5,7},{6,4},{7,5},{8,10},{9,11},{10,... | collective-permute-start | bytes 12296 | tf_op jit(solution)/shard_map/ppermute | solution.py:31
  94.5 7.7 %collective-permute-start.18 = (f32[1024]{0:T(1024)S(1)}, f32[1024]{0:T(1024)S(1)}, u32[]{:S(2)}, u32[]{:S(2)}) collective-permute-start(f32[1024]{0:T(1024)S(1)} %add.146), channel_id=1, source_target_pairs={{0,4},{1,5},{2,6},{3,7},{4,0},{5,1},{6,2},{7,3},{8,12},{9,13},{10,... | collective-permute-start | bytes 12296 | tf_op jit(solution)/shard_map/ppermute | solution.py:31
  102.3 18.9 %copy-start.1 = (f32[1024,1024]{1,0:T(8,128)S(1)}, f32[1024,1024]{1,0:T(8,128)}, u32[]{:S(2)}) copy-start(f32[1024,1024]{1,0:T(8,128)} %copy-done) | copy-start | bytes 12582916
  102.3 13.8 %collective-permute-start.19 = (f32[1024]{0:T(1024)S(1)}, f32[1024]{0:T(1024)S(1)}, u32[]{:S(2)}, u32[]{:S(2)}) collective-permute-start(f32[1024]{0:T(1024)S(1)} %add.147), channel_id=1, source_target_pairs={{0,8},{1,9},{2,10},{3,11},{4,12},{5,13},{6,14},{7,15},{8,0},{9,1},... | collective-permute-start | bytes 12296 | tf_op jit(solution)/shard_map/ppermute | solution.py:31
  116.1 5.1 %collective-permute-start.20 = (f32[1024]{0:T(1024)S(1)}, f32[1024]{0:T(1024)S(1)}, u32[]{:S(2)}, u32[]{:S(2)}) collective-permute-start(f32[1024]{0:T(1024)S(1)} %add.148), channel_id=1, source_target_pairs={{0,16},{1,17},{2,18},{3,19},{4,20},{5,21},{6,22},{7,23},{8,24},{9,... | collective-permute-start | bytes 12296 | tf_op jit(solution)/shard_map/ppermute | solution.py:31
  121.6 3.7 %collective-permute-start.21 = (f32[1024]{0:T(1024)S(1)}, f32[1024]{0:T(1024)S(1)}, u32[]{:S(2)}, u32[]{:S(2)}) collective-permute-start(f32[1024]{0:T(1024)S(1)} %multiply_reduce_fusion.1), channel_id=1, source_target_pairs={{0,32},{32,0},{64,96},{96,64},{128,160},{160,128},{192,224},{224,1... | collective-permute-start | bytes 12296 | tf_op jit(solution)/shard_map/ppermute | solution.py:40
  125.3 18.6 %collective-permute-start.22 = (f32[1024]{0:T(1024)S(1)}, f32[1024]{0:T(1024)S(1)}, u32[]{:S(2)}, u32[]{:S(2)}) collective-permute-start(f32[1024]{0:T(1024)S(1)} %add.150), channel_id=1, source_target_pairs={{0,64},{32,96},{64,0},{96,32},{128,192},{160,224},{192,128},{224,1... | collective-permute-start | bytes 12296 | tf_op jit(solution)/shard_map/ppermute | solution.py:40
  143.6 5.6 %collective-permute-start.24 = (f32[1024]{0:T(1024)S(1)}, f32[1024]{0:T(1024)S(1)}, u32[]{:S(2)}, u32[]{:S(2)}) collective-permute-start(f32[1024]{0:T(1024)S(1)} %reduce_sum.119), channel_id=1, source_target_pairs={{0,32},{32,0},{64,96},{96,64},{128,160},{160,128},{192,224},{224,1... | collective-permute-start | bytes 12296 | tf_op jit(solution)/shard_map/ppermute | solution.py:40
  143.8 7.5 %collective-permute-start.23 = (f32[1024]{0:T(1024)S(1)}, f32[1024]{0:T(1024)S(1)}, u32[]{:S(2)}, u32[]{:S(2)}) collective-permute-start(f32[1024]{0:T(1024)S(1)} %add.151), channel_id=1, source_target_pairs={{0,128},{32,160},{64,192},{96,224},{128,0},{160,32},{192,64},{224,... | collective-permute-start | bytes 12296 | tf_op jit(solution)/shard_map/ppermute | solution.py:40
  149.2 4.5 %collective-permute-start.25 = (f32[1024]{0:T(1024)S(1)}, f32[1024]{0:T(1024)S(1)}, u32[]{:S(2)}, u32[]{:S(2)}) collective-permute-start(f32[1024]{0:T(1024)S(1)} %add.161), channel_id=1, source_target_pairs={{0,64},{32,96},{64,0},{96,32},{128,192},{160,224},{192,128},{224,1... | collective-permute-start | bytes 12296 | tf_op jit(solution)/shard_map/ppermute | solution.py:40
  153.7 7.5 %collective-permute-start.26 = (f32[1024]{0:T(1024)S(1)}, f32[1024]{0:T(1024)S(1)}, u32[]{:S(2)}, u32[]{:S(2)}) collective-permute-start(f32[1024]{0:T(1024)S(1)} %add.162), channel_id=1, source_target_pairs={{0,128},{32,160},{64,192},{96,224},{128,0},{160,32},{192,64},{224,... | collective-permute-start | bytes 12296 | tf_op jit(solution)/shard_map/ppermute | solution.py:40
  (2 other events, 12.3 us)
Sparse Core Ops, SparseCore 0:
  11.1 82.6 all-gather.1

commit v8 on v6

--- a/solution.py
+++ b/solution.py
@@ -103,7 +103,7 @@
         col_scale = 1.0 / dp_sum(col_part)
         row_part = jnp.sum(expo * col_scale[None, :], axis=1)
         if step + 1 < ITERS:
-            row_scale = 1.0 / cent_sum(row_part)
+            row_scale = 1.0 / lax.psum(row_part, "cent")
 
     row_total = cent_sum(row_part)
     denominator = cent_sum(denom_part)

time: 162 us -> 167 us (1.031)
  blocking collectives: 0 us -> 34.2 us
  starting transfers between devices: 62.2 us -> 42.8 us
  waiting for transfers between devices: 34.1 us -> 19 us
  other arithmetic: 15.8 us -> 20.3 us
    psum x0 -> x2, blocking collectives: none -> 34.2 us  [shards(): row_scale = 1.0 / lax.psum(row_part, 'cent')]
    ppermute x12 -> x6, starting transfers between devices: 33.5 us -> 11.7 us  [cent_sum(): lax.ppermute(values, 'cent', [(i, i ^ bit) for i in range(count)])]
    ppermute x12 -> x6, waiting for transfers between devices: 17.7 us -> 4.73 us  [cent_sum(): lax.ppermute(values, 'cent', [(i, i ^ bit) for i in range(count)])]
    reduce_sum x2, other arithmetic: 0.7 us -> 5.23 us  [shards(): col_part = jnp.sum(expo * row_scale[:, None], axis=0)]
    ppermute x21, starting transfers between devices: 28.7 us -> 31 us  [dp_sum(): lax.ppermute(values, 'dp', shift_pairs(count, stride, size, step))]
    ppermute x21, waiting for transfers between devices: 16.4 us -> 14.3 us  [dp_sum(): lax.ppermute(values, 'dp', shift_pairs(count, stride, size, step))]
  transfers between devices with their start and end apart: 34 -> 28, of which waited for: 25 -> 17; matrix products, arithmetic and copies ran while one was open for 28% -> 30% of each run, Pallas kernels for 0% -> 0%
where the time goes in v8:
time: 167 us; the launch traced here: 165 us
  starting transfers between devices  42.8 us (26%)
  blocking collectives  34.2 us (20%)
  matrix products  27 us (16%)
  other arithmetic  20.3 us (12%)
  waiting for transfers between devices  19 us (11%)
  between operations  14.4 us (9%)
  local copies, waits for them, and re-layouts  7.36 us (4%)
    psum x2, blocking collectives, shards(): row_scale = 1.0 / lax.psum(row_part, 'cent')  34.2 us
    ppermute x21, starting transfers between devices, dp_sum(): lax.ppermute(values, 'dp', shift_pairs(count, stride, size, step))  31 us
    ppermute x21, waiting for transfers between devices, dp_sum(): lax.ppermute(values, 'dp', shift_pairs(count, stride, size, step))  14.3 us
    dot_general x1, matrix products, shards(): jnp.dot(pick, points, preferred_element_type=jnp.float32)  12.4 us
    ppermute x6, starting transfers between devices, cent_sum(): lax.ppermute(values, 'cent', [(i, i ^ bit) for i in range(count)])  11.7 us
    dot_general x1, matrix products, shards(): jnp.einsum('gcd,gkd->gck', buffer, gathered, preferred_element_type=jnp.f...  11.3 us
    reduce_sum x3, other arithmetic, inverse_norm(): return lax.rsqrt(jnp.mean(values * values, axis=-1) + EPS)  5.65 us
    reduce_sum x2, other arithmetic, shards(): col_part = jnp.sum(expo * row_scale[:, None], axis=0)  5.23 us
  transfers between devices with their start and end apart: 28, of which 17 were waited for; matrix products, arithmetic and copies ran while one was open for 30% of the time, Pallas kernels for 0%

profile of v8, /device:TPU:32, one launch (start us, length us, event | category | flops | bytes accessed | tf_op | source)
XLA Modules:
  0.0 165.0 jit_solution(18020087442361700035)
XLA Ops:
  7.2 1.4 multiply_reduce_fusion.8
  8.7 2.0 %maximum_maximum_fusion = bf16[2,136,1024]{2,1,0:T(8,128)(2,1)} fusion(bf16[2,1,1024]{2,1,0:T(2,128)(2,1)S(1)} %copy.7, bf16[2,128,1024]{2,1,0:T(8,128)(2,1)} %param.7, bf16[136]{0:T(256)(128)(2,1)S(1)} %pad.2.clone), kind=kLoop, calls=%fused_computation.24 | loop fusion | flops 1671168 | bytes 1085712 | tf_op jit(solution)/shard_map/concatenate | solution.py:70
  10.8 2.2 %multiply_reduce_fusion.6 = f32[1024]{0:T(1024)S(1)} fusion(bf16[1024,1024]{1,0:T(8,128)(2,1)} %param.6), kind=kLoop, calls=%fused_computation.17 | loop fusion | flops 3144704 | bytes 2101248 | tf_op jit(solution)/shard_map/reduce_sum | solution.py:16
  13.0 2.1 %multiply_reduce_fusion.7 = f32[1024]{0:T(1024)S(1)} fusion(bf16[1024,1024]{1,0:T(8,128)(2,1)} %param.4), kind=kLoop, calls=%fused_computation.18 | loop fusion | flops 3144704 | bytes 2101248 | tf_op jit(solution)/shard_map/reduce_sum | solution.py:16
  15.1 2.7 %fusion.16 = (f32[1024]{0:T(1024)S(1)}, f32[1024,1024]{1,0:T(8,128)S(1)}) fusion(f32[1024]{0:T(1024)S(1)} %get-tuple-element.9, f32[1024]{0:T(1024)S(1)} %get-tuple-element.10, bf16[1024,1024]{1,0:T(8,128)(2,1)S(1)} %copy-done.4, bf16[1024,1024]{1,0:T(8,128)(2,1)S(1)} %copy-done.3), kind=kOutput, calls=%fused_computation.56 | convolution fusion | flops 2151676928 | bytes 8400896 | tf_op jit(solution)/shard_map/pd,kd->pk/dot_general | solution.py:95
  19.1 1.6 collective-permute-start.1
  20.7 2.9 %collective-permute-start.2 = (f32[1024]{0:T(1024)S(1)}, f32[1024]{0:T(1024)S(1)}, u32[]{:S(2)}, u32[]{:S(2)}) collective-permute-start(f32[1024]{0:T(1024)S(1)} %add.133), channel_id=1, source_target_pairs={{0,4},{1,5},{2,6},{3,7},{4,0},{5,1},{6,2},{7,3},{8,12},{9,13},{10,... | collective-permute-start | bytes 12296 | tf_op jit(solution)/shard_map/ppermute | solution.py:32
  25.8 1.4 collective-permute-done.3
  27.2 1.5 collective-permute-start.4
  28.7 2.7 %collective-permute-start.5 = (f32[1024]{0:T(1024)S(1)}, f32[1024]{0:T(1024)S(1)}, u32[]{:S(2)}, u32[]{:S(2)}) collective-permute-start(f32[1024]{0:T(1024)S(1)} %add_add_fusion.2), channel_id=1, source_target_pairs={{0,16},{1,17},{2,18},{3,19},{4,20},{5,21},{6,22},{7,23},{8,24},{9,... | collective-permute-start | bytes 12296 | tf_op jit(solution)/shard_map/ppermute | solution.py:32
  31.4 1.4 collective-permute-start.6
  35.4 17.8 %psum.14 = f32[1024]{0:T(1024)S(1)} all-reduce(f32[1024]{0:T(1024)S(1)} %multiply_reduce_fusion.5), channel_id=1, replica_groups=mesh['cent'=8,'dp'=32] {'cent'}, use_global_device_ids=true, to_apply=%region_4.0 | all-reduce | flops 1024 | bytes 8192 | tf_op jit(solution)/shard_map/psum | solution.py:106
  53.3 2.7 %multiply_reduce_fusion.4 = f32[1024]{0:T(1024)S(1)} fusion(f32[1024,1024]{1,0:T(8,128)} %copy-done, f32[1024]{0:T(1024)S(1)} %broadcast_divide_fusion.1), kind=kLoop, calls=%fused_computation.14 | loop fusion | flops 2096128 | bytes 4202496 | tf_op jit(solution)/shard_map/reduce_sum | solution.py:102
  57.3 2.7 %collective-permute-start.10 = (f32[1024]{0:T(1024)S(1)}, f32[1024]{0:T(1024)S(1)}, u32[]{:S(2)}, u32[]{:S(2)}) collective-permute-start(f32[1024]{0:T(1024)S(1)} %add.140), channel_id=1, source_target_pairs={{0,6},{1,7},{2,0},{3,1},{4,2},{5,3},{6,4},{7,5},{8,14},{9,15},{10,... | collective-permute-start | bytes 12296 | tf_op jit(solution)/shard_map/ppermute | solution.py:32
  60.0 2.1 %collective-permute-start.9 = (f32[1024]{0:T(1024)S(1)}, f32[1024]{0:T(1024)S(1)}, u32[]{:S(2)}, u32[]{:S(2)}) collective-permute-start(f32[1024]{0:T(1024)S(1)} %add.140), channel_id=1, source_target_pairs={{0,4},{1,5},{2,6},{3,7},{4,0},{5,1},{6,2},{7,3},{8,12},{9,13},{10,... | collective-permute-start | bytes 12296 | tf_op jit(solution)/shard_map/ppermute | solution.py:32
  62.1 2.9 %collective-permute-done.8 = f32[1024]{0:T(1024)S(1)} collective-permute-done((f32[1024]{0:T(1024)S(1)}, f32[1024]{0:T(1024)S(1)}, u32[]{:S(2)}, u32[]{:S(2)}) %collective-permute-start.8) | collective-permute-done | bytes 4128 | tf_op jit(solution)/shard_map/ppermute | solution.py:32
  65.3 1.5 collective-permute-start.11
  66.8 2.7 %collective-permute-start.12 = (f32[1024]{0:T(1024)S(1)}, f32[1024]{0:T(1024)S(1)}, u32[]{:S(2)}, u32[]{:S(2)}) collective-permute-start(f32[1024]{0:T(1024)S(1)} %add_add_fusion.1), channel_id=1, source_target_pairs={{0,16},{1,17},{2,18},{3,19},{4,20},{5,21},{6,22},{7,23},{8,24},{9,... | collective-permute-start | bytes 12296 | tf_op jit(solution)/shard_map/ppermute | solution.py:32
  73.7 16.4 %psum.15 = f32[1024]{0:T(1024)S(1)} all-reduce(f32[1024]{0:T(1024)S(1)} %multiply_reduce_fusion.3), channel_id=1, replica_groups=mesh['cent'=8,'dp'=32] {'cent'}, use_global_device_ids=true, to_apply=%region_7.0 | all-reduce | flops 1024 | bytes 8192 | tf_op jit(solution)/shard_map/psum | solution.py:106
  90.1 2.5 %multiply_reduce_fusion.2 = f32[1024]{0:T(1024)S(1)} fusion(f32[1024,1024]{1,0:T(8,128)} %copy-done, f32[1024]{0:T(1024)S(1)} %broadcast_divide_fusion), kind=kLoop, calls=%fused_computation.12 | loop fusion | flops 2096128 | bytes 4202496 | tf_op jit(solution)/shard_map/reduce_sum | solution.py:102
  92.7 4.3 %scatter_custom_fusion = s32[4096]{0:T(1024)S(1)} fusion(s32[1024]{0:T(1024)S(1)} %bitcast.23, s32[1024]{0:T(1024)S(1)} %iota.23, s32[]{:T(128)} %constant.18.clone.1), kind=kCustom, calls=%fused_computation.34 | custom fusion | bytes 16388 | tf_op jit(solution)/shard_map/scatter | solution.py:84
  97.9 4.0 %collective-permute-start.16 = (f32[1024]{0:T(1024)S(1)}, f32[1024]{0:T(1024)S(1)}, u32[]{:S(2)}, u32[]{:S(2)}) collective-permute-start(f32[1024]{0:T(1024)S(1)} %add.147), channel_id=1, source_target_pairs={{0,4},{1,5},{2,6},{3,7},{4,0},{5,1},{6,2},{7,3},{8,12},{9,13},{10,... | collective-permute-start | bytes 12296 | tf_op jit(solution)/shard_map/ppermute | solution.py:32
  101.9 12.4 %multiply_reduce_fusion = (f32[4096]{0:T(1024)S(1)}, bf16[4096,1024]{1,0:T(8,128)(2,1)}) fusion(bf16[1024,1024]{1,0:T(8,128)(2,1)S(1)} %copy-done.5, s32[4096]{0:T(1024)S(1)} %scatter_custom_fusion), kind=kOutput, calls=%fused_computation.4 | convolution fusion | flops 8610902016 | bytes 10518528 | tf_op jit(solution)/shard_map/dot_general | solution.py:86
  114.4 2.8 %collective-permute-start.19 = (f32[1024]{0:T(1024)S(1)}, f32[1024]{0:T(1024)S(1)}, u32[]{:S(2)}, u32[]{:S(2)}) collective-permute-start(f32[1024]{0:T(1024)S(1)} %add_add_fusion), channel_id=1, source_target_pairs={{0,16},{1,17},{2,18},{3,19},{4,20},{5,21},{6,22},{7,23},{8,24},{9,... | collective-permute-start | bytes 12296 | tf_op jit(solution)/shard_map/ppermute | solution.py:32
  117.2 1.4 collective-permute-start.20
  122.3 2.5 %collective-permute-done.21 = f32[1024]{0:T(1024)S(1)} collective-permute-done((f32[1024]{0:T(1024)S(1)}, f32[1024]{0:T(1024)S(1)}, u32[]{:S(2)}, u32[]{:S(2)}) %collective-permute-start.21) | collective-permute-done | bytes 4128 | tf_op jit(solution)/shard_map/ppermute | solution.py:42
  127.0 11.3 %multiply_exponential_fusion.1 = f32[64,64,128]{2,1,0:T(8,128)S(1)} fusion(bf16[64,64,1024]{2,1,0:T(8,128)(2,1)} %bitcast.27, bf16[64,136,1024]{2,1,0:T(8,128)(2,1)} %all-gather.2.cloned.1.call-done, f32[64,128]{1,0:T(8,128)S(1)} %slice_add_fusion, f32[64,64]{1,0:T(8,128)S(1)} %rsqrt.31), kind=kOutput, calls=%fused_computation.20 | convolution fusion | flops 1075314688 | bytes 27312128 | tf_op jit(solution)/shard_map/gcd,gkd->gck/dot_general | solution.py:89
  138.3 2.8 %gather_fusion = f32[1024,128]{1,0:T(8,128)S(1)} fusion(f32[4096,128]{1,0:T(8,128)S(1)} %bitcast.21, s32[1024]{0:T(1024)S(1)} %broadcast_clamp_fusion), kind=kCustom, calls=%fused_computation | custom fusion | bytes 1052672 | tf_op jit(solution)/shard_map/gather | solution.py:91
  141.6 3.5 %collective-permute-start.23 = (f32[1024]{0:T(1024)S(1)}, f32[1024]{0:T(1024)S(1)}, u32[]{:S(2)}, u32[]{:S(2)}) collective-permute-start(f32[1024]{0:T(1024)S(1)} %add.155), channel_id=1, source_target_pairs={{0,128},{32,160},{64,192},{96,224},{128,0},{160,32},{192,64},{224,... | collective-permute-start | bytes 12296 | tf_op jit(solution)/shard_map/ppermute | solution.py:42
  145.2 2.7 %collective-permute-start.25 = (f32[1024]{0:T(1024)S(1)}, f32[1024]{0:T(1024)S(1)}, u32[]{:S(2)}, u32[]{:S(2)}) collective-permute-start(f32[1024]{0:T(1024)S(1)} %add.165), channel_id=1, source_target_pairs={{0,64},{32,96},{64,0},{96,32},{128,192},{160,224},{192,128},{224,1... | collective-permute-start | bytes 12296 | tf_op jit(solution)/shard_map/ppermute | solution.py:42
  149.7 3.1 %collective-permute-start.26 = (f32[1024]{0:T(1024)S(1)}, f32[1024]{0:T(1024)S(1)}, u32[]{:S(2)}, u32[]{:S(2)}) collective-permute-start(f32[1024]{0:T(1024)S(1)} %add.166), channel_id=1, source_target_pairs={{0,128},{32,160},{64,192},{96,224},{128,0},{160,32},{192,64},{224,... | collective-permute-start | bytes 12296 | tf_op jit(solution)/shard_map/ppermute | solution.py:42
  152.8 4.0 %multiply_convert_fusion = bf16[1024,1024]{1,0:T(8,128)(2,1)} fusion(f32[1024,1024]{1,0:T(8,128)} %copy-done, f32[1024]{0:T(1024)S(1)} %add_divide_fusion, f32[1024]{0:T(1024)S(1)} %add_divide_fusion.1), kind=kLoop, calls=%fused_computation.10 | loop fusion | flops 4194304 | bytes 6299648 | tf_op jit(solution)/shard_map/convert_element_type | solution.py:111
  (93 shorter events, 22.4 us)
Async XLA Ops:
  7.2 118.7 %all-gather.2.cloned.1.call-start = ((), (), s32[]{:S(2)}) async-start(), calls=%async_computation | async-start | bytes 18382848 | tf_op jit(solution)/shard_map/all_gather | solution.py:71
  17.9 1.3 collective-permute-start
  19.1 5.8 %collective-permute-start.1 = (f32[1024]{0:T(1024)S(1)}, f32[1024]{0:T(1024)S(1)}, u32[]{:S(2)}, u32[]{:S(2)}) collective-permute-start(f32[1024]{0:T(1024)S(1)} %add.133), channel_id=1, source_target_pairs={{0,2},{1,3},{2,4},{3,5},{4,6},{5,7},{6,0},{7,1},{8,10},{9,11},{10,... | collective-permute-start | bytes 12296 | tf_op jit(solution)/shard_map/ppermute | solution.py:32
  20.7 5.1 %collective-permute-start.2 = (f32[1024]{0:T(1024)S(1)}, f32[1024]{0:T(1024)S(1)}, u32[]{:S(2)}, u32[]{:S(2)}) collective-permute-start(f32[1024]{0:T(1024)S(1)} %add.133), channel_id=1, source_target_pairs={{0,4},{1,5},{2,6},{3,7},{4,0},{5,1},{6,2},{7,3},{8,12},{9,13},{10,... | collective-permute-start | bytes 12296 | tf_op jit(solution)/shard_map/ppermute | solution.py:32
  23.6 3.6 %collective-permute-start.3 = (f32[1024]{0:T(1024)S(1)}, f32[1024]{0:T(1024)S(1)}, u32[]{:S(2)}, u32[]{:S(2)}) collective-permute-start(f32[1024]{0:T(1024)S(1)} %add.133), channel_id=1, source_target_pairs={{0,6},{1,7},{2,0},{3,1},{4,2},{5,3},{6,4},{7,5},{8,14},{9,15},{10,... | collective-permute-start | bytes 12296 | tf_op jit(solution)/shard_map/ppermute | solution.py:32
  27.2 5.7 %collective-permute-start.4 = (f32[1024]{0:T(1024)S(1)}, f32[1024]{0:T(1024)S(1)}, u32[]{:S(2)}, u32[]{:S(2)}) collective-permute-start(f32[1024]{0:T(1024)S(1)} %add_add_fusion.2), channel_id=1, source_target_pairs={{0,8},{1,9},{2,10},{3,11},{4,12},{5,13},{6,14},{7,15},{8,16},{9,17... | collective-permute-start | bytes 12296 | tf_op jit(solution)/shard_map/ppermute | solution.py:32
  28.7 5.3 %collective-permute-start.5 = (f32[1024]{0:T(1024)S(1)}, f32[1024]{0:T(1024)S(1)}, u32[]{:S(2)}, u32[]{:S(2)}) collective-permute-start(f32[1024]{0:T(1024)S(1)} %add_add_fusion.2), channel_id=1, source_target_pairs={{0,16},{1,17},{2,18},{3,19},{4,20},{5,21},{6,22},{7,23},{8,24},{9,... | collective-permute-start | bytes 12296 | tf_op jit(solution)/shard_map/ppermute | solution.py:32
  31.4 3.6 %collective-permute-start.6 = (f32[1024]{0:T(1024)S(1)}, f32[1024]{0:T(1024)S(1)}, u32[]{:S(2)}, u32[]{:S(2)}) collective-permute-start(f32[1024]{0:T(1024)S(1)} %add_add_fusion.2), channel_id=1, source_target_pairs={{0,24},{1,25},{2,26},{3,27},{4,28},{5,29},{6,30},{7,31},{8,0},{9,1... | collective-permute-start | bytes 12296 | tf_op jit(solution)/shard_map/ppermute | solution.py:32
  35.1 35.5 %copy-start.6 = (s32[1024,1]{0,1:T(1,128)S(1)}, s32[1024,1]{0,1:T(1,128)}, u32[]{:S(2)}) copy-start(s32[1024,1]{0,1:T(1,128)} %param.5) | copy-start | bytes 12292
  53.3 20.0 %copy-start.1 = (f32[1024,1024]{1,0:T(8,128)S(1)}, f32[1024,1024]{1,0:T(8,128)}, u32[]{:S(2)}) copy-start(f32[1024,1024]{1,0:T(8,128)} %copy-done) | copy-start | bytes 12582916
  56.0 1.3 collective-permute-start.7
  57.3 4.9 %collective-permute-start.10 = (f32[1024]{0:T(1024)S(1)}, f32[1024]{0:T(1024)S(1)}, u32[]{:S(2)}, u32[]{:S(2)}) collective-permute-start(f32[1024]{0:T(1024)S(1)} %add.140), channel_id=1, source_target_pairs={{0,6},{1,7},{2,0},{3,1},{4,2},{5,3},{6,4},{7,5},{8,14},{9,15},{10,... | collective-permute-start | bytes 12296 | tf_op jit(solution)/shard_map/ppermute | solution.py:32
  60.0 5.0 %collective-permute-start.8 = (f32[1024]{0:T(1024)S(1)}, f32[1024]{0:T(1024)S(1)}, u32[]{:S(2)}, u32[]{:S(2)}) collective-permute-start(f32[1024]{0:T(1024)S(1)} %add.140), channel_id=1, source_target_pairs={{0,2},{1,3},{2,4},{3,5},{4,6},{5,7},{6,0},{7,1},{8,10},{9,11},{10,... | collective-permute-start | bytes 12296 | tf_op jit(solution)/shard_map/ppermute | solution.py:32
  60.0 5.3 %collective-permute-start.9 = (f32[1024]{0:T(1024)S(1)}, f32[1024]{0:T(1024)S(1)}, u32[]{:S(2)}, u32[]{:S(2)}) collective-permute-start(f32[1024]{0:T(1024)S(1)} %add.140), channel_id=1, source_target_pairs={{0,4},{1,5},{2,6},{3,7},{4,0},{5,1},{6,2},{7,3},{8,12},{9,13},{10,... | collective-permute-start | bytes 12296 | tf_op jit(solution)/shard_map/ppermute | solution.py:32
  65.3 5.8 %collective-permute-start.11 = (f32[1024]{0:T(1024)S(1)}, f32[1024]{0:T(1024)S(1)}, u32[]{:S(2)}, u32[]{:S(2)}) collective-permute-start(f32[1024]{0:T(1024)S(1)} %add_add_fusion.1), channel_id=1, source_target_pairs={{0,8},{1,9},{2,10},{3,11},{4,12},{5,13},{6,14},{7,15},{8,16},{9,17... | collective-permute-start | bytes 12296 | tf_op jit(solution)/shard_map/ppermute | solution.py:32
  66.8 5.3 %collective-permute-start.12 = (f32[1024]{0:T(1024)S(1)}, f32[1024]{0:T(1024)S(1)}, u32[]{:S(2)}, u32[]{:S(2)}) collective-permute-start(f32[1024]{0:T(1024)S(1)} %add_add_fusion.1), channel_id=1, source_target_pairs={{0,16},{1,17},{2,18},{3,19},{4,20},{5,21},{6,22},{7,23},{8,24},{9,... | collective-permute-start | bytes 12296 | tf_op jit(solution)/shard_map/ppermute | solution.py:32
  69.5 3.8 %collective-permute-start.13 = (f32[1024]{0:T(1024)S(1)}, f32[1024]{0:T(1024)S(1)}, u32[]{:S(2)}, u32[]{:S(2)}) collective-permute-start(f32[1024]{0:T(1024)S(1)} %add_add_fusion.1), channel_id=1, source_target_pairs={{0,24},{1,25},{2,26},{3,27},{4,28},{5,29},{6,30},{7,31},{8,0},{9,1... | collective-permute-start | bytes 12296 | tf_op jit(solution)/shard_map/ppermute | solution.py:32
  73.3 28.6 %copy-start.5 = (bf16[1024,1024]{1,0:T(8,128)(2,1)S(1)}, bf16[1024,1024]{1,0:T(8,128)(2,1)}, u32[]{:S(2)}) copy-start(bf16[1024,1024]{1,0:T(8,128)(2,1)} %param.4) | copy-start | bytes 6291460
  92.6 4.5 %collective-permute-start.14 = (f32[1024]{0:T(1024)S(1)}, f32[1024]{0:T(1024)S(1)}, u32[]{:S(2)}, u32[]{:S(2)}) collective-permute-start(f32[1024]{0:T(1024)S(1)} %multiply_reduce_fusion.2), channel_id=1, source_target_pairs={{0,1},{1,0},{2,3},{3,2},{4,5},{5,4},{6,7},{7,6},{8,9},{9,8},{10,11... | collective-permute-start | bytes 12296 | tf_op jit(solution)/shard_map/ppermute | solution.py:32
  97.1 23.7 %copy-start.2 = (f32[1024,1024]{1,0:T(8,128)S(1)}, f32[1024,1024]{1,0:T(8,128)}, u32[]{:S(2)}) copy-start(f32[1024,1024]{1,0:T(8,128)} %copy-done) | copy-start | bytes 12582916
  97.1 17.2 %collective-permute-start.15 = (f32[1024]{0:T(1024)S(1)}, f32[1024]{0:T(1024)S(1)}, u32[]{:S(2)}, u32[]{:S(2)}) collective-permute-start(f32[1024]{0:T(1024)S(1)} %add.147), channel_id=1, source_target_pairs={{0,2},{1,3},{2,4},{3,5},{4,6},{5,7},{6,0},{7,1},{8,10},{9,11},{10,... | collective-permute-start | bytes 12296 | tf_op jit(solution)/shard_map/ppermute | solution.py:32
  97.9 16.4 %collective-permute-start.16 = (f32[1024]{0:T(1024)S(1)}, f32[1024]{0:T(1024)S(1)}, u32[]{:S(2)}, u32[]{:S(2)}) collective-permute-start(f32[1024]{0:T(1024)S(1)} %add.147), channel_id=1, source_target_pairs={{0,4},{1,5},{2,6},{3,7},{4,0},{5,1},{6,2},{7,3},{8,12},{9,13},{10,... | collective-permute-start | bytes 12296 | tf_op jit(solution)/shard_map/ppermute | solution.py:32
  101.9 12.4 %collective-permute-start.17 = (f32[1024]{0:T(1024)S(1)}, f32[1024]{0:T(1024)S(1)}, u32[]{:S(2)}, u32[]{:S(2)}) collective-permute-start(f32[1024]{0:T(1024)S(1)} %add.147), channel_id=1, source_target_pairs={{0,6},{1,7},{2,0},{3,1},{4,2},{5,3},{6,4},{7,5},{8,14},{9,15},{10,... | collective-permute-start | bytes 12296 | tf_op jit(solution)/shard_map/ppermute | solution.py:32
  114.3 4.9 %collective-permute-start.18 = (f32[1024]{0:T(1024)S(1)}, f32[1024]{0:T(1024)S(1)}, u32[]{:S(2)}, u32[]{:S(2)}) collective-permute-start(f32[1024]{0:T(1024)S(1)} %add_add_fusion), channel_id=1, source_target_pairs={{0,8},{1,9},{2,10},{3,11},{4,12},{5,13},{6,14},{7,15},{8,16},{9,17... | collective-permute-start | bytes 12296 | tf_op jit(solution)/shard_map/ppermute | solution.py:32
  114.4 5.2 %collective-permute-start.19 = (f32[1024]{0:T(1024)S(1)}, f32[1024]{0:T(1024)S(1)}, u32[]{:S(2)}, u32[]{:S(2)}) collective-permute-start(f32[1024]{0:T(1024)S(1)} %add_add_fusion), channel_id=1, source_target_pairs={{0,16},{1,17},{2,18},{3,19},{4,20},{5,21},{6,22},{7,23},{8,24},{9,... | collective-permute-start | bytes 12296 | tf_op jit(solution)/shard_map/ppermute | solution.py:32
  117.2 3.6 %collective-permute-start.20 = (f32[1024]{0:T(1024)S(1)}, f32[1024]{0:T(1024)S(1)}, u32[]{:S(2)}, u32[]{:S(2)}) collective-permute-start(f32[1024]{0:T(1024)S(1)} %add_add_fusion), channel_id=1, source_target_pairs={{0,24},{1,25},{2,26},{3,27},{4,28},{5,29},{6,30},{7,31},{8,0},{9,1... | collective-permute-start | bytes 12296 | tf_op jit(solution)/shard_map/ppermute | solution.py:32
  121.2 3.7 %collective-permute-start.21 = (f32[1024]{0:T(1024)S(1)}, f32[1024]{0:T(1024)S(1)}, u32[]{:S(2)}, u32[]{:S(2)}) collective-permute-start(f32[1024]{0:T(1024)S(1)} %multiply_reduce_fusion.1), channel_id=1, source_target_pairs={{0,32},{32,0},{64,96},{96,64},{128,160},{160,128},{192,224},{224,1... | collective-permute-start | bytes 12296 | tf_op jit(solution)/shard_map/ppermute | solution.py:42
  124.9 16.8 %collective-permute-start.22 = (f32[1024]{0:T(1024)S(1)}, f32[1024]{0:T(1024)S(1)}, u32[]{:S(2)}, u32[]{:S(2)}) collective-permute-start(f32[1024]{0:T(1024)S(1)} %add.154), channel_id=1, source_target_pairs={{0,64},{32,96},{64,0},{96,32},{128,192},{160,224},{192,128},{224,1... | collective-permute-start | bytes 12296 | tf_op jit(solution)/shard_map/ppermute | solution.py:42
  141.3 3.9 %collective-permute-start.24 = (f32[1024]{0:T(1024)S(1)}, f32[1024]{0:T(1024)S(1)}, u32[]{:S(2)}, u32[]{:S(2)}) collective-permute-start(f32[1024]{0:T(1024)S(1)} %reduce_sum.119), channel_id=1, source_target_pairs={{0,32},{32,0},{64,96},{96,64},{128,160},{160,128},{192,224},{224,1... | collective-permute-start | bytes 12296 | tf_op jit(solution)/shard_map/ppermute | solution.py:42
  141.6 7.5 %collective-permute-start.23 = (f32[1024]{0:T(1024)S(1)}, f32[1024]{0:T(1024)S(1)}, u32[]{:S(2)}, u32[]{:S(2)}) collective-permute-start(f32[1024]{0:T(1024)S(1)} %add.155), channel_id=1, source_target_pairs={{0,128},{32,160},{64,192},{96,224},{128,0},{160,32},{192,64},{224,... | collective-permute-start | bytes 12296 | tf_op jit(solution)/shard_map/ppermute | solution.py:42
  145.2 4.5 %collective-permute-start.25 = (f32[1024]{0:T(1024)S(1)}, f32[1024]{0:T(1024)S(1)}, u32[]{:S(2)}, u32[]{:S(2)}) collective-permute-start(f32[1024]{0:T(1024)S(1)} %add.165), channel_id=1, source_target_pairs={{0,64},{32,96},{64,0},{96,32},{128,192},{160,224},{192,128},{224,1... | collective-permute-start | bytes 12296 | tf_op jit(solution)/shard_map/ppermute | solution.py:42
  149.7 7.5 %collective-permute-start.26 = (f32[1024]{0:T(1024)S(1)}, f32[1024]{0:T(1024)S(1)}, u32[]{:S(2)}, u32[]{:S(2)}) collective-permute-start(f32[1024]{0:T(1024)S(1)} %add.166), channel_id=1, source_target_pairs={{0,128},{32,160},{64,192},{96,224},{128,0},{160,32},{192,64},{224,... | collective-permute-start | bytes 12296 | tf_op jit(solution)/shard_map/ppermute | solution.py:42
  (3 other events, 29.5 us)
Sparse Core Ops, SparseCore 0:
  11.1 82.7 all-gather.1

commit v9 on v6

--- a/solution.py
+++ b/solution.py
@@ -81,8 +81,7 @@
     before = jnp.dot(earlier, onehot.astype(jnp.bfloat16), preferred_element_type=jnp.float32)
     rank = jnp.sum(before * onehot.astype(jnp.float32), axis=1).astype(jnp.int32)
     slot = ids * CAP + rank
-    source = jnp.zeros((clusters * CAP,), jnp.int32).at[slot].set(jnp.arange(pts_count, dtype=jnp.int32))
-    pick = (source[:, None] == lax.broadcasted_iota(jnp.int32, (clusters * CAP, pts_count), 1)).astype(points.dtype)
+    pick = (slot[None, :] == lax.broadcasted_iota(jnp.int32, (clusters * CAP, pts_count), 0)).astype(points.dtype)
     buffer = jnp.dot(pick, points, preferred_element_type=jnp.float32).astype(points.dtype)
     buffer = buffer.reshape(clusters, CAP, width)
     inv_rows = inverse_norm(buffer)

time: 162 us -> 159 us (0.981)
  local copies, waits for them, and re-layouts: 7.35 us -> 3.01 us
  waiting for transfers between devices: 34.1 us -> 36.3 us
    scatter x1 -> x0, local copies, waits for them, and re-layouts: 4.33 us -> none  [shards(): jnp.zeros((clusters * CAP,), jnp.int32).at[slot]]
    ppermute x21, waiting for transfers between devices: 16.4 us -> 18.6 us  [dp_sum(): lax.ppermute(values, 'dp', shift_pairs(count, stride, size, step))]
  transfers between devices with their start and end apart: 34 -> 34, of which waited for: 25 -> 28; matrix products, arithmetic and copies ran while one was open for 28% -> 26% of each run, Pallas kernels for 0% -> 0%
where the time goes in v9:
time: 159 us; the launch traced here: 158 us
  starting transfers between devices  62 us (39%)
  waiting for transfers between devices  36.3 us (23%)
  matrix products  26.2 us (16%)
  other arithmetic  15.8 us (10%)
  between operations  14.3 us (9%)
  local copies, waits for them, and re-layouts  3.01 us (2%)
    ppermute x12, starting transfers between devices, cent_sum(): lax.ppermute(values, 'cent', [(i, i ^ bit) for i in range(count)])  33.5 us
    ppermute x21, starting transfers between devices, dp_sum(): lax.ppermute(values, 'dp', shift_pairs(count, stride, size, step))  28.5 us
    ppermute x21, waiting for transfers between devices, dp_sum(): lax.ppermute(values, 'dp', shift_pairs(count, stride, size, step))  18.6 us
    ppermute x12, waiting for transfers between devices, cent_sum(): lax.ppermute(values, 'cent', [(i, i ^ bit) for i in range(count)])  17.7 us
    dot_general x1, matrix products, shards(): jnp.dot(pick, points, preferred_element_type=jnp.float32)  11.7 us
    dot_general x1, matrix products, shards(): jnp.einsum('gcd,gkd->gck', buffer, gathered, preferred_element_type=jnp.f...  11.3 us
    reduce_sum x3, other arithmetic, inverse_norm(): return lax.rsqrt(jnp.mean(values * values, axis=-1) + EPS)  5.65 us
    convert_element_type x1, other arithmetic, shards(): (expo * row_scale[:, None] * col_scale[None, :] * total_cent).astype(jnp....  4.05 us
  transfers between devices with their start and end apart: 34, of which 28 were waited for; matrix products, arithmetic and copies ran while one was open for 26% of the time, Pallas kernels for 0%

profile of v9, /device:TPU:32, one launch (start us, length us, event | category | flops | bytes accessed | tf_op | source)
XLA Modules:
  0.0 157.6 jit_solution(5348252288743760539)
XLA Ops:
  8.7 2.0 %maximum_maximum_fusion = bf16[2,136,1024]{2,1,0:T(8,128)(2,1)} fusion(bf16[2,1,1024]{2,1,0:T(2,128)(2,1)S(1)} %copy.7, bf16[2,128,1024]{2,1,0:T(8,128)(2,1)} %param.7, bf16[136]{0:T(256)(128)(2,1)S(1)} %pad.2.clone), kind=kLoop, calls=%fused_computation.23 | loop fusion | flops 1671168 | bytes 1085712 | tf_op jit(solution)/shard_map/concatenate | solution.py:70
  10.8 2.2 %multiply_reduce_fusion.6 = f32[1024]{0:T(1024)S(1)} fusion(bf16[1024,1024]{1,0:T(8,128)(2,1)} %param.6), kind=kLoop, calls=%fused_computation.16 | loop fusion | flops 3144704 | bytes 2101248 | tf_op jit(solution)/shard_map/reduce_sum | solution.py:16
  13.0 2.1 %multiply_reduce_fusion.7 = f32[1024]{0:T(1024)S(1)} fusion(bf16[1024,1024]{1,0:T(8,128)(2,1)} %param.4), kind=kLoop, calls=%fused_computation.17 | loop fusion | flops 3144704 | bytes 2101248 | tf_op jit(solution)/shard_map/reduce_sum | solution.py:16
  15.1 2.7 %fusion.14 = (f32[1024]{0:T(1024)S(1)}, f32[1024,1024]{1,0:T(8,128)S(1)}) fusion(f32[1024]{0:T(1024)S(1)} %get-tuple-element.9, f32[1024]{0:T(1024)S(1)} %get-tuple-element.10, bf16[1024,1024]{1,0:T(8,128)(2,1)S(1)} %copy-done.2, bf16[1024,1024]{1,0:T(8,128)(2,1)S(1)} %copy-done.1), kind=kOutput, calls=%fused_computation.54 | convolution fusion | flops 2151676928 | bytes 8400896 | tf_op jit(solution)/shard_map/pd,kd->pk/dot_general | solution.py:94
  19.0 1.6 %collective-permute-start.1 = (f32[1024]{0:T(1024)S(1)}, f32[1024]{0:T(1024)S(1)}, u32[]{:S(2)}, u32[]{:S(2)}) collective-permute-start(f32[1024]{0:T(1024)S(1)} %add.155), channel_id=1, source_target_pairs={{0,2},{1,3},{2,4},{3,5},{4,6},{5,7},{6,0},{7,1},{8,10},{9,11},{10,... | collective-permute-start | bytes 12296 | tf_op jit(solution)/shard_map/ppermute | solution.py:32
  20.6 2.9 %collective-permute-start.2 = (f32[1024]{0:T(1024)S(1)}, f32[1024]{0:T(1024)S(1)}, u32[]{:S(2)}, u32[]{:S(2)}) collective-permute-start(f32[1024]{0:T(1024)S(1)} %add.155), channel_id=1, source_target_pairs={{0,4},{1,5},{2,6},{3,7},{4,0},{5,1},{6,2},{7,3},{8,12},{9,13},{10,... | collective-permute-start | bytes 12296 | tf_op jit(solution)/shard_map/ppermute | solution.py:32
  28.6 2.7 %collective-permute-start.5 = (f32[1024]{0:T(1024)S(1)}, f32[1024]{0:T(1024)S(1)}, u32[]{:S(2)}, u32[]{:S(2)}) collective-permute-start(f32[1024]{0:T(1024)S(1)} %add_add_fusion.2), channel_id=1, source_target_pairs={{0,16},{1,17},{2,18},{3,19},{4,20},{5,21},{6,22},{7,23},{8,24},{9,... | collective-permute-start | bytes 12296 | tf_op jit(solution)/shard_map/ppermute | solution.py:32
  35.5 3.5 %collective-permute-done.7 = f32[1024]{0:T(1024)S(1)} collective-permute-done((f32[1024]{0:T(1024)S(1)}, f32[1024]{0:T(1024)S(1)}, u32[]{:S(2)}, u32[]{:S(2)}) %collective-permute-start.7) | collective-permute-done | bytes 4128 | tf_op jit(solution)/shard_map/ppermute | solution.py:42
  39.0 3.3 %collective-permute-start.8 = (f32[1024]{0:T(1024)S(1)}, f32[1024]{0:T(1024)S(1)}, u32[]{:S(2)}, u32[]{:S(2)}) collective-permute-start(f32[1024]{0:T(1024)S(1)} %add.162), channel_id=1, source_target_pairs={{0,64},{32,96},{64,0},{96,32},{128,192},{160,224},{192,128},{224,1... | collective-permute-start | bytes 12296 | tf_op jit(solution)/shard_map/ppermute | solution.py:42
  42.3 1.6 %collective-permute-done.8 = f32[1024]{0:T(1024)S(1)} collective-permute-done((f32[1024]{0:T(1024)S(1)}, f32[1024]{0:T(1024)S(1)}, u32[]{:S(2)}, u32[]{:S(2)}) %collective-permute-start.8) | collective-permute-done | bytes 4128 | tf_op jit(solution)/shard_map/ppermute | solution.py:42
  43.9 5.9 %collective-permute-start.9 = (f32[1024]{0:T(1024)S(1)}, f32[1024]{0:T(1024)S(1)}, u32[]{:S(2)}, u32[]{:S(2)}) collective-permute-start(f32[1024]{0:T(1024)S(1)} %add.163), channel_id=1, source_target_pairs={{0,128},{32,160},{64,192},{96,224},{128,0},{160,32},{192,64},{224,... | collective-permute-start | bytes 12296 | tf_op jit(solution)/shard_map/ppermute | solution.py:42
  49.8 1.6 %collective-permute-done.9 = f32[1024]{0:T(1024)S(1)} collective-permute-done((f32[1024]{0:T(1024)S(1)}, f32[1024]{0:T(1024)S(1)}, u32[]{:S(2)}, u32[]{:S(2)}) %collective-permute-start.9) | collective-permute-done | bytes 4128 | tf_op jit(solution)/shard_map/ppermute | solution.py:42
  53.3 3.8 %collective-permute-start.12 = (f32[1024]{0:T(1024)S(1)}, f32[1024]{0:T(1024)S(1)}, u32[]{:S(2)}, u32[]{:S(2)}) collective-permute-start(f32[1024]{0:T(1024)S(1)} %add.165), channel_id=1, source_target_pairs={{0,4},{1,5},{2,6},{3,7},{4,0},{5,1},{6,2},{7,3},{8,12},{9,13},{10,... | collective-permute-start | bytes 12296 | tf_op jit(solution)/shard_map/ppermute | solution.py:32
  59.0 1.9 %collective-permute-done.13 = f32[1024]{0:T(1024)S(1)} collective-permute-done((f32[1024]{0:T(1024)S(1)}, f32[1024]{0:T(1024)S(1)}, u32[]{:S(2)}, u32[]{:S(2)}) %collective-permute-start.13) | collective-permute-done | bytes 4128 | tf_op jit(solution)/shard_map/ppermute | solution.py:32
  61.3 3.8 %collective-permute-start.15 = (f32[1024]{0:T(1024)S(1)}, f32[1024]{0:T(1024)S(1)}, u32[]{:S(2)}, u32[]{:S(2)}) collective-permute-start(f32[1024]{0:T(1024)S(1)} %add_add_fusion.1), channel_id=1, source_target_pairs={{0,16},{1,17},{2,18},{3,19},{4,20},{5,21},{6,22},{7,23},{8,24},{9,... | collective-permute-start | bytes 12296 | tf_op jit(solution)/shard_map/ppermute | solution.py:32
  67.0 1.9 %collective-permute-done.16 = f32[1024]{0:T(1024)S(1)} collective-permute-done((f32[1024]{0:T(1024)S(1)}, f32[1024]{0:T(1024)S(1)}, u32[]{:S(2)}, u32[]{:S(2)}) %collective-permute-start.16) | collective-permute-done | bytes 4128 | tf_op jit(solution)/shard_map/ppermute | solution.py:32
  70.3 2.6 %collective-permute-done.17 = f32[1024]{0:T(1024)S(1)} collective-permute-done((f32[1024]{0:T(1024)S(1)}, f32[1024]{0:T(1024)S(1)}, u32[]{:S(2)}, u32[]{:S(2)}) %collective-permute-start.17) | collective-permute-done | bytes 4128 | tf_op jit(solution)/shard_map/ppermute | solution.py:42
  72.9 2.9 %collective-permute-start.18 = (f32[1024]{0:T(1024)S(1)}, f32[1024]{0:T(1024)S(1)}, u32[]{:S(2)}, u32[]{:S(2)}) collective-permute-start(f32[1024]{0:T(1024)S(1)} %add.172), channel_id=1, source_target_pairs={{0,64},{32,96},{64,0},{96,32},{128,192},{160,224},{192,128},{224,1... | collective-permute-start | bytes 12296 | tf_op jit(solution)/shard_map/ppermute | solution.py:42
  77.4 5.9 %collective-permute-start.19 = (f32[1024]{0:T(1024)S(1)}, f32[1024]{0:T(1024)S(1)}, u32[]{:S(2)}, u32[]{:S(2)}) collective-permute-start(f32[1024]{0:T(1024)S(1)} %add.173), channel_id=1, source_target_pairs={{0,128},{32,160},{64,192},{96,224},{128,0},{160,32},{192,64},{224,... | collective-permute-start | bytes 12296 | tf_op jit(solution)/shard_map/ppermute | solution.py:42
  83.4 1.6 %collective-permute-done.19 = f32[1024]{0:T(1024)S(1)} collective-permute-done((f32[1024]{0:T(1024)S(1)}, f32[1024]{0:T(1024)S(1)}, u32[]{:S(2)}, u32[]{:S(2)}) %collective-permute-start.19) | collective-permute-done | bytes 4128 | tf_op jit(solution)/shard_map/ppermute | solution.py:42
  85.4 11.7 %multiply_reduce_fusion = (f32[4096]{0:T(1024)S(1)}, bf16[4096,1024]{1,0:T(8,128)(2,1)}) fusion(bf16[1024,1024]{1,0:T(8,128)(2,1)S(1)} %copy-done.2, s32[1024]{0:T(1024)S(1)} %multiply_add_fusion), kind=kOutput, calls=%fused_computation.3 | convolution fusion | flops 8610902016 | bytes 10506240 | tf_op jit(solution)/shard_map/dot_general | solution.py:85
  97.1 2.8 %collective-permute-start.22 = (f32[1024]{0:T(1024)S(1)}, f32[1024]{0:T(1024)S(1)}, u32[]{:S(2)}, u32[]{:S(2)}) collective-permute-start(f32[1024]{0:T(1024)S(1)} %add.175), channel_id=1, source_target_pairs={{0,4},{1,5},{2,6},{3,7},{4,0},{5,1},{6,2},{7,3},{8,12},{9,13},{10,... | collective-permute-start | bytes 12296 | tf_op jit(solution)/shard_map/ppermute | solution.py:32
  103.6 2.8 %collective-permute-start.25 = (f32[1024]{0:T(1024)S(1)}, f32[1024]{0:T(1024)S(1)}, u32[]{:S(2)}, u32[]{:S(2)}) collective-permute-start(f32[1024]{0:T(1024)S(1)} %add_add_fusion), channel_id=1, source_target_pairs={{0,16},{1,17},{2,18},{3,19},{4,20},{5,21},{6,22},{7,23},{8,24},{9,... | collective-permute-start | bytes 12296 | tf_op jit(solution)/shard_map/ppermute | solution.py:32
  111.5 2.5 %collective-permute-done.27 = f32[1024]{0:T(1024)S(1)} collective-permute-done((f32[1024]{0:T(1024)S(1)}, f32[1024]{0:T(1024)S(1)}, u32[]{:S(2)}, u32[]{:S(2)}) %collective-permute-start.27) | collective-permute-done | bytes 4128 | tf_op jit(solution)/shard_map/ppermute | solution.py:42
  114.0 2.9 %collective-permute-start.28 = (f32[1024]{0:T(1024)S(1)}, f32[1024]{0:T(1024)S(1)}, u32[]{:S(2)}, u32[]{:S(2)}) collective-permute-start(f32[1024]{0:T(1024)S(1)} %add.182), channel_id=1, source_target_pairs={{0,64},{32,96},{64,0},{96,32},{128,192},{160,224},{192,128},{224,1... | collective-permute-start | bytes 12296 | tf_op jit(solution)/shard_map/ppermute | solution.py:42
  118.0 11.3 %multiply_exponential_fusion.1 = f32[64,64,128]{2,1,0:T(8,128)S(1)} fusion(bf16[64,64,1024]{2,1,0:T(8,128)(2,1)} %bitcast.27, bf16[64,136,1024]{2,1,0:T(8,128)(2,1)} %all-gather.2.cloned.1.call-done, f32[64,128]{1,0:T(8,128)S(1)} %slice_add_fusion, f32[64,64]{1,0:T(8,128)S(1)} %rsqrt.31), kind=kOutput, calls=%fused_computation.19 | convolution fusion | flops 1075314688 | bytes 27312128 | tf_op jit(solution)/shard_map/gcd,gkd->gck/dot_general | solution.py:88
  129.3 2.8 %gather_fusion = f32[1024,128]{1,0:T(8,128)S(1)} fusion(f32[4096,128]{1,0:T(8,128)S(1)} %bitcast.21, s32[1024]{0:T(1024)S(1)} %broadcast_clamp_fusion), kind=kCustom, calls=%fused_computation | custom fusion | bytes 1052672 | tf_op jit(solution)/shard_map/gather | solution.py:90
  132.5 5.3 %collective-permute-start.29 = (f32[1024]{0:T(1024)S(1)}, f32[1024]{0:T(1024)S(1)}, u32[]{:S(2)}, u32[]{:S(2)}) collective-permute-start(f32[1024]{0:T(1024)S(1)} %add.183), channel_id=1, source_target_pairs={{0,128},{32,160},{64,192},{96,224},{128,0},{160,32},{192,64},{224,... | collective-permute-start | bytes 12296 | tf_op jit(solution)/shard_map/ppermute | solution.py:42
  137.9 1.5 collective-permute-start.31
  140.1 2.3 %collective-permute-done.31 = f32[1024]{0:T(1024)S(1)} collective-permute-done((f32[1024]{0:T(1024)S(1)}, f32[1024]{0:T(1024)S(1)}, u32[]{:S(2)}, u32[]{:S(2)}) %collective-permute-start.31) | collective-permute-done | bytes 4128 | tf_op jit(solution)/shard_map/ppermute | solution.py:42
  142.4 3.1 %collective-permute-start.32 = (f32[1024]{0:T(1024)S(1)}, f32[1024]{0:T(1024)S(1)}, u32[]{:S(2)}, u32[]{:S(2)}) collective-permute-start(f32[1024]{0:T(1024)S(1)} %add.196), channel_id=1, source_target_pairs={{0,128},{32,160},{64,192},{96,224},{128,0},{160,32},{192,64},{224,... | collective-permute-start | bytes 12296 | tf_op jit(solution)/shard_map/ppermute | solution.py:42
  145.5 4.0 %multiply_convert_fusion = bf16[1024,1024]{1,0:T(8,128)(2,1)} fusion(f32[1024,1024]{1,0:T(8,128)} %copy-done, f32[1024]{0:T(1024)S(1)} %add_divide_fusion, f32[1024]{0:T(1024)S(1)} %add_divide_fusion.1), kind=kLoop, calls=%fused_computation.9 | loop fusion | flops 4194304 | bytes 6299648 | tf_op jit(solution)/shard_map/convert_element_type | solution.py:110
  (100 shorter events, 33.9 us)
Async XLA Ops:
  7.2 109.7 %all-gather.2.cloned.1.call-start = ((), (), s32[]{:S(2)}) async-start(), calls=%async_computation | async-start | bytes 18382848 | tf_op jit(solution)/shard_map/all_gather | solution.py:71
  19.0 5.9 %collective-permute-start.1 = (f32[1024]{0:T(1024)S(1)}, f32[1024]{0:T(1024)S(1)}, u32[]{:S(2)}, u32[]{:S(2)}) collective-permute-start(f32[1024]{0:T(1024)S(1)} %add.155), channel_id=1, source_target_pairs={{0,2},{1,3},{2,4},{3,5},{4,6},{5,7},{6,0},{7,1},{8,10},{9,11},{10,... | collective-permute-start | bytes 12296 | tf_op jit(solution)/shard_map/ppermute | solution.py:32
  20.6 5.1 %collective-permute-start.2 = (f32[1024]{0:T(1024)S(1)}, f32[1024]{0:T(1024)S(1)}, u32[]{:S(2)}, u32[]{:S(2)}) collective-permute-start(f32[1024]{0:T(1024)S(1)} %add.155), channel_id=1, source_target_pairs={{0,4},{1,5},{2,6},{3,7},{4,0},{5,1},{6,2},{7,3},{8,12},{9,13},{10,... | collective-permute-start | bytes 12296 | tf_op jit(solution)/shard_map/ppermute | solution.py:32
  23.5 3.6 %collective-permute-start.3 = (f32[1024]{0:T(1024)S(1)}, f32[1024]{0:T(1024)S(1)}, u32[]{:S(2)}, u32[]{:S(2)}) collective-permute-start(f32[1024]{0:T(1024)S(1)} %add.155), channel_id=1, source_target_pairs={{0,6},{1,7},{2,0},{3,1},{4,2},{5,3},{6,4},{7,5},{8,14},{9,15},{10,... | collective-permute-start | bytes 12296 | tf_op jit(solution)/shard_map/ppermute | solution.py:32
  27.2 5.6 %collective-permute-start.4 = (f32[1024]{0:T(1024)S(1)}, f32[1024]{0:T(1024)S(1)}, u32[]{:S(2)}, u32[]{:S(2)}) collective-permute-start(f32[1024]{0:T(1024)S(1)} %add_add_fusion.2), channel_id=1, source_target_pairs={{0,8},{1,9},{2,10},{3,11},{4,12},{5,13},{6,14},{7,15},{8,16},{9,17... | collective-permute-start | bytes 12296 | tf_op jit(solution)/shard_map/ppermute | solution.py:32
  28.6 5.3 %collective-permute-start.5 = (f32[1024]{0:T(1024)S(1)}, f32[1024]{0:T(1024)S(1)}, u32[]{:S(2)}, u32[]{:S(2)}) collective-permute-start(f32[1024]{0:T(1024)S(1)} %add_add_fusion.2), channel_id=1, source_target_pairs={{0,16},{1,17},{2,18},{3,19},{4,20},{5,21},{6,22},{7,23},{8,24},{9,... | collective-permute-start | bytes 12296 | tf_op jit(solution)/shard_map/ppermute | solution.py:32
  31.4 3.6 %collective-permute-start.6 = (f32[1024]{0:T(1024)S(1)}, f32[1024]{0:T(1024)S(1)}, u32[]{:S(2)}, u32[]{:S(2)}) collective-permute-start(f32[1024]{0:T(1024)S(1)} %add_add_fusion.2), channel_id=1, source_target_pairs={{0,24},{1,25},{2,26},{3,27},{4,28},{5,29},{6,30},{7,31},{8,0},{9,1... | collective-permute-start | bytes 12296 | tf_op jit(solution)/shard_map/ppermute | solution.py:32
  35.3 3.7 %collective-permute-start.7 = (f32[1024]{0:T(1024)S(1)}, f32[1024]{0:T(1024)S(1)}, u32[]{:S(2)}, u32[]{:S(2)}) collective-permute-start(f32[1024]{0:T(1024)S(1)} %multiply_reduce_fusion.5), channel_id=1, source_target_pairs={{0,32},{32,0},{64,96},{96,64},{128,160},{160,128},{192,224},{224,1... | collective-permute-start | bytes 12296 | tf_op jit(solution)/shard_map/ppermute | solution.py:42
  39.0 4.8 %collective-permute-start.8 = (f32[1024]{0:T(1024)S(1)}, f32[1024]{0:T(1024)S(1)}, u32[]{:S(2)}, u32[]{:S(2)}) collective-permute-start(f32[1024]{0:T(1024)S(1)} %add.162), channel_id=1, source_target_pairs={{0,64},{32,96},{64,0},{96,32},{128,192},{160,224},{192,128},{224,1... | collective-permute-start | bytes 12296 | tf_op jit(solution)/shard_map/ppermute | solution.py:42
  43.9 7.5 %collective-permute-start.9 = (f32[1024]{0:T(1024)S(1)}, f32[1024]{0:T(1024)S(1)}, u32[]{:S(2)}, u32[]{:S(2)}) collective-permute-start(f32[1024]{0:T(1024)S(1)} %add.163), channel_id=1, source_target_pairs={{0,128},{32,160},{64,192},{96,224},{128,0},{160,32},{192,64},{224,... | collective-permute-start | bytes 12296 | tf_op jit(solution)/shard_map/ppermute | solution.py:42
  53.1 5.1 %collective-permute-start.11 = (f32[1024]{0:T(1024)S(1)}, f32[1024]{0:T(1024)S(1)}, u32[]{:S(2)}, u32[]{:S(2)}) collective-permute-start(f32[1024]{0:T(1024)S(1)} %add.165), channel_id=1, source_target_pairs={{0,2},{1,3},{2,4},{3,5},{4,6},{5,7},{6,0},{7,1},{8,10},{9,11},{10,... | collective-permute-start | bytes 12296 | tf_op jit(solution)/shard_map/ppermute | solution.py:32
  53.3 5.7 %collective-permute-start.12 = (f32[1024]{0:T(1024)S(1)}, f32[1024]{0:T(1024)S(1)}, u32[]{:S(2)}, u32[]{:S(2)}) collective-permute-start(f32[1024]{0:T(1024)S(1)} %add.165), channel_id=1, source_target_pairs={{0,4},{1,5},{2,6},{3,7},{4,0},{5,1},{6,2},{7,3},{8,12},{9,13},{10,... | collective-permute-start | bytes 12296 | tf_op jit(solution)/shard_map/ppermute | solution.py:32
  57.1 3.8 %collective-permute-start.13 = (f32[1024]{0:T(1024)S(1)}, f32[1024]{0:T(1024)S(1)}, u32[]{:S(2)}, u32[]{:S(2)}) collective-permute-start(f32[1024]{0:T(1024)S(1)} %add.165), channel_id=1, source_target_pairs={{0,6},{1,7},{2,0},{3,1},{4,2},{5,3},{6,4},{7,5},{8,14},{9,15},{10,... | collective-permute-start | bytes 12296 | tf_op jit(solution)/shard_map/ppermute | solution.py:32
  60.9 5.0 %collective-permute-start.14 = (f32[1024]{0:T(1024)S(1)}, f32[1024]{0:T(1024)S(1)}, u32[]{:S(2)}, u32[]{:S(2)}) collective-permute-start(f32[1024]{0:T(1024)S(1)} %add_add_fusion.1), channel_id=1, source_target_pairs={{0,8},{1,9},{2,10},{3,11},{4,12},{5,13},{6,14},{7,15},{8,16},{9,17... | collective-permute-start | bytes 12296 | tf_op jit(solution)/shard_map/ppermute | solution.py:32
  61.3 5.7 %collective-permute-start.15 = (f32[1024]{0:T(1024)S(1)}, f32[1024]{0:T(1024)S(1)}, u32[]{:S(2)}, u32[]{:S(2)}) collective-permute-start(f32[1024]{0:T(1024)S(1)} %add_add_fusion.1), channel_id=1, source_target_pairs={{0,16},{1,17},{2,18},{3,19},{4,20},{5,21},{6,22},{7,23},{8,24},{9,... | collective-permute-start | bytes 12296 | tf_op jit(solution)/shard_map/ppermute | solution.py:32
  65.0 3.8 %collective-permute-start.16 = (f32[1024]{0:T(1024)S(1)}, f32[1024]{0:T(1024)S(1)}, u32[]{:S(2)}, u32[]{:S(2)}) collective-permute-start(f32[1024]{0:T(1024)S(1)} %add_add_fusion.1), channel_id=1, source_target_pairs={{0,24},{1,25},{2,26},{3,27},{4,28},{5,29},{6,30},{7,31},{8,0},{9,1... | collective-permute-start | bytes 12296 | tf_op jit(solution)/shard_map/ppermute | solution.py:32
  69.2 3.7 %collective-permute-start.17 = (f32[1024]{0:T(1024)S(1)}, f32[1024]{0:T(1024)S(1)}, u32[]{:S(2)}, u32[]{:S(2)}) collective-permute-start(f32[1024]{0:T(1024)S(1)} %multiply_reduce_fusion.3), channel_id=1, source_target_pairs={{0,32},{32,0},{64,96},{96,64},{128,160},{160,128},{192,224},{224,1... | collective-permute-start | bytes 12296 | tf_op jit(solution)/shard_map/ppermute | solution.py:42
  72.9 4.5 %collective-permute-start.18 = (f32[1024]{0:T(1024)S(1)}, f32[1024]{0:T(1024)S(1)}, u32[]{:S(2)}, u32[]{:S(2)}) collective-permute-start(f32[1024]{0:T(1024)S(1)} %add.172), channel_id=1, source_target_pairs={{0,64},{32,96},{64,0},{96,32},{128,192},{160,224},{192,128},{224,1... | collective-permute-start | bytes 12296 | tf_op jit(solution)/shard_map/ppermute | solution.py:42
  77.4 7.5 %collective-permute-start.19 = (f32[1024]{0:T(1024)S(1)}, f32[1024]{0:T(1024)S(1)}, u32[]{:S(2)}, u32[]{:S(2)}) collective-permute-start(f32[1024]{0:T(1024)S(1)} %add.173), channel_id=1, source_target_pairs={{0,128},{32,160},{64,192},{96,224},{128,0},{160,32},{192,64},{224,... | collective-permute-start | bytes 12296 | tf_op jit(solution)/shard_map/ppermute | solution.py:42
  85.3 11.8 %collective-permute-start.20 = (f32[1024]{0:T(1024)S(1)}, f32[1024]{0:T(1024)S(1)}, u32[]{:S(2)}, u32[]{:S(2)}) collective-permute-start(f32[1024]{0:T(1024)S(1)} %multiply_reduce_fusion.2), channel_id=1, source_target_pairs={{0,1},{1,0},{2,3},{3,2},{4,5},{5,4},{6,7},{7,6},{8,9},{9,8},{10,11... | collective-permute-start | bytes 12296 | tf_op jit(solution)/shard_map/ppermute | solution.py:32
  97.1 4.8 %collective-permute-start.21 = (f32[1024]{0:T(1024)S(1)}, f32[1024]{0:T(1024)S(1)}, u32[]{:S(2)}, u32[]{:S(2)}) collective-permute-start(f32[1024]{0:T(1024)S(1)} %add.175), channel_id=1, source_target_pairs={{0,2},{1,3},{2,4},{3,5},{4,6},{5,7},{6,0},{7,1},{8,10},{9,11},{10,... | collective-permute-start | bytes 12296 | tf_op jit(solution)/shard_map/ppermute | solution.py:32
  97.1 5.2 %collective-permute-start.22 = (f32[1024]{0:T(1024)S(1)}, f32[1024]{0:T(1024)S(1)}, u32[]{:S(2)}, u32[]{:S(2)}) collective-permute-start(f32[1024]{0:T(1024)S(1)} %add.175), channel_id=1, source_target_pairs={{0,4},{1,5},{2,6},{3,7},{4,0},{5,1},{6,2},{7,3},{8,12},{9,13},{10,... | collective-permute-start | bytes 12296 | tf_op jit(solution)/shard_map/ppermute | solution.py:32
  100.0 3.6 %collective-permute-start.23 = (f32[1024]{0:T(1024)S(1)}, f32[1024]{0:T(1024)S(1)}, u32[]{:S(2)}, u32[]{:S(2)}) collective-permute-start(f32[1024]{0:T(1024)S(1)} %add.175), channel_id=1, source_target_pairs={{0,6},{1,7},{2,0},{3,1},{4,2},{5,3},{6,4},{7,5},{8,14},{9,15},{10,... | collective-permute-start | bytes 12296 | tf_op jit(solution)/shard_map/ppermute | solution.py:32
  103.6 4.8 %collective-permute-start.24 = (f32[1024]{0:T(1024)S(1)}, f32[1024]{0:T(1024)S(1)}, u32[]{:S(2)}, u32[]{:S(2)}) collective-permute-start(f32[1024]{0:T(1024)S(1)} %add_add_fusion), channel_id=1, source_target_pairs={{0,8},{1,9},{2,10},{3,11},{4,12},{5,13},{6,14},{7,15},{8,16},{9,17... | collective-permute-start | bytes 12296 | tf_op jit(solution)/shard_map/ppermute | solution.py:32
  103.6 5.2 %collective-permute-start.25 = (f32[1024]{0:T(1024)S(1)}, f32[1024]{0:T(1024)S(1)}, u32[]{:S(2)}, u32[]{:S(2)}) collective-permute-start(f32[1024]{0:T(1024)S(1)} %add_add_fusion), channel_id=1, source_target_pairs={{0,16},{1,17},{2,18},{3,19},{4,20},{5,21},{6,22},{7,23},{8,24},{9,... | collective-permute-start | bytes 12296 | tf_op jit(solution)/shard_map/ppermute | solution.py:32
  106.3 3.6 %collective-permute-start.26 = (f32[1024]{0:T(1024)S(1)}, f32[1024]{0:T(1024)S(1)}, u32[]{:S(2)}, u32[]{:S(2)}) collective-permute-start(f32[1024]{0:T(1024)S(1)} %add_add_fusion), channel_id=1, source_target_pairs={{0,24},{1,25},{2,26},{3,27},{4,28},{5,29},{6,30},{7,31},{8,0},{9,1... | collective-permute-start | bytes 12296 | tf_op jit(solution)/shard_map/ppermute | solution.py:32
  110.3 3.7 %collective-permute-start.27 = (f32[1024]{0:T(1024)S(1)}, f32[1024]{0:T(1024)S(1)}, u32[]{:S(2)}, u32[]{:S(2)}) collective-permute-start(f32[1024]{0:T(1024)S(1)} %multiply_reduce_fusion.1), channel_id=1, source_target_pairs={{0,32},{32,0},{64,96},{96,64},{128,160},{160,128},{192,224},{224,1... | collective-permute-start | bytes 12296 | tf_op jit(solution)/shard_map/ppermute | solution.py:42
  114.0 18.5 %collective-permute-start.28 = (f32[1024]{0:T(1024)S(1)}, f32[1024]{0:T(1024)S(1)}, u32[]{:S(2)}, u32[]{:S(2)}) collective-permute-start(f32[1024]{0:T(1024)S(1)} %add.182), channel_id=1, source_target_pairs={{0,64},{32,96},{64,0},{96,32},{128,192},{160,224},{192,128},{224,1... | collective-permute-start | bytes 12296 | tf_op jit(solution)/shard_map/ppermute | solution.py:42
  132.3 5.5 %collective-permute-start.30 = (f32[1024]{0:T(1024)S(1)}, f32[1024]{0:T(1024)S(1)}, u32[]{:S(2)}, u32[]{:S(2)}) collective-permute-start(f32[1024]{0:T(1024)S(1)} %reduce_sum.119), channel_id=1, source_target_pairs={{0,32},{32,0},{64,96},{96,64},{128,160},{160,128},{192,224},{224,1... | collective-permute-start | bytes 12296 | tf_op jit(solution)/shard_map/ppermute | solution.py:42
  132.5 7.5 %collective-permute-start.29 = (f32[1024]{0:T(1024)S(1)}, f32[1024]{0:T(1024)S(1)}, u32[]{:S(2)}, u32[]{:S(2)}) collective-permute-start(f32[1024]{0:T(1024)S(1)} %add.183), channel_id=1, source_target_pairs={{0,128},{32,160},{64,192},{96,224},{128,0},{160,32},{192,64},{224,... | collective-permute-start | bytes 12296 | tf_op jit(solution)/shard_map/ppermute | solution.py:42
  137.9 4.5 %collective-permute-start.31 = (f32[1024]{0:T(1024)S(1)}, f32[1024]{0:T(1024)S(1)}, u32[]{:S(2)}, u32[]{:S(2)}) collective-permute-start(f32[1024]{0:T(1024)S(1)} %add.195), channel_id=1, source_target_pairs={{0,64},{32,96},{64,0},{96,32},{128,192},{160,224},{192,128},{224,1... | collective-permute-start | bytes 12296 | tf_op jit(solution)/shard_map/ppermute | solution.py:42
  142.4 7.5 %collective-permute-start.32 = (f32[1024]{0:T(1024)S(1)}, f32[1024]{0:T(1024)S(1)}, u32[]{:S(2)}, u32[]{:S(2)}) collective-permute-start(f32[1024]{0:T(1024)S(1)} %add.196), channel_id=1, source_target_pairs={{0,128},{32,160},{64,192},{96,224},{128,0},{160,32},{192,64},{224,... | collective-permute-start | bytes 12296 | tf_op jit(solution)/shard_map/ppermute | solution.py:42
  (6 other events, 131.3 us)
Sparse Core Ops, SparseCore 0:
  11.1 82.7 all-gather.1

commit v10 on v9

--- a/solution.py
+++ b/solution.py
@@ -87,8 +87,9 @@
     inv_rows = inverse_norm(buffer)
     dots = jnp.einsum("gcd,gkd->gck", buffer, gathered, preferred_element_type=jnp.float32)
     weights = jnp.exp(dots * inv_rows[..., None] * inv_u[:, None, :] * scale_two)
-    point_weights = weights.reshape(clusters * CAP, sub_dev)[slot]
-    denom_part = jnp.sum(point_weights, axis=1)
+    slot_weights = weights.reshape(clusters * CAP, sub_dev)
+    denom_part = jnp.sum(slot_weights, axis=1)[slot]
+    point_weights = slot_weights[slot]
 
     inv_c = inverse_norm(centroids)
     scores = jnp.einsum("pd,kd->pk", points, centroids, preferred_element_type=jnp.float32)

time: 159 us -> 164 us (1.031)
  local copies, waits for them, and re-layouts: 3.01 us -> 9.22 us
    gather x1 -> x2, local copies, waits for them, and re-layouts: 2.81 us -> 8.95 us  [the longest x1 6.15 us: shards(): denom_part = jnp.sum(slot_weights, axis=1)[slot]]
  transfers between devices with their start and end apart: 34 -> 34, of which waited for: 28 -> 27; matrix products, arithmetic and copies ran while one was open for 26% -> 29% of each run, Pallas kernels for 0% -> 0%
where the time goes in v10:
time: 164 us; the launch traced here: 163 us
  starting transfers between devices  62 us (38%)
  waiting for transfers between devices  36 us (22%)
  matrix products  26.3 us (16%)
  other arithmetic  15.6 us (10%)
  between operations  14.3 us (9%)
  local copies, waits for them, and re-layouts  9.22 us (6%)
    ppermute x12, starting transfers between devices, cent_sum(): lax.ppermute(values, 'cent', [(i, i ^ bit) for i in range(count)])  33.5 us
    ppermute x21, starting transfers between devices, dp_sum(): lax.ppermute(values, 'dp', shift_pairs(count, stride, size, step))  28.5 us
    ppermute x21, waiting for transfers between devices, dp_sum(): lax.ppermute(values, 'dp', shift_pairs(count, stride, size, step))  18.6 us
    ppermute x12, waiting for transfers between devices, cent_sum(): lax.ppermute(values, 'cent', [(i, i ^ bit) for i in range(count)])  17.4 us
    dot_general x1, matrix products, shards(): jnp.dot(pick, points, preferred_element_type=jnp.float32)  11.7 us
    dot_general x1, matrix products, shards(): jnp.einsum('gcd,gkd->gck', buffer, gathered, preferred_element_type=jnp.f...  11.4 us
    gather x1, local copies, waits for them, and re-layouts, shards(): denom_part = jnp.sum(slot_weights, axis=1)[slot]  6.15 us
    reduce_sum x3, other arithmetic, inverse_norm(): return lax.rsqrt(jnp.mean(values * values, axis=-1) + EPS)  5.65 us
  transfers between devices with their start and end apart: 34, of which 27 were waited for; matrix products, arithmetic and copies ran while one was open for 29% of the time, Pallas kernels for 0%

profile of v10, /device:TPU:32, one launch (start us, length us, event | category | flops | bytes accessed | tf_op | source)
XLA Modules:
  0.0 163.4 jit_solution(6588461113783032744)
XLA Ops:
  8.7 2.0 %maximum_maximum_fusion = bf16[2,136,1024]{2,1,0:T(8,128)(2,1)} fusion(bf16[2,1,1024]{2,1,0:T(2,128)(2,1)S(1)} %copy.7, bf16[2,128,1024]{2,1,0:T(8,128)(2,1)} %param.7, bf16[136]{0:T(256)(128)(2,1)S(1)} %pad.2.clone), kind=kLoop, calls=%fused_computation.24 | loop fusion | flops 1671168 | bytes 1085712 | tf_op jit(solution)/shard_map/concatenate | solution.py:70
  10.8 2.2 %multiply_reduce_fusion.6 = f32[1024]{0:T(1024)S(1)} fusion(bf16[1024,1024]{1,0:T(8,128)(2,1)} %param.6), kind=kLoop, calls=%fused_computation.17 | loop fusion | flops 3144704 | bytes 2101248 | tf_op jit(solution)/shard_map/reduce_sum | solution.py:16
  13.0 2.1 %multiply_reduce_fusion.7 = f32[1024]{0:T(1024)S(1)} fusion(bf16[1024,1024]{1,0:T(8,128)(2,1)} %param.4), kind=kLoop, calls=%fused_computation.18 | loop fusion | flops 3144704 | bytes 2101248 | tf_op jit(solution)/shard_map/reduce_sum | solution.py:16
  15.1 2.7 %fusion.14 = (f32[1024]{0:T(1024)S(1)}, f32[1024,1024]{1,0:T(8,128)S(1)}) fusion(f32[1024]{0:T(1024)S(1)} %get-tuple-element.11, f32[1024]{0:T(1024)S(1)} %get-tuple-element.12, bf16[1024,1024]{1,0:T(8,128)(2,1)S(1)} %copy-done.2, bf16[1024,1024]{1,0:T(8,128)(2,1)S(1)} %copy-done.1), kind=kOutput, calls=%fused_computation.55 | convolution fusion | flops 2151676928 | bytes 8400896 | tf_op jit(solution)/shard_map/pd,kd->pk/dot_general | solution.py:95
  19.0 1.6 collective-permute-start.1
  20.6 2.9 %collective-permute-start.2 = (f32[1024]{0:T(1024)S(1)}, f32[1024]{0:T(1024)S(1)}, u32[]{:S(2)}, u32[]{:S(2)}) collective-permute-start(f32[1024]{0:T(1024)S(1)} %add.153), channel_id=1, source_target_pairs={{0,4},{1,5},{2,6},{3,7},{4,0},{5,1},{6,2},{7,3},{8,12},{9,13},{10,... | collective-permute-start | bytes 12296 | tf_op jit(solution)/shard_map/ppermute | solution.py:32
  28.6 2.7 %collective-permute-start.5 = (f32[1024]{0:T(1024)S(1)}, f32[1024]{0:T(1024)S(1)}, u32[]{:S(2)}, u32[]{:S(2)}) collective-permute-start(f32[1024]{0:T(1024)S(1)} %add_add_fusion.2), channel_id=1, source_target_pairs={{0,16},{1,17},{2,18},{3,19},{4,20},{5,21},{6,22},{7,23},{8,24},{9,... | collective-permute-start | bytes 12296 | tf_op jit(solution)/shard_map/ppermute | solution.py:32
  35.5 3.5 %collective-permute-done.7 = f32[1024]{0:T(1024)S(1)} collective-permute-done((f32[1024]{0:T(1024)S(1)}, f32[1024]{0:T(1024)S(1)}, u32[]{:S(2)}, u32[]{:S(2)}) %collective-permute-start.7) | collective-permute-done | bytes 4128 | tf_op jit(solution)/shard_map/ppermute | solution.py:42
  39.0 3.3 %collective-permute-start.8 = (f32[1024]{0:T(1024)S(1)}, f32[1024]{0:T(1024)S(1)}, u32[]{:S(2)}, u32[]{:S(2)}) collective-permute-start(f32[1024]{0:T(1024)S(1)} %add.160), channel_id=1, source_target_pairs={{0,64},{32,96},{64,0},{96,32},{128,192},{160,224},{192,128},{224,1... | collective-permute-start | bytes 12296 | tf_op jit(solution)/shard_map/ppermute | solution.py:42
  42.3 1.6 collective-permute-done.8
  43.9 5.9 %collective-permute-start.9 = (f32[1024]{0:T(1024)S(1)}, f32[1024]{0:T(1024)S(1)}, u32[]{:S(2)}, u32[]{:S(2)}) collective-permute-start(f32[1024]{0:T(1024)S(1)} %add.161), channel_id=1, source_target_pairs={{0,128},{32,160},{64,192},{96,224},{128,0},{160,32},{192,64},{224,... | collective-permute-start | bytes 12296 | tf_op jit(solution)/shard_map/ppermute | solution.py:42
  49.8 1.6 collective-permute-done.9
  53.3 3.8 %collective-permute-start.12 = (f32[1024]{0:T(1024)S(1)}, f32[1024]{0:T(1024)S(1)}, u32[]{:S(2)}, u32[]{:S(2)}) collective-permute-start(f32[1024]{0:T(1024)S(1)} %add.163), channel_id=1, source_target_pairs={{0,4},{1,5},{2,6},{3,7},{4,0},{5,1},{6,2},{7,3},{8,12},{9,13},{10,... | collective-permute-start | bytes 12296 | tf_op jit(solution)/shard_map/ppermute | solution.py:32
  59.0 1.9 %collective-permute-done.13 = f32[1024]{0:T(1024)S(1)} collective-permute-done((f32[1024]{0:T(1024)S(1)}, f32[1024]{0:T(1024)S(1)}, u32[]{:S(2)}, u32[]{:S(2)}) %collective-permute-start.13) | collective-permute-done | bytes 4128 | tf_op jit(solution)/shard_map/ppermute | solution.py:32
  61.3 3.8 %collective-permute-start.15 = (f32[1024]{0:T(1024)S(1)}, f32[1024]{0:T(1024)S(1)}, u32[]{:S(2)}, u32[]{:S(2)}) collective-permute-start(f32[1024]{0:T(1024)S(1)} %add_add_fusion.1), channel_id=1, source_target_pairs={{0,16},{1,17},{2,18},{3,19},{4,20},{5,21},{6,22},{7,23},{8,24},{9,... | collective-permute-start | bytes 12296 | tf_op jit(solution)/shard_map/ppermute | solution.py:32
  67.0 1.9 %collective-permute-done.16 = f32[1024]{0:T(1024)S(1)} collective-permute-done((f32[1024]{0:T(1024)S(1)}, f32[1024]{0:T(1024)S(1)}, u32[]{:S(2)}, u32[]{:S(2)}) %collective-permute-start.16) | collective-permute-done | bytes 4128 | tf_op jit(solution)/shard_map/ppermute | solution.py:32
  70.3 2.6 %collective-permute-done.17 = f32[1024]{0:T(1024)S(1)} collective-permute-done((f32[1024]{0:T(1024)S(1)}, f32[1024]{0:T(1024)S(1)}, u32[]{:S(2)}, u32[]{:S(2)}) %collective-permute-start.17) | collective-permute-done | bytes 4128 | tf_op jit(solution)/shard_map/ppermute | solution.py:42
  72.9 2.9 %collective-permute-start.18 = (f32[1024]{0:T(1024)S(1)}, f32[1024]{0:T(1024)S(1)}, u32[]{:S(2)}, u32[]{:S(2)}) collective-permute-start(f32[1024]{0:T(1024)S(1)} %add.170), channel_id=1, source_target_pairs={{0,64},{32,96},{64,0},{96,32},{128,192},{160,224},{192,128},{224,1... | collective-permute-start | bytes 12296 | tf_op jit(solution)/shard_map/ppermute | solution.py:42
  77.4 5.9 %collective-permute-start.19 = (f32[1024]{0:T(1024)S(1)}, f32[1024]{0:T(1024)S(1)}, u32[]{:S(2)}, u32[]{:S(2)}) collective-permute-start(f32[1024]{0:T(1024)S(1)} %add.171), channel_id=1, source_target_pairs={{0,128},{32,160},{64,192},{96,224},{128,0},{160,32},{192,64},{224,... | collective-permute-start | bytes 12296 | tf_op jit(solution)/shard_map/ppermute | solution.py:42
  83.4 1.6 collective-permute-done.19
  85.4 11.7 %multiply_reduce_fusion = (f32[4096]{0:T(1024)S(1)}, bf16[4096,1024]{1,0:T(8,128)(2,1)}) fusion(bf16[1024,1024]{1,0:T(8,128)(2,1)S(1)} %copy-done.2, s32[1024]{0:T(1024)S(1)} %multiply_add_fusion), kind=kOutput, calls=%fused_computation.4 | convolution fusion | flops 8610902016 | bytes 10506240 | tf_op jit(solution)/shard_map/dot_general | solution.py:85
  97.1 2.8 %collective-permute-start.22 = (f32[1024]{0:T(1024)S(1)}, f32[1024]{0:T(1024)S(1)}, u32[]{:S(2)}, u32[]{:S(2)}) collective-permute-start(f32[1024]{0:T(1024)S(1)} %add.173), channel_id=1, source_target_pairs={{0,4},{1,5},{2,6},{3,7},{4,0},{5,1},{6,2},{7,3},{8,12},{9,13},{10,... | collective-permute-start | bytes 12296 | tf_op jit(solution)/shard_map/ppermute | solution.py:32
  103.6 2.8 %collective-permute-start.25 = (f32[1024]{0:T(1024)S(1)}, f32[1024]{0:T(1024)S(1)}, u32[]{:S(2)}, u32[]{:S(2)}) collective-permute-start(f32[1024]{0:T(1024)S(1)} %add_add_fusion), channel_id=1, source_target_pairs={{0,16},{1,17},{2,18},{3,19},{4,20},{5,21},{6,22},{7,23},{8,24},{9,... | collective-permute-start | bytes 12296 | tf_op jit(solution)/shard_map/ppermute | solution.py:32
  111.5 2.5 %collective-permute-done.27 = f32[1024]{0:T(1024)S(1)} collective-permute-done((f32[1024]{0:T(1024)S(1)}, f32[1024]{0:T(1024)S(1)}, u32[]{:S(2)}, u32[]{:S(2)}) %collective-permute-start.27) | collective-permute-done | bytes 4128 | tf_op jit(solution)/shard_map/ppermute | solution.py:42
  114.0 2.9 %collective-permute-start.28 = (f32[1024]{0:T(1024)S(1)}, f32[1024]{0:T(1024)S(1)}, u32[]{:S(2)}, u32[]{:S(2)}) collective-permute-start(f32[1024]{0:T(1024)S(1)} %add.180), channel_id=1, source_target_pairs={{0,64},{32,96},{64,0},{96,32},{128,192},{160,224},{192,128},{224,1... | collective-permute-start | bytes 12296 | tf_op jit(solution)/shard_map/ppermute | solution.py:42
  118.0 11.4 %fusion.15 = (f32[64,64]{1,0:T(8,128)S(1)}, f32[64,64,128]{2,1,0:T(8,128)S(1)}) fusion(f32[64,128]{1,0:T(8,128)S(1)} %slice_add_fusion, f32[64,64]{1,0:T(8,128)S(1)} %rsqrt.31, bf16[64,64,1024]{2,1,0:T(8,128)(2,1)} %bitcast.27, bf16[64,136,1024]{2,1,0:T(8,128)(2,1)} %all-gather.2.cloned.1.call-done), kind=kOutput, calls=%fused_computation.56 | convolution fusion | flops 1075834880 | bytes 27328512 | tf_op jit(solution)/shard_map/gcd,gkd->gck/dot_general | solution.py:88
  129.5 6.1 %gather_fusion.1 = f32[1024]{0:T(1024)S(1)} fusion(f32[4096]{0:T(1024)S(1)} %reduce_sum.122, s32[1024]{0:T(1024)S(1)} %broadcast_clamp_fusion), kind=kCustom, calls=%fused_computation.1 | custom fusion | bytes 12288 | tf_op jit(solution)/shard_map/gather | solution.py:91
  135.8 5.3 %collective-permute-start.29 = (f32[1024]{0:T(1024)S(1)}, f32[1024]{0:T(1024)S(1)}, u32[]{:S(2)}, u32[]{:S(2)}) collective-permute-start(f32[1024]{0:T(1024)S(1)} %add.181), channel_id=1, source_target_pairs={{0,128},{32,160},{64,192},{96,224},{128,0},{160,32},{192,64},{224,... | collective-permute-start | bytes 12296 | tf_op jit(solution)/shard_map/ppermute | solution.py:42
  143.4 2.3 %collective-permute-done.31 = f32[1024]{0:T(1024)S(1)} collective-permute-done((f32[1024]{0:T(1024)S(1)}, f32[1024]{0:T(1024)S(1)}, u32[]{:S(2)}, u32[]{:S(2)}) %collective-permute-start.31) | collective-permute-done | bytes 4128 | tf_op jit(solution)/shard_map/ppermute | solution.py:42
  145.7 3.1 %collective-permute-start.32 = (f32[1024]{0:T(1024)S(1)}, f32[1024]{0:T(1024)S(1)}, u32[]{:S(2)}, u32[]{:S(2)}) collective-permute-start(f32[1024]{0:T(1024)S(1)} %add.193), channel_id=1, source_target_pairs={{0,128},{32,160},{64,192},{96,224},{128,0},{160,32},{192,64},{224,... | collective-permute-start | bytes 12296 | tf_op jit(solution)/shard_map/ppermute | solution.py:42
  148.8 4.0 %multiply_convert_fusion = bf16[1024,1024]{1,0:T(8,128)(2,1)} fusion(f32[1024,1024]{1,0:T(8,128)} %copy-done, f32[1024]{0:T(1024)S(1)} %add_divide_fusion, f32[1024]{0:T(1024)S(1)} %add_divide_fusion.1), kind=kLoop, calls=%fused_computation.10 | loop fusion | flops 4194304 | bytes 6299648 | tf_op jit(solution)/shard_map/convert_element_type | solution.py:111
  152.8 2.8 %gather_fusion = f32[1024,128]{1,0:T(8,128)S(1)} fusion(f32[4096,128]{1,0:T(8,128)S(1)} %bitcast.21, s32[1024]{0:T(1024)S(1)} %broadcast_clamp_fusion), kind=kCustom, calls=%fused_computation | custom fusion | bytes 1052672 | tf_op jit(solution)/shard_map/gather | solution.py:92
  (101 shorter events, 35.0 us)
Async XLA Ops:
  7.2 109.7 %all-gather.2.cloned.1.call-start = ((), (), s32[]{:S(2)}) async-start(), calls=%async_computation | async-start | bytes 18382848 | tf_op jit(solution)/shard_map/all_gather | solution.py:71
  19.0 5.9 %collective-permute-start.1 = (f32[1024]{0:T(1024)S(1)}, f32[1024]{0:T(1024)S(1)}, u32[]{:S(2)}, u32[]{:S(2)}) collective-permute-start(f32[1024]{0:T(1024)S(1)} %add.153), channel_id=1, source_target_pairs={{0,2},{1,3},{2,4},{3,5},{4,6},{5,7},{6,0},{7,1},{8,10},{9,11},{10,... | collective-permute-start | bytes 12296 | tf_op jit(solution)/shard_map/ppermute | solution.py:32
  20.6 5.1 %collective-permute-start.2 = (f32[1024]{0:T(1024)S(1)}, f32[1024]{0:T(1024)S(1)}, u32[]{:S(2)}, u32[]{:S(2)}) collective-permute-start(f32[1024]{0:T(1024)S(1)} %add.153), channel_id=1, source_target_pairs={{0,4},{1,5},{2,6},{3,7},{4,0},{5,1},{6,2},{7,3},{8,12},{9,13},{10,... | collective-permute-start | bytes 12296 | tf_op jit(solution)/shard_map/ppermute | solution.py:32
  23.5 3.6 %collective-permute-start.3 = (f32[1024]{0:T(1024)S(1)}, f32[1024]{0:T(1024)S(1)}, u32[]{:S(2)}, u32[]{:S(2)}) collective-permute-start(f32[1024]{0:T(1024)S(1)} %add.153), channel_id=1, source_target_pairs={{0,6},{1,7},{2,0},{3,1},{4,2},{5,3},{6,4},{7,5},{8,14},{9,15},{10,... | collective-permute-start | bytes 12296 | tf_op jit(solution)/shard_map/ppermute | solution.py:32
  27.2 5.6 %collective-permute-start.4 = (f32[1024]{0:T(1024)S(1)}, f32[1024]{0:T(1024)S(1)}, u32[]{:S(2)}, u32[]{:S(2)}) collective-permute-start(f32[1024]{0:T(1024)S(1)} %add_add_fusion.2), channel_id=1, source_target_pairs={{0,8},{1,9},{2,10},{3,11},{4,12},{5,13},{6,14},{7,15},{8,16},{9,17... | collective-permute-start | bytes 12296 | tf_op jit(solution)/shard_map/ppermute | solution.py:32
  28.6 5.3 %collective-permute-start.5 = (f32[1024]{0:T(1024)S(1)}, f32[1024]{0:T(1024)S(1)}, u32[]{:S(2)}, u32[]{:S(2)}) collective-permute-start(f32[1024]{0:T(1024)S(1)} %add_add_fusion.2), channel_id=1, source_target_pairs={{0,16},{1,17},{2,18},{3,19},{4,20},{5,21},{6,22},{7,23},{8,24},{9,... | collective-permute-start | bytes 12296 | tf_op jit(solution)/shard_map/ppermute | solution.py:32
  31.4 3.6 %collective-permute-start.6 = (f32[1024]{0:T(1024)S(1)}, f32[1024]{0:T(1024)S(1)}, u32[]{:S(2)}, u32[]{:S(2)}) collective-permute-start(f32[1024]{0:T(1024)S(1)} %add_add_fusion.2), channel_id=1, source_target_pairs={{0,24},{1,25},{2,26},{3,27},{4,28},{5,29},{6,30},{7,31},{8,0},{9,1... | collective-permute-start | bytes 12296 | tf_op jit(solution)/shard_map/ppermute | solution.py:32
  35.3 3.7 %collective-permute-start.7 = (f32[1024]{0:T(1024)S(1)}, f32[1024]{0:T(1024)S(1)}, u32[]{:S(2)}, u32[]{:S(2)}) collective-permute-start(f32[1024]{0:T(1024)S(1)} %multiply_reduce_fusion.5), channel_id=1, source_target_pairs={{0,32},{32,0},{64,96},{96,64},{128,160},{160,128},{192,224},{224,1... | collective-permute-start | bytes 12296 | tf_op jit(solution)/shard_map/ppermute | solution.py:42
  39.0 4.8 %collective-permute-start.8 = (f32[1024]{0:T(1024)S(1)}, f32[1024]{0:T(1024)S(1)}, u32[]{:S(2)}, u32[]{:S(2)}) collective-permute-start(f32[1024]{0:T(1024)S(1)} %add.160), channel_id=1, source_target_pairs={{0,64},{32,96},{64,0},{96,32},{128,192},{160,224},{192,128},{224,1... | collective-permute-start | bytes 12296 | tf_op jit(solution)/shard_map/ppermute | solution.py:42
  43.9 7.5 %collective-permute-start.9 = (f32[1024]{0:T(1024)S(1)}, f32[1024]{0:T(1024)S(1)}, u32[]{:S(2)}, u32[]{:S(2)}) collective-permute-start(f32[1024]{0:T(1024)S(1)} %add.161), channel_id=1, source_target_pairs={{0,128},{32,160},{64,192},{96,224},{128,0},{160,32},{192,64},{224,... | collective-permute-start | bytes 12296 | tf_op jit(solution)/shard_map/ppermute | solution.py:42
  53.1 5.1 %collective-permute-start.11 = (f32[1024]{0:T(1024)S(1)}, f32[1024]{0:T(1024)S(1)}, u32[]{:S(2)}, u32[]{:S(2)}) collective-permute-start(f32[1024]{0:T(1024)S(1)} %add.163), channel_id=1, source_target_pairs={{0,2},{1,3},{2,4},{3,5},{4,6},{5,7},{6,0},{7,1},{8,10},{9,11},{10,... | collective-permute-start | bytes 12296 | tf_op jit(solution)/shard_map/ppermute | solution.py:32
  53.3 5.7 %collective-permute-start.12 = (f32[1024]{0:T(1024)S(1)}, f32[1024]{0:T(1024)S(1)}, u32[]{:S(2)}, u32[]{:S(2)}) collective-permute-start(f32[1024]{0:T(1024)S(1)} %add.163), channel_id=1, source_target_pairs={{0,4},{1,5},{2,6},{3,7},{4,0},{5,1},{6,2},{7,3},{8,12},{9,13},{10,... | collective-permute-start | bytes 12296 | tf_op jit(solution)/shard_map/ppermute | solution.py:32
  57.1 3.8 %collective-permute-start.13 = (f32[1024]{0:T(1024)S(1)}, f32[1024]{0:T(1024)S(1)}, u32[]{:S(2)}, u32[]{:S(2)}) collective-permute-start(f32[1024]{0:T(1024)S(1)} %add.163), channel_id=1, source_target_pairs={{0,6},{1,7},{2,0},{3,1},{4,2},{5,3},{6,4},{7,5},{8,14},{9,15},{10,... | collective-permute-start | bytes 12296 | tf_op jit(solution)/shard_map/ppermute | solution.py:32
  60.9 5.0 %collective-permute-start.14 = (f32[1024]{0:T(1024)S(1)}, f32[1024]{0:T(1024)S(1)}, u32[]{:S(2)}, u32[]{:S(2)}) collective-permute-start(f32[1024]{0:T(1024)S(1)} %add_add_fusion.1), channel_id=1, source_target_pairs={{0,8},{1,9},{2,10},{3,11},{4,12},{5,13},{6,14},{7,15},{8,16},{9,17... | collective-permute-start | bytes 12296 | tf_op jit(solution)/shard_map/ppermute | solution.py:32
  61.3 5.7 %collective-permute-start.15 = (f32[1024]{0:T(1024)S(1)}, f32[1024]{0:T(1024)S(1)}, u32[]{:S(2)}, u32[]{:S(2)}) collective-permute-start(f32[1024]{0:T(1024)S(1)} %add_add_fusion.1), channel_id=1, source_target_pairs={{0,16},{1,17},{2,18},{3,19},{4,20},{5,21},{6,22},{7,23},{8,24},{9,... | collective-permute-start | bytes 12296 | tf_op jit(solution)/shard_map/ppermute | solution.py:32
  65.0 3.8 %collective-permute-start.16 = (f32[1024]{0:T(1024)S(1)}, f32[1024]{0:T(1024)S(1)}, u32[]{:S(2)}, u32[]{:S(2)}) collective-permute-start(f32[1024]{0:T(1024)S(1)} %add_add_fusion.1), channel_id=1, source_target_pairs={{0,24},{1,25},{2,26},{3,27},{4,28},{5,29},{6,30},{7,31},{8,0},{9,1... | collective-permute-start | bytes 12296 | tf_op jit(solution)/shard_map/ppermute | solution.py:32
  69.2 3.7 %collective-permute-start.17 = (f32[1024]{0:T(1024)S(1)}, f32[1024]{0:T(1024)S(1)}, u32[]{:S(2)}, u32[]{:S(2)}) collective-permute-start(f32[1024]{0:T(1024)S(1)} %multiply_reduce_fusion.3), channel_id=1, source_target_pairs={{0,32},{32,0},{64,96},{96,64},{128,160},{160,128},{192,224},{224,1... | collective-permute-start | bytes 12296 | tf_op jit(solution)/shard_map/ppermute | solution.py:42
  72.9 4.5 %collective-permute-start.18 = (f32[1024]{0:T(1024)S(1)}, f32[1024]{0:T(1024)S(1)}, u32[]{:S(2)}, u32[]{:S(2)}) collective-permute-start(f32[1024]{0:T(1024)S(1)} %add.170), channel_id=1, source_target_pairs={{0,64},{32,96},{64,0},{96,32},{128,192},{160,224},{192,128},{224,1... | collective-permute-start | bytes 12296 | tf_op jit(solution)/shard_map/ppermute | solution.py:42
  77.4 7.5 %collective-permute-start.19 = (f32[1024]{0:T(1024)S(1)}, f32[1024]{0:T(1024)S(1)}, u32[]{:S(2)}, u32[]{:S(2)}) collective-permute-start(f32[1024]{0:T(1024)S(1)} %add.171), channel_id=1, source_target_pairs={{0,128},{32,160},{64,192},{96,224},{128,0},{160,32},{192,64},{224,... | collective-permute-start | bytes 12296 | tf_op jit(solution)/shard_map/ppermute | solution.py:42
  85.3 11.8 %collective-permute-start.20 = (f32[1024]{0:T(1024)S(1)}, f32[1024]{0:T(1024)S(1)}, u32[]{:S(2)}, u32[]{:S(2)}) collective-permute-start(f32[1024]{0:T(1024)S(1)} %multiply_reduce_fusion.2), channel_id=1, source_target_pairs={{0,1},{1,0},{2,3},{3,2},{4,5},{5,4},{6,7},{7,6},{8,9},{9,8},{10,11... | collective-permute-start | bytes 12296 | tf_op jit(solution)/shard_map/ppermute | solution.py:32
  97.1 4.8 %collective-permute-start.21 = (f32[1024]{0:T(1024)S(1)}, f32[1024]{0:T(1024)S(1)}, u32[]{:S(2)}, u32[]{:S(2)}) collective-permute-start(f32[1024]{0:T(1024)S(1)} %add.173), channel_id=1, source_target_pairs={{0,2},{1,3},{2,4},{3,5},{4,6},{5,7},{6,0},{7,1},{8,10},{9,11},{10,... | collective-permute-start | bytes 12296 | tf_op jit(solution)/shard_map/ppermute | solution.py:32
  97.1 5.2 %collective-permute-start.22 = (f32[1024]{0:T(1024)S(1)}, f32[1024]{0:T(1024)S(1)}, u32[]{:S(2)}, u32[]{:S(2)}) collective-permute-start(f32[1024]{0:T(1024)S(1)} %add.173), channel_id=1, source_target_pairs={{0,4},{1,5},{2,6},{3,7},{4,0},{5,1},{6,2},{7,3},{8,12},{9,13},{10,... | collective-permute-start | bytes 12296 | tf_op jit(solution)/shard_map/ppermute | solution.py:32
  99.9 3.6 %collective-permute-start.23 = (f32[1024]{0:T(1024)S(1)}, f32[1024]{0:T(1024)S(1)}, u32[]{:S(2)}, u32[]{:S(2)}) collective-permute-start(f32[1024]{0:T(1024)S(1)} %add.173), channel_id=1, source_target_pairs={{0,6},{1,7},{2,0},{3,1},{4,2},{5,3},{6,4},{7,5},{8,14},{9,15},{10,... | collective-permute-start | bytes 12296 | tf_op jit(solution)/shard_map/ppermute | solution.py:32
  103.6 4.8 %collective-permute-start.24 = (f32[1024]{0:T(1024)S(1)}, f32[1024]{0:T(1024)S(1)}, u32[]{:S(2)}, u32[]{:S(2)}) collective-permute-start(f32[1024]{0:T(1024)S(1)} %add_add_fusion), channel_id=1, source_target_pairs={{0,8},{1,9},{2,10},{3,11},{4,12},{5,13},{6,14},{7,15},{8,16},{9,17... | collective-permute-start | bytes 12296 | tf_op jit(solution)/shard_map/ppermute | solution.py:32
  103.6 5.2 %collective-permute-start.25 = (f32[1024]{0:T(1024)S(1)}, f32[1024]{0:T(1024)S(1)}, u32[]{:S(2)}, u32[]{:S(2)}) collective-permute-start(f32[1024]{0:T(1024)S(1)} %add_add_fusion), channel_id=1, source_target_pairs={{0,16},{1,17},{2,18},{3,19},{4,20},{5,21},{6,22},{7,23},{8,24},{9,... | collective-permute-start | bytes 12296 | tf_op jit(solution)/shard_map/ppermute | solution.py:32
  106.3 3.6 %collective-permute-start.26 = (f32[1024]{0:T(1024)S(1)}, f32[1024]{0:T(1024)S(1)}, u32[]{:S(2)}, u32[]{:S(2)}) collective-permute-start(f32[1024]{0:T(1024)S(1)} %add_add_fusion), channel_id=1, source_target_pairs={{0,24},{1,25},{2,26},{3,27},{4,28},{5,29},{6,30},{7,31},{8,0},{9,1... | collective-permute-start | bytes 12296 | tf_op jit(solution)/shard_map/ppermute | solution.py:32
  110.3 3.7 %collective-permute-start.27 = (f32[1024]{0:T(1024)S(1)}, f32[1024]{0:T(1024)S(1)}, u32[]{:S(2)}, u32[]{:S(2)}) collective-permute-start(f32[1024]{0:T(1024)S(1)} %multiply_reduce_fusion.1), channel_id=1, source_target_pairs={{0,32},{32,0},{64,96},{96,64},{128,160},{160,128},{192,224},{224,1... | collective-permute-start | bytes 12296 | tf_op jit(solution)/shard_map/ppermute | solution.py:42
  114.0 21.8 %collective-permute-start.28 = (f32[1024]{0:T(1024)S(1)}, f32[1024]{0:T(1024)S(1)}, u32[]{:S(2)}, u32[]{:S(2)}) collective-permute-start(f32[1024]{0:T(1024)S(1)} %add.180), channel_id=1, source_target_pairs={{0,64},{32,96},{64,0},{96,32},{128,192},{160,224},{192,128},{224,1... | collective-permute-start | bytes 12296 | tf_op jit(solution)/shard_map/ppermute | solution.py:42
  135.6 5.5 %collective-permute-start.30 = (f32[1024]{0:T(1024)S(1)}, f32[1024]{0:T(1024)S(1)}, u32[]{:S(2)}, u32[]{:S(2)}) collective-permute-start(f32[1024]{0:T(1024)S(1)} %gather_fusion.1), channel_id=1, source_target_pairs={{0,32},{32,0},{64,96},{96,64},{128,160},{160,128},{192,224},{224,1... | collective-permute-start | bytes 12296 | tf_op jit(solution)/shard_map/ppermute | solution.py:42
  135.8 7.5 %collective-permute-start.29 = (f32[1024]{0:T(1024)S(1)}, f32[1024]{0:T(1024)S(1)}, u32[]{:S(2)}, u32[]{:S(2)}) collective-permute-start(f32[1024]{0:T(1024)S(1)} %add.181), channel_id=1, source_target_pairs={{0,128},{32,160},{64,192},{96,224},{128,0},{160,32},{192,64},{224,... | collective-permute-start | bytes 12296 | tf_op jit(solution)/shard_map/ppermute | solution.py:42
  141.1 4.5 %collective-permute-start.31 = (f32[1024]{0:T(1024)S(1)}, f32[1024]{0:T(1024)S(1)}, u32[]{:S(2)}, u32[]{:S(2)}) collective-permute-start(f32[1024]{0:T(1024)S(1)} %add.192), channel_id=1, source_target_pairs={{0,64},{32,96},{64,0},{96,32},{128,192},{160,224},{192,128},{224,1... | collective-permute-start | bytes 12296 | tf_op jit(solution)/shard_map/ppermute | solution.py:42
  145.7 10.0 %collective-permute-start.32 = (f32[1024]{0:T(1024)S(1)}, f32[1024]{0:T(1024)S(1)}, u32[]{:S(2)}, u32[]{:S(2)}) collective-permute-start(f32[1024]{0:T(1024)S(1)} %add.193), channel_id=1, source_target_pairs={{0,128},{32,160},{64,192},{96,224},{128,0},{160,32},{192,64},{224,... | collective-permute-start | bytes 12296 | tf_op jit(solution)/shard_map/ppermute | solution.py:42
  (6 other events, 131.3 us)
Sparse Core Ops, SparseCore 0:
  11.1 82.7 all-gather.1

commit v11 on v9

--- a/solution.py
+++ b/solution.py
@@ -104,6 +104,7 @@
         if step + 1 < ITERS:
             row_scale = 1.0 / cent_sum(row_part)
 
+    row_part, denom_part = lax.optimization_barrier((row_part, denom_part))
     row_total = cent_sum(row_part)
     denominator = cent_sum(denom_part)
     row_scale = 1.0 / row_total

time: 159 us -> 156 us (0.981)
  starting transfers between devices: 62 us -> 49.4 us
  waiting for transfers between devices: 36.3 us -> 45 us
  other arithmetic: 15.8 us -> 18 us
    ppermute x21, waiting for transfers between devices: 18.6 us -> 28.4 us  [dp_sum(): lax.ppermute(values, 'dp', shift_pairs(count, stride, size, step))]
    ppermute x21, starting transfers between devices: 28.5 us -> 20.6 us  [dp_sum(): lax.ppermute(values, 'dp', shift_pairs(count, stride, size, step))]
    ppermute x12, starting transfers between devices: 33.5 us -> 28.7 us  [cent_sum(): lax.ppermute(values, 'cent', [(i, i ^ bit) for i in range(count)])]
    reduce_sum x3, other arithmetic: 1.06 us -> 3.25 us  [shards(): row_part = jnp.sum(expo * col_scale[None, :], axis=1)]
  transfers between devices with their start and end apart: 34 -> 34, of which waited for: 28 -> 28; matrix products, arithmetic and copies ran while one was open for 26% -> 18% of each run, Pallas kernels for 0% -> 0%
where the time goes in v11:
time: 156 us
  starting transfers between devices  49.4 us (32%)
  waiting for transfers between devices  45 us (29%)
  matrix products  26.2 us (17%)
  other arithmetic  18 us (12%)
  between operations  14.3 us (9%)
  local copies, waits for them, and re-layouts  3.01 us (2%)
    ppermute x12, starting transfers between devices, cent_sum(): lax.ppermute(values, 'cent', [(i, i ^ bit) for i in range(count)])  28.7 us
    ppermute x21, waiting for transfers between devices, dp_sum(): lax.ppermute(values, 'dp', shift_pairs(count, stride, size, step))  28.4 us
    ppermute x21, starting transfers between devices, dp_sum(): lax.ppermute(values, 'dp', shift_pairs(count, stride, size, step))  20.6 us
    ppermute x12, waiting for transfers between devices, cent_sum(): lax.ppermute(values, 'cent', [(i, i ^ bit) for i in range(count)])  16.5 us
    dot_general x1, matrix products, shards(): jnp.dot(pick, points, preferred_element_type=jnp.float32)  11.6 us
    dot_general x1, matrix products, shards(): jnp.einsum('gcd,gkd->gck', buffer, gathered, preferred_element_type=jnp.f...  11.3 us
    reduce_sum x3, other arithmetic, inverse_norm(): return lax.rsqrt(jnp.mean(values * values, axis=-1) + EPS)  5.65 us
    convert_element_type x1, other arithmetic, shards(): (expo * row_scale[:, None] * col_scale[None, :] * total_cent).astype(jnp....  4.06 us
  transfers between devices with their start and end apart: 34, of which 28 were waited for; matrix products, arithmetic and copies ran while one was open for 18% of the time, Pallas kernels for 0%

profile of v11, /device:TPU:32, one launch (start us, length us, event | category | flops | bytes accessed | tf_op | source)
XLA Modules:
  0.0 155.9 jit_solution(7807929740143248560)
XLA Ops:
  8.7 2.0 %maximum_maximum_fusion = bf16[2,136,1024]{2,1,0:T(8,128)(2,1)} fusion(bf16[2,1,1024]{2,1,0:T(2,128)(2,1)S(1)} %copy.7, bf16[2,128,1024]{2,1,0:T(8,128)(2,1)} %param.7, bf16[136]{0:T(256)(128)(2,1)S(1)} %pad.2.clone), kind=kLoop, calls=%fused_computation.23 | loop fusion | flops 1671168 | bytes 1085712 | tf_op jit(solution)/shard_map/concatenate | solution.py:70
  10.8 2.2 %multiply_reduce_fusion.6 = f32[1024]{0:T(1024)S(1)} fusion(bf16[1024,1024]{1,0:T(8,128)(2,1)} %param.6), kind=kLoop, calls=%fused_computation.16 | loop fusion | flops 3144704 | bytes 2101248 | tf_op jit(solution)/shard_map/reduce_sum | solution.py:16
  13.0 2.1 %multiply_reduce_fusion.7 = f32[1024]{0:T(1024)S(1)} fusion(bf16[1024,1024]{1,0:T(8,128)(2,1)} %param.4), kind=kLoop, calls=%fused_computation.17 | loop fusion | flops 3144704 | bytes 2101248 | tf_op jit(solution)/shard_map/reduce_sum | solution.py:16
  15.1 2.7 %fusion.14 = (f32[1024]{0:T(1024)S(1)}, f32[1024,1024]{1,0:T(8,128)S(1)}) fusion(f32[1024]{0:T(1024)S(1)} %get-tuple-element.13, f32[1024]{0:T(1024)S(1)} %get-tuple-element.14, bf16[1024,1024]{1,0:T(8,128)(2,1)S(1)} %copy-done.2, bf16[1024,1024]{1,0:T(8,128)(2,1)S(1)} %copy-done.1), kind=kOutput, calls=%fused_computation.54 | convolution fusion | flops 2151676928 | bytes 8400896 | tf_op jit(solution)/shard_map/pd,kd->pk/dot_general | solution.py:94
  19.1 3.0 %collective-permute-start.3 = (f32[1024]{0:T(1024)S(1)}, f32[1024]{0:T(1024)S(1)}, u32[]{:S(2)}, u32[]{:S(2)}) collective-permute-start(f32[1024]{0:T(1024)S(1)} %add.155), channel_id=1, source_target_pairs={{0,6},{1,7},{2,0},{3,1},{4,2},{5,3},{6,4},{7,5},{8,14},{9,15},{10,... | collective-permute-start | bytes 12296 | tf_op jit(solution)/shard_map/ppermute | solution.py:32
  23.7 3.5 %collective-permute-done.2 = f32[1024]{0:T(1024)S(1)} collective-permute-done((f32[1024]{0:T(1024)S(1)}, f32[1024]{0:T(1024)S(1)}, u32[]{:S(2)}, u32[]{:S(2)}) %collective-permute-start.2) | collective-permute-done | bytes 4128 | tf_op jit(solution)/shard_map/ppermute | solution.py:32
  27.5 2.7 %collective-permute-start.6 = (f32[1024]{0:T(1024)S(1)}, f32[1024]{0:T(1024)S(1)}, u32[]{:S(2)}, u32[]{:S(2)}) collective-permute-start(f32[1024]{0:T(1024)S(1)} %add_add_fusion.2), channel_id=1, source_target_pairs={{0,24},{1,25},{2,26},{3,27},{4,28},{5,29},{6,30},{7,31},{8,0},{9,1... | collective-permute-start | bytes 12296 | tf_op jit(solution)/shard_map/ppermute | solution.py:32
  32.0 3.4 %collective-permute-done.5 = f32[1024]{0:T(1024)S(1)} collective-permute-done((f32[1024]{0:T(1024)S(1)}, f32[1024]{0:T(1024)S(1)}, u32[]{:S(2)}, u32[]{:S(2)}) %collective-permute-start.5) | collective-permute-done | bytes 4128 | tf_op jit(solution)/shard_map/ppermute | solution.py:32
  36.4 3.5 %collective-permute-done.7 = f32[1024]{0:T(1024)S(1)} collective-permute-done((f32[1024]{0:T(1024)S(1)}, f32[1024]{0:T(1024)S(1)}, u32[]{:S(2)}, u32[]{:S(2)}) %collective-permute-start.7) | collective-permute-done | bytes 4128 | tf_op jit(solution)/shard_map/ppermute | solution.py:42
  40.0 3.3 %collective-permute-start.8 = (f32[1024]{0:T(1024)S(1)}, f32[1024]{0:T(1024)S(1)}, u32[]{:S(2)}, u32[]{:S(2)}) collective-permute-start(f32[1024]{0:T(1024)S(1)} %add.162), channel_id=1, source_target_pairs={{0,64},{32,96},{64,0},{96,32},{128,192},{160,224},{192,128},{224,1... | collective-permute-start | bytes 12296 | tf_op jit(solution)/shard_map/ppermute | solution.py:42
  43.2 1.6 %collective-permute-done.8 = f32[1024]{0:T(1024)S(1)} collective-permute-done((f32[1024]{0:T(1024)S(1)}, f32[1024]{0:T(1024)S(1)}, u32[]{:S(2)}, u32[]{:S(2)}) %collective-permute-start.8) | collective-permute-done | bytes 4128 | tf_op jit(solution)/shard_map/ppermute | solution.py:42
  44.8 5.9 %collective-permute-start.9 = (f32[1024]{0:T(1024)S(1)}, f32[1024]{0:T(1024)S(1)}, u32[]{:S(2)}, u32[]{:S(2)}) collective-permute-start(f32[1024]{0:T(1024)S(1)} %add.163), channel_id=1, source_target_pairs={{0,128},{32,160},{64,192},{96,224},{128,0},{160,32},{192,64},{224,... | collective-permute-start | bytes 12296 | tf_op jit(solution)/shard_map/ppermute | solution.py:42
  50.8 1.6 %collective-permute-done.9 = f32[1024]{0:T(1024)S(1)} collective-permute-done((f32[1024]{0:T(1024)S(1)}, f32[1024]{0:T(1024)S(1)}, u32[]{:S(2)}, u32[]{:S(2)}) %collective-permute-start.9) | collective-permute-done | bytes 4128 | tf_op jit(solution)/shard_map/ppermute | solution.py:42
  57.8 2.0 %collective-permute-done.12 = f32[1024]{0:T(1024)S(1)} collective-permute-done((f32[1024]{0:T(1024)S(1)}, f32[1024]{0:T(1024)S(1)}, u32[]{:S(2)}, u32[]{:S(2)}) %collective-permute-start.12) | collective-permute-done | bytes 4128 | tf_op jit(solution)/shard_map/ppermute | solution.py:32
  64.7 1.9 %collective-permute-done.15 = f32[1024]{0:T(1024)S(1)} collective-permute-done((f32[1024]{0:T(1024)S(1)}, f32[1024]{0:T(1024)S(1)}, u32[]{:S(2)}, u32[]{:S(2)}) %collective-permute-start.15) | collective-permute-done | bytes 4128 | tf_op jit(solution)/shard_map/ppermute | solution.py:32
  69.7 2.0 %collective-permute-done.17 = f32[1024]{0:T(1024)S(1)} collective-permute-done((f32[1024]{0:T(1024)S(1)}, f32[1024]{0:T(1024)S(1)}, u32[]{:S(2)}, u32[]{:S(2)}) %collective-permute-start.17) | collective-permute-done | bytes 4128 | tf_op jit(solution)/shard_map/ppermute | solution.py:42
  71.7 2.9 %collective-permute-start.18 = (f32[1024]{0:T(1024)S(1)}, f32[1024]{0:T(1024)S(1)}, u32[]{:S(2)}, u32[]{:S(2)}) collective-permute-start(f32[1024]{0:T(1024)S(1)} %add.172), channel_id=1, source_target_pairs={{0,64},{32,96},{64,0},{96,32},{128,192},{160,224},{192,128},{224,1... | collective-permute-start | bytes 12296 | tf_op jit(solution)/shard_map/ppermute | solution.py:42
  74.6 1.6 %collective-permute-done.18 = f32[1024]{0:T(1024)S(1)} collective-permute-done((f32[1024]{0:T(1024)S(1)}, f32[1024]{0:T(1024)S(1)}, u32[]{:S(2)}, u32[]{:S(2)}) %collective-permute-start.18) | collective-permute-done | bytes 4128 | tf_op jit(solution)/shard_map/ppermute | solution.py:42
  76.2 5.9 %collective-permute-start.19 = (f32[1024]{0:T(1024)S(1)}, f32[1024]{0:T(1024)S(1)}, u32[]{:S(2)}, u32[]{:S(2)}) collective-permute-start(f32[1024]{0:T(1024)S(1)} %add.173), channel_id=1, source_target_pairs={{0,128},{32,160},{64,192},{96,224},{128,0},{160,32},{192,64},{224,... | collective-permute-start | bytes 12296 | tf_op jit(solution)/shard_map/ppermute | solution.py:42
  82.1 11.6 %multiply_reduce_fusion = (f32[4096]{0:T(1024)S(1)}, bf16[4096,1024]{1,0:T(8,128)(2,1)}) fusion(bf16[1024,1024]{1,0:T(8,128)(2,1)S(1)} %copy-done.2, s32[1024]{0:T(1024)S(1)} %multiply_add_fusion), kind=kOutput, calls=%fused_computation.3 | convolution fusion | flops 8610902016 | bytes 10506240 | tf_op jit(solution)/shard_map/dot_general | solution.py:85
  95.4 1.7 %collective-permute-start.23 = (f32[1024]{0:T(1024)S(1)}, f32[1024]{0:T(1024)S(1)}, u32[]{:S(2)}, u32[]{:S(2)}) collective-permute-start(f32[1024]{0:T(1024)S(1)} %add.175), channel_id=1, source_target_pairs={{0,6},{1,7},{2,0},{3,1},{4,2},{5,3},{6,4},{7,5},{8,14},{9,15},{10,... | collective-permute-start | bytes 12296 | tf_op jit(solution)/shard_map/ppermute | solution.py:32
  99.0 3.2 %collective-permute-done.22 = f32[1024]{0:T(1024)S(1)} collective-permute-done((f32[1024]{0:T(1024)S(1)}, f32[1024]{0:T(1024)S(1)}, u32[]{:S(2)}, u32[]{:S(2)}) %collective-permute-start.22) | collective-permute-done | bytes 4128 | tf_op jit(solution)/shard_map/ppermute | solution.py:32
  102.9 1.7 %collective-permute-start.26 = (f32[1024]{0:T(1024)S(1)}, f32[1024]{0:T(1024)S(1)}, u32[]{:S(2)}, u32[]{:S(2)}) collective-permute-start(f32[1024]{0:T(1024)S(1)} %add_add_fusion), channel_id=1, source_target_pairs={{0,24},{1,25},{2,26},{3,27},{4,28},{5,29},{6,30},{7,31},{8,0},{9,1... | collective-permute-start | bytes 12296 | tf_op jit(solution)/shard_map/ppermute | solution.py:32
  106.5 3.2 %collective-permute-done.25 = f32[1024]{0:T(1024)S(1)} collective-permute-done((f32[1024]{0:T(1024)S(1)}, f32[1024]{0:T(1024)S(1)}, u32[]{:S(2)}, u32[]{:S(2)}) %collective-permute-start.25) | collective-permute-done | bytes 4128 | tf_op jit(solution)/shard_map/ppermute | solution.py:32
  110.3 2.5 %multiply_reduce_fusion.1 = f32[1024]{0:T(1024)S(1)} fusion(f32[1024,1024]{1,0:T(8,128)} %copy-done, f32[1024]{0:T(1024)S(1)} %add_divide_fusion.1), kind=kLoop, calls=%fused_computation.10 | loop fusion | flops 2096128 | bytes 4202496 | tf_op jit(solution)/shard_map/reduce_sum | solution.py:103
  114.0 11.3 %multiply_exponential_fusion.1 = f32[64,64,128]{2,1,0:T(8,128)S(1)} fusion(bf16[64,64,1024]{2,1,0:T(8,128)(2,1)} %bitcast.27, bf16[64,136,1024]{2,1,0:T(8,128)(2,1)} %all-gather.2.cloned.1.call-done, f32[64,128]{1,0:T(8,128)S(1)} %slice_add_fusion, f32[64,64]{1,0:T(8,128)S(1)} %rsqrt.31), kind=kOutput, calls=%fused_computation.19 | convolution fusion | flops 1075314688 | bytes 27312128 | tf_op jit(solution)/shard_map/gcd,gkd->gck/dot_general | solution.py:88
  125.3 2.8 %gather_fusion = f32[1024,128]{1,0:T(8,128)S(1)} fusion(f32[4096,128]{1,0:T(8,128)S(1)} %bitcast.21, s32[1024]{0:T(1024)S(1)} %broadcast_clamp_fusion), kind=kCustom, calls=%fused_computation | custom fusion | bytes 1052672 | tf_op jit(solution)/shard_map/gather | solution.py:90
  130.4 1.6 %collective-permute-done.27 = f32[1024]{0:T(1024)S(1)} collective-permute-done((f32[1024]{0:T(1024)S(1)}, f32[1024]{0:T(1024)S(1)}, u32[]{:S(2)}, u32[]{:S(2)}) %collective-permute-start.27) | collective-permute-done | bytes 4128 | tf_op jit(solution)/shard_map/ppermute | solution.py:42
  134.9 1.6 %collective-permute-done.28 = f32[1024]{0:T(1024)S(1)} collective-permute-done((f32[1024]{0:T(1024)S(1)}, f32[1024]{0:T(1024)S(1)}, u32[]{:S(2)}, u32[]{:S(2)}) %collective-permute-start.28) | collective-permute-done | bytes 4128 | tf_op jit(solution)/shard_map/ppermute | solution.py:42
  138.0 4.4 %collective-permute-start.32 = (f32[1024]{0:T(1024)S(1)}, f32[1024]{0:T(1024)S(1)}, u32[]{:S(2)}, u32[]{:S(2)}) collective-permute-start(f32[1024]{0:T(1024)S(1)} %add.196), channel_id=1, source_target_pairs={{0,128},{32,160},{64,192},{96,224},{128,0},{160,32},{192,64},{224,... | collective-permute-start | bytes 12296 | tf_op jit(solution)/shard_map/ppermute | solution.py:42
  142.5 1.6 %collective-permute-done.29 = f32[1024]{0:T(1024)S(1)} collective-permute-done((f32[1024]{0:T(1024)S(1)}, f32[1024]{0:T(1024)S(1)}, u32[]{:S(2)}, u32[]{:S(2)}) %collective-permute-start.29) | collective-permute-done | bytes 4128 | tf_op jit(solution)/shard_map/ppermute | solution.py:42
  144.0 4.1 %multiply_convert_fusion = bf16[1024,1024]{1,0:T(8,128)(2,1)} fusion(f32[1024,1024]{1,0:T(8,128)} %copy-done, f32[1024]{0:T(1024)S(1)} %add_divide_fusion, f32[1024]{0:T(1024)S(1)} %add_divide_fusion.1), kind=kLoop, calls=%fused_computation.9 | loop fusion | flops 4194304 | bytes 6299648 | tf_op jit(solution)/shard_map/convert_element_type | solution.py:111
  (100 shorter events, 36.4 us)
Async XLA Ops:
  7.2 105.7 %all-gather.2.cloned.1.call-start = ((), (), s32[]{:S(2)}) async-start(), calls=%async_computation | async-start | bytes 18382848 | tf_op jit(solution)/shard_map/all_gather | solution.py:71
  19.1 4.6 %collective-permute-start.3 = (f32[1024]{0:T(1024)S(1)}, f32[1024]{0:T(1024)S(1)}, u32[]{:S(2)}, u32[]{:S(2)}) collective-permute-start(f32[1024]{0:T(1024)S(1)} %add.155), channel_id=1, source_target_pairs={{0,6},{1,7},{2,0},{3,1},{4,2},{5,3},{6,4},{7,5},{8,14},{9,15},{10,... | collective-permute-start | bytes 12296 | tf_op jit(solution)/shard_map/ppermute | solution.py:32
  22.1 5.1 %collective-permute-start.2 = (f32[1024]{0:T(1024)S(1)}, f32[1024]{0:T(1024)S(1)}, u32[]{:S(2)}, u32[]{:S(2)}) collective-permute-start(f32[1024]{0:T(1024)S(1)} %add.155), channel_id=1, source_target_pairs={{0,4},{1,5},{2,6},{3,7},{4,0},{5,1},{6,2},{7,3},{8,12},{9,13},{10,... | collective-permute-start | bytes 12296 | tf_op jit(solution)/shard_map/ppermute | solution.py:32
  22.7 4.8 %collective-permute-start.1 = (f32[1024]{0:T(1024)S(1)}, f32[1024]{0:T(1024)S(1)}, u32[]{:S(2)}, u32[]{:S(2)}) collective-permute-start(f32[1024]{0:T(1024)S(1)} %add.155), channel_id=1, source_target_pairs={{0,2},{1,3},{2,4},{3,5},{4,6},{5,7},{6,0},{7,1},{8,10},{9,11},{10,... | collective-permute-start | bytes 12296 | tf_op jit(solution)/shard_map/ppermute | solution.py:32
  27.5 4.4 %collective-permute-start.6 = (f32[1024]{0:T(1024)S(1)}, f32[1024]{0:T(1024)S(1)}, u32[]{:S(2)}, u32[]{:S(2)}) collective-permute-start(f32[1024]{0:T(1024)S(1)} %add_add_fusion.2), channel_id=1, source_target_pairs={{0,24},{1,25},{2,26},{3,27},{4,28},{5,29},{6,30},{7,31},{8,0},{9,1... | collective-permute-start | bytes 12296 | tf_op jit(solution)/shard_map/ppermute | solution.py:32
  30.3 5.1 %collective-permute-start.5 = (f32[1024]{0:T(1024)S(1)}, f32[1024]{0:T(1024)S(1)}, u32[]{:S(2)}, u32[]{:S(2)}) collective-permute-start(f32[1024]{0:T(1024)S(1)} %add_add_fusion.2), channel_id=1, source_target_pairs={{0,16},{1,17},{2,18},{3,19},{4,20},{5,21},{6,22},{7,23},{8,24},{9,... | collective-permute-start | bytes 12296 | tf_op jit(solution)/shard_map/ppermute | solution.py:32
  31.1 4.8 %collective-permute-start.4 = (f32[1024]{0:T(1024)S(1)}, f32[1024]{0:T(1024)S(1)}, u32[]{:S(2)}, u32[]{:S(2)}) collective-permute-start(f32[1024]{0:T(1024)S(1)} %add_add_fusion.2), channel_id=1, source_target_pairs={{0,8},{1,9},{2,10},{3,11},{4,12},{5,13},{6,14},{7,15},{8,16},{9,17... | collective-permute-start | bytes 12296 | tf_op jit(solution)/shard_map/ppermute | solution.py:32
  36.3 3.7 %collective-permute-start.7 = (f32[1024]{0:T(1024)S(1)}, f32[1024]{0:T(1024)S(1)}, u32[]{:S(2)}, u32[]{:S(2)}) collective-permute-start(f32[1024]{0:T(1024)S(1)} %multiply_reduce_fusion.5), channel_id=1, source_target_pairs={{0,32},{32,0},{64,96},{96,64},{128,160},{160,128},{192,224},{224,1... | collective-permute-start | bytes 12296 | tf_op jit(solution)/shard_map/ppermute | solution.py:42
  40.0 4.8 %collective-permute-start.8 = (f32[1024]{0:T(1024)S(1)}, f32[1024]{0:T(1024)S(1)}, u32[]{:S(2)}, u32[]{:S(2)}) collective-permute-start(f32[1024]{0:T(1024)S(1)} %add.162), channel_id=1, source_target_pairs={{0,64},{32,96},{64,0},{96,32},{128,192},{160,224},{192,128},{224,1... | collective-permute-start | bytes 12296 | tf_op jit(solution)/shard_map/ppermute | solution.py:42
  44.8 7.5 %collective-permute-start.9 = (f32[1024]{0:T(1024)S(1)}, f32[1024]{0:T(1024)S(1)}, u32[]{:S(2)}, u32[]{:S(2)}) collective-permute-start(f32[1024]{0:T(1024)S(1)} %add.163), channel_id=1, source_target_pairs={{0,128},{32,160},{64,192},{96,224},{128,0},{160,32},{192,64},{224,... | collective-permute-start | bytes 12296 | tf_op jit(solution)/shard_map/ppermute | solution.py:42
  52.7 1.3 collective-permute-start.10
  54.0 3.8 %collective-permute-start.13 = (f32[1024]{0:T(1024)S(1)}, f32[1024]{0:T(1024)S(1)}, u32[]{:S(2)}, u32[]{:S(2)}) collective-permute-start(f32[1024]{0:T(1024)S(1)} %add.165), channel_id=1, source_target_pairs={{0,6},{1,7},{2,0},{3,1},{4,2},{5,3},{6,4},{7,5},{8,14},{9,15},{10,... | collective-permute-start | bytes 12296 | tf_op jit(solution)/shard_map/ppermute | solution.py:32
  54.5 5.3 %collective-permute-start.12 = (f32[1024]{0:T(1024)S(1)}, f32[1024]{0:T(1024)S(1)}, u32[]{:S(2)}, u32[]{:S(2)}) collective-permute-start(f32[1024]{0:T(1024)S(1)} %add.165), channel_id=1, source_target_pairs={{0,4},{1,5},{2,6},{3,7},{4,0},{5,1},{6,2},{7,3},{8,12},{9,13},{10,... | collective-permute-start | bytes 12296 | tf_op jit(solution)/shard_map/ppermute | solution.py:32
  55.8 5.0 %collective-permute-start.11 = (f32[1024]{0:T(1024)S(1)}, f32[1024]{0:T(1024)S(1)}, u32[]{:S(2)}, u32[]{:S(2)}) collective-permute-start(f32[1024]{0:T(1024)S(1)} %add.165), channel_id=1, source_target_pairs={{0,2},{1,3},{2,4},{3,5},{4,6},{5,7},{6,0},{7,1},{8,10},{9,11},{10,... | collective-permute-start | bytes 12296 | tf_op jit(solution)/shard_map/ppermute | solution.py:32
  60.9 3.8 %collective-permute-start.16 = (f32[1024]{0:T(1024)S(1)}, f32[1024]{0:T(1024)S(1)}, u32[]{:S(2)}, u32[]{:S(2)}) collective-permute-start(f32[1024]{0:T(1024)S(1)} %add_add_fusion.1), channel_id=1, source_target_pairs={{0,24},{1,25},{2,26},{3,27},{4,28},{5,29},{6,30},{7,31},{8,0},{9,1... | collective-permute-start | bytes 12296 | tf_op jit(solution)/shard_map/ppermute | solution.py:32
  61.3 5.3 %collective-permute-start.15 = (f32[1024]{0:T(1024)S(1)}, f32[1024]{0:T(1024)S(1)}, u32[]{:S(2)}, u32[]{:S(2)}) collective-permute-start(f32[1024]{0:T(1024)S(1)} %add_add_fusion.1), channel_id=1, source_target_pairs={{0,16},{1,17},{2,18},{3,19},{4,20},{5,21},{6,22},{7,23},{8,24},{9,... | collective-permute-start | bytes 12296 | tf_op jit(solution)/shard_map/ppermute | solution.py:32
  62.6 5.0 %collective-permute-start.14 = (f32[1024]{0:T(1024)S(1)}, f32[1024]{0:T(1024)S(1)}, u32[]{:S(2)}, u32[]{:S(2)}) collective-permute-start(f32[1024]{0:T(1024)S(1)} %add_add_fusion.1), channel_id=1, source_target_pairs={{0,8},{1,9},{2,10},{3,11},{4,12},{5,13},{6,14},{7,15},{8,16},{9,17... | collective-permute-start | bytes 12296 | tf_op jit(solution)/shard_map/ppermute | solution.py:32
  68.0 3.7 %collective-permute-start.17 = (f32[1024]{0:T(1024)S(1)}, f32[1024]{0:T(1024)S(1)}, u32[]{:S(2)}, u32[]{:S(2)}) collective-permute-start(f32[1024]{0:T(1024)S(1)} %multiply_reduce_fusion.3), channel_id=1, source_target_pairs={{0,32},{32,0},{64,96},{96,64},{128,160},{160,128},{192,224},{224,1... | collective-permute-start | bytes 12296 | tf_op jit(solution)/shard_map/ppermute | solution.py:42
  71.7 4.5 %collective-permute-start.18 = (f32[1024]{0:T(1024)S(1)}, f32[1024]{0:T(1024)S(1)}, u32[]{:S(2)}, u32[]{:S(2)}) collective-permute-start(f32[1024]{0:T(1024)S(1)} %add.172), channel_id=1, source_target_pairs={{0,64},{32,96},{64,0},{96,32},{128,192},{160,224},{192,128},{224,1... | collective-permute-start | bytes 12296 | tf_op jit(solution)/shard_map/ppermute | solution.py:42
  76.2 17.6 %collective-permute-start.19 = (f32[1024]{0:T(1024)S(1)}, f32[1024]{0:T(1024)S(1)}, u32[]{:S(2)}, u32[]{:S(2)}) collective-permute-start(f32[1024]{0:T(1024)S(1)} %add.173), channel_id=1, source_target_pairs={{0,128},{32,160},{64,192},{96,224},{128,0},{160,32},{192,64},{224,... | collective-permute-start | bytes 12296 | tf_op jit(solution)/shard_map/ppermute | solution.py:42
  95.4 3.6 %collective-permute-start.23 = (f32[1024]{0:T(1024)S(1)}, f32[1024]{0:T(1024)S(1)}, u32[]{:S(2)}, u32[]{:S(2)}) collective-permute-start(f32[1024]{0:T(1024)S(1)} %add.175), channel_id=1, source_target_pairs={{0,6},{1,7},{2,0},{3,1},{4,2},{5,3},{6,4},{7,5},{8,14},{9,15},{10,... | collective-permute-start | bytes 12296 | tf_op jit(solution)/shard_map/ppermute | solution.py:32
  97.1 5.1 %collective-permute-start.22 = (f32[1024]{0:T(1024)S(1)}, f32[1024]{0:T(1024)S(1)}, u32[]{:S(2)}, u32[]{:S(2)}) collective-permute-start(f32[1024]{0:T(1024)S(1)} %add.175), channel_id=1, source_target_pairs={{0,4},{1,5},{2,6},{3,7},{4,0},{5,1},{6,2},{7,3},{8,12},{9,13},{10,... | collective-permute-start | bytes 12296 | tf_op jit(solution)/shard_map/ppermute | solution.py:32
  98.0 4.8 %collective-permute-start.21 = (f32[1024]{0:T(1024)S(1)}, f32[1024]{0:T(1024)S(1)}, u32[]{:S(2)}, u32[]{:S(2)}) collective-permute-start(f32[1024]{0:T(1024)S(1)} %add.175), channel_id=1, source_target_pairs={{0,2},{1,3},{2,4},{3,5},{4,6},{5,7},{6,0},{7,1},{8,10},{9,11},{10,... | collective-permute-start | bytes 12296 | tf_op jit(solution)/shard_map/ppermute | solution.py:32
  102.9 3.6 %collective-permute-start.26 = (f32[1024]{0:T(1024)S(1)}, f32[1024]{0:T(1024)S(1)}, u32[]{:S(2)}, u32[]{:S(2)}) collective-permute-start(f32[1024]{0:T(1024)S(1)} %add_add_fusion), channel_id=1, source_target_pairs={{0,24},{1,25},{2,26},{3,27},{4,28},{5,29},{6,30},{7,31},{8,0},{9,1... | collective-permute-start | bytes 12296 | tf_op jit(solution)/shard_map/ppermute | solution.py:32
  104.6 5.1 %collective-permute-start.25 = (f32[1024]{0:T(1024)S(1)}, f32[1024]{0:T(1024)S(1)}, u32[]{:S(2)}, u32[]{:S(2)}) collective-permute-start(f32[1024]{0:T(1024)S(1)} %add_add_fusion), channel_id=1, source_target_pairs={{0,16},{1,17},{2,18},{3,19},{4,20},{5,21},{6,22},{7,23},{8,24},{9,... | collective-permute-start | bytes 12296 | tf_op jit(solution)/shard_map/ppermute | solution.py:32
  105.5 4.8 %collective-permute-start.24 = (f32[1024]{0:T(1024)S(1)}, f32[1024]{0:T(1024)S(1)}, u32[]{:S(2)}, u32[]{:S(2)}) collective-permute-start(f32[1024]{0:T(1024)S(1)} %add_add_fusion), channel_id=1, source_target_pairs={{0,8},{1,9},{2,10},{3,11},{4,12},{5,13},{6,14},{7,15},{8,16},{9,17... | collective-permute-start | bytes 12296 | tf_op jit(solution)/shard_map/ppermute | solution.py:32
  128.3 3.7 %collective-permute-start.27 = (f32[1024]{0:T(1024)S(1)}, f32[1024]{0:T(1024)S(1)}, u32[]{:S(2)}, u32[]{:S(2)}) collective-permute-start(f32[1024]{0:T(1024)S(1)} %multiply_reduce_fusion.1), channel_id=1, source_target_pairs={{0,32},{32,0},{64,96},{96,64},{128,160},{160,128},{192,224},{224,1... | collective-permute-start | bytes 12296 | tf_op jit(solution)/shard_map/ppermute | solution.py:42
  129.5 4.0 %collective-permute-start.30 = (f32[1024]{0:T(1024)S(1)}, f32[1024]{0:T(1024)S(1)}, u32[]{:S(2)}, u32[]{:S(2)}) collective-permute-start(f32[1024]{0:T(1024)S(1)} %reduce_sum.119), channel_id=1, source_target_pairs={{0,32},{32,0},{64,96},{96,64},{128,160},{160,128},{192,224},{224,1... | collective-permute-start | bytes 12296 | tf_op jit(solution)/shard_map/ppermute | solution.py:42
  132.0 4.5 %collective-permute-start.28 = (f32[1024]{0:T(1024)S(1)}, f32[1024]{0:T(1024)S(1)}, u32[]{:S(2)}, u32[]{:S(2)}) collective-permute-start(f32[1024]{0:T(1024)S(1)} %add.192), channel_id=1, source_target_pairs={{0,64},{32,96},{64,0},{96,32},{128,192},{160,224},{192,128},{224,1... | collective-permute-start | bytes 12296 | tf_op jit(solution)/shard_map/ppermute | solution.py:42
  133.5 4.5 %collective-permute-start.31 = (f32[1024]{0:T(1024)S(1)}, f32[1024]{0:T(1024)S(1)}, u32[]{:S(2)}, u32[]{:S(2)}) collective-permute-start(f32[1024]{0:T(1024)S(1)} %add.195), channel_id=1, source_target_pairs={{0,64},{32,96},{64,0},{96,32},{128,192},{160,224},{192,128},{224,1... | collective-permute-start | bytes 12296 | tf_op jit(solution)/shard_map/ppermute | solution.py:42
  136.5 7.5 %collective-permute-start.29 = (f32[1024]{0:T(1024)S(1)}, f32[1024]{0:T(1024)S(1)}, u32[]{:S(2)}, u32[]{:S(2)}) collective-permute-start(f32[1024]{0:T(1024)S(1)} %add.193), channel_id=1, source_target_pairs={{0,128},{32,160},{64,192},{96,224},{128,0},{160,32},{192,64},{224,... | collective-permute-start | bytes 12296 | tf_op jit(solution)/shard_map/ppermute | solution.py:42
  138.0 10.1 %collective-permute-start.32 = (f32[1024]{0:T(1024)S(1)}, f32[1024]{0:T(1024)S(1)}, u32[]{:S(2)}, u32[]{:S(2)}) collective-permute-start(f32[1024]{0:T(1024)S(1)} %add.196), channel_id=1, source_target_pairs={{0,128},{32,160},{64,192},{96,224},{128,0},{160,32},{192,64},{224,... | collective-permute-start | bytes 12296 | tf_op jit(solution)/shard_map/ppermute | solution.py:42
  (6 other events, 107.5 us)
Sparse Core Ops, SparseCore 0:
  11.1 82.7 all-gather.1

commit v12 on v10

--- a/solution.py
+++ b/solution.py
@@ -105,6 +105,7 @@
         if step + 1 < ITERS:
             row_scale = 1.0 / cent_sum(row_part)
 
+    row_part, denom_part = lax.optimization_barrier((row_part, denom_part))
     row_total = cent_sum(row_part)
     denominator = cent_sum(denom_part)
     row_scale = 1.0 / row_total

time: 164 us -> 161 us (0.982)
  starting transfers between devices: 62 us -> 51 us
  waiting for transfers between devices: 36 us -> 41.9 us
  other arithmetic: 15.6 us -> 17.8 us
    ppermute x21, waiting for transfers between devices: 18.6 us -> 28.4 us  [dp_sum(): lax.ppermute(values, 'dp', shift_pairs(count, stride, size, step))]
    ppermute x21, starting transfers between devices: 28.5 us -> 20.6 us  [dp_sum(): lax.ppermute(values, 'dp', shift_pairs(count, stride, size, step))]
    ppermute x12, waiting for transfers between devices: 17.4 us -> 13.5 us  [cent_sum(): lax.ppermute(values, 'cent', [(i, i ^ bit) for i in range(count)])]
    ppermute x12, starting transfers between devices: 33.5 us -> 30.3 us  [cent_sum(): lax.ppermute(values, 'cent', [(i, i ^ bit) for i in range(count)])]
    reduce_sum x3, other arithmetic: 1.06 us -> 3.25 us  [shards(): row_part = jnp.sum(expo * col_scale[None, :], axis=1)]
  transfers between devices with their start and end apart: 34 -> 34, of which waited for: 27 -> 26; matrix products, arithmetic and copies ran while one was open for 29% -> 19% of each run, Pallas kernels for 0% -> 0%
where the time goes in v12:
time: 161 us; the launch traced here: 160 us
  starting transfers between devices  51 us (32%)
  waiting for transfers between devices  41.9 us (26%)
  matrix products  26.3 us (16%)
  other arithmetic  17.8 us (11%)
  between operations  14.3 us (9%)
  local copies, waits for them, and re-layouts  9.22 us (6%)
    ppermute x12, starting transfers between devices, cent_sum(): lax.ppermute(values, 'cent', [(i, i ^ bit) for i in range(count)])  30.3 us
    ppermute x21, waiting for transfers between devices, dp_sum(): lax.ppermute(values, 'dp', shift_pairs(count, stride, size, step))  28.4 us
    ppermute x21, starting transfers between devices, dp_sum(): lax.ppermute(values, 'dp', shift_pairs(count, stride, size, step))  20.6 us
    ppermute x12, waiting for transfers between devices, cent_sum(): lax.ppermute(values, 'cent', [(i, i ^ bit) for i in range(count)])  13.5 us
    dot_general x1, matrix products, shards(): jnp.dot(pick, points, preferred_element_type=jnp.float32)  11.6 us
    dot_general x1, matrix products, shards(): jnp.einsum('gcd,gkd->gck', buffer, gathered, preferred_element_type=jnp.f...  11.4 us
    gather x1, local copies, waits for them, and re-layouts, shards(): denom_part = jnp.sum(slot_weights, axis=1)[slot]  6.15 us
    reduce_sum x3, other arithmetic, inverse_norm(): return lax.rsqrt(jnp.mean(values * values, axis=-1) + EPS)  5.65 us
  transfers between devices with their start and end apart: 34, of which 26 were waited for; matrix products, arithmetic and copies ran while one was open for 19% of the time, Pallas kernels for 0%

profile of v12, /device:TPU:32, one launch (start us, length us, event | category | flops | bytes accessed | tf_op | source)
XLA Modules:
  0.0 160.5 jit_solution(4654029797482089004)
XLA Ops:
  8.7 2.0 %maximum_maximum_fusion = bf16[2,136,1024]{2,1,0:T(8,128)(2,1)} fusion(bf16[2,1,1024]{2,1,0:T(2,128)(2,1)S(1)} %copy.7, bf16[2,128,1024]{2,1,0:T(8,128)(2,1)} %param.7, bf16[136]{0:T(256)(128)(2,1)S(1)} %pad.2.clone), kind=kLoop, calls=%fused_computation.24 | loop fusion | flops 1671168 | bytes 1085712 | tf_op jit(solution)/shard_map/concatenate | solution.py:70
  10.8 2.2 %multiply_reduce_fusion.6 = f32[1024]{0:T(1024)S(1)} fusion(bf16[1024,1024]{1,0:T(8,128)(2,1)} %param.6), kind=kLoop, calls=%fused_computation.17 | loop fusion | flops 3144704 | bytes 2101248 | tf_op jit(solution)/shard_map/reduce_sum | solution.py:16
  13.0 2.1 %multiply_reduce_fusion.7 = f32[1024]{0:T(1024)S(1)} fusion(bf16[1024,1024]{1,0:T(8,128)(2,1)} %param.4), kind=kLoop, calls=%fused_computation.18 | loop fusion | flops 3144704 | bytes 2101248 | tf_op jit(solution)/shard_map/reduce_sum | solution.py:16
  15.1 2.7 %fusion.14 = (f32[1024]{0:T(1024)S(1)}, f32[1024,1024]{1,0:T(8,128)S(1)}) fusion(f32[1024]{0:T(1024)S(1)} %get-tuple-element.15, f32[1024]{0:T(1024)S(1)} %get-tuple-element.16, bf16[1024,1024]{1,0:T(8,128)(2,1)S(1)} %copy-done.2, bf16[1024,1024]{1,0:T(8,128)(2,1)S(1)} %copy-done.1), kind=kOutput, calls=%fused_computation.55 | convolution fusion | flops 2151676928 | bytes 8400896 | tf_op jit(solution)/shard_map/pd,kd->pk/dot_general | solution.py:95
  19.1 3.0 %collective-permute-start.3 = (f32[1024]{0:T(1024)S(1)}, f32[1024]{0:T(1024)S(1)}, u32[]{:S(2)}, u32[]{:S(2)}) collective-permute-start(f32[1024]{0:T(1024)S(1)} %add.153), channel_id=1, source_target_pairs={{0,6},{1,7},{2,0},{3,1},{4,2},{5,3},{6,4},{7,5},{8,14},{9,15},{10,... | collective-permute-start | bytes 12296 | tf_op jit(solution)/shard_map/ppermute | solution.py:32
  23.7 3.5 %collective-permute-done.2 = f32[1024]{0:T(1024)S(1)} collective-permute-done((f32[1024]{0:T(1024)S(1)}, f32[1024]{0:T(1024)S(1)}, u32[]{:S(2)}, u32[]{:S(2)}) %collective-permute-start.2) | collective-permute-done | bytes 4128 | tf_op jit(solution)/shard_map/ppermute | solution.py:32
  27.5 2.7 %collective-permute-start.6 = (f32[1024]{0:T(1024)S(1)}, f32[1024]{0:T(1024)S(1)}, u32[]{:S(2)}, u32[]{:S(2)}) collective-permute-start(f32[1024]{0:T(1024)S(1)} %add_add_fusion.2), channel_id=1, source_target_pairs={{0,24},{1,25},{2,26},{3,27},{4,28},{5,29},{6,30},{7,31},{8,0},{9,1... | collective-permute-start | bytes 12296 | tf_op jit(solution)/shard_map/ppermute | solution.py:32
  32.0 3.4 %collective-permute-done.5 = f32[1024]{0:T(1024)S(1)} collective-permute-done((f32[1024]{0:T(1024)S(1)}, f32[1024]{0:T(1024)S(1)}, u32[]{:S(2)}, u32[]{:S(2)}) %collective-permute-start.5) | collective-permute-done | bytes 4128 | tf_op jit(solution)/shard_map/ppermute | solution.py:32
  36.4 3.5 %collective-permute-done.7 = f32[1024]{0:T(1024)S(1)} collective-permute-done((f32[1024]{0:T(1024)S(1)}, f32[1024]{0:T(1024)S(1)}, u32[]{:S(2)}, u32[]{:S(2)}) %collective-permute-start.7) | collective-permute-done | bytes 4128 | tf_op jit(solution)/shard_map/ppermute | solution.py:42
  40.0 3.3 %collective-permute-start.8 = (f32[1024]{0:T(1024)S(1)}, f32[1024]{0:T(1024)S(1)}, u32[]{:S(2)}, u32[]{:S(2)}) collective-permute-start(f32[1024]{0:T(1024)S(1)} %add.160), channel_id=1, source_target_pairs={{0,64},{32,96},{64,0},{96,32},{128,192},{160,224},{192,128},{224,1... | collective-permute-start | bytes 12296 | tf_op jit(solution)/shard_map/ppermute | solution.py:42
  43.2 1.6 collective-permute-done.8
  44.8 5.9 %collective-permute-start.9 = (f32[1024]{0:T(1024)S(1)}, f32[1024]{0:T(1024)S(1)}, u32[]{:S(2)}, u32[]{:S(2)}) collective-permute-start(f32[1024]{0:T(1024)S(1)} %add.161), channel_id=1, source_target_pairs={{0,128},{32,160},{64,192},{96,224},{128,0},{160,32},{192,64},{224,... | collective-permute-start | bytes 12296 | tf_op jit(solution)/shard_map/ppermute | solution.py:42
  50.8 1.6 collective-permute-done.9
  57.8 2.0 %collective-permute-done.12 = f32[1024]{0:T(1024)S(1)} collective-permute-done((f32[1024]{0:T(1024)S(1)}, f32[1024]{0:T(1024)S(1)}, u32[]{:S(2)}, u32[]{:S(2)}) %collective-permute-start.12) | collective-permute-done | bytes 4128 | tf_op jit(solution)/shard_map/ppermute | solution.py:32
  64.7 1.9 %collective-permute-done.15 = f32[1024]{0:T(1024)S(1)} collective-permute-done((f32[1024]{0:T(1024)S(1)}, f32[1024]{0:T(1024)S(1)}, u32[]{:S(2)}, u32[]{:S(2)}) %collective-permute-start.15) | collective-permute-done | bytes 4128 | tf_op jit(solution)/shard_map/ppermute | solution.py:32
  69.7 2.0 %collective-permute-done.17 = f32[1024]{0:T(1024)S(1)} collective-permute-done((f32[1024]{0:T(1024)S(1)}, f32[1024]{0:T(1024)S(1)}, u32[]{:S(2)}, u32[]{:S(2)}) %collective-permute-start.17) | collective-permute-done | bytes 4128 | tf_op jit(solution)/shard_map/ppermute | solution.py:42
  71.7 2.9 %collective-permute-start.18 = (f32[1024]{0:T(1024)S(1)}, f32[1024]{0:T(1024)S(1)}, u32[]{:S(2)}, u32[]{:S(2)}) collective-permute-start(f32[1024]{0:T(1024)S(1)} %add.170), channel_id=1, source_target_pairs={{0,64},{32,96},{64,0},{96,32},{128,192},{160,224},{192,128},{224,1... | collective-permute-start | bytes 12296 | tf_op jit(solution)/shard_map/ppermute | solution.py:42
  74.6 1.6 collective-permute-done.18
  76.2 5.9 %collective-permute-start.19 = (f32[1024]{0:T(1024)S(1)}, f32[1024]{0:T(1024)S(1)}, u32[]{:S(2)}, u32[]{:S(2)}) collective-permute-start(f32[1024]{0:T(1024)S(1)} %add.171), channel_id=1, source_target_pairs={{0,128},{32,160},{64,192},{96,224},{128,0},{160,32},{192,64},{224,... | collective-permute-start | bytes 12296 | tf_op jit(solution)/shard_map/ppermute | solution.py:42
  82.1 11.6 %multiply_reduce_fusion = (f32[4096]{0:T(1024)S(1)}, bf16[4096,1024]{1,0:T(8,128)(2,1)}) fusion(bf16[1024,1024]{1,0:T(8,128)(2,1)S(1)} %copy-done.2, s32[1024]{0:T(1024)S(1)} %multiply_add_fusion), kind=kOutput, calls=%fused_computation.4 | convolution fusion | flops 8610902016 | bytes 10506240 | tf_op jit(solution)/shard_map/dot_general | solution.py:85
  95.4 1.7 %collective-permute-start.23 = (f32[1024]{0:T(1024)S(1)}, f32[1024]{0:T(1024)S(1)}, u32[]{:S(2)}, u32[]{:S(2)}) collective-permute-start(f32[1024]{0:T(1024)S(1)} %add.173), channel_id=1, source_target_pairs={{0,6},{1,7},{2,0},{3,1},{4,2},{5,3},{6,4},{7,5},{8,14},{9,15},{10,... | collective-permute-start | bytes 12296 | tf_op jit(solution)/shard_map/ppermute | solution.py:32
  99.0 3.2 %collective-permute-done.22 = f32[1024]{0:T(1024)S(1)} collective-permute-done((f32[1024]{0:T(1024)S(1)}, f32[1024]{0:T(1024)S(1)}, u32[]{:S(2)}, u32[]{:S(2)}) %collective-permute-start.22) | collective-permute-done | bytes 4128 | tf_op jit(solution)/shard_map/ppermute | solution.py:32
  102.9 1.7 %collective-permute-start.26 = (f32[1024]{0:T(1024)S(1)}, f32[1024]{0:T(1024)S(1)}, u32[]{:S(2)}, u32[]{:S(2)}) collective-permute-start(f32[1024]{0:T(1024)S(1)} %add_add_fusion), channel_id=1, source_target_pairs={{0,24},{1,25},{2,26},{3,27},{4,28},{5,29},{6,30},{7,31},{8,0},{9,1... | collective-permute-start | bytes 12296 | tf_op jit(solution)/shard_map/ppermute | solution.py:32
  106.5 3.2 %collective-permute-done.25 = f32[1024]{0:T(1024)S(1)} collective-permute-done((f32[1024]{0:T(1024)S(1)}, f32[1024]{0:T(1024)S(1)}, u32[]{:S(2)}, u32[]{:S(2)}) %collective-permute-start.25) | collective-permute-done | bytes 4128 | tf_op jit(solution)/shard_map/ppermute | solution.py:32
  110.3 2.5 %multiply_reduce_fusion.1 = f32[1024]{0:T(1024)S(1)} fusion(f32[1024,1024]{1,0:T(8,128)} %copy-done, f32[1024]{0:T(1024)S(1)} %add_divide_fusion.1), kind=kLoop, calls=%fused_computation.11 | loop fusion | flops 2096128 | bytes 4202496 | tf_op jit(solution)/shard_map/reduce_sum | solution.py:104
  114.0 11.4 %fusion.15 = (f32[64,64]{1,0:T(8,128)S(1)}, f32[64,64,128]{2,1,0:T(8,128)S(1)}) fusion(f32[64,128]{1,0:T(8,128)S(1)} %slice_add_fusion, f32[64,64]{1,0:T(8,128)S(1)} %rsqrt.31, bf16[64,64,1024]{2,1,0:T(8,128)(2,1)} %bitcast.27, bf16[64,136,1024]{2,1,0:T(8,128)(2,1)} %all-gather.2.cloned.1.call-done), kind=kOutput, calls=%fused_computation.56 | convolution fusion | flops 1075834880 | bytes 27328512 | tf_op jit(solution)/shard_map/gcd,gkd->gck/dot_general | solution.py:88
  125.5 6.1 %gather_fusion = f32[1024]{0:T(1024)S(1)} fusion(f32[4096]{0:T(1024)S(1)} %reduce_sum.122, s32[1024]{0:T(1024)S(1)} %broadcast_clamp_fusion), kind=kCustom, calls=%fused_computation | custom fusion | bytes 12288 | tf_op jit(solution)/shard_map/gather | solution.py:91
  133.7 1.6 collective-permute-done.27
  138.2 1.6 collective-permute-done.28
  139.8 2.8 %gather_fusion.1 = f32[1024,128]{1,0:T(8,128)S(1)} fusion(f32[4096,128]{1,0:T(8,128)S(1)} %bitcast.21, s32[1024]{0:T(1024)S(1)} %broadcast_clamp_fusion), kind=kCustom, calls=%fused_computation.1 | custom fusion | bytes 1052672 | tf_op jit(solution)/shard_map/gather | solution.py:92
  142.7 6.0 %collective-permute-start.32 = (f32[1024]{0:T(1024)S(1)}, f32[1024]{0:T(1024)S(1)}, u32[]{:S(2)}, u32[]{:S(2)}) collective-permute-start(f32[1024]{0:T(1024)S(1)} %add.193), channel_id=1, source_target_pairs={{0,128},{32,160},{64,192},{96,224},{128,0},{160,32},{192,64},{224,... | collective-permute-start | bytes 12296 | tf_op jit(solution)/shard_map/ppermute | solution.py:42
  148.7 4.1 %multiply_convert_fusion = bf16[1024,1024]{1,0:T(8,128)(2,1)} fusion(f32[1024,1024]{1,0:T(8,128)} %copy-done, f32[1024]{0:T(1024)S(1)} %add_divide_fusion, f32[1024]{0:T(1024)S(1)} %add_divide_fusion.1), kind=kLoop, calls=%fused_computation.10 | loop fusion | flops 4194304 | bytes 6299648 | tf_op jit(solution)/shard_map/convert_element_type | solution.py:112
  (101 shorter events, 34.8 us)
Async XLA Ops:
  7.2 105.7 %all-gather.2.cloned.1.call-start = ((), (), s32[]{:S(2)}) async-start(), calls=%async_computation | async-start | bytes 18382848 | tf_op jit(solution)/shard_map/all_gather | solution.py:71
  19.1 4.6 %collective-permute-start.3 = (f32[1024]{0:T(1024)S(1)}, f32[1024]{0:T(1024)S(1)}, u32[]{:S(2)}, u32[]{:S(2)}) collective-permute-start(f32[1024]{0:T(1024)S(1)} %add.153), channel_id=1, source_target_pairs={{0,6},{1,7},{2,0},{3,1},{4,2},{5,3},{6,4},{7,5},{8,14},{9,15},{10,... | collective-permute-start | bytes 12296 | tf_op jit(solution)/shard_map/ppermute | solution.py:32
  22.1 5.1 %collective-permute-start.2 = (f32[1024]{0:T(1024)S(1)}, f32[1024]{0:T(1024)S(1)}, u32[]{:S(2)}, u32[]{:S(2)}) collective-permute-start(f32[1024]{0:T(1024)S(1)} %add.153), channel_id=1, source_target_pairs={{0,4},{1,5},{2,6},{3,7},{4,0},{5,1},{6,2},{7,3},{8,12},{9,13},{10,... | collective-permute-start | bytes 12296 | tf_op jit(solution)/shard_map/ppermute | solution.py:32
  22.7 4.8 %collective-permute-start.1 = (f32[1024]{0:T(1024)S(1)}, f32[1024]{0:T(1024)S(1)}, u32[]{:S(2)}, u32[]{:S(2)}) collective-permute-start(f32[1024]{0:T(1024)S(1)} %add.153), channel_id=1, source_target_pairs={{0,2},{1,3},{2,4},{3,5},{4,6},{5,7},{6,0},{7,1},{8,10},{9,11},{10,... | collective-permute-start | bytes 12296 | tf_op jit(solution)/shard_map/ppermute | solution.py:32
  27.5 4.4 %collective-permute-start.6 = (f32[1024]{0:T(1024)S(1)}, f32[1024]{0:T(1024)S(1)}, u32[]{:S(2)}, u32[]{:S(2)}) collective-permute-start(f32[1024]{0:T(1024)S(1)} %add_add_fusion.2), channel_id=1, source_target_pairs={{0,24},{1,25},{2,26},{3,27},{4,28},{5,29},{6,30},{7,31},{8,0},{9,1... | collective-permute-start | bytes 12296 | tf_op jit(solution)/shard_map/ppermute | solution.py:32
  30.3 5.1 %collective-permute-start.5 = (f32[1024]{0:T(1024)S(1)}, f32[1024]{0:T(1024)S(1)}, u32[]{:S(2)}, u32[]{:S(2)}) collective-permute-start(f32[1024]{0:T(1024)S(1)} %add_add_fusion.2), channel_id=1, source_target_pairs={{0,16},{1,17},{2,18},{3,19},{4,20},{5,21},{6,22},{7,23},{8,24},{9,... | collective-permute-start | bytes 12296 | tf_op jit(solution)/shard_map/ppermute | solution.py:32
  31.1 4.8 %collective-permute-start.4 = (f32[1024]{0:T(1024)S(1)}, f32[1024]{0:T(1024)S(1)}, u32[]{:S(2)}, u32[]{:S(2)}) collective-permute-start(f32[1024]{0:T(1024)S(1)} %add_add_fusion.2), channel_id=1, source_target_pairs={{0,8},{1,9},{2,10},{3,11},{4,12},{5,13},{6,14},{7,15},{8,16},{9,17... | collective-permute-start | bytes 12296 | tf_op jit(solution)/shard_map/ppermute | solution.py:32
  36.3 3.7 %collective-permute-start.7 = (f32[1024]{0:T(1024)S(1)}, f32[1024]{0:T(1024)S(1)}, u32[]{:S(2)}, u32[]{:S(2)}) collective-permute-start(f32[1024]{0:T(1024)S(1)} %multiply_reduce_fusion.5), channel_id=1, source_target_pairs={{0,32},{32,0},{64,96},{96,64},{128,160},{160,128},{192,224},{224,1... | collective-permute-start | bytes 12296 | tf_op jit(solution)/shard_map/ppermute | solution.py:42
  40.0 4.8 %collective-permute-start.8 = (f32[1024]{0:T(1024)S(1)}, f32[1024]{0:T(1024)S(1)}, u32[]{:S(2)}, u32[]{:S(2)}) collective-permute-start(f32[1024]{0:T(1024)S(1)} %add.160), channel_id=1, source_target_pairs={{0,64},{32,96},{64,0},{96,32},{128,192},{160,224},{192,128},{224,1... | collective-permute-start | bytes 12296 | tf_op jit(solution)/shard_map/ppermute | solution.py:42
  44.8 7.5 %collective-permute-start.9 = (f32[1024]{0:T(1024)S(1)}, f32[1024]{0:T(1024)S(1)}, u32[]{:S(2)}, u32[]{:S(2)}) collective-permute-start(f32[1024]{0:T(1024)S(1)} %add.161), channel_id=1, source_target_pairs={{0,128},{32,160},{64,192},{96,224},{128,0},{160,32},{192,64},{224,... | collective-permute-start | bytes 12296 | tf_op jit(solution)/shard_map/ppermute | solution.py:42
  52.7 1.3 collective-permute-start.10
  54.0 3.8 %collective-permute-start.13 = (f32[1024]{0:T(1024)S(1)}, f32[1024]{0:T(1024)S(1)}, u32[]{:S(2)}, u32[]{:S(2)}) collective-permute-start(f32[1024]{0:T(1024)S(1)} %add.163), channel_id=1, source_target_pairs={{0,6},{1,7},{2,0},{3,1},{4,2},{5,3},{6,4},{7,5},{8,14},{9,15},{10,... | collective-permute-start | bytes 12296 | tf_op jit(solution)/shard_map/ppermute | solution.py:32
  54.5 5.3 %collective-permute-start.12 = (f32[1024]{0:T(1024)S(1)}, f32[1024]{0:T(1024)S(1)}, u32[]{:S(2)}, u32[]{:S(2)}) collective-permute-start(f32[1024]{0:T(1024)S(1)} %add.163), channel_id=1, source_target_pairs={{0,4},{1,5},{2,6},{3,7},{4,0},{5,1},{6,2},{7,3},{8,12},{9,13},{10,... | collective-permute-start | bytes 12296 | tf_op jit(solution)/shard_map/ppermute | solution.py:32
  55.8 5.0 %collective-permute-start.11 = (f32[1024]{0:T(1024)S(1)}, f32[1024]{0:T(1024)S(1)}, u32[]{:S(2)}, u32[]{:S(2)}) collective-permute-start(f32[1024]{0:T(1024)S(1)} %add.163), channel_id=1, source_target_pairs={{0,2},{1,3},{2,4},{3,5},{4,6},{5,7},{6,0},{7,1},{8,10},{9,11},{10,... | collective-permute-start | bytes 12296 | tf_op jit(solution)/shard_map/ppermute | solution.py:32
  60.9 3.8 %collective-permute-start.16 = (f32[1024]{0:T(1024)S(1)}, f32[1024]{0:T(1024)S(1)}, u32[]{:S(2)}, u32[]{:S(2)}) collective-permute-start(f32[1024]{0:T(1024)S(1)} %add_add_fusion.1), channel_id=1, source_target_pairs={{0,24},{1,25},{2,26},{3,27},{4,28},{5,29},{6,30},{7,31},{8,0},{9,1... | collective-permute-start | bytes 12296 | tf_op jit(solution)/shard_map/ppermute | solution.py:32
  61.3 5.3 %collective-permute-start.15 = (f32[1024]{0:T(1024)S(1)}, f32[1024]{0:T(1024)S(1)}, u32[]{:S(2)}, u32[]{:S(2)}) collective-permute-start(f32[1024]{0:T(1024)S(1)} %add_add_fusion.1), channel_id=1, source_target_pairs={{0,16},{1,17},{2,18},{3,19},{4,20},{5,21},{6,22},{7,23},{8,24},{9,... | collective-permute-start | bytes 12296 | tf_op jit(solution)/shard_map/ppermute | solution.py:32
  62.6 5.0 %collective-permute-start.14 = (f32[1024]{0:T(1024)S(1)}, f32[1024]{0:T(1024)S(1)}, u32[]{:S(2)}, u32[]{:S(2)}) collective-permute-start(f32[1024]{0:T(1024)S(1)} %add_add_fusion.1), channel_id=1, source_target_pairs={{0,8},{1,9},{2,10},{3,11},{4,12},{5,13},{6,14},{7,15},{8,16},{9,17... | collective-permute-start | bytes 12296 | tf_op jit(solution)/shard_map/ppermute | solution.py:32
  68.0 3.7 %collective-permute-start.17 = (f32[1024]{0:T(1024)S(1)}, f32[1024]{0:T(1024)S(1)}, u32[]{:S(2)}, u32[]{:S(2)}) collective-permute-start(f32[1024]{0:T(1024)S(1)} %multiply_reduce_fusion.3), channel_id=1, source_target_pairs={{0,32},{32,0},{64,96},{96,64},{128,160},{160,128},{192,224},{224,1... | collective-permute-start | bytes 12296 | tf_op jit(solution)/shard_map/ppermute | solution.py:42
  71.7 4.5 %collective-permute-start.18 = (f32[1024]{0:T(1024)S(1)}, f32[1024]{0:T(1024)S(1)}, u32[]{:S(2)}, u32[]{:S(2)}) collective-permute-start(f32[1024]{0:T(1024)S(1)} %add.170), channel_id=1, source_target_pairs={{0,64},{32,96},{64,0},{96,32},{128,192},{160,224},{192,128},{224,1... | collective-permute-start | bytes 12296 | tf_op jit(solution)/shard_map/ppermute | solution.py:42
  76.2 17.6 %collective-permute-start.19 = (f32[1024]{0:T(1024)S(1)}, f32[1024]{0:T(1024)S(1)}, u32[]{:S(2)}, u32[]{:S(2)}) collective-permute-start(f32[1024]{0:T(1024)S(1)} %add.171), channel_id=1, source_target_pairs={{0,128},{32,160},{64,192},{96,224},{128,0},{160,32},{192,64},{224,... | collective-permute-start | bytes 12296 | tf_op jit(solution)/shard_map/ppermute | solution.py:42
  95.4 3.6 %collective-permute-start.23 = (f32[1024]{0:T(1024)S(1)}, f32[1024]{0:T(1024)S(1)}, u32[]{:S(2)}, u32[]{:S(2)}) collective-permute-start(f32[1024]{0:T(1024)S(1)} %add.173), channel_id=1, source_target_pairs={{0,6},{1,7},{2,0},{3,1},{4,2},{5,3},{6,4},{7,5},{8,14},{9,15},{10,... | collective-permute-start | bytes 12296 | tf_op jit(solution)/shard_map/ppermute | solution.py:32
  97.1 5.1 %collective-permute-start.22 = (f32[1024]{0:T(1024)S(1)}, f32[1024]{0:T(1024)S(1)}, u32[]{:S(2)}, u32[]{:S(2)}) collective-permute-start(f32[1024]{0:T(1024)S(1)} %add.173), channel_id=1, source_target_pairs={{0,4},{1,5},{2,6},{3,7},{4,0},{5,1},{6,2},{7,3},{8,12},{9,13},{10,... | collective-permute-start | bytes 12296 | tf_op jit(solution)/shard_map/ppermute | solution.py:32
  98.0 4.8 %collective-permute-start.21 = (f32[1024]{0:T(1024)S(1)}, f32[1024]{0:T(1024)S(1)}, u32[]{:S(2)}, u32[]{:S(2)}) collective-permute-start(f32[1024]{0:T(1024)S(1)} %add.173), channel_id=1, source_target_pairs={{0,2},{1,3},{2,4},{3,5},{4,6},{5,7},{6,0},{7,1},{8,10},{9,11},{10,... | collective-permute-start | bytes 12296 | tf_op jit(solution)/shard_map/ppermute | solution.py:32
  102.9 3.6 %collective-permute-start.26 = (f32[1024]{0:T(1024)S(1)}, f32[1024]{0:T(1024)S(1)}, u32[]{:S(2)}, u32[]{:S(2)}) collective-permute-start(f32[1024]{0:T(1024)S(1)} %add_add_fusion), channel_id=1, source_target_pairs={{0,24},{1,25},{2,26},{3,27},{4,28},{5,29},{6,30},{7,31},{8,0},{9,1... | collective-permute-start | bytes 12296 | tf_op jit(solution)/shard_map/ppermute | solution.py:32
  104.6 5.1 %collective-permute-start.25 = (f32[1024]{0:T(1024)S(1)}, f32[1024]{0:T(1024)S(1)}, u32[]{:S(2)}, u32[]{:S(2)}) collective-permute-start(f32[1024]{0:T(1024)S(1)} %add_add_fusion), channel_id=1, source_target_pairs={{0,16},{1,17},{2,18},{3,19},{4,20},{5,21},{6,22},{7,23},{8,24},{9,... | collective-permute-start | bytes 12296 | tf_op jit(solution)/shard_map/ppermute | solution.py:32
  105.5 4.8 %collective-permute-start.24 = (f32[1024]{0:T(1024)S(1)}, f32[1024]{0:T(1024)S(1)}, u32[]{:S(2)}, u32[]{:S(2)}) collective-permute-start(f32[1024]{0:T(1024)S(1)} %add_add_fusion), channel_id=1, source_target_pairs={{0,8},{1,9},{2,10},{3,11},{4,12},{5,13},{6,14},{7,15},{8,16},{9,17... | collective-permute-start | bytes 12296 | tf_op jit(solution)/shard_map/ppermute | solution.py:32
  131.6 3.7 %collective-permute-start.27 = (f32[1024]{0:T(1024)S(1)}, f32[1024]{0:T(1024)S(1)}, u32[]{:S(2)}, u32[]{:S(2)}) collective-permute-start(f32[1024]{0:T(1024)S(1)} %multiply_reduce_fusion.1), channel_id=1, source_target_pairs={{0,32},{32,0},{64,96},{96,64},{128,160},{160,128},{192,224},{224,1... | collective-permute-start | bytes 12296 | tf_op jit(solution)/shard_map/ppermute | solution.py:42
  132.8 4.0 %collective-permute-start.30 = (f32[1024]{0:T(1024)S(1)}, f32[1024]{0:T(1024)S(1)}, u32[]{:S(2)}, u32[]{:S(2)}) collective-permute-start(f32[1024]{0:T(1024)S(1)} %gather_fusion), channel_id=1, source_target_pairs={{0,32},{32,0},{64,96},{96,64},{128,160},{160,128},{192,224},{224,1... | collective-permute-start | bytes 12296 | tf_op jit(solution)/shard_map/ppermute | solution.py:42
  135.3 4.5 %collective-permute-start.28 = (f32[1024]{0:T(1024)S(1)}, f32[1024]{0:T(1024)S(1)}, u32[]{:S(2)}, u32[]{:S(2)}) collective-permute-start(f32[1024]{0:T(1024)S(1)} %add.189), channel_id=1, source_target_pairs={{0,64},{32,96},{64,0},{96,32},{128,192},{160,224},{192,128},{224,1... | collective-permute-start | bytes 12296 | tf_op jit(solution)/shard_map/ppermute | solution.py:42
  136.8 5.8 %collective-permute-start.31 = (f32[1024]{0:T(1024)S(1)}, f32[1024]{0:T(1024)S(1)}, u32[]{:S(2)}, u32[]{:S(2)}) collective-permute-start(f32[1024]{0:T(1024)S(1)} %add.192), channel_id=1, source_target_pairs={{0,64},{32,96},{64,0},{96,32},{128,192},{160,224},{192,128},{224,1... | collective-permute-start | bytes 12296 | tf_op jit(solution)/shard_map/ppermute | solution.py:42
  139.8 8.9 %collective-permute-start.29 = (f32[1024]{0:T(1024)S(1)}, f32[1024]{0:T(1024)S(1)}, u32[]{:S(2)}, u32[]{:S(2)}) collective-permute-start(f32[1024]{0:T(1024)S(1)} %add.190), channel_id=1, source_target_pairs={{0,128},{32,160},{64,192},{96,224},{128,0},{160,32},{192,64},{224,... | collective-permute-start | bytes 12296 | tf_op jit(solution)/shard_map/ppermute | solution.py:42
  142.7 10.1 %collective-permute-start.32 = (f32[1024]{0:T(1024)S(1)}, f32[1024]{0:T(1024)S(1)}, u32[]{:S(2)}, u32[]{:S(2)}) collective-permute-start(f32[1024]{0:T(1024)S(1)} %add.193), channel_id=1, source_target_pairs={{0,128},{32,160},{64,192},{96,224},{128,0},{160,32},{192,64},{224,... | collective-permute-start | bytes 12296 | tf_op jit(solution)/shard_map/ppermute | solution.py:42
  (6 other events, 107.5 us)
Sparse Core Ops, SparseCore 0:
  11.1 82.7 all-gather.1
